TPU v7x, 32 devices: a whole 2x2x4 slice. The times are simulated.
32 devices in a mesh: seq: 8 (over y, x, core), head: 4 (over z).
Axes of the slice: x: 2, y: 2, z: 4, core: 2. Of those that a mesh axis runs over, the one named last changes fastest.
Arguments:
- tokens: bfloat16 [4096, 5376], P('seq', 'head'), may hold values from -32 to 32
- query_weight: bfloat16 [5376, 4096], P(None, 'head'), may hold values from -1 to 1
- key_weight: bfloat16 [5376, 2048], P(None, 'head'), may hold values from -1 to 1
- value_weight: bfloat16 [5376, 2048], P(None, 'head'), may hold values from -0.078125 to 0.078125
- output_grad: bfloat16 [4096, 4096], P('seq', 'head'), may hold values from -48 to 48
- segments: int32 [4096], replicated, may hold values from 0 to 3, never falling along the last dimension, each value on 1 to 2048 neighbouring positions
Outputs:
- token_grad: bfloat16 [4096, 5376], P('seq', 'head')
- query_weight_grad: bfloat16 [5376, 4096], P('seq', 'head')
- key_weight_grad: bfloat16 [5376, 2048], P('seq', 'head')
- value_weight_grad: bfloat16 [5376, 2048], P('seq', 'head')
Inputs may be any that keep to these rules, and one draw needn't show every extreme that they name: `segments`: segment numbers never fall along the tokens; a segment has at most 2048 tokens.
All inputs are finite; a program needn't handle non-finite values.
Results may differ from a plain program's by a relative error of at most 0.015.
The roundings to bfloat16 on the way count: a program that leaves them out, or rounds other values in their place, can miss the bound.
Values may be sent and summed in bfloat16 or wider, within the bound.
No kernel may reach another device: no remote copies, remote signals or barrier semaphores. Data moves between devices by JAX's collectives and lax.ppermute only.
A program may use at most 192 MiB of HBM per device.

v0:
```python
import jax
import jax.numpy as jnp
from jax import lax
from jax.sharding import PartitionSpec as P

D = 5376
HEADS = 32
KV_HEADS = 16
HEAD_DIM = 128
WINDOW = 1024
HOPS = 2


neg_large = -1e30


def passed_along(x, axis, by):
    count = lax.axis_size(axis)
    pairs = [(i, i + by) for i in range(count) if 0 <= i + by < count]
    return lax.ppermute(x, axis, pairs)


def contract_last(left, right):
    return lax.dot_general(
        left, right, (((1,), (1,)), ((), ())), preferred_element_type=jnp.float32
    )


def contract_first(left, right):
    return lax.dot_general(
        left, right, (((0,), (0,)), ((), ())), preferred_element_type=jnp.float32
    )


def attend(queries, key_value, grads, query_first, key_first, seg_query, seg_key):
    tok_rows = queries.shape[0]
    key_rows = key_value.shape[1]
    groups = HEADS // KV_HEADS
    kv_local = key_value.shape[2] // HEAD_DIM
    score_scale = (D / HEADS) ** (-0.5)
    query_four = queries.reshape(tok_rows, kv_local, groups, HEAD_DIM)
    grad_four = grads.reshape(tok_rows, kv_local, groups, HEAD_DIM)
    key_three = key_value[0].reshape(key_rows, kv_local, HEAD_DIM)
    value_three = key_value[1].reshape(key_rows, kv_local, HEAD_DIM)
    query_pos = query_first + jnp.arange(tok_rows, dtype=jnp.int32)
    key_pos = key_first + jnp.arange(key_rows, dtype=jnp.int32)
    spacing = query_pos[:, None] - key_pos[None, :]
    allowed = (
        (key_pos >= 0)[None, :]
        & (spacing >= 0)
        & (spacing < WINDOW)
        & (seg_query[:, None] == seg_key[None, :])
    )
    scores = (
        jnp.einsum("akgd,ckd->kgac", query_four, key_three, preferred_element_type=jnp.float32)
        * score_scale
    )
    masked = jnp.where(allowed, scores, neg_large)
    row_max = jnp.max(masked, axis=-1, keepdims=True)
    expo = jnp.where(allowed, jnp.exp(masked - row_max), 0.0)
    probs = expo / jnp.sum(expo, axis=-1, keepdims=True)
    dprobs = jnp.einsum(
        "akgd,ckd->kgac", grad_four, value_three, preferred_element_type=jnp.float32
    )
    center = jnp.sum(probs * dprobs, axis=-1, keepdims=True)
    dscores = (probs * (dprobs - center)).astype(jnp.bfloat16)
    probs_low = probs.astype(jnp.bfloat16)
    query_grad = (
        (
            jnp.einsum("kgac,ckd->akgd", dscores, key_three, preferred_element_type=jnp.float32)
            * score_scale
        )
        .reshape(tok_rows, -1)
        .astype(jnp.bfloat16)
    )
    key_grad = (
        jnp.einsum("kgac,akgd->ckd", dscores, query_four, preferred_element_type=jnp.float32)
        * score_scale
    ).reshape(key_rows, -1)
    value_grad = jnp.einsum(
        "kgac,akgd->ckd", probs_low, grad_four, preferred_element_type=jnp.float32
    ).reshape(key_rows, -1)
    return (query_grad, jnp.stack([key_grad, value_grad]))


def per_device(tokens, query_weight, key_weight, value_weight, output_grad, segments):
    tok_rows = tokens.shape[0]
    hop_count = HOPS
    margin = hop_count * tok_rows
    gathered = lax.all_gather(tokens, "head", axis=1, tiled=True)
    queries = jnp.dot(gathered, query_weight, preferred_element_type=jnp.float32).astype(
        jnp.bfloat16
    )
    keys_own = jnp.dot(gathered, key_weight, preferred_element_type=jnp.float32).astype(
        jnp.bfloat16
    )
    values_own = jnp.dot(gathered, value_weight, preferred_element_type=jnp.float32).astype(
        jnp.bfloat16
    )
    key_value = jnp.stack([keys_own, values_own])
    blocks = [key_value] * (hop_count + 1)
    moving = key_value
    for distance in range(1, hop_count + 1):
        moving = passed_along(moving, "seq", 1)
        blocks[hop_count - distance] = moving
    keys_all = jnp.concatenate(blocks, axis=1)
    position = lax.axis_index("seq")
    query_first = position * tok_rows
    seg_query = lax.dynamic_slice_in_dim(segments, query_first, tok_rows, 0)
    seg_padded = jnp.concatenate([jnp.full((margin,), -1, jnp.int32), segments], axis=0)
    seg_key = lax.dynamic_slice_in_dim(seg_padded, query_first, (hop_count + 1) * tok_rows, 0)
    query_grad, kv_grad = attend(
        queries, keys_all, output_grad, query_first, query_first - margin, seg_query, seg_key
    )
    pieces = [
        kv_grad[:, block * tok_rows : (block + 1) * tok_rows] for block in range(hop_count + 1)
    ]
    carried = pieces[0]
    for distance in range(1, hop_count + 1):
        carried = pieces[distance] + passed_along(carried.astype(jnp.bfloat16), "seq", -1).astype(
            carried.dtype
        )
    key_grad = carried[0].astype(jnp.bfloat16)
    value_grad = carried[1].astype(jnp.bfloat16)
    partial_term = (
        contract_last(query_grad, query_weight)
        + contract_last(key_grad, key_weight)
        + contract_last(value_grad, value_weight)
    )
    token_grad = lax.psum_scatter(
        partial_term.astype(jnp.bfloat16), "head", scatter_dimension=1, tiled=True
    )
    proj_grads = jnp.concatenate([query_grad, key_grad, value_grad], axis=1)
    summed = lax.psum_scatter(
        contract_first(gathered, proj_grads).astype(jnp.bfloat16),
        "seq",
        scatter_dimension=0,
        tiled=True,
    ).astype(jnp.float32)
    summed = summed * (tok_rows * lax.axis_size("seq")) ** (-0.5)
    q_width = query_weight.shape[1]
    k_width = key_weight.shape[1]
    query_weight_grad = summed[:, :q_width].astype(jnp.bfloat16)
    key_weight_grad = summed[:, q_width : q_width + k_width].astype(jnp.bfloat16)
    value_weight_grad = summed[:, q_width + k_width :].astype(jnp.bfloat16)
    return (token_grad, query_weight_grad, key_weight_grad, value_weight_grad)


def solution(mesh):
    in_specs = (
        P("seq", "head"),
        P(None, "head"),
        P(None, "head"),
        P(None, "head"),
        P("seq", "head"),
        P(),
    )
    out_specs = (P("seq", "head"), P("seq", "head"), P("seq", "head"), P("seq", "head"))
    return jax.shard_map(
        per_device, mesh=mesh, in_specs=in_specs, out_specs=out_specs, check_vma=False
    )
```

profile of v0, /device:TPU:11, one launch (start us, length us, event | category | flops | bytes accessed | tf_op | source)
XLA Modules:
  0.0 567.5 jit_solution(12160398720478876539)
XLA Ops:
  7.9 102.5 %all-gather.2.cloned.1.call-done = bf16[512,5376]{0,1:T(8,128)(2,1)} async-done(((bf16[512,1344]{0,1:T(8,128)(2,1)}), bf16[512,5376]{0,1:T(8,128)(2,1)}) %all-gather.2.cloned.1.call-update) | async-done | bytes 5505040 | tf_op jit(solution)/shard_map/all_gather | solution.py:90
  110.5 7.3 %fusion.32 = bf16[1,512,512]{2,1,0:T(8,128)(2,1)S(1)} fusion(bf16[512,5376]{0,1:T(8,128)(2,1)} %all-gather.2.cloned.1.call-done, bf16[5376,512]{1,0:T(8,128)(2,1)} %param.9), kind=kOutput, calls=%fused_computation.52 | convolution fusion | flops 2818834432 | bytes 11534336 | tf_op jit(solution)/shard_map/dot_general | solution.py:97
  117.9 5.7 %fusion.31 = bf16[1,512,512]{2,1,0:T(8,128)(2,1)S(1)} fusion(bf16[512,5376]{0,1:T(8,128)(2,1)S(1)} %copy-done.8, bf16[5376,512]{1,0:T(8,128)(2,1)} %param.8), kind=kOutput, calls=%fused_computation.51 | convolution fusion | flops 2818834432 | bytes 11534336 | tf_op jit(solution)/shard_map/dot_general | solution.py:94
  123.7 3.7 collective-permute-start
  131.5 7.6 %collective-permute-done = bf16[2,512,512]{2,1,0:T(8,128)(2,1)} collective-permute-done((bf16[2,512,512]{2,1,0:T(8,128)(2,1)S(1)}, bf16[2,512,512]{2,1,0:T(8,128)(2,1)}, u32[]{:S(2)}, u32[]{:S(2)}) %collective-permute-start) | collective-permute-done | bytes 1048608 | tf_op jit(solution)/shard_map/ppermute | solution.py:20
  139.1 5.6 collective-permute-start.1
  144.6 10.4 %convolution_convert_fusion.1 = bf16[512,1024]{1,0:T(8,128)(2,1)S(1)} fusion(bf16[512,5376]{0,1:T(8,128)(2,1)} %all-gather.2.cloned.1.call-done, bf16[5376,1024]{1,0:T(8,128)(2,1)} %param.7), kind=kOutput, calls=%fused_computation.48 | convolution fusion | flops 5637668864 | bytes 17563648 | tf_op jit(solution)/shard_map/dot_general | solution.py:91
  160.6 2.8 reshape_squeeze.7
  163.4 17.4 %fusion.39 = (f32[4,2,512]{2,1,0:T(2,128)S(1)}, f32[4,2,512,1536]{2,3,1,0:T(8,128)}) fusion(pred[512,1536]{0,1:T(8,128)(4,1)} %fusion.16, bf16[1536,4,128,1]{0,2,3,1:T(8,128)(2,1)S(1)} %copy.38, bf16[512,4,2,128]{0,3,2,1:T(8,128)(2,1)} %bitcast.77), kind=kOutput, calls=%fused_computation.66 | convolution fusion | flops 1642071552 | bytes 28590080 | tf_op jit(solution)/shard_map/sub | solution.py:60
  180.8 12.5 %fusion.6 = f32[4,1536,128,1]{1,2,3,0:T(8,128)} fusion(bf16[512,4,2,128]{0,3,2,1:T(8,128)(2,1)} %bitcast.80, f32[4,2,512,1536]{2,3,1,0:T(8,128)} %get-tuple-element.19, f32[4,2,512]{2,1,0:T(2,128)S(1)} %get-tuple-element.18), kind=kOutput, calls=%fused_computation.11 | convolution fusion | flops 1623195648 | bytes 29376512 | tf_op jit(solution)/shard_map/kgac,akgd->ckd/dot_general | solution.py:80
  193.3 16.6 %fusion.1 = (f32[4,2,512]{2,1,0:T(2,128)S(1)}, f32[4,1536,512,2]{2,1,3,0:T(8,128)}) fusion(f32[4,2,512,1536]{2,3,1,0:T(8,128)} %get-tuple-element.19, f32[4,2,512]{2,1,0:T(2,128)S(1)} %get-tuple-element.18, bf16[512,4,2,128]{0,3,2,1:T(8,128)(2,1)S(1)} %bitcast.81, bf16[1536,4,128,1]{2,1,0,3:T(4,128)(2,1)S(1)} %bitcast.79), kind=kOutput, calls=%fused_computation.3 | convolution fusion | flops 1629483008 | bytes 52985856 | tf_op jit(solution)/shard_map/akgd,ckd->kgac/dot_general | solution.py:62
  210.0 16.8 %fusion.3 = bf16[4,2,512,1536]{2,3,1,0:T(8,128)(2,1)S(1)} fusion(f32[4,1536,512,2]{2,1,3,0:T(8,128)} %get-tuple-element.21, f32[4,2,512]{2,1,0:T(2,128)S(1)} %get-tuple-element.20, f32[4,2,512,1536]{2,3,1,0:T(8,128)} %get-tuple-element.19, f32[4,2,512]{2,1,0:T(2,128)S(1)} %get-tuple-element.18), kind=kLoop, calls=%fused_computation.5 | loop fusion | flops 25165824 | bytes 62947328 | tf_op jit(solution)/shard_map/convert_element_type | solution.py:66
  226.8 7.0 %fusion.13 = f32[4,128,1536]{2,1,0:T(8,128)} fusion(bf16[512,4,2,128]{0,3,2,1:T(8,128)(2,1)} %bitcast.78, bf16[4,2,512,1536]{2,3,1,0:T(8,128)(2,1)S(1)} %fusion.3), kind=kOutput, calls=%fused_computation.27 | convolution fusion | flops 1611399168 | bytes 16777216 | tf_op jit(solution)/shard_map/kgac,akgd->ckd/dot_general | solution.py:77
  238.2 15.3 %collective-permute-done.2 = bf16[2,512,512]{1,2,0:T(8,128)(2,1)S(1)} collective-permute-done((bf16[2,512,512]{1,2,0:T(8,128)(2,1)S(1)}, bf16[2,512,512]{1,2,0:T(8,128)(2,1)S(1)}, u32[]{:S(2)}, u32[]{:S(2)}) %collective-permute-start.2) | collective-permute-done | bytes 1048608 | tf_op jit(solution)/shard_map/ppermute | solution.py:20
  255.9 2.8 multiply_convert_fusion.1
  258.7 12.3 %collective-permute-done.3 = bf16[2,512,512]{1,2,0:T(8,128)(2,1)S(1)} collective-permute-done((bf16[2,512,512]{1,2,0:T(8,128)(2,1)S(1)}, bf16[2,512,512]{1,2,0:T(8,128)(2,1)S(1)}, u32[]{:S(2)}, u32[]{:S(2)}) %collective-permute-start.3) | collective-permute-done | bytes 1048608 | tf_op jit(solution)/shard_map/ppermute | solution.py:20
  271.4 20.0 %fusion.5 = bf16[5376,2048]{0,1:T(8,128)(2,1)} fusion(bf16[512,5376]{0,1:T(8,128)(2,1)} %all-gather.2.cloned.1.call-done, bf16[512,512]{0,1:T(8,128)(2,1)S(1)} %get-tuple-element.17, bf16[512,512]{0,1:T(8,128)(2,1)S(1)} %get-tuple-element.16, bf16[512,1024]{0,1:T(8,128)(2,1)S(1)} %bitcast.82), kind=kOutput, calls=%fused_computation.10 | convolution fusion | flops 11291590656 | bytes 29622272 | tf_op jit(solution)/shard_map/dot_general | solution.py:30
  291.4 28.2 %copy.50 = bf16[5376,2048]{1,0:T(8,128)(2,1)} copy(bf16[5376,2048]{0,1:T(8,128)(2,1)} %fusion.5) | data formatting | bytes 44040192
  319.7 14.0 %fusion.40 = f32[512,5376]{0,1:T(8,128)} fusion(bf16[5376,1024]{1,0:T(8,128)(2,1)} %param.7, bf16[512,1024]{0,1:T(8,128)(2,1)S(1)} %bitcast.83), kind=kOutput, calls=%fused_computation.67 | convolution fusion | flops 5637144576 | bytes 23068672 | tf_op jit(solution)/shard_map/dot_general | solution.py:24
  333.7 11.5 %fusion.36 = f32[512,5376]{0,1:T(8,128)} fusion(bf16[5376,512]{1,0:T(8,128)(2,1)} %param.8, bf16[2,512,512]{1,2,0:T(8,128)(2,1)S(1)} %fusion.22), kind=kOutput, calls=%fused_computation.63 | convolution fusion | flops 2818572288 | bytes 17039360 | tf_op jit(solution)/shard_map/dot_general | solution.py:24
  345.3 15.2 %add_convert_fusion = bf16[512,5376]{0,1:T(8,128)(2,1)} fusion(f32[512,5376]{0,1:T(8,128)} %fusion.40, f32[512,5376]{0,1:T(8,128)} %fusion.36, bf16[5376,512]{1,0:T(8,128)(2,1)} %param.9, bf16[2,512,512]{1,2,0:T(8,128)(2,1)S(1)} %fusion.22), kind=kOutput, calls=%fused_computation.17 | convolution fusion | flops 2826829824 | bytes 33554432 | tf_op jit(solution)/shard_map/dot_general | solution.py:24
  360.5 99.4 %reduce-scatter.7.cloned.1.call-done = bf16[672,2048]{1,0:T(8,128)(2,1)} async-done(((bf16[5376,2048]{1,0:T(8,128)(2,1)}), bf16[672,2048]{1,0:T(8,128)(2,1)}) %reduce-scatter.7.cloned.1.call-update) | async-done | bytes 2752528
  459.9 4.6 copy.51
  476.5 84.5 %reduce-scatter.5.cloned.1.call-done = bf16[512,1344]{0,1:T(8,128)(2,1)} async-done(((bf16[512,5376]{0,1:T(8,128)(2,1)}), bf16[512,1344]{0,1:T(8,128)(2,1)}) %reduce-scatter.5.cloned.1.call-update) | async-done | bytes 1376272 | tf_op jit(solution)/shard_map/reduce_scatter | solution.py:130
  (49 shorter events, 29.9 us)
Async XLA Ops:
  7.2 103.3 %all-gather.2.cloned.1.call-start = ((), (), s32[]{:S(2)}) async-start(), calls=%async_computation.2 | async-start | bytes 6881280 | tf_op jit(solution)/shard_map/all_gather | solution.py:90
  7.9 452.0 %reduce-scatter.7.cloned.1.call-start = ((), (), s32[]{:S(2)}) async-start(), calls=%async_computation.4 | async-start | bytes 24772608
  110.5 7.4 %copy-start.8 = (bf16[512,5376]{0,1:T(8,128)(2,1)S(1)}, bf16[512,5376]{0,1:T(8,128)(2,1)}, u32[]{:S(2)}) copy-start(bf16[512,5376]{0,1:T(8,128)(2,1)} %all-gather.2.cloned.1.call-done) | copy-start | bytes 16515076
  117.9 9.5 %copy-start.4 = (bf16[512,1024]{1,0:T(8,128)(2,1)S(1)}, bf16[512,1024]{1,0:T(8,128)(2,1)}, u32[]{:S(2)}) copy-start(bf16[512,1024]{1,0:T(8,128)(2,1)} %param.10) | copy-start | bytes 3145732
  117.9 10.8 %copy-start.7 = (s32[4096]{0:T(1024)S(1)}, s32[4096]{0:T(1024)}, u32[]{:S(2)}) copy-start(s32[4096]{0:T(1024)} %param.11) | copy-start | bytes 49156
  123.7 15.4 %collective-permute-start = (bf16[2,512,512]{2,1,0:T(8,128)(2,1)S(1)}, bf16[2,512,512]{2,1,0:T(8,128)(2,1)}, u32[]{:S(2)}, u32[]{:S(2)}) collective-permute-start(bf16[2,512,512]{2,1,0:T(8,128)(2,1)S(1)} %pad_maximum_fusion.1), channel_id=1, source_target_pairs={{0,4},{4,8},{8,12},{12,16},{16,20},{20,24},{24,28},{1,5},{5,9},{9,... | collective-permute-start | bytes 3145736 | tf_op jit(solution)/shard_map/ppermute | solution.py:20
  139.1 17.4 %collective-permute-start.1 = (bf16[2,512,512]{2,1,0:T(8,128)(2,1)}, bf16[2,512,512]{2,1,0:T(8,128)(2,1)S(1)}, u32[]{:S(2)}, u32[]{:S(2)}) collective-permute-start(bf16[2,512,512]{2,1,0:T(8,128)(2,1)} %collective-permute-done), channel_id=1, source_target_pairs={{0,4},{4,8},{8,12},{12,16},{16,20},{20,24},{24,28},{1,5},{5,9},{9,... | collective-permute-start | bytes 3145736 | tf_op jit(solution)/shard_map/ppermute | solution.py:20
  160.6 20.2 %copy-start.2 = (bf16[1536,4,128,1]{0,2,3,1:T(8,128)(2,1)}, bf16[1536,4,128,1]{0,2,3,1:T(8,128)(2,1)S(1)}, u32[]{:S(2)}) copy-start(bf16[1536,4,128,1]{0,2,3,1:T(8,128)(2,1)S(1)} %copy.38) | copy-start | bytes 4718596
  180.8 12.5 %copy-start.5 = (bf16[512,1024]{0,1:T(8,128)(2,1)S(1)}, bf16[512,1024]{0,1:T(8,128)(2,1)}, u32[]{:S(2)}) copy-start(bf16[512,1024]{0,1:T(8,128)(2,1)} %copy.53) | copy-start | bytes 3145732
  233.8 19.8 %copy-start = (f32[4,128,1536]{2,1,0:T(8,128)S(1)}, f32[4,128,1536]{2,1,0:T(8,128)}, u32[]{:S(2)}) copy-start(f32[4,128,1536]{2,1,0:T(8,128)} %fusion.13) | copy-start | bytes 9437188
  233.8 19.8 %copy-start.1 = (f32[4,1536,128,1]{1,2,3,0:T(8,128)S(1)}, f32[4,1536,128,1]{1,2,3,0:T(8,128)}, u32[]{:S(2)}) copy-start(f32[4,1536,128,1]{1,2,3,0:T(8,128)} %fusion.6) | copy-start | bytes 9437188
  235.6 20.3 %copy-start.3 = (bf16[1536,4,128,1]{0,2,3,1:T(8,128)(2,1)S(1)}, bf16[1536,4,128,1]{0,2,3,1:T(8,128)(2,1)}, u32[]{:S(2)}) copy-start(bf16[1536,4,128,1]{0,2,3,1:T(8,128)(2,1)} %copy-done.2) | copy-start | bytes 4718596
  235.6 17.9 %collective-permute-start.2 = (bf16[2,512,512]{1,2,0:T(8,128)(2,1)S(1)}, bf16[2,512,512]{1,2,0:T(8,128)(2,1)S(1)}, u32[]{:S(2)}, u32[]{:S(2)}) collective-permute-start(bf16[2,512,512]{1,2,0:T(8,128)(2,1)S(1)} %fusion.23), channel_id=1, source_target_pairs={{4,0},{8,4},{12,8},{16,12},{20,16},{24,20},{28,24},{5,1},{9,5},{13... | collective-permute-start | bytes 3145736 | tf_op jit(solution)/shard_map/ppermute | solution.py:20
  253.9 17.0 %collective-permute-start.3 = (bf16[2,512,512]{1,2,0:T(8,128)(2,1)S(1)}, bf16[2,512,512]{1,2,0:T(8,128)(2,1)S(1)}, u32[]{:S(2)}, u32[]{:S(2)}) collective-permute-start(bf16[2,512,512]{1,2,0:T(8,128)(2,1)S(1)} %fusion.19), channel_id=1, source_target_pairs={{4,0},{8,4},{12,8},{16,12},{20,16},{24,20},{28,24},{5,1},{9,5},{13... | collective-permute-start | bytes 3145736 | tf_op jit(solution)/shard_map/ppermute | solution.py:20
  258.7 12.8 %copy-start.6 = (bf16[4,128,2,512]{3,1,2,0:T(8,128)(2,1)S(1)}, bf16[4,128,2,512]{3,1,2,0:T(8,128)(2,1)}, u32[]{:S(2)}) copy-start(bf16[4,128,2,512]{3,1,2,0:T(8,128)(2,1)} %multiply_convert_fusion.1) | copy-start | bytes 3145732
  319.6 241.4 %reduce-scatter.5.cloned.1.call-start = ((), (), s32[]{:S(2)}) async-start(), calls=%async_computation.3 | async-start | bytes 6881280 | tf_op jit(solution)/shard_map/reduce_scatter | solution.py:130
Sparse Core Ops, SparseCore 0:
  9.6 100.8 all-gather.1
  319.8 140.0 reduce-scatter.6
  462.8 98.1 reduce-scatter.4
where the time goes:
time: 570 us; the launch traced here: 568 us
  waiting for transfers between devices  323 us (57%)
  matrix products  140 us (25%)
  local copies, waits for them, and re-layouts  50.7 us (9%)
  other arithmetic  26 us (5%)
  between operations  14 us (2%)
  starting transfers between devices  13.8 us (2%)
    all_gather x1, waiting for transfers between devices, per_device(): gathered = lax.all_gather(tokens, 'head', axis=1, tiled=True)  103 us
    unnamed x4, waiting for transfers between devices  100 us
    reduce_scatter x1, waiting for transfers between devices, per_device(): lax.psum_scatter(partial_term.astype(jnp.bfloat16), 'head', scatter_dimen...  84.5 us
    dot_general x3, matrix products, contract_last(): lax.dot_general(left, right, (((1,), (1,)), ((), ())), preferred_element_...  40.7 us
    unnamed x23, local copies, waits for them, and re-layouts  39.8 us
    ppermute x4, waiting for transfers between devices, passed_along(): return lax.ppermute(x, axis, pairs)  35.4 us
    dot_general x1, matrix products, contract_first(): lax.dot_general(left, right, (((0,), (0,)), ((), ())), preferred_element_...  20 us
    sub x1, matrix products, attend(): expo = jnp.where(allowed, jnp.exp(masked - row_max), 0.0)  17.4 us
  transfers between devices with their start and end apart: 7, of which 7 were waited for; matrix products, arithmetic and copies ran while one was open for 13% of the time, Pallas kernels for 0%

commit v1 on v0

--- a/solution.py
+++ b/solution.py
@@ -122,27 +122,38 @@
         )
     key_grad = carried[0].astype(jnp.bfloat16)
     value_grad = carried[1].astype(jnp.bfloat16)
-    partial_term = (
-        contract_last(query_grad, query_weight)
-        + contract_last(key_grad, key_weight)
-        + contract_last(value_grad, value_weight)
-    )
-    token_grad = lax.psum_scatter(
-        partial_term.astype(jnp.bfloat16), "head", scatter_dimension=1, tiled=True
-    )
+    n_head = lax.axis_size("head")
+    me = lax.axis_index("head")
+    width = tokens.shape[1]
+
+    def term(dest):
+        start = dest * width
+        part = contract_last(query_grad, lax.dynamic_slice_in_dim(query_weight, start, width, 0))
+        part = part + contract_last(key_grad, lax.dynamic_slice_in_dim(key_weight, start, width, 0))
+        part = part + contract_last(value_grad, lax.dynamic_slice_in_dim(value_weight, start, width, 0))
+        return part.astype(jnp.bfloat16)
+
+    token_sum = None
+    for shift in range(n_head - 1, 0, -1):
+        sent = term((me + shift) % n_head)
+        pairs = [(i, (i + shift) % n_head) for i in range(n_head)]
+        got = lax.ppermute(sent, "head", pairs).astype(jnp.float32)
+        token_sum = got if token_sum is None else token_sum + got
+    own = term(me).astype(jnp.float32)
+    token_grad = (own if token_sum is None else token_sum + own).astype(jnp.bfloat16)
     proj_grads = jnp.concatenate([query_grad, key_grad, value_grad], axis=1)
     summed = lax.psum_scatter(
-        contract_first(gathered, proj_grads).astype(jnp.bfloat16),
+        contract_first(proj_grads, gathered).astype(jnp.bfloat16),
         "seq",
-        scatter_dimension=0,
+        scatter_dimension=1,
         tiled=True,
     ).astype(jnp.float32)
-    summed = summed * (tok_rows * lax.axis_size("seq")) ** (-0.5)
+    summed = (summed * (tok_rows * lax.axis_size("seq")) ** (-0.5)).astype(jnp.bfloat16).T
     q_width = query_weight.shape[1]
     k_width = key_weight.shape[1]
-    query_weight_grad = summed[:, :q_width].astype(jnp.bfloat16)
-    key_weight_grad = summed[:, q_width : q_width + k_width].astype(jnp.bfloat16)
-    value_weight_grad = summed[:, q_width + k_width :].astype(jnp.bfloat16)
+    query_weight_grad = summed[:, :q_width]
+    key_weight_grad = summed[:, q_width : q_width + k_width]
+    value_weight_grad = summed[:, q_width + k_width :]
     return (token_grad, query_weight_grad, key_weight_grad, value_weight_grad)
 
 

time: 570 us -> 443 us (0.78)
  waiting for transfers between devices: 323 us -> 242 us
  local copies, waits for them, and re-layouts: 50.7 us -> 12.1 us
  matrix products: 140 us -> 127 us
    ppermute x0 -> x3, waiting for transfers between devices: none -> 103 us  [per_device(): got = lax.ppermute(sent, 'head', pairs).astype(jnp.float32)]
    unnamed x4 -> x2, waiting for transfers between devices: 100 us -> 0.7 us
    reduce_scatter x1, waiting for transfers between devices: 84.5 us -> 0.56 us  [per_device(): lax.psum_scatter(contract_first(proj_grads, gathered).astype(jnp.bfloat16...]
    unnamed x23 -> x32, local copies, waits for them, and re-layouts: 39.8 us -> 0.09 us
    dot_general x3 -> x12, matrix products: 40.7 us -> 31.3 us  [contract_last(): lax.dot_general(left, right, (((1,), (1,)), ((), ())), preferred_element_...]
  transfers between devices with their start and end apart: 7 -> 9, of which waited for: 7 -> 9; matrix products, arithmetic and copies ran while one was open for 13% -> 11% of each run, Pallas kernels for 0% -> 0%
where the time goes in v1:
time: 443 us; the launch traced here: 441 us
  waiting for transfers between devices  242 us (55%)
  matrix products  127 us (29%)
  other arithmetic  26.2 us (6%)
  starting transfers between devices  19.4 us (4%)
  between operations  14.5 us (3%)
  local copies, waits for them, and re-layouts  12.1 us (3%)
    ppermute x3, waiting for transfers between devices, per_device(): got = lax.ppermute(sent, 'head', pairs).astype(jnp.float32)  103 us
    all_gather x1, waiting for transfers between devices, per_device(): gathered = lax.all_gather(tokens, 'head', axis=1, tiled=True)  103 us
    ppermute x4, waiting for transfers between devices, passed_along(): return lax.ppermute(x, axis, pairs)  35.4 us
    dot_general x12, matrix products, contract_last(): lax.dot_general(left, right, (((1,), (1,)), ((), ())), preferred_element_...  31.3 us
    dot_general x1, matrix products, contract_first(): lax.dot_general(left, right, (((0,), (0,)), ((), ())), preferred_element_...  20.3 us
    convert_element_type x1, other arithmetic, attend(): dscores = (probs * (dprobs - center)).astype(jnp.bfloat16)  17 us
    dot_general x1, matrix products, attend(): jnp.einsum('akgd,ckd->kgac', grad_four, value_three, preferred_element_ty...  16.4 us
    ppermute x4, starting transfers between devices, passed_along(): return lax.ppermute(x, axis, pairs)  13.7 us
  transfers between devices with their start and end apart: 9, of which 9 were waited for; matrix products, arithmetic and copies ran while one was open for 11% of the time, Pallas kernels for 0%

profile of v1, /device:TPU:11, one launch (start us, length us, event | category | flops | bytes accessed | tf_op | source)
XLA Modules:
  0.0 441.2 jit_solution(16275509124751445466)
XLA Ops:
  7.9 102.5 %all-gather.2.cloned.1.call-done = bf16[512,5376]{0,1:T(8,128)(2,1)} async-done(((bf16[512,1344]{0,1:T(8,128)(2,1)}), bf16[512,5376]{0,1:T(8,128)(2,1)}) %all-gather.2.cloned.1.call-update) | async-done | bytes 5505040 | tf_op jit(solution)/shard_map/all_gather | solution.py:90
  110.5 7.3 %fusion.55 = bf16[1,512,512]{2,1,0:T(8,128)(2,1)S(1)} fusion(bf16[512,5376]{0,1:T(8,128)(2,1)} %all-gather.2.cloned.1.call-done, bf16[5376,512]{1,0:T(8,128)(2,1)} %param.9), kind=kOutput, calls=%fused_computation.81 | convolution fusion | flops 2818834432 | bytes 11534336 | tf_op jit(solution)/shard_map/dot_general | solution.py:97
  117.9 5.7 %fusion.54 = bf16[1,512,512]{2,1,0:T(8,128)(2,1)S(1)} fusion(bf16[512,5376]{0,1:T(8,128)(2,1)S(1)} %copy-done.11, bf16[5376,512]{1,0:T(8,128)(2,1)} %param.8), kind=kOutput, calls=%fused_computation.80 | convolution fusion | flops 2818834432 | bytes 11534336 | tf_op jit(solution)/shard_map/dot_general | solution.py:94
  123.7 3.7 collective-permute-start
  131.5 7.6 %collective-permute-done = bf16[2,512,512]{2,1,0:T(8,128)(2,1)} collective-permute-done((bf16[2,512,512]{2,1,0:T(8,128)(2,1)S(1)}, bf16[2,512,512]{2,1,0:T(8,128)(2,1)}, u32[]{:S(2)}, u32[]{:S(2)}) %collective-permute-start) | collective-permute-done | bytes 1048608 | tf_op jit(solution)/shard_map/ppermute | solution.py:20
  139.1 5.6 %collective-permute-start.1 = (bf16[2,512,512]{2,1,0:T(8,128)(2,1)}, bf16[2,512,512]{2,1,0:T(8,128)(2,1)S(1)}, u32[]{:S(2)}, u32[]{:S(2)}) collective-permute-start(bf16[2,512,512]{2,1,0:T(8,128)(2,1)} %collective-permute-done), channel_id=1, source_target_pairs={{0,4},{4,8},{8,12},{12,16},{16,20},{20,24},{24,28},{1,5},{5,9},{9,... | collective-permute-start | bytes 3145736 | tf_op jit(solution)/shard_map/ppermute | solution.py:20
  144.6 10.3 %convolution_convert_fusion.1 = bf16[512,1024]{1,0:T(8,128)(2,1)S(1)} fusion(bf16[512,5376]{0,1:T(8,128)(2,1)} %all-gather.2.cloned.1.call-done, bf16[5376,1024]{1,0:T(8,128)(2,1)} %param.7), kind=kOutput, calls=%fused_computation.69 | convolution fusion | flops 5637668864 | bytes 17563648 | tf_op jit(solution)/shard_map/dot_general | solution.py:91
  160.7 4.0 reshape_squeeze.7
  164.7 13.6 %fusion.73 = (f32[4,2,512]{2,1,0:T(2,128)S(1)}, f32[4,2,512,1536]{2,3,1,0:T(8,128)}) fusion(pred[512,1536]{0,1:T(8,128)(4,1)S(1)} %copy-done.9, bf16[1536,4,128,1]{0,2,3,1:T(8,128)(2,1)S(1)} %copy.22, bf16[512,4,2,128]{0,3,2,1:T(8,128)(2,1)S(1)} %bitcast.87), kind=kOutput, calls=%fused_computation.106 | convolution fusion | flops 1642071552 | bytes 28590080 | tf_op jit(solution)/shard_map/sub | solution.py:60
  178.3 12.6 %fusion.5 = f32[4,1536,128,1]{1,2,3,0:T(8,128)} fusion(bf16[512,4,2,128]{0,3,2,1:T(8,128)(2,1)} %bitcast.89, f32[4,2,512,1536]{2,3,1,0:T(8,128)} %get-tuple-element.11, f32[4,2,512]{2,1,0:T(2,128)S(1)} %get-tuple-element.10), kind=kOutput, calls=%fused_computation.10 | convolution fusion | flops 1623195648 | bytes 29376512 | tf_op jit(solution)/shard_map/kgac,akgd->ckd/dot_general | solution.py:80
  190.9 16.4 %fusion.1 = (f32[4,2,512]{2,1,0:T(2,128)S(1)}, f32[4,1536,512,2]{2,1,3,0:T(8,128)}) fusion(f32[4,2,512,1536]{2,3,1,0:T(8,128)} %get-tuple-element.11, f32[4,2,512]{2,1,0:T(2,128)S(1)} %get-tuple-element.10, bf16[512,4,2,128]{0,3,2,1:T(8,128)(2,1)S(1)} %bitcast.90, bf16[1536,4,128,1]{2,1,0,3:T(4,128)(2,1)S(1)} %bitcast.88), kind=kOutput, calls=%fused_computation.3 | convolution fusion | flops 1629483008 | bytes 52985856 | tf_op jit(solution)/shard_map/akgd,ckd->kgac/dot_general | solution.py:62
  207.3 17.0 %fusion.3 = bf16[4,2,512,1536]{2,3,1,0:T(8,128)(2,1)S(1)} fusion(f32[4,1536,512,2]{2,1,3,0:T(8,128)} %get-tuple-element.13, f32[4,2,512]{2,1,0:T(2,128)S(1)} %get-tuple-element.12, f32[4,2,512,1536]{2,3,1,0:T(8,128)} %get-tuple-element.11, f32[4,2,512]{2,1,0:T(2,128)S(1)} %get-tuple-element.10), kind=kLoop, calls=%fused_computation.5 | loop fusion | flops 25165824 | bytes 62947328 | tf_op jit(solution)/shard_map/convert_element_type | solution.py:66
  224.4 7.0 %fusion.12 = f32[4,128,1536]{2,1,0:T(8,128)} fusion(bf16[512,4,2,128]{0,3,2,1:T(8,128)(2,1)} %bitcast.86, bf16[4,2,512,1536]{2,3,1,0:T(8,128)(2,1)S(1)} %fusion.3), kind=kOutput, calls=%fused_computation.33 | convolution fusion | flops 1611399168 | bytes 16777216 | tf_op jit(solution)/shard_map/kgac,akgd->ckd/dot_general | solution.py:77
  235.8 15.3 %collective-permute-done.2 = bf16[2,512,512]{1,2,0:T(8,128)(2,1)S(1)} collective-permute-done((bf16[2,512,512]{1,2,0:T(8,128)(2,1)S(1)}, bf16[2,512,512]{1,2,0:T(8,128)(2,1)S(1)}, u32[]{:S(2)}, u32[]{:S(2)}) %collective-permute-start.2) | collective-permute-done | bytes 1048608 | tf_op jit(solution)/shard_map/ppermute | solution.py:20
  256.2 12.3 %collective-permute-done.3 = bf16[2,512,512]{1,2,0:T(8,128)(2,1)S(1)} collective-permute-done((bf16[2,512,512]{1,2,0:T(8,128)(2,1)S(1)}, bf16[2,512,512]{1,2,0:T(8,128)(2,1)S(1)}, u32[]{:S(2)}, u32[]{:S(2)}) %collective-permute-start.3) | collective-permute-done | bytes 1048608 | tf_op jit(solution)/shard_map/ppermute | solution.py:20
  269.0 20.3 %convolution_convert_fusion = bf16[2048,5376]{0,1:T(8,128)(2,1)} fusion(bf16[512,5376]{0,1:T(8,128)(2,1)} %all-gather.2.cloned.1.call-done, bf16[512,512]{0,1:T(8,128)(2,1)S(1)} %get-tuple-element.9, bf16[512,512]{0,1:T(8,128)(2,1)S(1)} %get-tuple-element.8, bf16[512,1024]{0,1:T(8,128)(2,1)S(1)} %bitcast.91), kind=kOutput, calls=%fused_computation.8 | convolution fusion | flops 11291590656 | bytes 29622272 | tf_op jit(solution)/shard_map/dot_general | solution.py:30
  289.3 3.4 fusion.24
  292.7 3.5 fusion.26
  296.3 4.9 %fusion.28 = f32[512,1344]{0,1:T(8,128)S(1)} fusion(bf16[512,1024]{0,1:T(8,128)(2,1)S(1)} %bitcast.94, bf16[5376,1024]{1,0:T(8,128)(2,1)} %param.7, s32[]{:T(128)S(6)} %select_n.53), kind=kOutput, calls=%fused_computation.51 | convolution fusion | flops 1409286144 | bytes 6553604 | tf_op jit(solution)/shard_map/dot_general | solution.py:24
  315.4 4.0 fusion.22
  321.8 74.8 %collective-permute-done.6 = bf16[512,1344]{0,1:T(8,128)(2,1)S(1)} collective-permute-done((bf16[512,1344]{0,1:T(8,128)(2,1)}, bf16[512,1344]{0,1:T(8,128)(2,1)S(1)}, u32[]{:S(2)}, u32[]{:S(2)}) %collective-permute-start.6) | collective-permute-done | bytes 1376288 | tf_op jit(solution)/shard_map/ppermute | solution.py:140
  396.6 23.7 %collective-permute-done.5 = bf16[512,1344]{0,1:T(8,128)(2,1)} collective-permute-done((bf16[512,1344]{0,1:T(8,128)(2,1)}, bf16[512,1344]{0,1:T(8,128)(2,1)}, u32[]{:S(2)}, u32[]{:S(2)}) %collective-permute-start.5) | collective-permute-done | bytes 1376288 | tf_op jit(solution)/shard_map/ppermute | solution.py:140
  420.2 4.1 collective-permute-done.4
  424.3 4.6 %add_convert_fusion = bf16[512,1344]{0,1:T(8,128)(2,1)} fusion(bf16[512,1344]{0,1:T(8,128)(2,1)S(1)} %collective-permute-done.6, bf16[512,1344]{0,1:T(8,128)(2,1)} %collective-permute-done.5, bf16[512,1344]{0,1:T(8,128)(2,1)} %collective-permute-done.4, f32[512,1344]{0,1:T(8,128)S(1)} %convolution_add_fusion.1, bf16[5376,512]{1,0:T(8,128)(2,1)} %param.9, ...), kind=kOutput, calls=%fused_computation.44 | convolution fusion | flops 711524352 | bytes 10158084 | tf_op jit(solution)/shard_map/dot_general | solution.py:24
  (72 shorter events, 42.5 us)
Async XLA Ops:
  7.2 103.3 %all-gather.2.cloned.1.call-start = ((), (), s32[]{:S(2)}) async-start(), calls=%async_computation.1 | async-start | bytes 6881280 | tf_op jit(solution)/shard_map/all_gather | solution.py:90
  7.9 421.6 %reduce-scatter.2.cloned.1.call-start = ((), (), s32[]{:S(2)}) async-start(), calls=%async_computation.2 | async-start | bytes 24772608 | tf_op jit(solution)/shard_map/reduce_scatter | solution.py:145
  110.5 7.4 %copy-start.11 = (bf16[512,5376]{0,1:T(8,128)(2,1)S(1)}, bf16[512,5376]{0,1:T(8,128)(2,1)}, u32[]{:S(2)}) copy-start(bf16[512,5376]{0,1:T(8,128)(2,1)} %all-gather.2.cloned.1.call-done) | copy-start | bytes 16515076
  117.9 9.5 %copy-start.6 = (bf16[512,1024]{1,0:T(8,128)(2,1)S(1)}, bf16[512,1024]{1,0:T(8,128)(2,1)}, u32[]{:S(2)}) copy-start(bf16[512,1024]{1,0:T(8,128)(2,1)} %param.10) | copy-start | bytes 3145732
  123.6 5.1 %copy-start.10 = (s32[4096]{0:T(1024)S(1)}, s32[4096]{0:T(1024)}, u32[]{:S(2)}) copy-start(s32[4096]{0:T(1024)} %param.11) | copy-start | bytes 49156
  123.7 15.4 %collective-permute-start = (bf16[2,512,512]{2,1,0:T(8,128)(2,1)S(1)}, bf16[2,512,512]{2,1,0:T(8,128)(2,1)}, u32[]{:S(2)}, u32[]{:S(2)}) collective-permute-start(bf16[2,512,512]{2,1,0:T(8,128)(2,1)S(1)} %pad_maximum_fusion.1), channel_id=1, source_target_pairs={{0,4},{4,8},{8,12},{12,16},{16,20},{20,24},{24,28},{1,5},{5,9},{9,... | collective-permute-start | bytes 3145736 | tf_op jit(solution)/shard_map/ppermute | solution.py:20
  139.1 17.4 %collective-permute-start.1 = (bf16[2,512,512]{2,1,0:T(8,128)(2,1)}, bf16[2,512,512]{2,1,0:T(8,128)(2,1)S(1)}, u32[]{:S(2)}, u32[]{:S(2)}) collective-permute-start(bf16[2,512,512]{2,1,0:T(8,128)(2,1)} %collective-permute-done), channel_id=1, source_target_pairs={{0,4},{4,8},{8,12},{12,16},{16,20},{20,24},{24,28},{1,5},{5,9},{9,... | collective-permute-start | bytes 3145736 | tf_op jit(solution)/shard_map/ppermute | solution.py:20
  160.6 17.7 %copy-start.2 = (bf16[1536,4,128,1]{0,2,3,1:T(8,128)(2,1)}, bf16[1536,4,128,1]{0,2,3,1:T(8,128)(2,1)S(1)}, u32[]{:S(2)}) copy-start(bf16[1536,4,128,1]{0,2,3,1:T(8,128)(2,1)S(1)} %copy.22) | copy-start | bytes 4718596
  160.7 4.1 copy-start.4
  178.3 12.6 %copy-start.5 = (bf16[1536,4,128]{2,1,0:T(4,128)(2,1)S(1)}, bf16[1536,4,128]{2,1,0:T(4,128)(2,1)}, u32[]{:S(2)}) copy-start(bf16[1536,4,128]{2,1,0:T(4,128)(2,1)} %reshape_squeeze.7) | copy-start | bytes 4718596
  178.3 12.6 %copy-start.7 = (bf16[512,1024]{0,1:T(8,128)(2,1)S(1)}, bf16[512,1024]{0,1:T(8,128)(2,1)}, u32[]{:S(2)}) copy-start(bf16[512,1024]{0,1:T(8,128)(2,1)} %copy.35) | copy-start | bytes 3145732
  231.4 19.8 %copy-start = (f32[4,128,1536]{2,1,0:T(8,128)S(1)}, f32[4,128,1536]{2,1,0:T(8,128)}, u32[]{:S(2)}) copy-start(f32[4,128,1536]{2,1,0:T(8,128)} %fusion.12) | copy-start | bytes 9437188
  231.4 19.8 %copy-start.1 = (f32[4,1536,128,1]{1,2,3,0:T(8,128)S(1)}, f32[4,1536,128,1]{1,2,3,0:T(8,128)}, u32[]{:S(2)}) copy-start(f32[4,1536,128,1]{1,2,3,0:T(8,128)} %fusion.5) | copy-start | bytes 9437188
  233.2 20.2 %copy-start.3 = (bf16[1536,4,128,1]{0,2,3,1:T(8,128)(2,1)S(1)}, bf16[1536,4,128,1]{0,2,3,1:T(8,128)(2,1)}, u32[]{:S(2)}) copy-start(bf16[1536,4,128,1]{0,2,3,1:T(8,128)(2,1)} %copy-done.2) | copy-start | bytes 4718596
  233.2 17.9 %collective-permute-start.2 = (bf16[2,512,512]{1,2,0:T(8,128)(2,1)S(1)}, bf16[2,512,512]{1,2,0:T(8,128)(2,1)S(1)}, u32[]{:S(2)}, u32[]{:S(2)}) collective-permute-start(bf16[2,512,512]{1,2,0:T(8,128)(2,1)S(1)} %fusion.36), channel_id=1, source_target_pairs={{4,0},{8,4},{12,8},{16,12},{20,16},{24,20},{28,24},{5,1},{9,5},{13... | collective-permute-start | bytes 3145736 | tf_op jit(solution)/shard_map/ppermute | solution.py:20
  251.5 17.0 %collective-permute-start.3 = (bf16[2,512,512]{1,2,0:T(8,128)(2,1)S(1)}, bf16[2,512,512]{1,2,0:T(8,128)(2,1)S(1)}, u32[]{:S(2)}, u32[]{:S(2)}) collective-permute-start(bf16[2,512,512]{1,2,0:T(8,128)(2,1)S(1)} %fusion.32), channel_id=1, source_target_pairs={{4,0},{8,4},{12,8},{16,12},{20,16},{24,20},{28,24},{5,1},{9,5},{13... | collective-permute-start | bytes 3145736 | tf_op jit(solution)/shard_map/ppermute | solution.py:20
  256.2 12.8 %copy-start.8 = (bf16[4,128,2,512]{3,1,2,0:T(8,128)(2,1)S(1)}, bf16[4,128,2,512]{3,1,2,0:T(8,128)(2,1)}, u32[]{:S(2)}) copy-start(bf16[4,128,2,512]{3,1,2,0:T(8,128)(2,1)} %multiply_convert_fusion.1) | copy-start | bytes 3145732
  292.7 8.5 %slice-start.2 = ((s8[5505024]{0:T(1024)(128)(4,1)}), s8[4194304]{0:T(1024)(128)(4,1)S(1)}, s32[]{:S(2)}) async-start(s8[5505024]{0:T(1024)(128)(4,1)} %bitcast.84), calls=%async_computation.5 | async-start | bytes 8388608
  292.7 9.4 %slice-start = ((s8[5505024]{0:T(1024)(128)(4,1)}), s8[4194304]{0:T(1024)(128)(4,1)S(1)}, s32[]{:S(2)}) async-start(s8[5505024]{0:T(1024)(128)(4,1)} %bitcast.82), calls=%async_computation.3 | async-start | bytes 8388608
  296.2 5.0 %slice-start.3 = ((s8[5505024]{0:T(1024)(128)(4,1)}), s8[1310720]{0:T(1024)(128)(4,1)S(1)}, s32[]{:S(2)}) async-start(s8[5505024]{0:T(1024)(128)(4,1)} %bitcast.84), calls=%async_computation.6 | async-start | bytes 2621440
  296.3 5.9 %slice-start.1 = ((s8[5505024]{0:T(1024)(128)(4,1)}), s8[1310720]{0:T(1024)(128)(4,1)S(1)}, s32[]{:S(2)}) async-start(s8[5505024]{0:T(1024)(128)(4,1)} %bitcast.82), calls=%async_computation.4 | async-start | bytes 2621440
  304.1 92.4 %collective-permute-start.6 = (bf16[512,1344]{0,1:T(8,128)(2,1)}, bf16[512,1344]{0,1:T(8,128)(2,1)S(1)}, u32[]{:S(2)}, u32[]{:S(2)}) collective-permute-start(bf16[512,1344]{0,1:T(8,128)(2,1)} %fusion.18), channel_id=1, source_target_pairs={{0,1},{1,2},{2,3},{3,0},{4,5},{5,6},{6,7},{7,4},{8,9},{9,10},{10,1... | collective-permute-start | bytes 4128776 | tf_op jit(solution)/shard_map/ppermute | solution.py:140
  310.0 110.2 %collective-permute-start.5 = (bf16[512,1344]{0,1:T(8,128)(2,1)}, bf16[512,1344]{0,1:T(8,128)(2,1)}, u32[]{:S(2)}, u32[]{:S(2)}) collective-permute-start(bf16[512,1344]{0,1:T(8,128)(2,1)} %fusion.17), channel_id=1, source_target_pairs={{0,2},{1,3},{2,0},{3,1},{4,6},{5,7},{6,4},{7,5},{8,10},{9,11},{10,... | collective-permute-start | bytes 4128776 | tf_op jit(solution)/shard_map/ppermute | solution.py:140
  315.4 109.0 %collective-permute-start.4 = (bf16[512,1344]{0,1:T(8,128)(2,1)}, bf16[512,1344]{0,1:T(8,128)(2,1)}, u32[]{:S(2)}, u32[]{:S(2)}) collective-permute-start(bf16[512,1344]{0,1:T(8,128)(2,1)} %fusion.16), channel_id=1, source_target_pairs={{0,3},{1,0},{2,1},{3,2},{4,7},{5,4},{6,5},{7,6},{8,11},{9,8},{10,9... | collective-permute-start | bytes 4128776 | tf_op jit(solution)/shard_map/ppermute | solution.py:140
  (1 other events, 4.1 us)
Sparse Core Ops, SparseCore 0:
  9.6 100.8 all-gather.1
  289.4 140.0 reduce-scatter.1

commit v2 on v1

--- a/solution.py
+++ b/solution.py
@@ -1,7 +1,7 @@
 import jax
 import jax.numpy as jnp
 from jax import lax
-from jax.sharding import PartitionSpec as P
+from jax.sharding import Mesh, PartitionSpec as P
 
 D = 5376
 HEADS = 32
@@ -9,6 +9,7 @@
 HEAD_DIM = 128
 WINDOW = 1024
 HOPS = 2
+SEQ = ("seq_hi", "core")
 
 
 neg_large = -1e30
@@ -99,12 +100,10 @@
     )
     key_value = jnp.stack([keys_own, values_own])
     blocks = [key_value] * (hop_count + 1)
-    moving = key_value
     for distance in range(1, hop_count + 1):
-        moving = passed_along(moving, "seq", 1)
-        blocks[hop_count - distance] = moving
+        blocks[hop_count - distance] = passed_along(key_value, SEQ, distance)
     keys_all = jnp.concatenate(blocks, axis=1)
-    position = lax.axis_index("seq")
+    position = lax.axis_index(SEQ)
     query_first = position * tok_rows
     seg_query = lax.dynamic_slice_in_dim(segments, query_first, tok_rows, 0)
     seg_padded = jnp.concatenate([jnp.full((margin,), -1, jnp.int32), segments], axis=0)
@@ -115,11 +114,10 @@
     pieces = [
         kv_grad[:, block * tok_rows : (block + 1) * tok_rows] for block in range(hop_count + 1)
     ]
-    carried = pieces[0]
+    carried = pieces[hop_count]
     for distance in range(1, hop_count + 1):
-        carried = pieces[distance] + passed_along(carried.astype(jnp.bfloat16), "seq", -1).astype(
-            carried.dtype
-        )
+        back = passed_along(pieces[hop_count - distance].astype(jnp.bfloat16), SEQ, -distance)
+        carried = carried + back.astype(jnp.float32)
     key_grad = carried[0].astype(jnp.bfloat16)
     value_grad = carried[1].astype(jnp.bfloat16)
     n_head = lax.axis_size("head")
@@ -142,13 +140,17 @@
     own = term(me).astype(jnp.float32)
     token_grad = (own if token_sum is None else token_sum + own).astype(jnp.bfloat16)
     proj_grads = jnp.concatenate([query_grad, key_grad, value_grad], axis=1)
-    summed = lax.psum_scatter(
-        contract_first(proj_grads, gathered).astype(jnp.bfloat16),
-        "seq",
-        scatter_dimension=1,
-        tiled=True,
-    ).astype(jnp.float32)
-    summed = (summed * (tok_rows * lax.axis_size("seq")) ** (-0.5)).astype(jnp.bfloat16).T
+    weight_part = contract_first(proj_grads, gathered)
+    n_hi = lax.axis_size("seq_hi")
+    quarter = weight_part.reshape(weight_part.shape[0], n_hi, 2, -1)
+    core = lax.axis_index("core")
+    keep = lax.dynamic_index_in_dim(quarter, core, 2, keepdims=False)
+    give = lax.dynamic_index_in_dim(quarter, 1 - core, 2, keepdims=False).astype(jnp.bfloat16)
+    got = lax.ppermute(give, "core", [(0, 1), (1, 0)])
+    pair_sum = (keep + got.astype(jnp.float32)).astype(jnp.bfloat16)
+    summed = lax.psum_scatter(pair_sum, "seq_hi", scatter_dimension=1, tiled=True)
+    summed = summed.reshape(summed.shape[0], -1).astype(jnp.float32)
+    summed = (summed * (tok_rows * lax.axis_size(SEQ)) ** (-0.5)).astype(jnp.bfloat16).T
     q_width = query_weight.shape[1]
     k_width = key_weight.shape[1]
     query_weight_grad = summed[:, :q_width]
@@ -158,15 +160,18 @@
 
 
 def solution(mesh):
+    n_seq = mesh.shape["seq"]
+    n_head = mesh.shape["head"]
+    view = Mesh(mesh.devices.reshape(n_seq // 2, 2, n_head), ("seq_hi", "core", "head"))
     in_specs = (
-        P("seq", "head"),
+        P(SEQ, "head"),
         P(None, "head"),
         P(None, "head"),
         P(None, "head"),
-        P("seq", "head"),
+        P(SEQ, "head"),
         P(),
     )
-    out_specs = (P("seq", "head"), P("seq", "head"), P("seq", "head"), P("seq", "head"))
+    out_specs = (P(SEQ, "head"),) * 4
     return jax.shard_map(
-        per_device, mesh=mesh, in_specs=in_specs, out_specs=out_specs, check_vma=False
+        per_device, mesh=view, in_specs=in_specs, out_specs=out_specs, check_vma=False
     )

time: 443 us -> 502 us (1.13)
  waiting for transfers between devices: 242 us -> 272 us
  other arithmetic: 26.2 us -> 43 us
  local copies, waits for them, and re-layouts: 12.1 us -> 25.5 us
    ppermute x0 -> x1, waiting for transfers between devices: none -> 17.2 us  [per_device(): got = lax.ppermute(give, 'core', [(0, 1), (1, 0)])]
    convert_element_type x1, other arithmetic: 0.37 us -> 15.4 us  [per_device(): pair_sum = (keep + got.astype(jnp.float32)).astype(jnp.bfloat16)]
    ppermute x4, waiting for transfers between devices: 35.4 us -> 48.6 us  [passed_along(): return lax.ppermute(x, axis, pairs)]
    convert_element_type x0 -> x1, local copies, waits for them, and re-layouts: none -> 12.1 us  [per_device(): lax.dynamic_index_in_dim(quarter, 1 - core, 2, keepdims=False)]
    ppermute x3, waiting for transfers between devices: 103 us -> 108 us  [per_device(): got = lax.ppermute(sent, 'head', pairs).astype(jnp.float32)]
    all_gather x1, waiting for transfers between devices: 103 us -> 97.5 us  [per_device(): gathered = lax.all_gather(tokens, 'head', axis=1, tiled=True)]
  transfers between devices with their start and end apart: 9 -> 10, of which waited for: 9 -> 9; matrix products, arithmetic and copies ran while one was open for 11% -> 9% of each run, Pallas kernels for 0% -> 0%
where the time goes in v2:
time: 502 us; the launch traced here: 496 us
  waiting for transfers between devices  272 us (54%)
  matrix products  123 us (25%)
  other arithmetic  43 us (9%)
  local copies, waits for them, and re-layouts  25.5 us (5%)
  starting transfers between devices  16.9 us (3%)
  between operations  15 us (3%)
    ppermute x3, waiting for transfers between devices, per_device(): got = lax.ppermute(sent, 'head', pairs).astype(jnp.float32)  108 us
    all_gather x1, waiting for transfers between devices, per_device(): gathered = lax.all_gather(tokens, 'head', axis=1, tiled=True)  97.5 us
    ppermute x4, waiting for transfers between devices, passed_along(): return lax.ppermute(x, axis, pairs)  48.6 us
    dot_general x12, matrix products, contract_last(): lax.dot_general(left, right, (((1,), (1,)), ((), ())), preferred_element_...  29.6 us
    dot_general x1, matrix products, contract_first(): lax.dot_general(left, right, (((0,), (0,)), ((), ())), preferred_element_...  22.2 us
    ppermute x1, waiting for transfers between devices, per_device(): got = lax.ppermute(give, 'core', [(0, 1), (1, 0)])  17.2 us
    convert_element_type x1, other arithmetic, attend(): dscores = (probs * (dprobs - center)).astype(jnp.bfloat16)  16.8 us
    dot_general x1, matrix products, attend(): jnp.einsum('akgd,ckd->kgac', grad_four, value_three, preferred_element_ty...  16.4 us
  transfers between devices with their start and end apart: 10, of which 9 were waited for; matrix products, arithmetic and copies ran while one was open for 9% of the time, Pallas kernels for 0%

profile of v2, /device:TPU:11, one launch (start us, length us, event | category | flops | bytes accessed | tf_op | source)
XLA Modules:
  0.0 495.6 jit_solution(10588061255750553206)
XLA Ops:
  13.0 97.5 %all-gather.2.cloned.1.call-done = bf16[512,5376]{0,1:T(8,128)(2,1)} async-done(((bf16[512,1344]{0,1:T(8,128)(2,1)}), bf16[512,5376]{0,1:T(8,128)(2,1)}) %all-gather.2.cloned.1.call-update) | async-done | bytes 5505040 | tf_op jit(solution)/shard_map/all_gather | solution.py:91
  110.5 7.3 %fusion.56 = bf16[1,512,512]{2,1,0:T(8,128)(2,1)S(1)} fusion(bf16[512,5376]{0,1:T(8,128)(2,1)} %all-gather.2.cloned.1.call-done, bf16[5376,512]{1,0:T(8,128)(2,1)} %param.9), kind=kOutput, calls=%fused_computation.81 | convolution fusion | flops 2818834432 | bytes 11534336 | tf_op jit(solution)/shard_map/dot_general | solution.py:98
  117.9 5.8 %fusion.55 = bf16[1,512,512]{2,1,0:T(8,128)(2,1)S(1)} fusion(bf16[512,5376]{0,1:T(8,128)(2,1)S(1)} %copy-done.10, bf16[5376,512]{1,0:T(8,128)(2,1)} %param.8), kind=kOutput, calls=%fused_computation.80 | convolution fusion | flops 2818834432 | bytes 11534336 | tf_op jit(solution)/shard_map/dot_general | solution.py:95
  123.7 3.7 collective-permute-start.1
  130.6 5.9 %convolution_convert_fusion = bf16[512,1024]{1,0:T(8,128)(2,1)S(1)} fusion(bf16[512,5376]{0,1:T(8,128)(2,1)S(1)} %copy-done.10, bf16[5376,1024]{1,0:T(8,128)(2,1)S(1)} %bitcast.107), kind=kOutput, calls=%fused_computation.69 | convolution fusion | flops 5637668864 | bytes 17563648 | tf_op jit(solution)/shard_map/dot_general | solution.py:92
  137.9 9.9 %collective-permute-done.1 = bf16[2,512,512]{2,1,0:T(8,128)(2,1)} collective-permute-done((bf16[2,512,512]{2,1,0:T(8,128)(2,1)S(1)}, bf16[2,512,512]{2,1,0:T(8,128)(2,1)}, u32[]{:S(2)}, u32[]{:S(2)}) %collective-permute-start.1) | collective-permute-done | bytes 1048608 | tf_op jit(solution)/shard_map/ppermute | solution.py:21
  147.8 14.6 %collective-permute-done = bf16[2,512,512]{2,1,0:T(8,128)(2,1)} collective-permute-done((bf16[2,512,512]{2,1,0:T(8,128)(2,1)S(1)}, bf16[2,512,512]{2,1,0:T(8,128)(2,1)}, u32[]{:S(2)}, u32[]{:S(2)}) %collective-permute-start) | collective-permute-done | bytes 1048608 | tf_op jit(solution)/shard_map/ppermute | solution.py:21
  166.9 4.0 reshape_squeeze.7
  170.9 13.6 %fusion.75 = (f32[4,2,512]{2,1,0:T(2,128)S(1)}, f32[4,2,512,1536]{2,3,1,0:T(8,128)}) fusion(pred[512,1536]{0,1:T(8,128)(4,1)S(1)} %copy-done.8, bf16[1536,4,128,1]{0,2,3,1:T(8,128)(2,1)S(1)} %copy.46, bf16[512,4,2,128]{0,3,2,1:T(8,128)(2,1)S(1)} %bitcast.97), kind=kOutput, calls=%fused_computation.107 | convolution fusion | flops 1642071552 | bytes 28590080 | tf_op jit(solution)/shard_map/sub | solution.py:61
  184.5 12.6 %fusion.6 = f32[4,1536,128,1]{1,2,3,0:T(8,128)} fusion(bf16[512,4,2,128]{0,3,2,1:T(8,128)(2,1)} %bitcast.99, f32[4,2,512,1536]{2,3,1,0:T(8,128)} %get-tuple-element.13, f32[4,2,512]{2,1,0:T(2,128)S(1)} %get-tuple-element.12), kind=kOutput, calls=%fused_computation.12 | convolution fusion | flops 1623195648 | bytes 29376512 | tf_op jit(solution)/shard_map/kgac,akgd->ckd/dot_general | solution.py:81
  197.2 16.4 %fusion.1 = (f32[4,2,512]{2,1,0:T(2,128)S(1)}, f32[4,1536,512,2]{2,1,3,0:T(8,128)}) fusion(f32[4,2,512,1536]{2,3,1,0:T(8,128)} %get-tuple-element.13, f32[4,2,512]{2,1,0:T(2,128)S(1)} %get-tuple-element.12, bf16[512,4,2,128]{0,3,2,1:T(8,128)(2,1)S(1)} %bitcast.100, bf16[1536,4,128,1]{2,1,0,3:T(4,128)(2,1)S(1)} %bitcast.98), kind=kOutput, calls=%fused_computation.3 | convolution fusion | flops 1629483008 | bytes 52985856 | tf_op jit(solution)/shard_map/akgd,ckd->kgac/dot_general | solution.py:63
  213.6 16.8 %fusion.3 = bf16[4,2,512,1536]{2,3,1,0:T(8,128)(2,1)S(1)} fusion(f32[4,1536,512,2]{2,1,3,0:T(8,128)} %get-tuple-element.15, f32[4,2,512]{2,1,0:T(2,128)S(1)} %get-tuple-element.14, f32[4,2,512,1536]{2,3,1,0:T(8,128)} %get-tuple-element.13, f32[4,2,512]{2,1,0:T(2,128)S(1)} %get-tuple-element.12), kind=kLoop, calls=%fused_computation.5 | loop fusion | flops 25165824 | bytes 62947328 | tf_op jit(solution)/shard_map/convert_element_type | solution.py:67
  230.4 7.0 %fusion.15 = f32[4,128,1536]{2,1,0:T(8,128)} fusion(bf16[512,4,2,128]{0,3,2,1:T(8,128)(2,1)} %bitcast.96, bf16[4,2,512,1536]{2,3,1,0:T(8,128)(2,1)S(1)} %fusion.3), kind=kOutput, calls=%fused_computation.36 | convolution fusion | flops 1611399168 | bytes 16777216 | tf_op jit(solution)/shard_map/kgac,akgd->ckd/dot_general | solution.py:78
  248.4 20.5 %collective-permute-done.3 = bf16[2,512,512]{1,2,0:T(8,128)(2,1)S(1)} collective-permute-done((bf16[2,512,512]{1,2,0:T(8,128)(2,1)S(1)}, bf16[2,512,512]{1,2,0:T(8,128)(2,1)S(1)}, u32[]{:S(2)}, u32[]{:S(2)}) %collective-permute-start.3) | collective-permute-done | bytes 1048608 | tf_op jit(solution)/shard_map/ppermute | solution.py:21
  268.9 3.7 collective-permute-done.2
  273.1 22.2 %fusion.37 = f32[2048,5376]{0,1:T(8,128)} fusion(bf16[512,5376]{0,1:T(8,128)(2,1)} %all-gather.2.cloned.1.call-done, bf16[512,512]{0,1:T(8,128)(2,1)S(1)} %get-tuple-element.11, bf16[512,512]{0,1:T(8,128)(2,1)S(1)} %get-tuple-element.10, bf16[512,1024]{0,1:T(8,128)(2,1)S(1)} %bitcast.101), kind=kOutput, calls=%fused_computation.60 | convolution fusion | flops 11280580608 | bytes 51642368 | tf_op jit(solution)/shard_map/dot_general | solution.py:31
  295.2 12.1 %fusion.11 = bf16[2048,4,672]{0,2,1:T(8,128)(2,1)} fusion(f32[2048,4,2,672]{0,3,2,1:T(8,128)} %bitcast.87, s32[]{:T(128)S(6)} %select_n.67), kind=kLoop, calls=%fused_computation.18 | loop fusion | bytes 22020100 | tf_op jit(solution)/shard_map/convert_element_type | solution.py:148
  307.3 17.2 %collective-permute-done.7 = bf16[2048,4,672]{0,2,1:T(8,128)(2,1)} collective-permute-done((bf16[2048,4,672]{0,2,1:T(8,128)(2,1)}, bf16[2048,4,672]{0,2,1:T(8,128)(2,1)}, u32[]{:S(2)}, u32[]{:S(2)}) %collective-permute-start.7) | collective-permute-done | bytes 11010080 | tf_op jit(solution)/shard_map/ppermute | solution.py:149
  324.5 15.4 %fusion.5 = bf16[2048,4,672]{0,2,1:T(8,128)(2,1)} fusion(bf16[2048,4,672]{0,2,1:T(8,128)(2,1)} %collective-permute-done.7, f32[2048,4,2,672]{0,3,2,1:T(8,128)} %bitcast.88, s32[]{:T(128)S(6)} %select_n.66), kind=kLoop, calls=%fused_computation.10 | loop fusion | flops 16515072 | bytes 44040196 | tf_op jit(solution)/shard_map/convert_element_type | solution.py:150
  347.0 4.0 fusion.31
  370.9 17.3 %collective-permute-done.6 = bf16[512,1344]{0,1:T(8,128)(2,1)S(1)} collective-permute-done((bf16[512,1344]{0,1:T(8,128)(2,1)}, bf16[512,1344]{0,1:T(8,128)(2,1)S(1)}, u32[]{:S(2)}, u32[]{:S(2)}) %collective-permute-start.6) | collective-permute-done | bytes 1376288 | tf_op jit(solution)/shard_map/ppermute | solution.py:138
  388.2 86.5 %collective-permute-done.5 = bf16[512,1344]{0,1:T(8,128)(2,1)} collective-permute-done((bf16[512,1344]{0,1:T(8,128)(2,1)}, bf16[512,1344]{0,1:T(8,128)(2,1)}, u32[]{:S(2)}, u32[]{:S(2)}) %collective-permute-start.5) | collective-permute-done | bytes 1376288 | tf_op jit(solution)/shard_map/ppermute | solution.py:138
  474.6 4.4 collective-permute-done.4
  479.0 4.5 add_convert_fusion
  (81 shorter events, 58.0 us)
Async XLA Ops:
  7.2 103.3 %all-gather.2.cloned.1.call-start = ((), (), s32[]{:S(2)}) async-start(), calls=%async_computation.1 | async-start | bytes 6881280 | tf_op jit(solution)/shard_map/all_gather | solution.py:91
  7.9 475.6 %reduce-scatter.4.cloned.1.call-start = ((), (), s32[]{:S(2)}) async-start(), calls=%async_computation.2 | async-start | bytes 13762560
  110.5 7.4 %copy-start.10 = (bf16[512,5376]{0,1:T(8,128)(2,1)S(1)}, bf16[512,5376]{0,1:T(8,128)(2,1)}, u32[]{:S(2)}) copy-start(bf16[512,5376]{0,1:T(8,128)(2,1)} %all-gather.2.cloned.1.call-done) | copy-start | bytes 16515076
  110.5 20.0 %slice-start.4 = ((s8[11010048]{0:T(1024)(128)(4,1)}), s8[4194304]{0:T(1024)(128)(4,1)S(1)}, s32[]{:S(2)}) async-start(s8[11010048]{0:T(1024)(128)(4,1)} %bitcast.106), calls=%async_computation.7 | async-start | bytes 8388608
  110.5 20.0 %slice-start.5 = ((s8[11010048]{0:T(1024)(128)(4,1)}), s8[4194304]{0:T(1024)(128)(4,1)S(1)}, s32[]{:S(2)}) async-start(s8[11010048]{0:T(1024)(128)(4,1)} %bitcast.106), calls=%async_computation.8 | async-start | bytes 8388608
  117.9 12.7 %slice-start.6 = ((s8[11010048]{0:T(1024)(128)(4,1)}), s8[2621440]{0:T(1024)(128)(4,1)S(1)}, s32[]{:S(2)}) async-start(s8[11010048]{0:T(1024)(128)(4,1)} %bitcast.106), calls=%async_computation.9 | async-start | bytes 5242880
  123.7 24.0 %collective-permute-start.1 = (bf16[2,512,512]{2,1,0:T(8,128)(2,1)S(1)}, bf16[2,512,512]{2,1,0:T(8,128)(2,1)}, u32[]{:S(2)}, u32[]{:S(2)}) collective-permute-start(bf16[2,512,512]{2,1,0:T(8,128)(2,1)S(1)} %pad_maximum_fusion.1), channel_id=1, source_target_pairs={{0,4},{4,8},{8,12},{12,16},{16,20},{20,24},{24,28},{1,5},{5,9},{9,... | collective-permute-start | bytes 3145736 | tf_op jit(solution)/shard_map/ppermute | solution.py:21
  127.4 35.0 %collective-permute-start = (bf16[2,512,512]{2,1,0:T(8,128)(2,1)S(1)}, bf16[2,512,512]{2,1,0:T(8,128)(2,1)}, u32[]{:S(2)}, u32[]{:S(2)}) collective-permute-start(bf16[2,512,512]{2,1,0:T(8,128)(2,1)S(1)} %pad_maximum_fusion.1), channel_id=1, source_target_pairs={{0,8},{4,12},{8,16},{12,20},{16,24},{20,28},{1,9},{5,13},{9,17},{1... | collective-permute-start | bytes 3145736 | tf_op jit(solution)/shard_map/ppermute | solution.py:21
  166.9 17.6 %copy-start.2 = (bf16[1536,4,128,1]{0,2,3,1:T(8,128)(2,1)}, bf16[1536,4,128,1]{0,2,3,1:T(8,128)(2,1)S(1)}, u32[]{:S(2)}) copy-start(bf16[1536,4,128,1]{0,2,3,1:T(8,128)(2,1)S(1)} %copy.46) | copy-start | bytes 4718596
  184.5 12.6 %copy-start.5 = (bf16[1536,4,128]{2,1,0:T(4,128)(2,1)S(1)}, bf16[1536,4,128]{2,1,0:T(4,128)(2,1)}, u32[]{:S(2)}) copy-start(bf16[1536,4,128]{2,1,0:T(4,128)(2,1)} %reshape_squeeze.7) | copy-start | bytes 4718596
  184.5 12.6 %copy-start.6 = (bf16[512,1024]{0,1:T(8,128)(2,1)S(1)}, bf16[512,1024]{0,1:T(8,128)(2,1)}, u32[]{:S(2)}) copy-start(bf16[512,1024]{0,1:T(8,128)(2,1)} %copy.60) | copy-start | bytes 3145732
  240.8 4.8 copy-start.3
  241.0 27.9 %collective-permute-start.3 = (bf16[2,512,512]{1,2,0:T(8,128)(2,1)S(1)}, bf16[2,512,512]{1,2,0:T(8,128)(2,1)S(1)}, u32[]{:S(2)}, u32[]{:S(2)}) collective-permute-start(bf16[2,512,512]{1,2,0:T(8,128)(2,1)S(1)} %get-tuple-element.5), channel_id=1, source_target_pairs={{8,0},{12,4},{16,8},{20,12},{24,16},{28,20},{9,1},{13,5},{17,9},{2... | collective-permute-start | bytes 3145736 | tf_op jit(solution)/shard_map/ppermute | solution.py:21
  243.1 29.5 %copy-start = (f32[4,128,1536]{2,1,0:T(8,128)S(1)}, f32[4,128,1536]{2,1,0:T(8,128)}, u32[]{:S(2)}) copy-start(f32[4,128,1536]{2,1,0:T(8,128)} %fusion.15) | copy-start | bytes 9437188
  243.1 29.5 %copy-start.1 = (f32[4,1536,128,1]{1,2,3,0:T(8,128)S(1)}, f32[4,1536,128,1]{1,2,3,0:T(8,128)}, u32[]{:S(2)}) copy-start(f32[4,1536,128,1]{1,2,3,0:T(8,128)} %fusion.6) | copy-start | bytes 9437188
  243.1 29.4 %collective-permute-start.2 = (bf16[2,512,512]{1,2,0:T(8,128)(2,1)S(1)}, bf16[2,512,512]{1,2,0:T(8,128)(2,1)S(1)}, u32[]{:S(2)}, u32[]{:S(2)}) collective-permute-start(bf16[2,512,512]{1,2,0:T(8,128)(2,1)S(1)} %get-tuple-element.4), channel_id=1, source_target_pairs={{4,0},{8,4},{12,8},{16,12},{20,16},{24,20},{28,24},{5,1},{9,5},{13... | collective-permute-start | bytes 3145736 | tf_op jit(solution)/shard_map/ppermute | solution.py:21
  248.4 24.7 %copy-start.7 = (bf16[4,128,2,512]{3,1,2,0:T(8,128)(2,1)S(1)}, bf16[4,128,2,512]{3,1,2,0:T(8,128)(2,1)}, u32[]{:S(2)}) copy-start(bf16[4,128,2,512]{3,1,2,0:T(8,128)(2,1)} %multiply_convert_fusion.1) | copy-start | bytes 3145732
  307.3 17.2 %collective-permute-start.7 = (bf16[2048,4,672]{0,2,1:T(8,128)(2,1)}, bf16[2048,4,672]{0,2,1:T(8,128)(2,1)}, u32[]{:S(2)}, u32[]{:S(2)}) collective-permute-start(bf16[2048,4,672]{0,2,1:T(8,128)(2,1)} %fusion.11), channel_id=1, source_target_pairs={{0,4},{4,0},{1,5},{5,1},{2,6},{6,2},{3,7},{7,3},{8,12},{12,8},{9,1... | collective-permute-start | bytes 33030152 | tf_op jit(solution)/shard_map/ppermute | solution.py:149
  343.4 7.6 %slice-start.2 = ((s8[5505024]{0:T(1024)(128)(4,1)}), s8[4194304]{0:T(1024)(128)(4,1)S(1)}, s32[]{:S(2)}) async-start(s8[5505024]{0:T(1024)(128)(4,1)} %bitcast.94), calls=%async_computation.5 | async-start | bytes 8388608
  343.4 8.5 %slice-start = ((s8[5505024]{0:T(1024)(128)(4,1)}), s8[4194304]{0:T(1024)(128)(4,1)S(1)}, s32[]{:S(2)}) async-start(s8[5505024]{0:T(1024)(128)(4,1)} %bitcast.92), calls=%async_computation.3 | async-start | bytes 8388608
  347.0 5.0 %slice-start.1 = ((s8[5505024]{0:T(1024)(128)(4,1)}), s8[1310720]{0:T(1024)(128)(4,1)S(1)}, s32[]{:S(2)}) async-start(s8[5505024]{0:T(1024)(128)(4,1)} %bitcast.92), calls=%async_computation.4 | async-start | bytes 2621440
  354.0 34.2 %collective-permute-start.6 = (bf16[512,1344]{0,1:T(8,128)(2,1)}, bf16[512,1344]{0,1:T(8,128)(2,1)S(1)}, u32[]{:S(2)}, u32[]{:S(2)}) collective-permute-start(bf16[512,1344]{0,1:T(8,128)(2,1)} %fusion.21), channel_id=1, source_target_pairs={{0,1},{1,2},{2,3},{3,0},{4,5},{5,6},{6,7},{7,4},{8,9},{9,10},{10,1... | collective-permute-start | bytes 4128776 | tf_op jit(solution)/shard_map/ppermute | solution.py:138
  359.2 115.4 %collective-permute-start.5 = (bf16[512,1344]{0,1:T(8,128)(2,1)}, bf16[512,1344]{0,1:T(8,128)(2,1)}, u32[]{:S(2)}, u32[]{:S(2)}) collective-permute-start(bf16[512,1344]{0,1:T(8,128)(2,1)} %fusion.20), channel_id=1, source_target_pairs={{0,2},{1,3},{2,0},{3,1},{4,6},{5,7},{6,4},{7,5},{8,10},{9,11},{10,... | collective-permute-start | bytes 4128776 | tf_op jit(solution)/shard_map/ppermute | solution.py:138
  365.2 113.8 %collective-permute-start.4 = (bf16[512,1344]{0,1:T(8,128)(2,1)}, bf16[512,1344]{0,1:T(8,128)(2,1)}, u32[]{:S(2)}, u32[]{:S(2)}) collective-permute-start(bf16[512,1344]{0,1:T(8,128)(2,1)} %fusion.19), channel_id=1, source_target_pairs={{0,3},{1,0},{2,1},{3,2},{4,7},{5,4},{6,5},{7,6},{8,11},{9,8},{10,9... | collective-permute-start | bytes 4128776 | tf_op jit(solution)/shard_map/ppermute | solution.py:138
  (4 other events, 15.2 us)
Sparse Core Ops, SparseCore 0:
  9.6 100.8 all-gather.1
  340.1 107.2 reduce-scatter.3

commit v3 on v2

--- a/solution.py
+++ b/solution.py
@@ -140,14 +140,18 @@
     own = term(me).astype(jnp.float32)
     token_grad = (own if token_sum is None else token_sum + own).astype(jnp.bfloat16)
     proj_grads = jnp.concatenate([query_grad, key_grad, value_grad], axis=1)
-    weight_part = contract_first(proj_grads, gathered)
     n_hi = lax.axis_size("seq_hi")
-    quarter = weight_part.reshape(weight_part.shape[0], n_hi, 2, -1)
     core = lax.axis_index("core")
-    keep = lax.dynamic_index_in_dim(quarter, core, 2, keepdims=False)
-    give = lax.dynamic_index_in_dim(quarter, 1 - core, 2, keepdims=False).astype(jnp.bfloat16)
-    got = lax.ppermute(give, "core", [(0, 1), (1, 0)])
-    pair_sum = (keep + got.astype(jnp.float32)).astype(jnp.bfloat16)
+    swap = [(0, 1), (1, 0)]
+    halves = gathered.reshape(tok_rows, n_hi, 2, -1)
+    own_cols = lax.dynamic_index_in_dim(halves, core, 2, keepdims=False).reshape(tok_rows, -1)
+    partner_cols = lax.dynamic_index_in_dim(halves, 1 - core, 2, keepdims=False).reshape(tok_rows, -1)
+    partner_tokens = lax.ppermute(partner_cols, "core", swap)
+    partner_grads = lax.ppermute(proj_grads, "core", swap)
+    pair_tokens = jnp.concatenate([own_cols, partner_tokens], axis=0)
+    pair_grads = jnp.concatenate([proj_grads, partner_grads], axis=0)
+    pair_sum = contract_first(pair_grads, pair_tokens).astype(jnp.bfloat16)
+    pair_sum = pair_sum.reshape(pair_sum.shape[0], n_hi, -1)
     summed = lax.psum_scatter(pair_sum, "seq_hi", scatter_dimension=1, tiled=True)
     summed = summed.reshape(summed.shape[0], -1).astype(jnp.float32)
     summed = (summed * (tok_rows * lax.axis_size(SEQ)) ** (-0.5)).astype(jnp.bfloat16).T

time: 502 us -> 480 us (0.956)
  waiting for transfers between devices: 272 us -> 255 us
  other arithmetic: 43 us -> 27.8 us
  local copies, waits for them, and re-layouts: 25.5 us -> 36.3 us
    convert_element_type x1 -> x0, other arithmetic: 15.4 us -> none  [per_device(): pair_sum = (keep + got.astype(jnp.float32)).astype(jnp.bfloat16)]
    ppermute x1 -> x2, waiting for transfers between devices: 17.2 us -> 4.14 us  [the longest x1 4.14 us: per_device(): partner_grads = lax.ppermute(proj_grads, 'core', swap)]
    dynamic_slice x0 -> x1, local copies, waits for them, and re-layouts: none -> 5.4 us  [per_device(): lax.dynamic_index_in_dim(halves, core, 2, keepdims=False)]
  transfers between devices with their start and end apart: 10 -> 11, of which waited for: 9 -> 9; matrix products, arithmetic and copies ran while one was open for 9% -> 27% of each run, Pallas kernels for 0% -> 0%
where the time goes in v3:
time: 480 us; the launch traced here: 473 us
  waiting for transfers between devices  255 us (53%)
  matrix products  123 us (26%)
  local copies, waits for them, and re-layouts  36.3 us (8%)
  other arithmetic  27.8 us (6%)
  starting transfers between devices  16.1 us (3%)
  between operations  15 us (3%)
    ppermute x3, waiting for transfers between devices, per_device(): got = lax.ppermute(sent, 'head', pairs).astype(jnp.float32)  108 us
    all_gather x1, waiting for transfers between devices, per_device(): gathered = lax.all_gather(tokens, 'head', axis=1, tiled=True)  97.4 us
    ppermute x4, waiting for transfers between devices, passed_along(): return lax.ppermute(x, axis, pairs)  44.2 us
    dot_general x12, matrix products, contract_last(): lax.dot_general(left, right, (((1,), (1,)), ((), ())), preferred_element_...  29.6 us
    dot_general x1, matrix products, contract_first(): lax.dot_general(left, right, (((0,), (0,)), ((), ())), preferred_element_...  23.1 us
    convert_element_type x1, other arithmetic, attend(): dscores = (probs * (dprobs - center)).astype(jnp.bfloat16)  16.8 us
    dot_general x1, matrix products, attend(): jnp.einsum('akgd,ckd->kgac', grad_four, value_three, preferred_element_ty...  16.4 us
    convert_element_type x1, local copies, waits for them, and re-layouts, per_device(): pair_sum = contract_first(pair_grads, pair_tokens).astype(jnp.bfloat16)  15 us
  transfers between devices with their start and end apart: 11, of which 9 were waited for; matrix products, arithmetic and copies ran while one was open for 27% of the time, Pallas kernels for 0%

profile of v3, /device:TPU:11, one launch (start us, length us, event | category | flops | bytes accessed | tf_op | source)
XLA Modules:
  0.0 472.9 jit_solution(3988718019263584472)
XLA Ops:
  13.1 97.4 %all-gather.2.cloned.1.call-done = bf16[512,5376]{0,1:T(8,128)(2,1)} async-done(((bf16[512,1344]{0,1:T(8,128)(2,1)}), bf16[512,5376]{0,1:T(8,128)(2,1)}) %all-gather.2.cloned.1.call-update) | async-done | bytes 5505040 | tf_op jit(solution)/shard_map/all_gather | solution.py:91
  110.5 7.3 %fusion.58 = bf16[1,512,512]{2,1,0:T(8,128)(2,1)S(1)} fusion(bf16[512,5376]{0,1:T(8,128)(2,1)} %all-gather.2.cloned.1.call-done, bf16[5376,512]{1,0:T(8,128)(2,1)} %param.9), kind=kOutput, calls=%fused_computation.83 | convolution fusion | flops 2818834432 | bytes 11534336 | tf_op jit(solution)/shard_map/dot_general | solution.py:98
  117.9 5.8 %fusion.57 = bf16[1,512,512]{2,1,0:T(8,128)(2,1)S(1)} fusion(bf16[512,5376]{0,1:T(8,128)(2,1)S(1)} %copy-done.4, bf16[5376,512]{1,0:T(8,128)(2,1)} %param.8), kind=kOutput, calls=%fused_computation.82 | convolution fusion | flops 2818834432 | bytes 11534336 | tf_op jit(solution)/shard_map/dot_general | solution.py:95
  123.7 3.7 collective-permute-start.1
  130.6 5.9 %convolution_convert_fusion.1 = bf16[512,1024]{1,0:T(8,128)(2,1)S(1)} fusion(bf16[512,5376]{0,1:T(8,128)(2,1)S(1)} %copy-done.4, bf16[5376,1024]{1,0:T(8,128)(2,1)S(1)} %bitcast.105), kind=kOutput, calls=%fused_computation.71 | convolution fusion | flops 5637668864 | bytes 17563648 | tf_op jit(solution)/shard_map/dot_general | solution.py:92
  137.9 5.4 %constant_dynamic-slice_fusion.1 = (bf16[512,4,1,672]{0,3,2,1:T(8,128)(2,1)}, bf16[512,4,1,672]{0,3,2,1:T(8,128)(2,1)}) fusion(bf16[512,4,2,672]{0,3,2,1:T(8,128)(2,1)} %bitcast.89, s32[]{:T(128)S(6)} %select_n.66, s32[]{:T(128)S(6)} %select_n.67), kind=kLoop, calls=%fused_computation.91 | loop fusion | bytes 11010056 | tf_op jit(solution)/shard_map/jit(dynamic_index_in_dim)/dynamic_slice | solution.py:147
  143.3 4.5 collective-permute-done.1
  147.8 14.6 %collective-permute-done = bf16[2,512,512]{2,1,0:T(8,128)(2,1)} collective-permute-done((bf16[2,512,512]{2,1,0:T(8,128)(2,1)S(1)}, bf16[2,512,512]{2,1,0:T(8,128)(2,1)}, u32[]{:S(2)}, u32[]{:S(2)}) %collective-permute-start) | collective-permute-done | bytes 1048608 | tf_op jit(solution)/shard_map/ppermute | solution.py:21
  167.0 4.0 reshape_squeeze.7
  171.0 13.6 %fusion.77 = (f32[4,2,512]{2,1,0:T(2,128)S(1)}, f32[4,2,512,1536]{2,3,1,0:T(8,128)}) fusion(pred[512,1536]{0,1:T(8,128)(4,1)S(1)} %copy-done.10, bf16[1536,4,128,1]{0,2,3,1:T(8,128)(2,1)S(1)} %copy.45, bf16[512,4,2,128]{0,3,2,1:T(8,128)(2,1)S(1)} %bitcast.93), kind=kOutput, calls=%fused_computation.111 | convolution fusion | flops 1642071552 | bytes 28590080 | tf_op jit(solution)/shard_map/sub | solution.py:61
  184.6 12.7 %fusion.5 = f32[4,1536,128,1]{1,2,3,0:T(8,128)} fusion(bf16[512,4,2,128]{0,3,2,1:T(8,128)(2,1)} %bitcast.102, f32[4,2,512,1536]{2,3,1,0:T(8,128)} %get-tuple-element.15, f32[4,2,512]{2,1,0:T(2,128)S(1)} %get-tuple-element.14), kind=kOutput, calls=%fused_computation.9 | convolution fusion | flops 1623195648 | bytes 29376512 | tf_op jit(solution)/shard_map/kgac,akgd->ckd/dot_general | solution.py:81
  197.3 16.4 %fusion.1 = (f32[4,2,512]{2,1,0:T(2,128)S(1)}, f32[4,1536,512,2]{2,1,3,0:T(8,128)}) fusion(f32[4,2,512,1536]{2,3,1,0:T(8,128)} %get-tuple-element.15, f32[4,2,512]{2,1,0:T(2,128)S(1)} %get-tuple-element.14, bf16[512,4,2,128]{0,3,2,1:T(8,128)(2,1)S(1)} %bitcast.103, bf16[1536,4,128,1]{2,1,0,3:T(4,128)(2,1)S(1)} %bitcast.101), kind=kOutput, calls=%fused_computation.3 | convolution fusion | flops 1629483008 | bytes 52985856 | tf_op jit(solution)/shard_map/akgd,ckd->kgac/dot_general | solution.py:63
  213.7 16.8 %fusion.3 = bf16[4,2,512,1536]{2,3,1,0:T(8,128)(2,1)S(1)} fusion(f32[4,1536,512,2]{2,1,3,0:T(8,128)} %get-tuple-element.17, f32[4,2,512]{2,1,0:T(2,128)S(1)} %get-tuple-element.16, f32[4,2,512,1536]{2,3,1,0:T(8,128)} %get-tuple-element.15, f32[4,2,512]{2,1,0:T(2,128)S(1)} %get-tuple-element.14), kind=kLoop, calls=%fused_computation.5 | loop fusion | flops 25165824 | bytes 62947328 | tf_op jit(solution)/shard_map/convert_element_type | solution.py:67
  230.6 7.0 %fusion.23 = f32[4,128,1536]{2,1,0:T(8,128)} fusion(bf16[512,4,2,128]{0,3,2,1:T(8,128)(2,1)} %bitcast.92, bf16[4,2,512,1536]{2,3,1,0:T(8,128)(2,1)S(1)} %fusion.3), kind=kOutput, calls=%fused_computation.43 | convolution fusion | flops 1611399168 | bytes 16777216 | tf_op jit(solution)/shard_map/kgac,akgd->ckd/dot_general | solution.py:78
  247.6 21.4 %collective-permute-done.3 = bf16[2,512,512]{1,2,0:T(8,128)(2,1)S(1)} collective-permute-done((bf16[2,512,512]{1,2,0:T(8,128)(2,1)S(1)}, bf16[2,512,512]{1,2,0:T(8,128)(2,1)S(1)}, u32[]{:S(2)}, u32[]{:S(2)}) %collective-permute-start.3) | collective-permute-done | bytes 1048608 | tf_op jit(solution)/shard_map/ppermute | solution.py:21
  269.1 3.6 collective-permute-done.2
  273.5 4.1 collective-permute-done.7
  279.0 23.1 %convolution_convert_fusion = bf16[2048,2688]{1,0:T(8,128)(2,1)} fusion(bf16[512,2688]{0,1:T(8,128)(2,1)} %collective-permute-done.8, bf16[512,2688]{0,1:T(8,128)(2,1)} %bitcast.100, bf16[512,2048]{0,1:T(8,128)(2,1)} %copy-done.12, bf16[512,512]{0,1:T(8,128)(2,1)S(1)} %get-tuple-element.13, bf16[512,512]{0,1:T(8,128)(2,1)S(1)} %get-tuple-element.12, ...), kind=kOutput, calls=%fused_computation.15 | convolution fusion | flops 11307581440 | bytes 20709376 | tf_op jit(solution)/shard_map/dot_general | solution.py:31
  302.1 15.0 %copy.42 = bf16[2048,2688]{0,1:T(8,128)(2,1)} copy(bf16[2048,2688]{1,0:T(8,128)(2,1)} %convolution_convert_fusion) | data formatting | bytes 22020096 | tf_op jit(solution)/shard_map/convert_element_type | solution.py:153
  321.7 3.5 fusion.37
  325.2 4.0 fusion.39
  348.1 17.3 %collective-permute-done.6 = bf16[512,1344]{0,1:T(8,128)(2,1)S(1)} collective-permute-done((bf16[512,1344]{0,1:T(8,128)(2,1)}, bf16[512,1344]{0,1:T(8,128)(2,1)S(1)}, u32[]{:S(2)}, u32[]{:S(2)}) %collective-permute-start.6) | collective-permute-done | bytes 1376288 | tf_op jit(solution)/shard_map/ppermute | solution.py:138
  365.4 87.4 %collective-permute-done.5 = bf16[512,1344]{0,1:T(8,128)(2,1)} collective-permute-done((bf16[512,1344]{0,1:T(8,128)(2,1)}, bf16[512,1344]{0,1:T(8,128)(2,1)}, u32[]{:S(2)}, u32[]{:S(2)}) %collective-permute-start.5) | collective-permute-done | bytes 1376288 | tf_op jit(solution)/shard_map/ppermute | solution.py:138
  456.3 4.5 add_convert_fusion
  (88 shorter events, 58.8 us)
Async XLA Ops:
  7.2 103.3 %all-gather.2.cloned.1.call-start = ((), (), s32[]{:S(2)}) async-start(), calls=%async_computation.1 | async-start | bytes 6881280 | tf_op jit(solution)/shard_map/all_gather | solution.py:91
  7.9 452.9 %reduce-scatter.4.cloned.1.call-start = ((), (), s32[]{:S(2)}) async-start(), calls=%async_computation.2 | async-start | bytes 13762560
  110.5 7.4 %copy-start.4 = (bf16[512,5376]{0,1:T(8,128)(2,1)S(1)}, bf16[512,5376]{0,1:T(8,128)(2,1)}, u32[]{:S(2)}) copy-start(bf16[512,5376]{0,1:T(8,128)(2,1)} %all-gather.2.cloned.1.call-done) | copy-start | bytes 16515076
  110.5 20.0 %slice-start.4 = ((s8[11010048]{0:T(1024)(128)(4,1)}), s8[4194304]{0:T(1024)(128)(4,1)S(1)}, s32[]{:S(2)}) async-start(s8[11010048]{0:T(1024)(128)(4,1)} %bitcast.104), calls=%async_computation.7 | async-start | bytes 8388608
  110.5 20.0 %slice-start.5 = ((s8[11010048]{0:T(1024)(128)(4,1)}), s8[4194304]{0:T(1024)(128)(4,1)S(1)}, s32[]{:S(2)}) async-start(s8[11010048]{0:T(1024)(128)(4,1)} %bitcast.104), calls=%async_computation.8 | async-start | bytes 8388608
  117.9 12.7 %slice-start.6 = ((s8[11010048]{0:T(1024)(128)(4,1)}), s8[2621440]{0:T(1024)(128)(4,1)S(1)}, s32[]{:S(2)}) async-start(s8[11010048]{0:T(1024)(128)(4,1)} %bitcast.104), calls=%async_computation.9 | async-start | bytes 5242880
  123.7 24.0 %collective-permute-start.1 = (bf16[2,512,512]{2,1,0:T(8,128)(2,1)S(1)}, bf16[2,512,512]{2,1,0:T(8,128)(2,1)}, u32[]{:S(2)}, u32[]{:S(2)}) collective-permute-start(bf16[2,512,512]{2,1,0:T(8,128)(2,1)S(1)} %pad_maximum_fusion.2), channel_id=1, source_target_pairs={{0,4},{4,8},{8,12},{12,16},{16,20},{20,24},{24,28},{1,5},{5,9},{9,... | collective-permute-start | bytes 3145736 | tf_op jit(solution)/shard_map/ppermute | solution.py:21
  127.4 35.0 %collective-permute-start = (bf16[2,512,512]{2,1,0:T(8,128)(2,1)S(1)}, bf16[2,512,512]{2,1,0:T(8,128)(2,1)}, u32[]{:S(2)}, u32[]{:S(2)}) collective-permute-start(bf16[2,512,512]{2,1,0:T(8,128)(2,1)S(1)} %pad_maximum_fusion.2), channel_id=1, source_target_pairs={{0,8},{4,12},{8,16},{12,20},{16,24},{20,28},{1,9},{5,13},{9,17},{1... | collective-permute-start | bytes 3145736 | tf_op jit(solution)/shard_map/ppermute | solution.py:21
  143.3 130.2 %collective-permute-start.8 = (bf16[512,2688]{0,1:T(8,128)(2,1)}, bf16[512,2688]{0,1:T(8,128)(2,1)}, u32[]{:S(2)}, u32[]{:S(2)}) collective-permute-start(bf16[512,2688]{0,1:T(8,128)(2,1)} %bitcast.22), channel_id=1, source_target_pairs={{0,4},{4,0},{1,5},{5,1},{2,6},{6,2},{3,7},{7,3},{8,12},{12,8},{9,1... | collective-permute-start | bytes 8257544 | tf_op jit(solution)/shard_map/ppermute | solution.py:149
  166.9 17.7 %copy-start.2 = (bf16[1536,4,128,1]{0,2,3,1:T(8,128)(2,1)}, bf16[1536,4,128,1]{0,2,3,1:T(8,128)(2,1)S(1)}, u32[]{:S(2)}) copy-start(bf16[1536,4,128,1]{0,2,3,1:T(8,128)(2,1)S(1)} %copy.45) | copy-start | bytes 4718596
  184.6 12.7 %copy-start.8 = (bf16[1536,4,128]{2,1,0:T(4,128)(2,1)S(1)}, bf16[1536,4,128]{2,1,0:T(4,128)(2,1)}, u32[]{:S(2)}) copy-start(bf16[1536,4,128]{2,1,0:T(4,128)(2,1)} %reshape_squeeze.7) | copy-start | bytes 4718596
  184.6 12.7 %copy-start.9 = (bf16[512,1024]{0,1:T(8,128)(2,1)S(1)}, bf16[512,1024]{0,1:T(8,128)(2,1)}, u32[]{:S(2)}) copy-start(bf16[512,1024]{0,1:T(8,128)(2,1)} %copy.58) | copy-start | bytes 3145732
  241.2 27.9 %collective-permute-start.3 = (bf16[2,512,512]{1,2,0:T(8,128)(2,1)S(1)}, bf16[2,512,512]{1,2,0:T(8,128)(2,1)S(1)}, u32[]{:S(2)}, u32[]{:S(2)}) collective-permute-start(bf16[2,512,512]{1,2,0:T(8,128)(2,1)S(1)} %get-tuple-element.7), channel_id=1, source_target_pairs={{8,0},{12,4},{16,8},{20,12},{24,16},{28,20},{9,1},{13,5},{17,9},{2... | collective-permute-start | bytes 3145736 | tf_op jit(solution)/shard_map/ppermute | solution.py:21
  243.5 29.2 %copy-start = (f32[4,128,1536]{2,1,0:T(8,128)S(1)}, f32[4,128,1536]{2,1,0:T(8,128)}, u32[]{:S(2)}) copy-start(f32[4,128,1536]{2,1,0:T(8,128)} %fusion.23) | copy-start | bytes 9437188
  243.5 29.2 %copy-start.1 = (f32[4,1536,128,1]{1,2,3,0:T(8,128)S(1)}, f32[4,1536,128,1]{1,2,3,0:T(8,128)}, u32[]{:S(2)}) copy-start(f32[4,1536,128,1]{1,2,3,0:T(8,128)} %fusion.5) | copy-start | bytes 9437188
  243.5 29.2 %collective-permute-start.2 = (bf16[2,512,512]{1,2,0:T(8,128)(2,1)S(1)}, bf16[2,512,512]{1,2,0:T(8,128)(2,1)S(1)}, u32[]{:S(2)}, u32[]{:S(2)}) collective-permute-start(bf16[2,512,512]{1,2,0:T(8,128)(2,1)S(1)} %get-tuple-element.6), channel_id=1, source_target_pairs={{4,0},{8,4},{12,8},{16,12},{20,16},{24,20},{28,24},{5,1},{9,5},{13... | collective-permute-start | bytes 3145736 | tf_op jit(solution)/shard_map/ppermute | solution.py:21
  247.6 25.6 %copy-start.6 = (bf16[4,128,2,512]{3,1,2,0:T(8,128)(2,1)}, bf16[4,128,2,512]{3,1,2,0:T(8,128)(2,1)S(1)}, u32[]{:S(2)}) copy-start(bf16[4,128,2,512]{3,1,2,0:T(8,128)(2,1)S(1)} %multiply_convert_fusion.1) | copy-start | bytes 3145732
  273.4 4.2 collective-permute-start.7
  321.6 7.6 %slice-start.2 = ((s8[5505024]{0:T(1024)(128)(4,1)}), s8[4194304]{0:T(1024)(128)(4,1)S(1)}, s32[]{:S(2)}) async-start(s8[5505024]{0:T(1024)(128)(4,1)} %bitcast.90), calls=%async_computation.5 | async-start | bytes 8388608
  321.6 8.5 %slice-start = ((s8[5505024]{0:T(1024)(128)(4,1)}), s8[4194304]{0:T(1024)(128)(4,1)S(1)}, s32[]{:S(2)}) async-start(s8[5505024]{0:T(1024)(128)(4,1)} %bitcast.87), calls=%async_computation.3 | async-start | bytes 8388608
  325.2 5.0 %slice-start.1 = ((s8[5505024]{0:T(1024)(128)(4,1)}), s8[1310720]{0:T(1024)(128)(4,1)S(1)}, s32[]{:S(2)}) async-start(s8[5505024]{0:T(1024)(128)(4,1)} %bitcast.87), calls=%async_computation.4 | async-start | bytes 2621440
  332.2 33.2 %collective-permute-start.6 = (bf16[512,1344]{0,1:T(8,128)(2,1)}, bf16[512,1344]{0,1:T(8,128)(2,1)S(1)}, u32[]{:S(2)}, u32[]{:S(2)}) collective-permute-start(bf16[512,1344]{0,1:T(8,128)(2,1)} %fusion.29), channel_id=1, source_target_pairs={{0,1},{1,2},{2,3},{3,0},{4,5},{5,6},{6,7},{7,4},{8,9},{9,10},{10,1... | collective-permute-start | bytes 4128776 | tf_op jit(solution)/shard_map/ppermute | solution.py:138
  337.3 115.5 %collective-permute-start.5 = (bf16[512,1344]{0,1:T(8,128)(2,1)}, bf16[512,1344]{0,1:T(8,128)(2,1)}, u32[]{:S(2)}, u32[]{:S(2)}) collective-permute-start(bf16[512,1344]{0,1:T(8,128)(2,1)} %fusion.28), channel_id=1, source_target_pairs={{0,2},{1,3},{2,0},{3,1},{4,6},{5,7},{6,4},{7,5},{8,10},{9,11},{10,... | collective-permute-start | bytes 4128776 | tf_op jit(solution)/shard_map/ppermute | solution.py:138
  342.5 113.8 %collective-permute-start.4 = (bf16[512,1344]{0,1:T(8,128)(2,1)}, bf16[512,1344]{0,1:T(8,128)(2,1)}, u32[]{:S(2)}, u32[]{:S(2)}) collective-permute-start(bf16[512,1344]{0,1:T(8,128)(2,1)} %fusion.27), channel_id=1, source_target_pairs={{0,3},{1,0},{2,1},{3,2},{4,7},{5,4},{6,5},{7,6},{8,11},{9,8},{10,9... | collective-permute-start | bytes 4128776 | tf_op jit(solution)/shard_map/ppermute | solution.py:138
  (7 other events, 22.7 us)
Sparse Core Ops, SparseCore 0:
  9.6 100.8 all-gather.1
  317.2 107.2 reduce-scatter.3

commit v4 on v3

--- a/solution.py
+++ b/solution.py
@@ -139,27 +139,26 @@
         token_sum = got if token_sum is None else token_sum + got
     own = term(me).astype(jnp.float32)
     token_grad = (own if token_sum is None else token_sum + own).astype(jnp.bfloat16)
-    proj_grads = jnp.concatenate([query_grad, key_grad, value_grad], axis=1)
     n_hi = lax.axis_size("seq_hi")
     core = lax.axis_index("core")
     swap = [(0, 1), (1, 0)]
     halves = gathered.reshape(tok_rows, n_hi, 2, -1)
     own_cols = lax.dynamic_index_in_dim(halves, core, 2, keepdims=False).reshape(tok_rows, -1)
     partner_cols = lax.dynamic_index_in_dim(halves, 1 - core, 2, keepdims=False).reshape(tok_rows, -1)
-    partner_tokens = lax.ppermute(partner_cols, "core", swap)
-    partner_grads = lax.ppermute(proj_grads, "core", swap)
-    pair_tokens = jnp.concatenate([own_cols, partner_tokens], axis=0)
-    pair_grads = jnp.concatenate([proj_grads, partner_grads], axis=0)
-    pair_sum = contract_first(pair_grads, pair_tokens).astype(jnp.bfloat16)
-    pair_sum = pair_sum.reshape(pair_sum.shape[0], n_hi, -1)
-    summed = lax.psum_scatter(pair_sum, "seq_hi", scatter_dimension=1, tiled=True)
-    summed = summed.reshape(summed.shape[0], -1).astype(jnp.float32)
-    summed = (summed * (tok_rows * lax.axis_size(SEQ)) ** (-0.5)).astype(jnp.bfloat16).T
-    q_width = query_weight.shape[1]
+    pair_tokens = jnp.concatenate([own_cols, lax.ppermute(partner_cols, "core", swap)], axis=0)
+    weight_scale = (tok_rows * lax.axis_size(SEQ)) ** (-0.5)
+
+    def weight_grad(grads):
+        pair_grads = jnp.concatenate([grads, lax.ppermute(grads, "core", swap)], axis=0)
+        pair_sum = contract_first(pair_grads, pair_tokens).astype(jnp.bfloat16)
+        summed = lax.psum_scatter(pair_sum, "seq_hi", scatter_dimension=1, tiled=True)
+        return (summed.astype(jnp.float32) * weight_scale).astype(jnp.bfloat16).T
+
+    query_weight_grad = weight_grad(query_grad)
+    kv_weight_grad = weight_grad(jnp.concatenate([key_grad, value_grad], axis=1))
     k_width = key_weight.shape[1]
-    query_weight_grad = summed[:, :q_width]
-    key_weight_grad = summed[:, q_width : q_width + k_width]
-    value_weight_grad = summed[:, q_width + k_width :]
+    key_weight_grad = kv_weight_grad[:, :k_width]
+    value_weight_grad = kv_weight_grad[:, k_width:]
     return (token_grad, query_weight_grad, key_weight_grad, value_weight_grad)
 
 

time: 480 us -> 500 us (1.042)
  waiting for transfers between devices: 255 us -> 292 us
  local copies, waits for them, and re-layouts: 36.3 us -> 21.6 us
    ppermute x4, waiting for transfers between devices: 44.2 us -> 81.7 us  [passed_along(): return lax.ppermute(x, axis, pairs)]
    convert_element_type x1 -> x0, local copies, waits for them, and re-layouts: 15 us -> none  [per_device(): pair_sum = contract_first(pair_grads, pair_tokens).astype(jnp.bfloat16)]
    dot_general x1 -> x2, matrix products: 23.1 us -> 21.5 us  [contract_first(): lax.dot_general(left, right, (((0,), (0,)), ((), ())), preferred_element_...]
  transfers between devices with their start and end apart: 11 -> 13, of which waited for: 9 -> 10; matrix products, arithmetic and copies ran while one was open for 27% -> 29% of each run, Pallas kernels for 0% -> 0%
where the time goes in v4:
time: 500 us; the launch traced here: 493 us
  waiting for transfers between devices  292 us (58%)
  matrix products  123 us (25%)
  other arithmetic  26.8 us (5%)
  local copies, waits for them, and re-layouts  21.6 us (4%)
  starting transfers between devices  14.9 us (3%)
  between operations  14.7 us (3%)
    ppermute x3, waiting for transfers between devices, per_device(): got = lax.ppermute(sent, 'head', pairs).astype(jnp.float32)  107 us
    all_gather x1, waiting for transfers between devices, per_device(): gathered = lax.all_gather(tokens, 'head', axis=1, tiled=True)  97.4 us
    ppermute x4, waiting for transfers between devices, passed_along(): return lax.ppermute(x, axis, pairs)  81.7 us
    dot_general x12, matrix products, contract_last(): lax.dot_general(left, right, (((1,), (1,)), ((), ())), preferred_element_...  29.6 us
    dot_general x2, matrix products, contract_first(): lax.dot_general(left, right, (((0,), (0,)), ((), ())), preferred_element_...  21.5 us
    dot_general x1, matrix products, attend(): jnp.einsum('akgd,ckd->kgac', grad_four, value_three, preferred_element_ty...  17.8 us
    convert_element_type x1, other arithmetic, attend(): dscores = (probs * (dprobs - center)).astype(jnp.bfloat16)  16.8 us
    sub x1, matrix products, attend(): expo = jnp.where(allowed, jnp.exp(masked - row_max), 0.0)  13.6 us
  transfers between devices with their start and end apart: 13, of which 10 were waited for; matrix products, arithmetic and copies ran while one was open for 29% of the time, Pallas kernels for 0%

profile of v4, /device:TPU:11, one launch (start us, length us, event | category | flops | bytes accessed | tf_op | source)
XLA Modules:
  0.0 492.8 jit_solution(1891360205692647250)
XLA Ops:
  13.1 97.4 %all-gather.2.cloned.1.call-done = bf16[512,5376]{0,1:T(8,128)(2,1)} async-done(((bf16[512,1344]{0,1:T(8,128)(2,1)}), bf16[512,5376]{0,1:T(8,128)(2,1)}) %all-gather.2.cloned.1.call-update) | async-done | bytes 5505040 | tf_op jit(solution)/shard_map/all_gather | solution.py:91
  110.5 7.3 %fusion.57 = bf16[1,512,512]{2,1,0:T(8,128)(2,1)S(1)} fusion(bf16[512,5376]{0,1:T(8,128)(2,1)} %all-gather.2.cloned.1.call-done, bf16[5376,512]{1,0:T(8,128)(2,1)} %param.9), kind=kOutput, calls=%fused_computation.84 | convolution fusion | flops 2818834432 | bytes 11534336 | tf_op jit(solution)/shard_map/dot_general | solution.py:98
  117.9 5.8 %fusion.56 = bf16[1,512,512]{2,1,0:T(8,128)(2,1)S(1)} fusion(bf16[512,5376]{0,1:T(8,128)(2,1)S(1)} %copy-done.1, bf16[5376,512]{1,0:T(8,128)(2,1)} %param.8), kind=kOutput, calls=%fused_computation.83 | convolution fusion | flops 2818834432 | bytes 11534336 | tf_op jit(solution)/shard_map/dot_general | solution.py:95
  123.7 3.7 collective-permute-start.1
  130.6 5.9 %convolution_convert_fusion.2 = bf16[512,1024]{1,0:T(8,128)(2,1)S(1)} fusion(bf16[512,5376]{0,1:T(8,128)(2,1)S(1)} %copy-done.1, bf16[5376,1024]{1,0:T(8,128)(2,1)S(1)} %bitcast.103), kind=kOutput, calls=%fused_computation.70 | convolution fusion | flops 5637668864 | bytes 17563648 | tf_op jit(solution)/shard_map/dot_general | solution.py:92
  137.9 5.4 %constant_dynamic-slice_fusion.1 = (bf16[512,4,1,672]{0,3,2,1:T(8,128)(2,1)}, bf16[512,4,1,672]{0,3,2,1:T(8,128)(2,1)}) fusion(bf16[512,4,2,672]{0,3,2,1:T(8,128)(2,1)} %bitcast.86, s32[]{:T(128)S(6)} %select_n.66, s32[]{:T(128)S(6)} %select_n.67), kind=kLoop, calls=%fused_computation.93 | loop fusion | bytes 11010056 | tf_op jit(solution)/shard_map/jit(dynamic_index_in_dim)/dynamic_slice | solution.py:146
  143.3 4.5 collective-permute-done.1
  147.8 14.6 %collective-permute-done = bf16[2,512,512]{2,1,0:T(8,128)(2,1)} collective-permute-done((bf16[2,512,512]{2,1,0:T(8,128)(2,1)S(1)}, bf16[2,512,512]{2,1,0:T(8,128)(2,1)}, u32[]{:S(2)}, u32[]{:S(2)}) %collective-permute-start) | collective-permute-done | bytes 1048608 | tf_op jit(solution)/shard_map/ppermute | solution.py:21
  166.9 3.6 reshape_squeeze.7
  170.6 13.6 %fusion.77 = (f32[4,2,512]{2,1,0:T(2,128)S(1)}, f32[4,2,512,1536]{2,3,1,0:T(8,128)}) fusion(pred[512,1536]{0,1:T(8,128)(4,1)S(1)} %copy-done.8, bf16[1536,4,128,1]{0,2,3,1:T(8,128)(2,1)S(1)} %copy.22, bf16[512,4,2,128]{0,3,2,1:T(8,128)(2,1)S(1)} %bitcast.89), kind=kOutput, calls=%fused_computation.114 | convolution fusion | flops 1642071552 | bytes 28590080 | tf_op jit(solution)/shard_map/sub | solution.py:61
  184.2 17.8 %fusion.1 = (f32[4,2,512]{2,1,0:T(2,128)S(1)}, f32[4,1536,512,2]{2,1,3,0:T(8,128)}) fusion(f32[4,2,512,1536]{2,3,1,0:T(8,128)} %get-tuple-element.15, f32[4,2,512]{2,1,0:T(2,128)S(1)} %get-tuple-element.14, bf16[512,4,2,128]{0,3,2,1:T(8,128)(2,1)} %bitcast.94, bf16[1536,4,128,1]{2,1,0,3:T(4,128)(2,1)} %bitcast.93), kind=kOutput, calls=%fused_computation.3 | convolution fusion | flops 1629483008 | bytes 52985856 | tf_op jit(solution)/shard_map/akgd,ckd->kgac/dot_general | solution.py:63
  202.0 16.8 %fusion.3 = bf16[4,2,512,1536]{2,3,1,0:T(8,128)(2,1)S(1)} fusion(f32[4,1536,512,2]{2,1,3,0:T(8,128)} %get-tuple-element.17, f32[4,2,512]{2,1,0:T(2,128)S(1)} %get-tuple-element.16, f32[4,2,512,1536]{2,3,1,0:T(8,128)} %get-tuple-element.15, f32[4,2,512]{2,1,0:T(2,128)S(1)} %get-tuple-element.14), kind=kLoop, calls=%fused_computation.5 | loop fusion | flops 25165824 | bytes 62947328 | tf_op jit(solution)/shard_map/convert_element_type | solution.py:67
  226.7 9.6 %convolution_convert_fusion.1 = bf16[1024,2688]{0,1:T(8,128)(2,1)} fusion(bf16[512,2688]{0,1:T(8,128)(2,1)} %collective-permute-done.8, bf16[512,2688]{0,1:T(8,128)(2,1)S(1)} %bitcast.91, bf16[512,1024]{0,1:T(8,128)(2,1)S(1)} %collective-permute-done.7, bf16[512,1024]{0,1:T(8,128)(2,1)S(1)} %bitcast.97), kind=kOutput, calls=%fused_computation.21 | convolution fusion | flops 5655101440 | bytes 13107200 | tf_op jit(solution)/shard_map/dot_general | solution.py:31
  236.6 8.7 %fusion.13 = f32[4,128,1536]{2,1,0:T(8,128)S(1)} fusion(bf16[512,4,2,128]{0,3,2,1:T(8,128)(2,1)S(1)} %bitcast.90, bf16[4,2,512,1536]{2,3,1,0:T(8,128)(2,1)} %copy-done), kind=kOutput, calls=%fused_computation.34 | convolution fusion | flops 1611399168 | bytes 16777216 | tf_op jit(solution)/shard_map/kgac,akgd->ckd/dot_general | solution.py:78
  245.3 10.7 %fusion.5 = f32[4,1536,128,1]{1,2,3,0:T(8,128)S(1)} fusion(bf16[512,4,2,128]{0,3,2,1:T(8,128)(2,1)S(1)} %bitcast.95, f32[4,2,512,1536]{2,3,1,0:T(8,128)} %get-tuple-element.15, f32[4,2,512]{2,1,0:T(2,128)S(1)} %get-tuple-element.14), kind=kOutput, calls=%fused_computation.9 | convolution fusion | flops 1623195648 | bytes 29376512 | tf_op jit(solution)/shard_map/kgac,akgd->ckd/dot_general | solution.py:81
  260.8 36.7 %collective-permute-done.3 = bf16[2,512,512]{1,2,0:T(8,128)(2,1)S(1)} collective-permute-done((bf16[2,512,512]{1,2,0:T(8,128)(2,1)S(1)}, bf16[2,512,512]{1,2,0:T(8,128)(2,1)S(1)}, u32[]{:S(2)}, u32[]{:S(2)}) %collective-permute-start.3) | collective-permute-done | bytes 1048608 | tf_op jit(solution)/shard_map/ppermute | solution.py:21
  297.5 25.9 %collective-permute-done.2 = bf16[2,512,512]{1,2,0:T(8,128)(2,1)S(1)} collective-permute-done((bf16[2,512,512]{1,2,0:T(8,128)(2,1)S(1)}, bf16[2,512,512]{1,2,0:T(8,128)(2,1)S(1)}, u32[]{:S(2)}, u32[]{:S(2)}) %collective-permute-start.2) | collective-permute-done | bytes 1048608 | tf_op jit(solution)/shard_map/ppermute | solution.py:21
  326.7 11.9 %convolution_convert_fusion = bf16[1024,2688]{0,1:T(8,128)(2,1)} fusion(bf16[512,2688]{0,1:T(8,128)(2,1)} %collective-permute-done.8, bf16[512,2688]{0,1:T(8,128)(2,1)S(1)} %bitcast.92, bf16[512,1024]{0,1:T(8,128)(2,1)S(1)} %collective-permute-done.9, bf16[512,512]{0,1:T(8,128)(2,1)S(1)} %get-tuple-element.13, bf16[512,512]{0,1:T(8,128)(2,1)S(1)} %get-tuple-element.12), kind=kOutput, calls=%fused_computation.20 | convolution fusion | flops 5657198592 | bytes 13107200 | tf_op jit(solution)/shard_map/dot_general | solution.py:31
  343.3 3.5 fusion.26
  346.8 4.0 fusion.28
  363.3 3.4 fusion.22
  368.9 17.0 %collective-permute-done.6 = bf16[512,1344]{0,1:T(8,128)(2,1)S(1)} collective-permute-done((bf16[512,1344]{0,1:T(8,128)(2,1)}, bf16[512,1344]{0,1:T(8,128)(2,1)S(1)}, u32[]{:S(2)}, u32[]{:S(2)}) %collective-permute-start.6) | collective-permute-done | bytes 1376288 | tf_op jit(solution)/shard_map/ppermute | solution.py:138
  385.9 87.5 %collective-permute-done.5 = bf16[512,1344]{0,1:T(8,128)(2,1)} collective-permute-done((bf16[512,1344]{0,1:T(8,128)(2,1)}, bf16[512,1344]{0,1:T(8,128)(2,1)}, u32[]{:S(2)}, u32[]{:S(2)}) %collective-permute-start.5) | collective-permute-done | bytes 1376288 | tf_op jit(solution)/shard_map/ppermute | solution.py:138
  475.8 4.5 add_convert_fusion
  (87 shorter events, 58.3 us)
Async XLA Ops:
  7.2 103.3 %all-gather.2.cloned.1.call-start = ((), (), s32[]{:S(2)}) async-start(), calls=%async_computation.2 | async-start | bytes 6881280 | tf_op jit(solution)/shard_map/all_gather | solution.py:91
  7.9 472.4 %reduce-scatter.3.cloned.1.call-start = ((), (), s32[]{:S(2)}) async-start(), calls=%async_computation.3 | async-start | bytes 6881280 | tf_op jit(solution)/shard_map/reduce_scatter | solution.py:154
  110.5 7.4 %copy-start.1 = (bf16[512,5376]{0,1:T(8,128)(2,1)S(1)}, bf16[512,5376]{0,1:T(8,128)(2,1)}, u32[]{:S(2)}) copy-start(bf16[512,5376]{0,1:T(8,128)(2,1)} %all-gather.2.cloned.1.call-done) | copy-start | bytes 16515076
  110.5 20.0 %slice-start.4 = ((s8[11010048]{0:T(1024)(128)(4,1)}), s8[4194304]{0:T(1024)(128)(4,1)S(1)}, s32[]{:S(2)}) async-start(s8[11010048]{0:T(1024)(128)(4,1)} %bitcast.102), calls=%async_computation.9 | async-start | bytes 8388608
  110.5 20.0 %slice-start.5 = ((s8[11010048]{0:T(1024)(128)(4,1)}), s8[4194304]{0:T(1024)(128)(4,1)S(1)}, s32[]{:S(2)}) async-start(s8[11010048]{0:T(1024)(128)(4,1)} %bitcast.102), calls=%async_computation.10 | async-start | bytes 8388608
  117.9 12.7 %slice-start.6 = ((s8[11010048]{0:T(1024)(128)(4,1)}), s8[2621440]{0:T(1024)(128)(4,1)S(1)}, s32[]{:S(2)}) async-start(s8[11010048]{0:T(1024)(128)(4,1)} %bitcast.102), calls=%async_computation.11 | async-start | bytes 5242880
  123.7 24.0 %collective-permute-start.1 = (bf16[2,512,512]{2,1,0:T(8,128)(2,1)S(1)}, bf16[2,512,512]{2,1,0:T(8,128)(2,1)}, u32[]{:S(2)}, u32[]{:S(2)}) collective-permute-start(bf16[2,512,512]{2,1,0:T(8,128)(2,1)S(1)} %pad_maximum_fusion.4), channel_id=1, source_target_pairs={{0,4},{4,8},{8,12},{12,16},{16,20},{20,24},{24,28},{1,5},{5,9},{9,... | collective-permute-start | bytes 3145736 | tf_op jit(solution)/shard_map/ppermute | solution.py:21
  127.4 35.0 %collective-permute-start = (bf16[2,512,512]{2,1,0:T(8,128)(2,1)S(1)}, bf16[2,512,512]{2,1,0:T(8,128)(2,1)}, u32[]{:S(2)}, u32[]{:S(2)}) collective-permute-start(bf16[2,512,512]{2,1,0:T(8,128)(2,1)S(1)} %pad_maximum_fusion.4), channel_id=1, source_target_pairs={{0,8},{4,12},{8,16},{12,20},{16,24},{20,28},{1,9},{5,13},{9,17},{1... | collective-permute-start | bytes 3145736 | tf_op jit(solution)/shard_map/ppermute | solution.py:21
  143.3 83.4 %collective-permute-start.8 = (bf16[512,2688]{0,1:T(8,128)(2,1)}, bf16[512,2688]{0,1:T(8,128)(2,1)}, u32[]{:S(2)}, u32[]{:S(2)}) collective-permute-start(bf16[512,2688]{0,1:T(8,128)(2,1)} %bitcast.22), channel_id=1, source_target_pairs={{0,4},{4,0},{1,5},{5,1},{2,6},{6,2},{3,7},{7,3},{8,12},{12,8},{9,1... | collective-permute-start | bytes 8257544 | tf_op jit(solution)/shard_map/ppermute | solution.py:148
  218.8 5.2 %copy-start = (bf16[4,2,512,1536]{2,3,1,0:T(8,128)(2,1)}, bf16[4,2,512,1536]{2,3,1,0:T(8,128)(2,1)S(1)}, u32[]{:S(2)}) copy-start(bf16[4,2,512,1536]{2,3,1,0:T(8,128)(2,1)S(1)} %fusion.3) | copy-start | bytes 37748740
  218.9 7.8 %copy-start.3 = (bf16[512,4,1,672]{0,3,2,1:T(8,128)(2,1)S(1)}, bf16[512,4,1,672]{0,3,2,1:T(8,128)(2,1)}, u32[]{:S(2)}) copy-start(bf16[512,4,1,672]{0,3,2,1:T(8,128)(2,1)} %get-tuple-element.4) | copy-start | bytes 8257540
  224.0 2.7 collective-permute-start.7
  236.3 9.0 %copy-start.5 = (bf16[512,1024]{0,1:T(8,128)(2,1)S(1)}, bf16[512,1024]{0,1:T(8,128)(2,1)}, u32[]{:S(2)}) copy-start(bf16[512,1024]{0,1:T(8,128)(2,1)} %copy.35) | copy-start | bytes 3145732
  236.3 246.8 %reduce-scatter.5.cloned.1.call-start = ((), (), s32[]{:S(2)}) async-start(), calls=%async_computation.4 | async-start | bytes 6881280 | tf_op jit(solution)/shard_map/reduce_scatter | solution.py:154
  256.9 40.6 %collective-permute-start.3 = (bf16[2,512,512]{1,2,0:T(8,128)(2,1)S(1)}, bf16[2,512,512]{1,2,0:T(8,128)(2,1)S(1)}, u32[]{:S(2)}, u32[]{:S(2)}) collective-permute-start(bf16[2,512,512]{1,2,0:T(8,128)(2,1)S(1)} %get-tuple-element.7), channel_id=1, source_target_pairs={{8,0},{12,4},{16,8},{20,12},{24,16},{28,20},{9,1},{13,5},{17,9},{2... | collective-permute-start | bytes 3145736 | tf_op jit(solution)/shard_map/ppermute | solution.py:21
  258.8 64.6 %collective-permute-start.2 = (bf16[2,512,512]{1,2,0:T(8,128)(2,1)S(1)}, bf16[2,512,512]{1,2,0:T(8,128)(2,1)S(1)}, u32[]{:S(2)}, u32[]{:S(2)}) collective-permute-start(bf16[2,512,512]{1,2,0:T(8,128)(2,1)S(1)} %get-tuple-element.6), channel_id=1, source_target_pairs={{4,0},{8,4},{12,8},{16,12},{20,16},{24,20},{28,24},{5,1},{9,5},{13... | collective-permute-start | bytes 3145736 | tf_op jit(solution)/shard_map/ppermute | solution.py:21
  324.0 2.7 collective-permute-start.9
  343.2 7.6 %slice-start.2 = ((s8[5505024]{0:T(1024)(128)(4,1)}), s8[4194304]{0:T(1024)(128)(4,1)S(1)}, s32[]{:S(2)}) async-start(s8[5505024]{0:T(1024)(128)(4,1)} %bitcast.87), calls=%async_computation.7 | async-start | bytes 8388608
  343.2 8.5 %slice-start = ((s8[5505024]{0:T(1024)(128)(4,1)}), s8[4194304]{0:T(1024)(128)(4,1)S(1)}, s32[]{:S(2)}) async-start(s8[5505024]{0:T(1024)(128)(4,1)} %bitcast.84), calls=%async_computation.5 | async-start | bytes 8388608
  346.8 4.1 slice-start.3
  346.8 5.0 %slice-start.1 = ((s8[5505024]{0:T(1024)(128)(4,1)}), s8[1310720]{0:T(1024)(128)(4,1)S(1)}, s32[]{:S(2)}) async-start(s8[5505024]{0:T(1024)(128)(4,1)} %bitcast.84), calls=%async_computation.6 | async-start | bytes 2621440
  353.8 32.2 %collective-permute-start.6 = (bf16[512,1344]{0,1:T(8,128)(2,1)}, bf16[512,1344]{0,1:T(8,128)(2,1)S(1)}, u32[]{:S(2)}, u32[]{:S(2)}) collective-permute-start(bf16[512,1344]{0,1:T(8,128)(2,1)} %fusion.19), channel_id=1, source_target_pairs={{0,1},{1,2},{2,3},{3,0},{4,5},{5,6},{6,7},{7,4},{8,9},{9,10},{10,1... | collective-permute-start | bytes 4128776 | tf_op jit(solution)/shard_map/ppermute | solution.py:138
  358.0 115.4 %collective-permute-start.5 = (bf16[512,1344]{0,1:T(8,128)(2,1)}, bf16[512,1344]{0,1:T(8,128)(2,1)}, u32[]{:S(2)}, u32[]{:S(2)}) collective-permute-start(bf16[512,1344]{0,1:T(8,128)(2,1)} %fusion.18), channel_id=1, source_target_pairs={{0,2},{1,3},{2,0},{3,1},{4,6},{5,7},{6,4},{7,5},{8,10},{9,11},{10,... | collective-permute-start | bytes 4128776 | tf_op jit(solution)/shard_map/ppermute | solution.py:138
  362.0 113.8 %collective-permute-start.4 = (bf16[512,1344]{0,1:T(8,128)(2,1)}, bf16[512,1344]{0,1:T(8,128)(2,1)}, u32[]{:S(2)}, u32[]{:S(2)}) collective-permute-start(bf16[512,1344]{0,1:T(8,128)(2,1)} %fusion.17), channel_id=1, source_target_pairs={{0,3},{1,0},{2,1},{3,2},{4,7},{5,4},{6,5},{7,6},{8,11},{9,8},{10,9... | collective-permute-start | bytes 4128776 | tf_op jit(solution)/shard_map/ppermute | solution.py:138
  (6 other events, 17.2 us)
Sparse Core Ops, SparseCore 0:
  9.6 100.8 all-gather.1
  236.4 84.8 reduce-scatter.2
  338.8 62.9 reduce-scatter.4

commit v5 on v2

--- a/solution.py
+++ b/solution.py
@@ -140,17 +140,19 @@
     own = term(me).astype(jnp.float32)
     token_grad = (own if token_sum is None else token_sum + own).astype(jnp.bfloat16)
     proj_grads = jnp.concatenate([query_grad, key_grad, value_grad], axis=1)
-    weight_part = contract_first(proj_grads, gathered)
-    n_hi = lax.axis_size("seq_hi")
-    quarter = weight_part.reshape(weight_part.shape[0], n_hi, 2, -1)
-    core = lax.axis_index("core")
-    keep = lax.dynamic_index_in_dim(quarter, core, 2, keepdims=False)
-    give = lax.dynamic_index_in_dim(quarter, 1 - core, 2, keepdims=False).astype(jnp.bfloat16)
-    got = lax.ppermute(give, "core", [(0, 1), (1, 0)])
-    pair_sum = (keep + got.astype(jnp.float32)).astype(jnp.bfloat16)
-    summed = lax.psum_scatter(pair_sum, "seq_hi", scatter_dimension=1, tiled=True)
-    summed = summed.reshape(summed.shape[0], -1).astype(jnp.float32)
-    summed = (summed * (tok_rows * lax.axis_size(SEQ)) ** (-0.5)).astype(jnp.bfloat16).T
+    weight_part = contract_first(proj_grads, gathered).astype(jnp.bfloat16)
+    n_seq = lax.axis_size(SEQ)
+    block = weight_part.shape[1] // n_seq
+
+    def weight_block(dest):
+        return lax.dynamic_slice_in_dim(weight_part, dest * block, block, 1)
+
+    weight_sum = weight_block(position).astype(jnp.float32)
+    for shift in range(n_seq - 1, 0, -1):
+        sent = weight_block((position + shift) % n_seq)
+        pairs = [(i, (i + shift) % n_seq) for i in range(n_seq)]
+        weight_sum = weight_sum + lax.ppermute(sent, SEQ, pairs).astype(jnp.float32)
+    summed = (weight_sum * (tok_rows * n_seq) ** (-0.5)).astype(jnp.bfloat16).T
     q_width = query_weight.shape[1]
     k_width = key_weight.shape[1]
     query_weight_grad = summed[:, :q_width]

time: 502 us -> 646 us (1.29)
  waiting for transfers between devices: 272 us -> 419 us
  other arithmetic: 43 us -> 32.4 us
    ppermute x1 -> x7, waiting for transfers between devices: 17.2 us -> 196 us  [per_device(): weight_sum = weight_sum + lax.ppermute(sent, SEQ, pairs).astype(jnp.float32)]
    ppermute x3, waiting for transfers between devices: 108 us -> 83.1 us  [per_device(): got = lax.ppermute(sent, 'head', pairs).astype(jnp.float32)]
    convert_element_type x1 -> x0, other arithmetic: 15.4 us -> none  [per_device(): pair_sum = (keep + got.astype(jnp.float32)).astype(jnp.bfloat16)]
    dynamic_slice x0 -> x1, local copies, waits for them, and re-layouts: none -> 12.4 us  [weight_block(): return lax.dynamic_slice_in_dim(weight_part, dest * block, block, 1)]
    convert_element_type x1 -> x0, local copies, waits for them, and re-layouts: 12.1 us -> none  [per_device(): lax.dynamic_index_in_dim(quarter, 1 - core, 2, keepdims=False)]
    transpose x1, other arithmetic: 2.39 us -> 9.95 us  [per_device(): summed = (weight_sum * (tok_rows * n_seq) ** (-0.5)).astype(jnp.bfloat16).T]
    ppermute x4, waiting for transfers between devices: 48.6 us -> 42 us  [passed_along(): return lax.ppermute(x, axis, pairs)]
  transfers between devices with their start and end apart: 10 -> 15, of which waited for: 9 -> 10; matrix products, arithmetic and copies ran while one was open for 9% -> 11% of each run, Pallas kernels for 0% -> 0%
where the time goes in v5:
time: 646 us; the launch traced here: 638 us
  waiting for transfers between devices  419 us (65%)
  matrix products  124 us (19%)
  other arithmetic  32.4 us (5%)
  local copies, waits for them, and re-layouts  26.8 us (4%)
  starting transfers between devices  20.4 us (3%)
  between operations  15.1 us (2%)
    ppermute x7, waiting for transfers between devices, per_device(): weight_sum = weight_sum + lax.ppermute(sent, SEQ, pairs).astype(jnp.float32)  196 us
    all_gather x1, waiting for transfers between devices, per_device(): gathered = lax.all_gather(tokens, 'head', axis=1, tiled=True)  97.4 us
    ppermute x3, waiting for transfers between devices, per_device(): got = lax.ppermute(sent, 'head', pairs).astype(jnp.float32)  83.1 us
    ppermute x4, waiting for transfers between devices, passed_along(): return lax.ppermute(x, axis, pairs)  42 us
    dot_general x12, matrix products, contract_last(): lax.dot_general(left, right, (((1,), (1,)), ((), ())), preferred_element_...  34 us
    dot_general x1, matrix products, contract_first(): lax.dot_general(left, right, (((0,), (0,)), ((), ())), preferred_element_...  19.3 us
    dot_general x1, matrix products, attend(): jnp.einsum('akgd,ckd->kgac', grad_four, value_three, preferred_element_ty...  17.5 us
    convert_element_type x1, other arithmetic, attend(): dscores = (probs * (dprobs - center)).astype(jnp.bfloat16)  17 us
  transfers between devices with their start and end apart: 15, of which 10 were waited for; matrix products, arithmetic and copies ran while one was open for 11% of the time, Pallas kernels for 0%

profile of v5, /device:TPU:11, one launch (start us, length us, event | category | flops | bytes accessed | tf_op | source)
XLA Modules:
  0.0 638.3 jit_solution(9430814455776416603)
XLA Ops:
  13.1 97.4 %all-gather.2.cloned.1.call-done = bf16[512,5376]{0,1:T(8,128)(2,1)} async-done(((bf16[512,1344]{0,1:T(8,128)(2,1)}), bf16[512,5376]{0,1:T(8,128)(2,1)}) %all-gather.2.cloned.1.call-update) | async-done | bytes 5505040 | tf_op jit(solution)/shard_map/all_gather | solution.py:91
  110.5 7.4 %fusion.53 = bf16[1,512,512]{2,1,0:T(8,128)(2,1)S(1)} fusion(bf16[512,5376]{0,1:T(8,128)(2,1)} %all-gather.2.cloned.1.call-done, bf16[5376,512]{1,0:T(8,128)(2,1)} %param.9), kind=kOutput, calls=%fused_computation.77 | convolution fusion | flops 2818834432 | bytes 11534336 | tf_op jit(solution)/shard_map/dot_general | solution.py:98
  117.9 5.7 fusion.52
  123.7 3.7 collective-permute-start.1
  130.6 5.9 convolution_convert_fusion.1
  137.9 9.9 %collective-permute-done.1 = bf16[2,512,512]{2,1,0:T(8,128)(2,1)} collective-permute-done((bf16[2,512,512]{2,1,0:T(8,128)(2,1)S(1)}, bf16[2,512,512]{2,1,0:T(8,128)(2,1)}, u32[]{:S(2)}, u32[]{:S(2)}) %collective-permute-start.1) | collective-permute-done | bytes 1048608 | tf_op jit(solution)/shard_map/ppermute | solution.py:21
  147.8 14.6 %collective-permute-done = bf16[2,512,512]{2,1,0:T(8,128)(2,1)} collective-permute-done((bf16[2,512,512]{2,1,0:T(8,128)(2,1)S(1)}, bf16[2,512,512]{2,1,0:T(8,128)(2,1)}, u32[]{:S(2)}, u32[]{:S(2)}) %collective-permute-start) | collective-permute-done | bytes 1048608 | tf_op jit(solution)/shard_map/ppermute | solution.py:21
  167.0 4.0 reshape_squeeze.7
  171.0 13.6 %fusion.72 = (f32[4,2,512]{2,1,0:T(2,128)S(1)}, f32[4,2,512,1536]{2,3,1,0:T(8,128)}) fusion(pred[512,1536]{0,1:T(8,128)(4,1)S(1)} %copy-done.11, bf16[1536,4,128,1]{0,2,3,1:T(8,128)(2,1)S(1)} %copy.63, bf16[512,4,2,128]{0,3,2,1:T(8,128)(2,1)S(1)} %bitcast.81), kind=kOutput, calls=%fused_computation.110 | convolution fusion | flops 1642071552 | bytes 28590080 | tf_op jit(solution)/shard_map/sub | solution.py:61
  184.6 17.5 %fusion.1 = (f32[4,2,512]{2,1,0:T(2,128)S(1)}, f32[4,1536,512,2]{2,1,3,0:T(8,128)}) fusion(f32[4,2,512,1536]{2,3,1,0:T(8,128)} %get-tuple-element.28, f32[4,2,512]{2,1,0:T(2,128)S(1)} %get-tuple-element.27, bf16[512,4,2,128]{0,3,2,1:T(8,128)(2,1)} %bitcast.83, bf16[1536,4,128,1]{2,1,0,3:T(4,128)(2,1)} %bitcast.82), kind=kOutput, calls=%fused_computation.3 | convolution fusion | flops 1629483008 | bytes 52985856 | tf_op jit(solution)/shard_map/akgd,ckd->kgac/dot_general | solution.py:63
  202.1 17.0 %fusion.3 = bf16[4,2,512,1536]{2,3,1,0:T(8,128)(2,1)S(1)} fusion(f32[4,1536,512,2]{2,1,3,0:T(8,128)} %get-tuple-element.30, f32[4,2,512]{2,1,0:T(2,128)S(1)} %get-tuple-element.29, f32[4,2,512,1536]{2,3,1,0:T(8,128)} %get-tuple-element.28, f32[4,2,512]{2,1,0:T(2,128)S(1)} %get-tuple-element.27), kind=kLoop, calls=%fused_computation.5 | loop fusion | flops 25165824 | bytes 62947328 | tf_op jit(solution)/shard_map/convert_element_type | solution.py:67
  221.9 7.0 %fusion.13 = f32[4,128,1536]{2,1,0:T(8,128)} fusion(bf16[512,4,2,128]{0,3,2,1:T(8,128)(2,1)} %bitcast.80, bf16[4,2,512,1536]{2,3,1,0:T(8,128)(2,1)S(1)} %fusion.3), kind=kOutput, calls=%fused_computation.33 | convolution fusion | flops 1611399168 | bytes 16777216 | tf_op jit(solution)/shard_map/kgac,akgd->ckd/dot_general | solution.py:78
  228.9 11.0 %fusion.5 = f32[4,1536,128,1]{1,2,3,0:T(8,128)S(1)} fusion(bf16[512,4,2,128]{0,3,2,1:T(8,128)(2,1)} %bitcast.84, f32[4,2,512,1536]{2,3,1,0:T(8,128)} %get-tuple-element.28, f32[4,2,512]{2,1,0:T(2,128)S(1)} %get-tuple-element.27), kind=kOutput, calls=%fused_computation.10 | convolution fusion | flops 1623195648 | bytes 29376512 | tf_op jit(solution)/shard_map/kgac,akgd->ckd/dot_general | solution.py:81
  244.9 3.5 fusion.25
  254.9 13.9 %collective-permute-done.3 = bf16[2,512,512]{1,2,0:T(8,128)(2,1)S(1)} collective-permute-done((bf16[2,512,512]{1,2,0:T(8,128)(2,1)S(1)}, bf16[2,512,512]{1,2,0:T(8,128)(2,1)S(1)}, u32[]{:S(2)}, u32[]{:S(2)}) %collective-permute-start.3) | collective-permute-done | bytes 1048608 | tf_op jit(solution)/shard_map/ppermute | solution.py:21
  268.8 3.7 collective-permute-done.2
  281.7 19.3 %convolution_convert_fusion = bf16[2048,5376]{0,1:T(8,128)(2,1)} fusion(bf16[512,5376]{0,1:T(8,128)(2,1)} %all-gather.2.cloned.1.call-done, bf16[512,512]{0,1:T(8,128)(2,1)} %get-tuple-element.26, bf16[512,512]{0,1:T(8,128)(2,1)} %get-tuple-element.25, bf16[512,1024]{0,1:T(8,128)(2,1)S(1)} %bitcast.88), kind=kOutput, calls=%fused_computation.8 | convolution fusion | flops 11291590656 | bytes 29622272 | tf_op jit(solution)/shard_map/dot_general | solution.py:31
  301.0 12.4 %constant_dynamic-slice_fusion.6 = (bf16[2048,672]{0,1:T(8,128)(2,1)}, bf16[2048,672]{0,1:T(8,128)(2,1)S(1)}, bf16[2048,672]{0,1:T(8,128)(2,1)S(1)}, bf16[2048,6...) fusion(bf16[2048,5376]{0,1:T(8,128)(2,1)} %convolution_convert_fusion, ...), kind=kLoop, calls=%fused_computation.89 | loop fusion | bytes 38535196 | tf_op jit(solution)/shard_map/dynamic_slice | solution.py:148
  326.8 82.6 %collective-permute-done.5 = bf16[512,1344]{0,1:T(8,128)(2,1)S(1)} collective-permute-done((bf16[512,1344]{0,1:T(8,128)(2,1)S(1)}, bf16[512,1344]{0,1:T(8,128)(2,1)S(1)}, u32[]{:S(2)}, u32[]{:S(2)}) %collective-permute-start.5) | collective-permute-done | bytes 1376288 | tf_op jit(solution)/shard_map/ppermute | solution.py:138
  412.8 17.2 %collective-permute-done.12 = bf16[2048,672]{0,1:T(8,128)(2,1)} collective-permute-done((bf16[2048,672]{0,1:T(8,128)(2,1)S(1)}, bf16[2048,672]{0,1:T(8,128)(2,1)}, u32[]{:S(2)}, u32[]{:S(2)}) %collective-permute-start.12) | collective-permute-done | bytes 2752544 | tf_op jit(solution)/shard_map/ppermute | solution.py:154
  436.1 3.7 add_convert_fusion
  439.8 148.7 %collective-permute-done.10 = bf16[2048,672]{0,1:T(8,128)(2,1)} collective-permute-done((bf16[2048,672]{0,1:T(8,128)(2,1)}, bf16[2048,672]{0,1:T(8,128)(2,1)}, u32[]{:S(2)}, u32[]{:S(2)}) %collective-permute-start.10) | collective-permute-done | bytes 2752544 | tf_op jit(solution)/shard_map/ppermute | solution.py:154
  588.5 30.1 %collective-permute-done.9 = bf16[2048,672]{0,1:T(8,128)(2,1)} collective-permute-done((bf16[2048,672]{0,1:T(8,128)(2,1)}, bf16[2048,672]{0,1:T(8,128)(2,1)}, u32[]{:S(2)}, u32[]{:S(2)}) %collective-permute-start.9) | collective-permute-done | bytes 2752544 | tf_op jit(solution)/shard_map/ppermute | solution.py:154
  618.6 9.9 %fusion.22 = bf16[672,2048]{1,0:T(8,128)(2,1)S(1)} fusion(bf16[2048,672]{0,1:T(8,128)(2,1)} %collective-permute-done.13, bf16[2048,672]{0,1:T(8,128)(2,1)} %collective-permute-done.12, bf16[2048,672]{0,1:T(8,128)(2,1)} %collective-permute-done.11, bf16[2048,672]{0,1:T(8,128)(2,1)} %collective-permute-done.10, bf16[2048,672]{0,1:T(8,128)(2,1)} %collective-permute-done.9, ...), kind=kLoop, calls=%fused_computation.43 | loop fusion | flops 23396352 | bytes 24772612 | tf_op jit(solution)/shard_map/transpose | solution.py:155
  (92 shorter events, 63.5 us)
Async XLA Ops:
  7.2 103.3 %all-gather.2.cloned.1.call-start = ((), (), s32[]{:S(2)}) async-start(), calls=%async_computation | async-start | bytes 6881280 | tf_op jit(solution)/shard_map/all_gather | solution.py:91
  110.5 20.0 %slice-start = ((s8[11010048]{0:T(1024)(128)(4,1)}), s8[4194304]{0:T(1024)(128)(4,1)S(1)}, s32[]{:S(2)}) async-start(s8[11010048]{0:T(1024)(128)(4,1)} %bitcast.90), calls=%async_computation.1 | async-start | bytes 8388608
  110.5 20.0 %slice-start.1 = ((s8[11010048]{0:T(1024)(128)(4,1)}), s8[4194304]{0:T(1024)(128)(4,1)S(1)}, s32[]{:S(2)}) async-start(s8[11010048]{0:T(1024)(128)(4,1)} %bitcast.90), calls=%async_computation.2 | async-start | bytes 8388608
  117.9 12.7 %slice-start.2 = ((s8[11010048]{0:T(1024)(128)(4,1)}), s8[2621440]{0:T(1024)(128)(4,1)S(1)}, s32[]{:S(2)}) async-start(s8[11010048]{0:T(1024)(128)(4,1)} %bitcast.90), calls=%async_computation.3 | async-start | bytes 5242880
  123.7 24.1 %collective-permute-start.1 = (bf16[2,512,512]{2,1,0:T(8,128)(2,1)S(1)}, bf16[2,512,512]{2,1,0:T(8,128)(2,1)}, u32[]{:S(2)}, u32[]{:S(2)}) collective-permute-start(bf16[2,512,512]{2,1,0:T(8,128)(2,1)S(1)} %pad_maximum_fusion.1), channel_id=1, source_target_pairs={{0,4},{4,8},{8,12},{12,16},{16,20},{20,24},{24,28},{1,5},{5,9},{9,... | collective-permute-start | bytes 3145736 | tf_op jit(solution)/shard_map/ppermute | solution.py:21
  127.4 35.0 %collective-permute-start = (bf16[2,512,512]{2,1,0:T(8,128)(2,1)S(1)}, bf16[2,512,512]{2,1,0:T(8,128)(2,1)}, u32[]{:S(2)}, u32[]{:S(2)}) collective-permute-start(bf16[2,512,512]{2,1,0:T(8,128)(2,1)S(1)} %pad_maximum_fusion.1), channel_id=1, source_target_pairs={{0,8},{4,12},{8,16},{12,20},{16,24},{20,28},{1,9},{5,13},{9,17},{1... | collective-permute-start | bytes 3145736 | tf_op jit(solution)/shard_map/ppermute | solution.py:21
  166.9 17.7 %copy-start.1 = (bf16[1536,4,128,1]{0,2,3,1:T(8,128)(2,1)}, bf16[1536,4,128,1]{0,2,3,1:T(8,128)(2,1)S(1)}, u32[]{:S(2)}) copy-start(bf16[1536,4,128,1]{0,2,3,1:T(8,128)(2,1)S(1)} %copy.63) | copy-start | bytes 4718596
  202.1 17.0 %copy-start.2 = (bf16[1536,4,128,1]{0,2,3,1:T(8,128)(2,1)S(1)}, bf16[1536,4,128,1]{0,2,3,1:T(8,128)(2,1)}, u32[]{:S(2)}) copy-start(bf16[1536,4,128,1]{0,2,3,1:T(8,128)(2,1)} %copy-done.1) | copy-start | bytes 4718596
  228.9 11.0 %copy-start = (f32[4,128,1536]{2,1,0:T(8,128)S(1)}, f32[4,128,1536]{2,1,0:T(8,128)}, u32[]{:S(2)}) copy-start(f32[4,128,1536]{2,1,0:T(8,128)} %fusion.13) | copy-start | bytes 9437188
  240.8 28.0 %collective-permute-start.3 = (bf16[2,512,512]{1,2,0:T(8,128)(2,1)S(1)}, bf16[2,512,512]{1,2,0:T(8,128)(2,1)S(1)}, u32[]{:S(2)}, u32[]{:S(2)}) collective-permute-start(bf16[2,512,512]{1,2,0:T(8,128)(2,1)S(1)} %get-tuple-element.20), channel_id=1, source_target_pairs={{8,0},{12,4},{16,8},{20,12},{24,16},{28,20},{9,1},{13,5},{17,9},{2... | collective-permute-start | bytes 3145736 | tf_op jit(solution)/shard_map/ppermute | solution.py:21
  243.0 29.5 %collective-permute-start.2 = (bf16[2,512,512]{1,2,0:T(8,128)(2,1)S(1)}, bf16[2,512,512]{1,2,0:T(8,128)(2,1)S(1)}, u32[]{:S(2)}, u32[]{:S(2)}) collective-permute-start(bf16[2,512,512]{1,2,0:T(8,128)(2,1)S(1)} %get-tuple-element.19), channel_id=1, source_target_pairs={{4,0},{8,4},{12,8},{16,12},{20,16},{24,20},{28,24},{5,1},{9,5},{13... | collective-permute-start | bytes 3145736 | tf_op jit(solution)/shard_map/ppermute | solution.py:21
  279.5 47.3 %collective-permute-start.6 = (bf16[512,1344]{0,1:T(8,128)(2,1)}, bf16[512,1344]{0,1:T(8,128)(2,1)S(1)}, u32[]{:S(2)}, u32[]{:S(2)}) collective-permute-start(bf16[512,1344]{0,1:T(8,128)(2,1)} %fusion.19), channel_id=1, source_target_pairs={{0,1},{1,2},{2,3},{3,0},{4,5},{5,6},{6,7},{7,4},{8,9},{9,10},{10,1... | collective-permute-start | bytes 4128776 | tf_op jit(solution)/shard_map/ppermute | solution.py:138
  301.0 13.7 %copy-start.5 = (f32[512,1344]{0,1:T(8,128)S(1)}, f32[512,1344]{0,1:T(8,128)}, u32[]{:S(2)}) copy-start(f32[512,1344]{0,1:T(8,128)} %fusion.27) | copy-start | bytes 8257540
  313.4 98.2 %collective-permute-start.13 = (bf16[2048,672]{0,1:T(8,128)(2,1)S(1)}, bf16[2048,672]{0,1:T(8,128)(2,1)}, u32[]{:S(2)}, u32[]{:S(2)}) collective-permute-start(bf16[2048,672]{0,1:T(8,128)(2,1)S(1)} %get-tuple-element.13), channel_id=1, source_target_pairs={{0,4},{4,8},{8,12},{12,16},{16,20},{20,24},{24,28},{28,0},{1,5},{5... | collective-permute-start | bytes 8257544 | tf_op jit(solution)/shard_map/ppermute | solution.py:154
  313.6 116.4 %collective-permute-start.12 = (bf16[2048,672]{0,1:T(8,128)(2,1)S(1)}, bf16[2048,672]{0,1:T(8,128)(2,1)}, u32[]{:S(2)}, u32[]{:S(2)}) collective-permute-start(bf16[2048,672]{0,1:T(8,128)(2,1)S(1)} %get-tuple-element.14), channel_id=1, source_target_pairs={{0,8},{4,12},{8,16},{12,20},{16,24},{20,28},{24,0},{28,4},{1,9},{5... | collective-permute-start | bytes 8257544 | tf_op jit(solution)/shard_map/ppermute | solution.py:154
  319.4 90.1 %collective-permute-start.5 = (bf16[512,1344]{0,1:T(8,128)(2,1)S(1)}, bf16[512,1344]{0,1:T(8,128)(2,1)S(1)}, u32[]{:S(2)}, u32[]{:S(2)}) collective-permute-start(bf16[512,1344]{0,1:T(8,128)(2,1)S(1)} %fusion.18), channel_id=1, source_target_pairs={{0,2},{1,3},{2,0},{3,1},{4,6},{5,7},{6,4},{7,5},{8,10},{9,11},{10,... | collective-permute-start | bytes 4128776 | tf_op jit(solution)/shard_map/ppermute | solution.py:138
  326.7 83.3 %collective-permute-start.4 = (bf16[512,1344]{0,1:T(8,128)(2,1)S(1)}, bf16[512,1344]{0,1:T(8,128)(2,1)S(1)}, u32[]{:S(2)}, u32[]{:S(2)}) collective-permute-start(bf16[512,1344]{0,1:T(8,128)(2,1)S(1)} %fusion.17), channel_id=1, source_target_pairs={{0,3},{1,0},{2,1},{3,2},{4,7},{5,4},{6,5},{7,6},{8,11},{9,8},{10,9... | collective-permute-start | bytes 4128776 | tf_op jit(solution)/shard_map/ppermute | solution.py:138
  326.8 113.0 %collective-permute-start.11 = (bf16[2048,672]{0,1:T(8,128)(2,1)}, bf16[2048,672]{0,1:T(8,128)(2,1)}, u32[]{:S(2)}, u32[]{:S(2)}) collective-permute-start(bf16[2048,672]{0,1:T(8,128)(2,1)} %get-tuple-element.15), channel_id=1, source_target_pairs={{0,12},{4,16},{8,20},{12,24},{16,28},{20,0},{24,4},{28,8},{1,13},{... | collective-permute-start | bytes 8257544 | tf_op jit(solution)/shard_map/ppermute | solution.py:154
  409.4 20.5 %copy-start.6 = (bf16[512,1344]{0,1:T(8,128)(2,1)}, bf16[512,1344]{0,1:T(8,128)(2,1)S(1)}, u32[]{:S(2)}) copy-start(bf16[512,1344]{0,1:T(8,128)(2,1)S(1)} %collective-permute-done.5) | copy-start | bytes 4128772
  409.4 179.0 %collective-permute-start.10 = (bf16[2048,672]{0,1:T(8,128)(2,1)}, bf16[2048,672]{0,1:T(8,128)(2,1)}, u32[]{:S(2)}, u32[]{:S(2)}) collective-permute-start(bf16[2048,672]{0,1:T(8,128)(2,1)} %get-tuple-element.16), channel_id=1, source_target_pairs={{0,16},{4,20},{8,24},{12,28},{16,0},{20,4},{24,8},{28,12},{1,17},{... | collective-permute-start | bytes 8257544 | tf_op jit(solution)/shard_map/ppermute | solution.py:154
  410.0 20.0 %copy-start.8 = (bf16[512,1344]{0,1:T(8,128)(2,1)}, bf16[512,1344]{0,1:T(8,128)(2,1)S(1)}, u32[]{:S(2)}) copy-start(bf16[512,1344]{0,1:T(8,128)(2,1)S(1)} %collective-permute-done.4) | copy-start | bytes 4128772
  410.0 208.6 %collective-permute-start.9 = (bf16[2048,672]{0,1:T(8,128)(2,1)}, bf16[2048,672]{0,1:T(8,128)(2,1)}, u32[]{:S(2)}, u32[]{:S(2)}) collective-permute-start(bf16[2048,672]{0,1:T(8,128)(2,1)} %get-tuple-element.17), channel_id=1, source_target_pairs={{0,20},{4,24},{8,28},{12,0},{16,4},{20,8},{24,12},{28,16},{1,21},{... | collective-permute-start | bytes 8257544 | tf_op jit(solution)/shard_map/ppermute | solution.py:154
  411.6 207.0 %collective-permute-start.8 = (bf16[2048,672]{0,1:T(8,128)(2,1)}, bf16[2048,672]{0,1:T(8,128)(2,1)}, u32[]{:S(2)}, u32[]{:S(2)}) collective-permute-start(bf16[2048,672]{0,1:T(8,128)(2,1)} %get-tuple-element.18), channel_id=1, source_target_pairs={{0,24},{4,28},{8,0},{12,4},{16,8},{20,12},{24,16},{28,20},{1,25},{... | collective-permute-start | bytes 8257544 | tf_op jit(solution)/shard_map/ppermute | solution.py:154
  430.0 188.6 %collective-permute-start.7 = (bf16[2048,672]{0,1:T(8,128)(2,1)}, bf16[2048,672]{0,1:T(8,128)(2,1)}, u32[]{:S(2)}, u32[]{:S(2)}) collective-permute-start(bf16[2048,672]{0,1:T(8,128)(2,1)} %get-tuple-element.12), channel_id=1, source_target_pairs={{0,28},{4,0},{8,4},{12,8},{16,12},{20,16},{24,20},{28,24},{1,29},{... | collective-permute-start | bytes 8257544 | tf_op jit(solution)/shard_map/ppermute | solution.py:154
  (11 other events, 53.8 us)
Sparse Core Ops, SparseCore 0:
  9.6 100.8 all-gather.1

commit v6 on v3

--- a/solution.py
+++ b/solution.py
@@ -151,9 +151,8 @@
     pair_tokens = jnp.concatenate([own_cols, partner_tokens], axis=0)
     pair_grads = jnp.concatenate([proj_grads, partner_grads], axis=0)
     pair_sum = contract_first(pair_grads, pair_tokens).astype(jnp.bfloat16)
-    pair_sum = pair_sum.reshape(pair_sum.shape[0], n_hi, -1)
     summed = lax.psum_scatter(pair_sum, "seq_hi", scatter_dimension=1, tiled=True)
-    summed = summed.reshape(summed.shape[0], -1).astype(jnp.float32)
+    summed = summed.astype(jnp.float32)
     summed = (summed * (tok_rows * lax.axis_size(SEQ)) ** (-0.5)).astype(jnp.bfloat16).T
     q_width = query_weight.shape[1]
     k_width = key_weight.shape[1]

time: 480 us -> 456 us (0.950)
  local copies, waits for them, and re-layouts: 36.3 us -> 20 us
  matrix products: 123 us -> 116 us
    convert_element_type x1 -> x0, local copies, waits for them, and re-layouts: 15 us -> none  [per_device(): pair_sum = contract_first(pair_grads, pair_tokens).astype(jnp.bfloat16)]
    dot_general x1, matrix products: 23.1 us -> 16 us  [contract_first(): lax.dot_general(left, right, (((0,), (0,)), ((), ())), preferred_element_...]
  transfers between devices with their start and end apart: 11 -> 11, of which waited for: 9 -> 9; matrix products, arithmetic and copies ran while one was open for 27% -> 29% of each run, Pallas kernels for 0% -> 0%
where the time goes in v6:
time: 456 us; the launch traced here: 450 us
  waiting for transfers between devices  255 us (56%)
  matrix products  116 us (25%)
  other arithmetic  27.8 us (6%)
  local copies, waits for them, and re-layouts  20 us (4%)
  starting transfers between devices  16.3 us (4%)
  between operations  15 us (3%)
    ppermute x3, waiting for transfers between devices, per_device(): got = lax.ppermute(sent, 'head', pairs).astype(jnp.float32)  108 us
    all_gather x1, waiting for transfers between devices, per_device(): gathered = lax.all_gather(tokens, 'head', axis=1, tiled=True)  97.4 us
    ppermute x4, waiting for transfers between devices, passed_along(): return lax.ppermute(x, axis, pairs)  44.2 us
    dot_general x12, matrix products, contract_last(): lax.dot_general(left, right, (((1,), (1,)), ((), ())), preferred_element_...  29.6 us
    convert_element_type x1, other arithmetic, attend(): dscores = (probs * (dprobs - center)).astype(jnp.bfloat16)  16.8 us
    dot_general x1, matrix products, attend(): jnp.einsum('akgd,ckd->kgac', grad_four, value_three, preferred_element_ty...  16.4 us
    dot_general x1, matrix products, contract_first(): lax.dot_general(left, right, (((0,), (0,)), ((), ())), preferred_element_...  16 us
    sub x1, matrix products, attend(): expo = jnp.where(allowed, jnp.exp(masked - row_max), 0.0)  13.6 us
  transfers between devices with their start and end apart: 11, of which 9 were waited for; matrix products, arithmetic and copies ran while one was open for 29% of the time, Pallas kernels for 0%

profile of v6, /device:TPU:11, one launch (start us, length us, event | category | flops | bytes accessed | tf_op | source)
XLA Modules:
  0.0 449.6 jit_solution(3506449158721040569)
XLA Ops:
  13.1 97.4 %all-gather.2.cloned.1.call-done = bf16[512,5376]{0,1:T(8,128)(2,1)} async-done(((bf16[512,1344]{0,1:T(8,128)(2,1)}), bf16[512,5376]{0,1:T(8,128)(2,1)}) %all-gather.2.cloned.1.call-update) | async-done | bytes 5505040 | tf_op jit(solution)/shard_map/all_gather | solution.py:91
  110.5 7.3 %fusion.58 = bf16[1,512,512]{2,1,0:T(8,128)(2,1)S(1)} fusion(bf16[512,5376]{0,1:T(8,128)(2,1)} %all-gather.2.cloned.1.call-done, bf16[5376,512]{1,0:T(8,128)(2,1)} %param.9), kind=kOutput, calls=%fused_computation.83 | convolution fusion | flops 2818834432 | bytes 11534336 | tf_op jit(solution)/shard_map/dot_general | solution.py:98
  117.9 5.8 %fusion.57 = bf16[1,512,512]{2,1,0:T(8,128)(2,1)S(1)} fusion(bf16[512,5376]{0,1:T(8,128)(2,1)S(1)} %copy-done.4, bf16[5376,512]{1,0:T(8,128)(2,1)} %param.8), kind=kOutput, calls=%fused_computation.82 | convolution fusion | flops 2818834432 | bytes 11534336 | tf_op jit(solution)/shard_map/dot_general | solution.py:95
  123.7 3.7 collective-permute-start.1
  130.6 5.9 %convolution_convert_fusion.1 = bf16[512,1024]{1,0:T(8,128)(2,1)S(1)} fusion(bf16[512,5376]{0,1:T(8,128)(2,1)S(1)} %copy-done.4, bf16[5376,1024]{1,0:T(8,128)(2,1)S(1)} %bitcast.100), kind=kOutput, calls=%fused_computation.71 | convolution fusion | flops 5637668864 | bytes 17563648 | tf_op jit(solution)/shard_map/dot_general | solution.py:92
  137.9 5.4 %constant_dynamic-slice_fusion.1 = (bf16[512,4,1,672]{0,3,2,1:T(8,128)(2,1)}, bf16[512,4,1,672]{0,3,2,1:T(8,128)(2,1)}) fusion(bf16[512,4,2,672]{0,3,2,1:T(8,128)(2,1)} %bitcast.84, s32[]{:T(128)S(6)} %select_n.66, s32[]{:T(128)S(6)} %select_n.67), kind=kLoop, calls=%fused_computation.91 | loop fusion | bytes 11010056 | tf_op jit(solution)/shard_map/jit(dynamic_index_in_dim)/dynamic_slice | solution.py:147
  143.3 4.5 %collective-permute-done.1 = bf16[2,512,512]{2,1,0:T(8,128)(2,1)} collective-permute-done((bf16[2,512,512]{2,1,0:T(8,128)(2,1)S(1)}, bf16[2,512,512]{2,1,0:T(8,128)(2,1)}, u32[]{:S(2)}, u32[]{:S(2)}) %collective-permute-start.1) | collective-permute-done | bytes 1048608 | tf_op jit(solution)/shard_map/ppermute | solution.py:21
  147.8 14.6 %collective-permute-done = bf16[2,512,512]{2,1,0:T(8,128)(2,1)} collective-permute-done((bf16[2,512,512]{2,1,0:T(8,128)(2,1)S(1)}, bf16[2,512,512]{2,1,0:T(8,128)(2,1)}, u32[]{:S(2)}, u32[]{:S(2)}) %collective-permute-start) | collective-permute-done | bytes 1048608 | tf_op jit(solution)/shard_map/ppermute | solution.py:21
  167.0 4.0 reshape_squeeze.7
  171.0 13.6 %fusion.77 = (f32[4,2,512]{2,1,0:T(2,128)S(1)}, f32[4,2,512,1536]{2,3,1,0:T(8,128)}) fusion(pred[512,1536]{0,1:T(8,128)(4,1)S(1)} %copy-done.11, bf16[1536,4,128,1]{0,2,3,1:T(8,128)(2,1)S(1)} %copy.22, bf16[512,4,2,128]{0,3,2,1:T(8,128)(2,1)S(1)} %bitcast.88), kind=kOutput, calls=%fused_computation.111 | convolution fusion | flops 1642071552 | bytes 28590080 | tf_op jit(solution)/shard_map/sub | solution.py:61
  184.6 12.7 %fusion.5 = f32[4,1536,128,1]{1,2,3,0:T(8,128)} fusion(bf16[512,4,2,128]{0,3,2,1:T(8,128)(2,1)} %bitcast.97, f32[4,2,512,1536]{2,3,1,0:T(8,128)} %get-tuple-element.15, f32[4,2,512]{2,1,0:T(2,128)S(1)} %get-tuple-element.14), kind=kOutput, calls=%fused_computation.9 | convolution fusion | flops 1623195648 | bytes 29376512 | tf_op jit(solution)/shard_map/kgac,akgd->ckd/dot_general | solution.py:81
  197.3 16.4 %fusion.1 = (f32[4,2,512]{2,1,0:T(2,128)S(1)}, f32[4,1536,512,2]{2,1,3,0:T(8,128)}) fusion(f32[4,2,512,1536]{2,3,1,0:T(8,128)} %get-tuple-element.15, f32[4,2,512]{2,1,0:T(2,128)S(1)} %get-tuple-element.14, bf16[512,4,2,128]{0,3,2,1:T(8,128)(2,1)S(1)} %bitcast.98, bf16[1536,4,128,1]{2,1,0,3:T(4,128)(2,1)S(1)} %bitcast.96), kind=kOutput, calls=%fused_computation.3 | convolution fusion | flops 1629483008 | bytes 52985856 | tf_op jit(solution)/shard_map/akgd,ckd->kgac/dot_general | solution.py:63
  213.7 16.8 %fusion.3 = bf16[4,2,512,1536]{2,3,1,0:T(8,128)(2,1)S(1)} fusion(f32[4,1536,512,2]{2,1,3,0:T(8,128)} %get-tuple-element.17, f32[4,2,512]{2,1,0:T(2,128)S(1)} %get-tuple-element.16, f32[4,2,512,1536]{2,3,1,0:T(8,128)} %get-tuple-element.15, f32[4,2,512]{2,1,0:T(2,128)S(1)} %get-tuple-element.14), kind=kLoop, calls=%fused_computation.5 | loop fusion | flops 25165824 | bytes 62947328 | tf_op jit(solution)/shard_map/convert_element_type | solution.py:67
  230.6 7.0 %fusion.23 = f32[4,128,1536]{2,1,0:T(8,128)} fusion(bf16[512,4,2,128]{0,3,2,1:T(8,128)(2,1)} %bitcast.87, bf16[4,2,512,1536]{2,3,1,0:T(8,128)(2,1)S(1)} %fusion.3), kind=kOutput, calls=%fused_computation.43 | convolution fusion | flops 1611399168 | bytes 16777216 | tf_op jit(solution)/shard_map/kgac,akgd->ckd/dot_general | solution.py:78
  247.6 21.4 %collective-permute-done.3 = bf16[2,512,512]{1,2,0:T(8,128)(2,1)S(1)} collective-permute-done((bf16[2,512,512]{1,2,0:T(8,128)(2,1)S(1)}, bf16[2,512,512]{1,2,0:T(8,128)(2,1)S(1)}, u32[]{:S(2)}, u32[]{:S(2)}) %collective-permute-start.3) | collective-permute-done | bytes 1048608 | tf_op jit(solution)/shard_map/ppermute | solution.py:21
  269.1 3.6 collective-permute-done.2
  273.5 4.1 collective-permute-done.7
  277.6 16.0 %convolution_convert_fusion = bf16[2048,2688]{0,1:T(8,128)(2,1)} fusion(bf16[512,2688]{0,1:T(8,128)(2,1)} %collective-permute-done.8, bf16[512,2688]{0,1:T(8,128)(2,1)S(1)} %bitcast.95, bf16[512,2048]{0,1:T(8,128)(2,1)S(1)} %collective-permute-done.7, bf16[512,512]{0,1:T(8,128)(2,1)S(1)} %get-tuple-element.13, bf16[512,512]{0,1:T(8,128)(2,1)S(1)} %get-tuple-element.12, ...), kind=kOutput, calls=%fused_computation.15 | convolution fusion | flops 11307581440 | bytes 20709376 | tf_op jit(solution)/shard_map/dot_general | solution.py:31
  298.2 3.5 fusion.37
  301.8 4.0 fusion.39
  324.9 17.4 %collective-permute-done.6 = bf16[512,1344]{0,1:T(8,128)(2,1)S(1)} collective-permute-done((bf16[512,1344]{0,1:T(8,128)(2,1)}, bf16[512,1344]{0,1:T(8,128)(2,1)S(1)}, u32[]{:S(2)}, u32[]{:S(2)}) %collective-permute-start.6) | collective-permute-done | bytes 1376288 | tf_op jit(solution)/shard_map/ppermute | solution.py:138
  342.2 87.3 %collective-permute-done.5 = bf16[512,1344]{0,1:T(8,128)(2,1)} collective-permute-done((bf16[512,1344]{0,1:T(8,128)(2,1)}, bf16[512,1344]{0,1:T(8,128)(2,1)}, u32[]{:S(2)}, u32[]{:S(2)}) %collective-permute-start.5) | collective-permute-done | bytes 1376288 | tf_op jit(solution)/shard_map/ppermute | solution.py:138
  429.6 3.5 collective-permute-done.4
  433.0 4.5 %add_convert_fusion = bf16[512,1344]{0,1:T(8,128)(2,1)} fusion(bf16[512,1344]{0,1:T(8,128)(2,1)S(1)} %collective-permute-done.6, bf16[512,1344]{0,1:T(8,128)(2,1)} %collective-permute-done.5, bf16[512,1344]{0,1:T(8,128)(2,1)} %collective-permute-done.4, f32[512,1344]{0,1:T(8,128)S(1)} %convolution_add_fusion.1, bf16[5376,512]{1,0:T(8,128)(2,1)} %param.9, ...), kind=kOutput, calls=%fused_computation.54 | convolution fusion | flops 711524352 | bytes 10158084 | tf_op jit(solution)/shard_map/dot_general | solution.py:25
  (87 shorter events, 54.2 us)
Async XLA Ops:
  7.2 103.3 %all-gather.2.cloned.1.call-start = ((), (), s32[]{:S(2)}) async-start(), calls=%async_computation.1 | async-start | bytes 6881280 | tf_op jit(solution)/shard_map/all_gather | solution.py:91
  7.9 429.6 %reduce-scatter.2.cloned.1.call-start = ((), (), s32[]{:S(2)}) async-start(), calls=%async_computation.2 | async-start | bytes 13762560 | tf_op jit(solution)/shard_map/reduce_scatter | solution.py:154
  110.5 7.4 %copy-start.4 = (bf16[512,5376]{0,1:T(8,128)(2,1)S(1)}, bf16[512,5376]{0,1:T(8,128)(2,1)}, u32[]{:S(2)}) copy-start(bf16[512,5376]{0,1:T(8,128)(2,1)} %all-gather.2.cloned.1.call-done) | copy-start | bytes 16515076
  110.5 20.0 %slice-start.4 = ((s8[11010048]{0:T(1024)(128)(4,1)}), s8[4194304]{0:T(1024)(128)(4,1)S(1)}, s32[]{:S(2)}) async-start(s8[11010048]{0:T(1024)(128)(4,1)} %bitcast.99), calls=%async_computation.7 | async-start | bytes 8388608
  110.5 20.0 %slice-start.5 = ((s8[11010048]{0:T(1024)(128)(4,1)}), s8[4194304]{0:T(1024)(128)(4,1)S(1)}, s32[]{:S(2)}) async-start(s8[11010048]{0:T(1024)(128)(4,1)} %bitcast.99), calls=%async_computation.8 | async-start | bytes 8388608
  117.9 12.7 %slice-start.6 = ((s8[11010048]{0:T(1024)(128)(4,1)}), s8[2621440]{0:T(1024)(128)(4,1)S(1)}, s32[]{:S(2)}) async-start(s8[11010048]{0:T(1024)(128)(4,1)} %bitcast.99), calls=%async_computation.9 | async-start | bytes 5242880
  123.7 24.0 %collective-permute-start.1 = (bf16[2,512,512]{2,1,0:T(8,128)(2,1)S(1)}, bf16[2,512,512]{2,1,0:T(8,128)(2,1)}, u32[]{:S(2)}, u32[]{:S(2)}) collective-permute-start(bf16[2,512,512]{2,1,0:T(8,128)(2,1)S(1)} %pad_maximum_fusion.2), channel_id=1, source_target_pairs={{0,4},{4,8},{8,12},{12,16},{16,20},{20,24},{24,28},{1,5},{5,9},{9,... | collective-permute-start | bytes 3145736 | tf_op jit(solution)/shard_map/ppermute | solution.py:21
  127.4 35.0 %collective-permute-start = (bf16[2,512,512]{2,1,0:T(8,128)(2,1)S(1)}, bf16[2,512,512]{2,1,0:T(8,128)(2,1)}, u32[]{:S(2)}, u32[]{:S(2)}) collective-permute-start(bf16[2,512,512]{2,1,0:T(8,128)(2,1)S(1)} %pad_maximum_fusion.2), channel_id=1, source_target_pairs={{0,8},{4,12},{8,16},{12,20},{16,24},{20,28},{1,9},{5,13},{9,17},{1... | collective-permute-start | bytes 3145736 | tf_op jit(solution)/shard_map/ppermute | solution.py:21
  143.3 130.2 %collective-permute-start.8 = (bf16[512,2688]{0,1:T(8,128)(2,1)}, bf16[512,2688]{0,1:T(8,128)(2,1)}, u32[]{:S(2)}, u32[]{:S(2)}) collective-permute-start(bf16[512,2688]{0,1:T(8,128)(2,1)} %bitcast.22), channel_id=1, source_target_pairs={{0,4},{4,0},{1,5},{5,1},{2,6},{6,2},{3,7},{7,3},{8,12},{12,8},{9,1... | collective-permute-start | bytes 8257544 | tf_op jit(solution)/shard_map/ppermute | solution.py:149
  166.9 17.7 %copy-start.2 = (bf16[1536,4,128,1]{0,2,3,1:T(8,128)(2,1)}, bf16[1536,4,128,1]{0,2,3,1:T(8,128)(2,1)S(1)}, u32[]{:S(2)}) copy-start(bf16[1536,4,128,1]{0,2,3,1:T(8,128)(2,1)S(1)} %copy.22) | copy-start | bytes 4718596
  184.6 12.7 %copy-start.9 = (bf16[1536,4,128]{2,1,0:T(4,128)(2,1)S(1)}, bf16[1536,4,128]{2,1,0:T(4,128)(2,1)}, u32[]{:S(2)}) copy-start(bf16[1536,4,128]{2,1,0:T(4,128)(2,1)} %reshape_squeeze.7) | copy-start | bytes 4718596
  184.6 12.7 %copy-start.10 = (bf16[512,1024]{0,1:T(8,128)(2,1)S(1)}, bf16[512,1024]{0,1:T(8,128)(2,1)}, u32[]{:S(2)}) copy-start(bf16[512,1024]{0,1:T(8,128)(2,1)} %copy.35) | copy-start | bytes 3145732
  241.2 27.9 %collective-permute-start.3 = (bf16[2,512,512]{1,2,0:T(8,128)(2,1)S(1)}, bf16[2,512,512]{1,2,0:T(8,128)(2,1)S(1)}, u32[]{:S(2)}, u32[]{:S(2)}) collective-permute-start(bf16[2,512,512]{1,2,0:T(8,128)(2,1)S(1)} %get-tuple-element.7), channel_id=1, source_target_pairs={{8,0},{12,4},{16,8},{20,12},{24,16},{28,20},{9,1},{13,5},{17,9},{2... | collective-permute-start | bytes 3145736 | tf_op jit(solution)/shard_map/ppermute | solution.py:21
  243.5 29.2 %copy-start = (f32[4,128,1536]{2,1,0:T(8,128)S(1)}, f32[4,128,1536]{2,1,0:T(8,128)}, u32[]{:S(2)}) copy-start(f32[4,128,1536]{2,1,0:T(8,128)} %fusion.23) | copy-start | bytes 9437188
  243.5 29.2 %copy-start.1 = (f32[4,1536,128,1]{1,2,3,0:T(8,128)S(1)}, f32[4,1536,128,1]{1,2,3,0:T(8,128)}, u32[]{:S(2)}) copy-start(f32[4,1536,128,1]{1,2,3,0:T(8,128)} %fusion.5) | copy-start | bytes 9437188
  243.5 29.2 %collective-permute-start.2 = (bf16[2,512,512]{1,2,0:T(8,128)(2,1)S(1)}, bf16[2,512,512]{1,2,0:T(8,128)(2,1)S(1)}, u32[]{:S(2)}, u32[]{:S(2)}) collective-permute-start(bf16[2,512,512]{1,2,0:T(8,128)(2,1)S(1)} %get-tuple-element.6), channel_id=1, source_target_pairs={{4,0},{8,4},{12,8},{16,12},{20,16},{24,20},{28,24},{5,1},{9,5},{13... | collective-permute-start | bytes 3145736 | tf_op jit(solution)/shard_map/ppermute | solution.py:21
  247.6 25.6 %copy-start.6 = (bf16[4,128,2,512]{3,1,2,0:T(8,128)(2,1)}, bf16[4,128,2,512]{3,1,2,0:T(8,128)(2,1)S(1)}, u32[]{:S(2)}) copy-start(bf16[4,128,2,512]{3,1,2,0:T(8,128)(2,1)S(1)} %multiply_convert_fusion.1) | copy-start | bytes 3145732
  273.4 4.2 collective-permute-start.7
  298.2 7.6 %slice-start.2 = ((s8[5505024]{0:T(1024)(128)(4,1)}), s8[4194304]{0:T(1024)(128)(4,1)S(1)}, s32[]{:S(2)}) async-start(s8[5505024]{0:T(1024)(128)(4,1)} %bitcast.85), calls=%async_computation.5 | async-start | bytes 8388608
  298.2 8.5 %slice-start = ((s8[5505024]{0:T(1024)(128)(4,1)}), s8[4194304]{0:T(1024)(128)(4,1)S(1)}, s32[]{:S(2)}) async-start(s8[5505024]{0:T(1024)(128)(4,1)} %bitcast.82), calls=%async_computation.3 | async-start | bytes 8388608
  301.8 5.0 %slice-start.1 = ((s8[5505024]{0:T(1024)(128)(4,1)}), s8[1310720]{0:T(1024)(128)(4,1)S(1)}, s32[]{:S(2)}) async-start(s8[5505024]{0:T(1024)(128)(4,1)} %bitcast.82), calls=%async_computation.4 | async-start | bytes 2621440
  308.7 33.5 %collective-permute-start.6 = (bf16[512,1344]{0,1:T(8,128)(2,1)}, bf16[512,1344]{0,1:T(8,128)(2,1)S(1)}, u32[]{:S(2)}, u32[]{:S(2)}) collective-permute-start(bf16[512,1344]{0,1:T(8,128)(2,1)} %fusion.29), channel_id=1, source_target_pairs={{0,1},{1,2},{2,3},{3,0},{4,5},{5,6},{6,7},{7,4},{8,9},{9,10},{10,1... | collective-permute-start | bytes 4128776 | tf_op jit(solution)/shard_map/ppermute | solution.py:138
  314.1 115.5 %collective-permute-start.5 = (bf16[512,1344]{0,1:T(8,128)(2,1)}, bf16[512,1344]{0,1:T(8,128)(2,1)}, u32[]{:S(2)}, u32[]{:S(2)}) collective-permute-start(bf16[512,1344]{0,1:T(8,128)(2,1)} %fusion.28), channel_id=1, source_target_pairs={{0,2},{1,3},{2,0},{3,1},{4,6},{5,7},{6,4},{7,5},{8,10},{9,11},{10,... | collective-permute-start | bytes 4128776 | tf_op jit(solution)/shard_map/ppermute | solution.py:138
  319.2 113.8 %collective-permute-start.4 = (bf16[512,1344]{0,1:T(8,128)(2,1)}, bf16[512,1344]{0,1:T(8,128)(2,1)}, u32[]{:S(2)}, u32[]{:S(2)}) collective-permute-start(bf16[512,1344]{0,1:T(8,128)(2,1)} %fusion.27), channel_id=1, source_target_pairs={{0,3},{1,0},{2,1},{3,2},{4,7},{5,4},{6,5},{7,6},{8,11},{9,8},{10,9... | collective-permute-start | bytes 4128776 | tf_op jit(solution)/shard_map/ppermute | solution.py:138
  (7 other events, 25.8 us)
Sparse Core Ops, SparseCore 0:
  9.6 100.8 all-gather.1
  293.7 107.2 reduce-scatter.1

commit v7 on v1

--- a/solution.py
+++ b/solution.py
@@ -88,40 +88,53 @@
     hop_count = HOPS
     margin = hop_count * tok_rows
     gathered = lax.all_gather(tokens, "head", axis=1, tiled=True)
-    queries = jnp.dot(gathered, query_weight, preferred_element_type=jnp.float32).astype(
-        jnp.bfloat16
-    )
-    keys_own = jnp.dot(gathered, key_weight, preferred_element_type=jnp.float32).astype(
-        jnp.bfloat16
-    )
-    values_own = jnp.dot(gathered, value_weight, preferred_element_type=jnp.float32).astype(
-        jnp.bfloat16
-    )
-    key_value = jnp.stack([keys_own, values_own])
-    blocks = [key_value] * (hop_count + 1)
-    moving = key_value
-    for distance in range(1, hop_count + 1):
-        moving = passed_along(moving, "seq", 1)
-        blocks[hop_count - distance] = moving
-    keys_all = jnp.concatenate(blocks, axis=1)
     position = lax.axis_index("seq")
     query_first = position * tok_rows
     seg_query = lax.dynamic_slice_in_dim(segments, query_first, tok_rows, 0)
     seg_padded = jnp.concatenate([jnp.full((margin,), -1, jnp.int32), segments], axis=0)
     seg_key = lax.dynamic_slice_in_dim(seg_padded, query_first, (hop_count + 1) * tok_rows, 0)
-    query_grad, kv_grad = attend(
-        queries, keys_all, output_grad, query_first, query_first - margin, seg_query, seg_key
-    )
-    pieces = [
-        kv_grad[:, block * tok_rows : (block + 1) * tok_rows] for block in range(hop_count + 1)
-    ]
-    carried = pieces[0]
-    for distance in range(1, hop_count + 1):
-        carried = pieces[distance] + passed_along(carried.astype(jnp.bfloat16), "seq", -1).astype(
-            carried.dtype
+    n_seq = lax.axis_size("seq")
+    weight_scale = (tok_rows * n_seq) ** (-0.5)
+    kv_local = key_weight.shape[1] // HEAD_DIM
+    n_split = 2 if kv_local % 2 == 0 else 1
+    q_cols = query_weight.shape[1] // n_split
+    k_cols = key_weight.shape[1] // n_split
+    query_grads, key_grads, value_grads, reduced = [], [], [], []
+    for part in range(n_split):
+        wq = query_weight[:, part * q_cols : (part + 1) * q_cols]
+        wk = key_weight[:, part * k_cols : (part + 1) * k_cols]
+        wv = value_weight[:, part * k_cols : (part + 1) * k_cols]
+        queries = jnp.dot(gathered, wq, preferred_element_type=jnp.float32).astype(jnp.bfloat16)
+        keys_own = jnp.dot(gathered, wk, preferred_element_type=jnp.float32).astype(jnp.bfloat16)
+        values_own = jnp.dot(gathered, wv, preferred_element_type=jnp.float32).astype(jnp.bfloat16)
+        key_value = jnp.stack([keys_own, values_own])
+        blocks = [key_value] * (hop_count + 1)
+        for distance in range(1, hop_count + 1):
+            blocks[hop_count - distance] = passed_along(key_value, "seq", distance)
+        keys_all = jnp.concatenate(blocks, axis=1)
+        grads = output_grad[:, part * q_cols : (part + 1) * q_cols]
+        query_grad, kv_grad = attend(
+            queries, keys_all, grads, query_first, query_first - margin, seg_query, seg_key
         )
-    key_grad = carried[0].astype(jnp.bfloat16)
-    value_grad = carried[1].astype(jnp.bfloat16)
+        pieces = [
+            kv_grad[:, block * tok_rows : (block + 1) * tok_rows]
+            for block in range(hop_count + 1)
+        ]
+        carried = pieces[hop_count]
+        for distance in range(1, hop_count + 1):
+            back = passed_along(pieces[hop_count - distance].astype(jnp.bfloat16), "seq", -distance)
+            carried = carried + back.astype(jnp.float32)
+        key_grad = carried[0].astype(jnp.bfloat16)
+        value_grad = carried[1].astype(jnp.bfloat16)
+        proj_grads = jnp.concatenate([query_grad, key_grad, value_grad], axis=1)
+        weight_part = contract_first(proj_grads, gathered).astype(jnp.bfloat16)
+        reduced.append(lax.psum_scatter(weight_part, "seq", scatter_dimension=1, tiled=True))
+        query_grads.append(query_grad)
+        key_grads.append(key_grad)
+        value_grads.append(value_grad)
+    query_grad = jnp.concatenate(query_grads, axis=1)
+    key_grad = jnp.concatenate(key_grads, axis=1)
+    value_grad = jnp.concatenate(value_grads, axis=1)
     n_head = lax.axis_size("head")
     me = lax.axis_index("head")
     width = tokens.shape[1]
@@ -141,19 +154,13 @@
         token_sum = got if token_sum is None else token_sum + got
     own = term(me).astype(jnp.float32)
     token_grad = (own if token_sum is None else token_sum + own).astype(jnp.bfloat16)
-    proj_grads = jnp.concatenate([query_grad, key_grad, value_grad], axis=1)
-    summed = lax.psum_scatter(
-        contract_first(proj_grads, gathered).astype(jnp.bfloat16),
-        "seq",
-        scatter_dimension=1,
-        tiled=True,
-    ).astype(jnp.float32)
-    summed = (summed * (tok_rows * lax.axis_size("seq")) ** (-0.5)).astype(jnp.bfloat16).T
-    q_width = query_weight.shape[1]
-    k_width = key_weight.shape[1]
-    query_weight_grad = summed[:, :q_width]
-    key_weight_grad = summed[:, q_width : q_width + k_width]
-    value_weight_grad = summed[:, q_width + k_width :]
+
+    def scaled(rows):
+        return (rows.astype(jnp.float32) * weight_scale).astype(jnp.bfloat16).T
+
+    query_weight_grad = jnp.concatenate([scaled(r[:q_cols]) for r in reduced], axis=1)
+    key_weight_grad = jnp.concatenate([scaled(r[q_cols : q_cols + k_cols]) for r in reduced], axis=1)
+    value_weight_grad = jnp.concatenate([scaled(r[q_cols + k_cols :]) for r in reduced], axis=1)
     return (token_grad, query_weight_grad, key_weight_grad, value_weight_grad)
 
 

time: 443 us -> 485 us (1.095)
  starting transfers between devices: 19.4 us -> 40.1 us
  waiting for transfers between devices: 242 us -> 253 us
  matrix products: 127 us -> 135 us
    ppermute x4 -> x8, starting transfers between devices: 13.7 us -> 28.6 us  [passed_along(): return lax.ppermute(x, axis, pairs)]
    ppermute x4 -> x8, waiting for transfers between devices: 35.4 us -> 49.8 us  [passed_along(): return lax.ppermute(x, axis, pairs)]
    unnamed x32 -> x64, local copies, waits for them, and re-layouts: 0.09 us -> 7.25 us
    sub x1 -> x2, matrix products: 13.6 us -> 20.6 us  [attend(): expo = jnp.where(allowed, jnp.exp(masked - row_max), 0.0)]
    all_gather x1, waiting for transfers between devices: 103 us -> 96.7 us  [per_device(): gathered = lax.all_gather(tokens, 'head', axis=1, tiled=True)]
    ppermute x3, starting transfers between devices: 5.57 us -> 11.4 us  [per_device(): got = lax.ppermute(sent, 'head', pairs).astype(jnp.float32)]
    dot_general x3 -> x6, matrix products: 23.3 us -> 29.1 us  [the longest x2 11.1 us: per_device(): jnp.dot(gathered, wk, preferred_element_type=jnp.float32)]
    convert_element_type x1 -> x2, other arithmetic: 17 us -> 13.6 us  [attend(): dscores = (probs * (dprobs - center)).astype(jnp.bfloat16)]
  transfers between devices with their start and end apart: 9 -> 14, of which waited for: 9 -> 11; matrix products, arithmetic and copies ran while one was open for 11% -> 23% of each run, Pallas kernels for 0% -> 0%
where the time goes in v7:
time: 485 us; the launch traced here: 479 us
  waiting for transfers between devices  253 us (52%)
  matrix products  135 us (28%)
  starting transfers between devices  40.1 us (8%)
  other arithmetic  23.6 us (5%)
  between operations  14.8 us (3%)
  local copies, waits for them, and re-layouts  12.7 us (3%)
    ppermute x3, waiting for transfers between devices, per_device(): got = lax.ppermute(sent, 'head', pairs).astype(jnp.float32)  106 us
    all_gather x1, waiting for transfers between devices, per_device(): gathered = lax.all_gather(tokens, 'head', axis=1, tiled=True)  96.7 us
    ppermute x8, waiting for transfers between devices, passed_along(): return lax.ppermute(x, axis, pairs)  49.8 us
    dot_general x12, matrix products, contract_last(): lax.dot_general(left, right, (((1,), (1,)), ((), ())), preferred_element_...  29.2 us
    ppermute x8, starting transfers between devices, passed_along(): return lax.ppermute(x, axis, pairs)  28.6 us
    sub x2, matrix products, attend(): expo = jnp.where(allowed, jnp.exp(masked - row_max), 0.0)  20.6 us
    dot_general x2, matrix products, attend(): jnp.einsum('akgd,ckd->kgac', grad_four, value_three, preferred_element_ty...  18.1 us
    dot_general x2, matrix products, contract_first(): lax.dot_general(left, right, (((0,), (0,)), ((), ())), preferred_element_...  17.4 us
  transfers between devices with their start and end apart: 14, of which 11 were waited for; matrix products, arithmetic and copies ran while one was open for 23% of the time, Pallas kernels for 0%

profile of v7, /device:TPU:11, one launch (start us, length us, event | category | flops | bytes accessed | tf_op | source)
XLA Modules:
  0.0 479.5 jit_solution(17212735160518549531)
XLA Ops:
  13.8 96.7 %all-gather.2.cloned.1.call-done = bf16[512,5376]{0,1:T(8,128)(2,1)} async-done(((bf16[512,1344]{0,1:T(8,128)(2,1)}), bf16[512,5376]{0,1:T(8,128)(2,1)}) %all-gather.2.cloned.1.call-update) | async-done | bytes 5505040 | tf_op jit(solution)/shard_map/all_gather | solution.py:90
  110.5 5.2 %fusion.92 = bf16[1,512,256]{2,1,0:T(8,128)(2,1)S(1)} fusion(bf16[512,5376]{0,1:T(8,128)(2,1)} %all-gather.2.cloned.1.call-done, bf16[5376,512]{1,0:T(8,128)(2,1)} %param.9), kind=kOutput, calls=%fused_computation.112 | convolution fusion | flops 1409417216 | bytes 8519680 | tf_op jit(solution)/shard_map/dot_general | solution.py:109
  134.7 5.8 %collective-permute-done.1 = bf16[2,512,256]{2,1,0:T(8,128)(2,1)S(1)} collective-permute-done((bf16[2,512,256]{2,1,0:T(8,128)(2,1)S(1)}, bf16[2,512,256]{2,1,0:T(8,128)(2,1)S(1)}, u32[]{:S(2)}, u32[]{:S(2)}) %collective-permute-start.1) | collective-permute-done | bytes 524320 | tf_op jit(solution)/shard_map/ppermute | solution.py:20
  142.5 10.3 %fusion.148 = (f32[2,2,512]{2,1,0:T(2,128)S(1)}, f32[2,2,512,1536]{2,3,1,0:T(8,128)}) fusion(pred[512,1536]{0,1:T(8,128)(4,1)} %fusion.28, bf16[1536,2,128,1]{0,2,3,1:T(8,128)(2,1)S(1)} %copy.48, bf16[512,2,2,128]{0,3,2,1:T(8,128)(2,1)} %bitcast.158), kind=kOutput, calls=%fused_computation.181 | convolution fusion | flops 821036544 | bytes 14688256 | tf_op jit(solution)/shard_map/sub | solution.py:60
  152.8 7.0 %fusion.12 = f32[2,1536,128,1]{1,2,3,0:T(8,128)S(1)} fusion(bf16[512,2,2,128]{0,3,2,1:T(8,128)(2,1)} %bitcast.162, f32[2,2,512,1536]{2,3,1,0:T(8,128)} %get-tuple-element.23, f32[2,2,512]{2,1,0:T(2,128)S(1)} %get-tuple-element.22), kind=kOutput, calls=%fused_computation.22 | convolution fusion | flops 811597824 | bytes 14688256 | tf_op jit(solution)/shard_map/kgac,akgd->ckd/dot_general | solution.py:80
  161.2 6.6 %fusion.5 = (f32[2,2,512]{2,1,0:T(2,128)S(1)}, f32[2,1536,512,2]{2,1,3,0:T(8,128)}) fusion(f32[2,2,512,1536]{2,3,1,0:T(8,128)S(1)} %copy-done, f32[2,2,512]{2,1,0:T(2,128)S(1)} %get-tuple-element.22, bf16[512,2,2,128]{0,3,2,1:T(8,128)(2,1)} %bitcast.163, bf16[1536,2,128,1]{2,1,0,3:T(2,128)(2,1)S(1)} %bitcast.156), kind=kOutput, calls=%fused_computation.10 | convolution fusion | flops 814741504 | bytes 26492928 | tf_op jit(solution)/shard_map/akgd,ckd->kgac/dot_general | solution.py:62
  167.9 6.8 %fusion.7 = bf16[2,2,512,1536]{2,3,1,0:T(8,128)(2,1)S(1)} fusion(f32[2,1536,512,2]{2,1,3,0:T(8,128)} %get-tuple-element.25, f32[2,2,512]{2,1,0:T(2,128)S(1)} %get-tuple-element.24, f32[2,2,512,1536]{2,3,1,0:T(8,128)S(1)} %copy-done, f32[2,2,512]{2,1,0:T(2,128)S(1)} %get-tuple-element.22), kind=kLoop, calls=%fused_computation.12 | loop fusion | flops 12582912 | bytes 31473664 | tf_op jit(solution)/shard_map/convert_element_type | solution.py:66
  184.2 8.9 %collective-permute-done.4 = bf16[2,512,256]{1,2,0:T(8,128)(2,1)S(1)} collective-permute-done((bf16[2,512,256]{1,2,0:T(8,128)(2,1)S(1)}, bf16[2,512,256]{1,2,0:T(8,128)(2,1)S(1)}, u32[]{:S(2)}, u32[]{:S(2)}) %collective-permute-start.4) | collective-permute-done | bytes 524320 | tf_op jit(solution)/shard_map/ppermute | solution.py:20
  193.0 4.7 collective-permute-done.5
  198.1 8.7 %convolution_convert_fusion.1 = bf16[1024,5376]{0,1:T(8,128)(2,1)} fusion(bf16[512,5376]{0,1:T(8,128)(2,1)S(1)} %bitcast.181, bf16[512,512]{0,1:T(8,128)(2,1)S(1)} %bitcast.166, bf16[512,256]{0,1:T(8,128)(2,1)S(1)} %get-tuple-element.18, bf16[512,256]{0,1:T(8,128)(2,1)S(1)} %get-tuple-element.19), kind=kOutput, calls=%fused_computation.17 | convolution fusion | flops 5645795328 | bytes 17563648 | tf_op jit(solution)/shard_map/dot_general | solution.py:30
  208.8 5.2 %fusion.86 = bf16[1,512,256]{2,1,0:T(8,128)(2,1)S(1)} fusion(bf16[512,5376]{0,1:T(8,128)(2,1)} %all-gather.2.cloned.1.call-done, bf16[5376,512]{1,0:T(8,128)(2,1)} %param.9), kind=kOutput, calls=%fused_computation.110 | convolution fusion | flops 1409417216 | bytes 8519680 | tf_op jit(solution)/shard_map/dot_general | solution.py:109
  214.0 6.8 %fusion.89 = bf16[1,512,256]{2,1,0:T(8,128)(2,1)S(1)} fusion(bf16[512,5376]{0,1:T(8,128)(2,1)} %all-gather.2.cloned.1.call-done, bf16[5376,512]{1,0:T(8,128)(2,1)} %param.8), kind=kOutput, calls=%fused_computation.111 | convolution fusion | flops 1409417216 | bytes 8519680 | tf_op jit(solution)/shard_map/dot_general | solution.py:108
  224.0 6.4 %collective-permute-start.3 = (bf16[2,512,256]{2,1,0:T(8,128)(2,1)S(1)}, bf16[2,512,256]{2,1,0:T(8,128)(2,1)S(1)}, u32[]{:S(2)}, u32[]{:S(2)}) collective-permute-start(bf16[2,512,256]{2,1,0:T(8,128)(2,1)S(1)} %pad_maximum_fusion.8), channel_id=1, source_target_pairs={{0,4},{4,8},{8,12},{12,16},{16,20},{20,24},{24,28},{1,5},{5,9},{9,... | collective-permute-start | bytes 1572872 | tf_op jit(solution)/shard_map/ppermute | solution.py:20
  234.4 11.4 %collective-permute-done.3 = bf16[2,512,256]{2,1,0:T(8,128)(2,1)S(1)} collective-permute-done((bf16[2,512,256]{2,1,0:T(8,128)(2,1)S(1)}, bf16[2,512,256]{2,1,0:T(8,128)(2,1)S(1)}, u32[]{:S(2)}, u32[]{:S(2)}) %collective-permute-start.3) | collective-permute-done | bytes 524320 | tf_op jit(solution)/shard_map/ppermute | solution.py:20
  247.0 10.3 %fusion.149 = (f32[2,2,512]{2,1,0:T(2,128)S(1)}, f32[2,2,512,1536]{2,3,1,0:T(8,128)}) fusion(pred[512,1536]{0,1:T(8,128)(4,1)} %fusion.28, bf16[1536,2,128,1]{0,2,3,1:T(8,128)(2,1)S(1)} %copy.54, bf16[512,2,2,128]{0,3,2,1:T(8,128)(2,1)} %bitcast.160), kind=kOutput, calls=%fused_computation.182 | convolution fusion | flops 821036544 | bytes 14688256 | tf_op jit(solution)/shard_map/sub | solution.py:60
  257.4 11.5 %fusion.2 = (f32[2,2,512]{2,1,0:T(2,128)S(1)}, f32[2,1536,512,2]{2,1,3,0:T(8,128)}) fusion(f32[2,2,512,1536]{2,3,1,0:T(8,128)} %get-tuple-element.27, f32[2,2,512]{2,1,0:T(2,128)S(1)} %get-tuple-element.26, bf16[512,2,2,128]{0,3,2,1:T(8,128)(2,1)S(1)} %bitcast.164, bf16[1536,2,128,1]{2,1,0,3:T(2,128)(2,1)S(1)} %bitcast.157), kind=kOutput, calls=%fused_computation.4 | convolution fusion | flops 814741504 | bytes 26492928 | tf_op jit(solution)/shard_map/akgd,ckd->kgac/dot_general | solution.py:62
  270.6 6.8 %fusion.4 = bf16[2,2,512,1536]{2,3,1,0:T(8,128)(2,1)S(1)} fusion(f32[2,1536,512,2]{2,1,3,0:T(8,128)} %get-tuple-element.29, f32[2,2,512]{2,1,0:T(2,128)S(1)} %get-tuple-element.28, f32[2,2,512,1536]{2,3,1,0:T(8,128)S(1)} %bitcast.145, f32[2,2,512]{2,1,0:T(2,128)S(1)} %get-tuple-element.26), kind=kLoop, calls=%fused_computation.6 | loop fusion | flops 12582912 | bytes 31473664 | tf_op jit(solution)/shard_map/convert_element_type | solution.py:66
  279.6 7.7 %fusion.10 = f32[2,1536,128,1]{1,2,3,0:T(8,128)S(1)} fusion(bf16[512,2,2,128]{0,3,2,1:T(8,128)(2,1)S(1)} %bitcast.165, f32[2,2,512,1536]{2,3,1,0:T(8,128)} %get-tuple-element.27, f32[2,2,512]{2,1,0:T(2,128)S(1)} %get-tuple-element.26), kind=kOutput, calls=%fused_computation.20 | convolution fusion | flops 811597824 | bytes 14688256 | tf_op jit(solution)/shard_map/kgac,akgd->ckd/dot_general | solution.py:80
  294.6 13.1 %collective-permute-done.6 = bf16[2,512,256]{1,2,0:T(8,128)(2,1)S(1)} collective-permute-done((bf16[2,512,256]{1,2,0:T(8,128)(2,1)S(1)}, bf16[2,512,256]{1,2,0:T(8,128)(2,1)S(1)}, u32[]{:S(2)}, u32[]{:S(2)}) %collective-permute-start.6) | collective-permute-done | bytes 524320 | tf_op jit(solution)/shard_map/ppermute | solution.py:20
  310.3 8.8 %convolution_convert_fusion = bf16[1024,5376]{0,1:T(8,128)(2,1)} fusion(bf16[512,5376]{0,1:T(8,128)(2,1)S(1)} %bitcast.185, bf16[512,256]{0,1:T(8,128)(2,1)S(1)} %get-tuple-element.20, bf16[512,256]{0,1:T(8,128)(2,1)S(1)} %get-tuple-element.21, bf16[512,512]{0,1:T(8,128)(2,1)S(1)} %bitcast.171), kind=kOutput, calls=%fused_computation.16 | convolution fusion | flops 5645795328 | bytes 17563648 | tf_op jit(solution)/shard_map/dot_general | solution.py:30
  333.6 10.0 %collective-permute-start.8 = (bf16[512,1344]{0,1:T(8,128)(2,1)}, bf16[512,1344]{0,1:T(8,128)(2,1)S(1)}, u32[]{:S(2)}, u32[]{:S(2)}) collective-permute-start(bf16[512,1344]{0,1:T(8,128)(2,1)} %fusion.29), channel_id=1, source_target_pairs={{0,3},{1,0},{2,1},{3,2},{4,7},{5,4},{6,5},{7,6},{8,11},{9,8},{10,9... | collective-permute-start | bytes 4128776 | tf_op jit(solution)/shard_map/ppermute | solution.py:153
  356.4 18.1 %collective-permute-done.8 = bf16[512,1344]{0,1:T(8,128)(2,1)S(1)} collective-permute-done((bf16[512,1344]{0,1:T(8,128)(2,1)}, bf16[512,1344]{0,1:T(8,128)(2,1)S(1)}, u32[]{:S(2)}, u32[]{:S(2)}) %collective-permute-start.8) | collective-permute-done | bytes 1376288 | tf_op jit(solution)/shard_map/ppermute | solution.py:153
  374.5 58.2 %collective-permute-done.9 = bf16[512,1344]{0,1:T(8,128)(2,1)} collective-permute-done((bf16[512,1344]{0,1:T(8,128)(2,1)}, bf16[512,1344]{0,1:T(8,128)(2,1)}, u32[]{:S(2)}, u32[]{:S(2)}) %collective-permute-start.9) | collective-permute-done | bytes 1376288 | tf_op jit(solution)/shard_map/ppermute | solution.py:153
  432.6 29.5 %collective-permute-done.10 = bf16[512,1344]{0,1:T(8,128)(2,1)} collective-permute-done((bf16[512,1344]{0,1:T(8,128)(2,1)}, bf16[512,1344]{0,1:T(8,128)(2,1)}, u32[]{:S(2)}, u32[]{:S(2)}) %collective-permute-start.10) | collective-permute-done | bytes 1376288 | tf_op jit(solution)/shard_map/ppermute | solution.py:153
  (144 shorter events, 100.3 us)
Async XLA Ops:
  7.2 103.3 %all-gather.2.cloned.1.call-start = ((), (), s32[]{:S(2)}) async-start(), calls=%async_computation.2 | async-start | bytes 6881280 | tf_op jit(solution)/shard_map/all_gather | solution.py:90
  7.9 458.7 %reduce-scatter.3.cloned.1.call-start = ((), (), s32[]{:S(2)}) async-start(), calls=%async_computation.3 | async-start | bytes 12386304 | tf_op jit(solution)/shard_map/reduce_scatter | solution.py:131
  110.5 16.8 %slice-start.7 = ((s8[11010048]{0:T(1024)(128)(4,1)}), s8[4194304]{0:T(1024)(128)(4,1)S(1)}, s32[]{:S(2)}) async-start(s8[11010048]{0:T(1024)(128)(4,1)} %bitcast.176), calls=%async_computation.12 | async-start | bytes 8388608
  110.5 16.8 %slice-start.8 = ((s8[11010048]{0:T(1024)(128)(4,1)}), s8[4194304]{0:T(1024)(128)(4,1)S(1)}, s32[]{:S(2)}) async-start(s8[11010048]{0:T(1024)(128)(4,1)} %bitcast.176), calls=%async_computation.13 | async-start | bytes 8388608
  120.0 14.7 %collective-permute-start = (bf16[2,512,256]{2,1,0:T(8,128)(2,1)S(1)}, bf16[2,512,256]{2,1,0:T(8,128)(2,1)S(1)}, u32[]{:S(2)}, u32[]{:S(2)}) collective-permute-start(bf16[2,512,256]{2,1,0:T(8,128)(2,1)S(1)} %pad_maximum_fusion.7), channel_id=1, source_target_pairs={{0,8},{4,12},{8,16},{12,20},{16,24},{20,28},{1,9},{5,13},{9,17},{1... | collective-permute-start | bytes 1572872 | tf_op jit(solution)/shard_map/ppermute | solution.py:20
  123.1 17.3 %collective-permute-start.1 = (bf16[2,512,256]{2,1,0:T(8,128)(2,1)S(1)}, bf16[2,512,256]{2,1,0:T(8,128)(2,1)S(1)}, u32[]{:S(2)}, u32[]{:S(2)}) collective-permute-start(bf16[2,512,256]{2,1,0:T(8,128)(2,1)S(1)} %pad_maximum_fusion.7), channel_id=1, source_target_pairs={{0,4},{4,8},{8,12},{12,16},{16,20},{20,24},{24,28},{1,5},{5,9},{9,... | collective-permute-start | bytes 1572872 | tf_op jit(solution)/shard_map/ppermute | solution.py:20
  176.8 21.2 %slice-start.13 = ((s8[5505024]{0:T(1024)(128)(4,1)}), s8[4194304]{0:T(1024)(128)(4,1)S(1)}, s32[]{:S(2)}) async-start(s8[5505024]{0:T(1024)(128)(4,1)} %bitcast.180), calls=%async_computation.18 | async-start | bytes 8388608
  177.2 15.8 %collective-permute-start.4 = (bf16[2,512,256]{1,2,0:T(8,128)(2,1)S(1)}, bf16[2,512,256]{1,2,0:T(8,128)(2,1)S(1)}, u32[]{:S(2)}, u32[]{:S(2)}) collective-permute-start(bf16[2,512,256]{1,2,0:T(8,128)(2,1)S(1)} %get-tuple-element.4), channel_id=1, source_target_pairs={{4,0},{8,4},{12,8},{16,12},{20,16},{24,20},{28,24},{5,1},{9,5},{13... | collective-permute-start | bytes 1572872 | tf_op jit(solution)/shard_map/ppermute | solution.py:20
  180.8 17.2 %slice-start.14 = ((s8[5505024]{0:T(1024)(128)(4,1)}), s8[1310720]{0:T(1024)(128)(4,1)S(1)}, s32[]{:S(2)}) async-start(s8[5505024]{0:T(1024)(128)(4,1)} %bitcast.180), calls=%async_computation.19 | async-start | bytes 2621440
  180.8 16.9 %collective-permute-start.5 = (bf16[2,512,256]{1,2,0:T(8,128)(2,1)S(1)}, bf16[2,512,256]{1,2,0:T(8,128)(2,1)S(1)}, u32[]{:S(2)}, u32[]{:S(2)}) collective-permute-start(bf16[2,512,256]{1,2,0:T(8,128)(2,1)S(1)} %get-tuple-element.5), channel_id=1, source_target_pairs={{8,0},{12,4},{16,8},{20,12},{24,16},{28,20},{9,1},{13,5},{17,9},{2... | collective-permute-start | bytes 1572872 | tf_op jit(solution)/shard_map/ppermute | solution.py:20
  206.8 261.2 %reduce-scatter.5.cloned.1.call-start = ((), (), s32[]{:S(2)}) async-start(), calls=%async_computation.4 | async-start | bytes 12386304 | tf_op jit(solution)/shard_map/reduce_scatter | solution.py:131
  208.8 21.7 %slice-start.10 = ((s8[11010048]{0:T(1024)(128)(4,1)}), s8[4194304]{0:T(1024)(128)(4,1)S(1)}, s32[]{:S(2)}) async-start(s8[11010048]{0:T(1024)(128)(4,1)} %bitcast.178), calls=%async_computation.15 | async-start | bytes 8388608
  208.8 21.7 %slice-start.11 = ((s8[11010048]{0:T(1024)(128)(4,1)}), s8[4194304]{0:T(1024)(128)(4,1)S(1)}, s32[]{:S(2)}) async-start(s8[11010048]{0:T(1024)(128)(4,1)} %bitcast.178), calls=%async_computation.16 | async-start | bytes 8388608
  208.8 21.7 %slice-start.15 = ((s8[5505024]{0:T(1024)(128)(4,1)}), s8[4194304]{0:T(1024)(128)(4,1)S(1)}, s32[]{:S(2)}) async-start(s8[5505024]{0:T(1024)(128)(4,1)} %bitcast.182), calls=%async_computation.20 | async-start | bytes 8388608
  214.0 16.5 %slice-start.12 = ((s8[11010048]{0:T(1024)(128)(4,1)}), s8[2621440]{0:T(1024)(128)(4,1)S(1)}, s32[]{:S(2)}) async-start(s8[11010048]{0:T(1024)(128)(4,1)} %bitcast.178), calls=%async_computation.17 | async-start | bytes 5242880
  220.9 13.5 %collective-permute-start.2 = (bf16[2,512,256]{2,1,0:T(8,128)(2,1)S(1)}, bf16[2,512,256]{2,1,0:T(8,128)(2,1)S(1)}, u32[]{:S(2)}, u32[]{:S(2)}) collective-permute-start(bf16[2,512,256]{2,1,0:T(8,128)(2,1)S(1)} %pad_maximum_fusion.8), channel_id=1, source_target_pairs={{0,8},{4,12},{8,16},{12,20},{16,24},{20,28},{1,9},{5,13},{9,17},{1... | collective-permute-start | bytes 1572872 | tf_op jit(solution)/shard_map/ppermute | solution.py:20
  224.0 21.8 %collective-permute-start.3 = (bf16[2,512,256]{2,1,0:T(8,128)(2,1)S(1)}, bf16[2,512,256]{2,1,0:T(8,128)(2,1)S(1)}, u32[]{:S(2)}, u32[]{:S(2)}) collective-permute-start(bf16[2,512,256]{2,1,0:T(8,128)(2,1)S(1)} %pad_maximum_fusion.8), channel_id=1, source_target_pairs={{0,4},{4,8},{8,12},{12,16},{16,20},{20,24},{24,28},{1,5},{5,9},{9,... | collective-permute-start | bytes 1572872 | tf_op jit(solution)/shard_map/ppermute | solution.py:20
  287.3 23.1 %slice-start.17 = ((s8[5505024]{0:T(1024)(128)(4,1)}), s8[4194304]{0:T(1024)(128)(4,1)S(1)}, s32[]{:S(2)}) async-start(s8[5505024]{0:T(1024)(128)(4,1)} %bitcast.184), calls=%async_computation.22 | async-start | bytes 8388608
  287.6 20.1 %collective-permute-start.6 = (bf16[2,512,256]{1,2,0:T(8,128)(2,1)S(1)}, bf16[2,512,256]{1,2,0:T(8,128)(2,1)S(1)}, u32[]{:S(2)}, u32[]{:S(2)}) collective-permute-start(bf16[2,512,256]{1,2,0:T(8,128)(2,1)S(1)} %get-tuple-element.6), channel_id=1, source_target_pairs={{4,0},{8,4},{12,8},{16,12},{20,16},{24,20},{28,24},{5,1},{9,5},{13... | collective-permute-start | bytes 1572872 | tf_op jit(solution)/shard_map/ppermute | solution.py:20
  291.4 19.0 %slice-start.18 = ((s8[5505024]{0:T(1024)(128)(4,1)}), s8[1310720]{0:T(1024)(128)(4,1)S(1)}, s32[]{:S(2)}) async-start(s8[5505024]{0:T(1024)(128)(4,1)} %bitcast.184), calls=%async_computation.23 | async-start | bytes 2621440
  291.4 18.7 %collective-permute-start.7 = (bf16[2,512,256]{1,2,0:T(8,128)(2,1)S(1)}, bf16[2,512,256]{1,2,0:T(8,128)(2,1)S(1)}, u32[]{:S(2)}, u32[]{:S(2)}) collective-permute-start(bf16[2,512,256]{1,2,0:T(8,128)(2,1)S(1)} %get-tuple-element.7), channel_id=1, source_target_pairs={{8,0},{12,4},{16,8},{20,12},{24,16},{28,20},{9,1},{13,5},{17,9},{2... | collective-permute-start | bytes 1572872 | tf_op jit(solution)/shard_map/ppermute | solution.py:20
  333.6 40.9 %collective-permute-start.8 = (bf16[512,1344]{0,1:T(8,128)(2,1)}, bf16[512,1344]{0,1:T(8,128)(2,1)S(1)}, u32[]{:S(2)}, u32[]{:S(2)}) collective-permute-start(bf16[512,1344]{0,1:T(8,128)(2,1)} %fusion.29), channel_id=1, source_target_pairs={{0,3},{1,0},{2,1},{3,2},{4,7},{5,4},{6,5},{7,6},{8,11},{9,8},{10,9... | collective-permute-start | bytes 4128776 | tf_op jit(solution)/shard_map/ppermute | solution.py:153
  346.5 86.1 %collective-permute-start.9 = (bf16[512,1344]{0,1:T(8,128)(2,1)}, bf16[512,1344]{0,1:T(8,128)(2,1)}, u32[]{:S(2)}, u32[]{:S(2)}) collective-permute-start(bf16[512,1344]{0,1:T(8,128)(2,1)} %fusion.30), channel_id=1, source_target_pairs={{0,2},{1,3},{2,0},{3,1},{4,6},{5,7},{6,4},{7,5},{8,10},{9,11},{10,... | collective-permute-start | bytes 4128776 | tf_op jit(solution)/shard_map/ppermute | solution.py:153
  349.4 112.8 %collective-permute-start.10 = (bf16[512,1344]{0,1:T(8,128)(2,1)}, bf16[512,1344]{0,1:T(8,128)(2,1)}, u32[]{:S(2)}, u32[]{:S(2)}) collective-permute-start(bf16[512,1344]{0,1:T(8,128)(2,1)} %fusion.31), channel_id=1, source_target_pairs={{0,1},{1,2},{2,3},{3,0},{4,5},{5,6},{6,7},{7,4},{8,9},{9,10},{10,1... | collective-permute-start | bytes 4128776 | tf_op jit(solution)/shard_map/ppermute | solution.py:153
  (21 other events, 161.0 us)
Sparse Core Ops, SparseCore 0:
  9.6 100.8 all-gather.1
  206.9 94.8 reduce-scatter.2
  319.2 90.1 reduce-scatter.4

commit v8 on v0

--- a/solution.py
+++ b/solution.py
@@ -122,27 +122,51 @@
         )
     key_grad = carried[0].astype(jnp.bfloat16)
     value_grad = carried[1].astype(jnp.bfloat16)
+    n_head = lax.axis_size("head")
+    me = lax.axis_index("head")
+    width = tokens.shape[1]
+    q_part = contract_first(query_grad, gathered).astype(jnp.bfloat16)
+    q_reduced = lax.psum_scatter(q_part, "seq", scatter_dimension=1, tiled=True)
+    kv_part = contract_first(
+        jnp.concatenate([key_grad, value_grad], axis=1), gathered
+    ).astype(jnp.bfloat16)
+    kv_reduced = lax.psum_scatter(kv_part, "seq", scatter_dimension=1, tiled=True)
     partial_term = (
         contract_last(query_grad, query_weight)
         + contract_last(key_grad, key_weight)
         + contract_last(value_grad, value_weight)
     )
-    token_grad = lax.psum_scatter(
-        partial_term.astype(jnp.bfloat16), "head", scatter_dimension=1, tiled=True
-    )
-    proj_grads = jnp.concatenate([query_grad, key_grad, value_grad], axis=1)
-    summed = lax.psum_scatter(
-        contract_first(gathered, proj_grads).astype(jnp.bfloat16),
-        "seq",
-        scatter_dimension=0,
-        tiled=True,
-    ).astype(jnp.float32)
-    summed = summed * (tok_rows * lax.axis_size("seq")) ** (-0.5)
-    q_width = query_weight.shape[1]
+
+    def block_of(dest):
+        return lax.dynamic_slice_in_dim(partial_term, dest * width, width, 1)
+
+    from_left = None
+    from_right = None
+    for step in range(1, n_head):
+        gap = n_head - step
+        rightward = block_of(jnp.minimum(me + gap, n_head - 1))
+        if from_left is not None:
+            rightward = rightward + from_left.astype(jnp.float32)
+        right_pairs = [(h, h + 1) for h in range(min(step, n_head - 1))]
+        from_left = lax.ppermute(rightward.astype(jnp.bfloat16), "head", right_pairs)
+        leftward = block_of(jnp.maximum(me - gap, 0))
+        if from_right is not None:
+            leftward = leftward + from_right.astype(jnp.float32)
+        left_pairs = [(h, h - 1) for h in range(max(gap, 1), n_head)]
+        from_right = lax.ppermute(leftward.astype(jnp.bfloat16), "head", left_pairs)
+    token_sum = block_of(me)
+    if from_left is not None:
+        token_sum = token_sum + from_left.astype(jnp.float32) + from_right.astype(jnp.float32)
+    token_grad = token_sum.astype(jnp.bfloat16)
+    weight_scale = (tok_rows * lax.axis_size("seq")) ** (-0.5)
+
+    def scaled(rows):
+        return (rows.astype(jnp.float32) * weight_scale).astype(jnp.bfloat16).T
+
     k_width = key_weight.shape[1]
-    query_weight_grad = summed[:, :q_width].astype(jnp.bfloat16)
-    key_weight_grad = summed[:, q_width : q_width + k_width].astype(jnp.bfloat16)
-    value_weight_grad = summed[:, q_width + k_width :].astype(jnp.bfloat16)
+    query_weight_grad = scaled(q_reduced)
+    key_weight_grad = scaled(kv_reduced[:k_width])
+    value_weight_grad = scaled(kv_reduced[k_width:])
     return (token_grad, query_weight_grad, key_weight_grad, value_weight_grad)
 
 

time: 570 us -> 535 us (0.939)
  waiting for transfers between devices: 323 us -> 286 us
  local copies, waits for them, and re-layouts: 50.7 us -> 18.7 us
  other arithmetic: 26 us -> 42.5 us
  starting transfers between devices: 13.8 us -> 26 us
    ppermute x0 -> x6, waiting for transfers between devices: none -> 121 us  [the longest x3 60.6 us: per_device(): from_right = lax.ppermute(leftward.astype(jnp.bfloat16), 'head', left_pairs)]
    unnamed x4 -> x3, waiting for transfers between devices: 100 us -> 0.71 us
    reduce_scatter x1 -> x2, waiting for transfers between devices: 84.5 us -> 0.01 us  [the longest x1 0.01 us: per_device(): q_reduced = lax.psum_scatter(q_part, 'seq', scatter_dimension=1, tiled=True)]
    unnamed x23 -> x28, local copies, waits for them, and re-layouts: 39.8 us -> 9.14 us
    ppermute x4, waiting for transfers between devices: 35.4 us -> 62.2 us  [passed_along(): return lax.ppermute(x, axis, pairs)]
    convert_element_type x0 -> x4, other arithmetic: none -> 15.2 us  [the longest x2 8.5 us: per_device(): rightward.astype(jnp.bfloat16)]
    ppermute x0 -> x6, starting transfers between devices: none -> 12.1 us  [the longest x3 7.2 us: per_device(): lax.ppermute(rightward.astype(jnp.bfloat16), 'head', right_pairs)]
    dot_general x1 -> x2, matrix products: 20 us -> 20.3 us  [contract_first(): lax.dot_general(left, right, (((0,), (0,)), ((), ())), preferred_element_...]
  transfers between devices with their start and end apart: 7 -> 13, of which waited for: 7 -> 9; matrix products, arithmetic and copies ran while one was open for 13% -> 21% of each run, Pallas kernels for 0% -> 0%
where the time goes in v8:
time: 535 us; the launch traced here: 530 us
  waiting for transfers between devices  286 us (53%)
  matrix products  142 us (27%)
  other arithmetic  42.5 us (8%)
  starting transfers between devices  26 us (5%)
  local copies, waits for them, and re-layouts  18.7 us (3%)
  between operations  14.6 us (3%)
    all_gather x1, waiting for transfers between devices, per_device(): gathered = lax.all_gather(tokens, 'head', axis=1, tiled=True)  103 us
    ppermute x4, waiting for transfers between devices, passed_along(): return lax.ppermute(x, axis, pairs)  62.2 us
    ppermute x3, waiting for transfers between devices, per_device(): from_right = lax.ppermute(leftward.astype(jnp.bfloat16), 'head', left_pairs)  60.6 us
    ppermute x3, waiting for transfers between devices, per_device(): lax.ppermute(rightward.astype(jnp.bfloat16), 'head', right_pairs)  60.3 us
    dot_general x3, matrix products, contract_last(): lax.dot_general(left, right, (((1,), (1,)), ((), ())), preferred_element_...  41.4 us
    dot_general x2, matrix products, contract_first(): lax.dot_general(left, right, (((0,), (0,)), ((), ())), preferred_element_...  20.3 us
    dot_general x1, matrix products, attend(): jnp.einsum('akgd,ckd->kgac', grad_four, value_three, preferred_element_ty...  17.7 us
    convert_element_type x1, other arithmetic, attend(): dscores = (probs * (dprobs - center)).astype(jnp.bfloat16)  16.8 us
  transfers between devices with their start and end apart: 13, of which 9 were waited for; matrix products, arithmetic and copies ran while one was open for 21% of the time, Pallas kernels for 0%

profile of v8, /device:TPU:11, one launch (start us, length us, event | category | flops | bytes accessed | tf_op | source)
XLA Modules:
  0.0 529.8 jit_solution(9086431407942935309)
XLA Ops:
  7.9 102.5 %all-gather.2.cloned.1.call-done = bf16[512,5376]{0,1:T(8,128)(2,1)} async-done(((bf16[512,1344]{0,1:T(8,128)(2,1)}), bf16[512,5376]{0,1:T(8,128)(2,1)}) %all-gather.2.cloned.1.call-update) | async-done | bytes 5505040 | tf_op jit(solution)/shard_map/all_gather | solution.py:90
  110.5 7.4 %fusion.27 = bf16[1,512,512]{2,1,0:T(8,128)(2,1)S(1)} fusion(bf16[512,5376]{0,1:T(8,128)(2,1)} %all-gather.2.cloned.1.call-done, bf16[5376,512]{1,0:T(8,128)(2,1)} %param.9), kind=kOutput, calls=%fused_computation.57 | convolution fusion | flops 2818834432 | bytes 11534336 | tf_op jit(solution)/shard_map/dot_general | solution.py:97
  117.9 5.7 %fusion.26 = bf16[1,512,512]{2,1,0:T(8,128)(2,1)S(1)} fusion(bf16[512,5376]{0,1:T(8,128)(2,1)S(1)} %copy-done.9, bf16[5376,512]{1,0:T(8,128)(2,1)} %param.8), kind=kOutput, calls=%fused_computation.56 | convolution fusion | flops 2818834432 | bytes 11534336 | tf_op jit(solution)/shard_map/dot_general | solution.py:94
  131.5 7.5 %collective-permute-done = bf16[2,512,512]{2,1,0:T(8,128)(2,1)} collective-permute-done((bf16[2,512,512]{2,1,0:T(8,128)(2,1)S(1)}, bf16[2,512,512]{2,1,0:T(8,128)(2,1)}, u32[]{:S(2)}, u32[]{:S(2)}) %collective-permute-start) | collective-permute-done | bytes 1048608 | tf_op jit(solution)/shard_map/ppermute | solution.py:20
  139.1 5.6 %collective-permute-start.1 = (bf16[2,512,512]{2,1,0:T(8,128)(2,1)}, bf16[2,512,512]{2,1,0:T(8,128)(2,1)S(1)}, u32[]{:S(2)}, u32[]{:S(2)}) collective-permute-start(bf16[2,512,512]{2,1,0:T(8,128)(2,1)} %collective-permute-done), channel_id=1, source_target_pairs={{0,4},{4,8},{8,12},{12,16},{16,20},{20,24},{24,28},{1,5},{5,9},{9,... | collective-permute-start | bytes 3145736 | tf_op jit(solution)/shard_map/ppermute | solution.py:20
  144.6 10.3 %convolution_convert_fusion.2 = bf16[512,1024]{1,0:T(8,128)(2,1)S(1)} fusion(bf16[512,5376]{0,1:T(8,128)(2,1)} %all-gather.2.cloned.1.call-done, bf16[5376,1024]{1,0:T(8,128)(2,1)} %param.7), kind=kOutput, calls=%fused_computation.50 | convolution fusion | flops 5637668864 | bytes 17563648 | tf_op jit(solution)/shard_map/dot_general | solution.py:91
  164.3 13.6 %fusion.38 = (f32[4,2,512]{2,1,0:T(2,128)S(1)}, f32[4,2,512,1536]{2,3,1,0:T(8,128)}) fusion(pred[512,1536]{0,1:T(8,128)(4,1)S(1)} %copy-done.7, bf16[1536,4,128,1]{0,2,3,1:T(8,128)(2,1)S(1)} %copy.59, bf16[512,4,2,128]{0,3,2,1:T(8,128)(2,1)S(1)} %bitcast.84), kind=kOutput, calls=%fused_computation.75 | convolution fusion | flops 1642071552 | bytes 28590080 | tf_op jit(solution)/shard_map/sub | solution.py:60
  177.9 17.7 %fusion.1 = (f32[4,2,512]{2,1,0:T(2,128)S(1)}, f32[4,1536,512,2]{2,1,3,0:T(8,128)}) fusion(f32[4,2,512,1536]{2,3,1,0:T(8,128)} %get-tuple-element.23, f32[4,2,512]{2,1,0:T(2,128)S(1)} %get-tuple-element.22, bf16[512,4,2,128]{0,3,2,1:T(8,128)(2,1)} %bitcast.87, bf16[1536,4,128,1]{2,1,0,3:T(4,128)(2,1)} %bitcast.86), kind=kOutput, calls=%fused_computation.3 | convolution fusion | flops 1629483008 | bytes 52985856 | tf_op jit(solution)/shard_map/akgd,ckd->kgac/dot_general | solution.py:62
  195.6 16.8 %fusion.3 = bf16[4,2,512,1536]{2,3,1,0:T(8,128)(2,1)S(1)} fusion(f32[4,1536,512,2]{2,1,3,0:T(8,128)} %get-tuple-element.25, f32[4,2,512]{2,1,0:T(2,128)S(1)} %get-tuple-element.24, f32[4,2,512,1536]{2,3,1,0:T(8,128)} %get-tuple-element.23, f32[4,2,512]{2,1,0:T(2,128)S(1)} %get-tuple-element.22), kind=kLoop, calls=%fused_computation.5 | loop fusion | flops 25165824 | bytes 62947328 | tf_op jit(solution)/shard_map/convert_element_type | solution.py:66
  218.0 11.4 %convolution_convert_fusion.1 = bf16[1024,5376]{0,1:T(8,128)(2,1)} fusion(bf16[512,1024]{0,1:T(8,128)(2,1)S(1)} %bitcast.89, bf16[512,5376]{0,1:T(8,128)(2,1)} %all-gather.2.cloned.1.call-done), kind=kOutput, calls=%fused_computation.16 | convolution fusion | flops 5642649600 | bytes 17563648 | tf_op jit(solution)/shard_map/dot_general | solution.py:30
  229.5 8.8 %fusion.12 = f32[4,128,1536]{2,1,0:T(8,128)S(1)} fusion(bf16[512,4,2,128]{0,3,2,1:T(8,128)(2,1)S(1)} %bitcast.85, bf16[4,2,512,1536]{2,3,1,0:T(8,128)(2,1)} %copy-done.1), kind=kOutput, calls=%fused_computation.26 | convolution fusion | flops 1611399168 | bytes 16777216 | tf_op jit(solution)/shard_map/kgac,akgd->ckd/dot_general | solution.py:77
  238.3 14.8 %fusion.5 = f32[4,1536,128,1]{1,2,3,0:T(8,128)S(1)} fusion(bf16[512,4,2,128]{0,3,2,1:T(8,128)(2,1)S(1)} %bitcast.88, f32[4,2,512,1536]{2,3,1,0:T(8,128)} %get-tuple-element.23, f32[4,2,512]{2,1,0:T(2,128)S(1)} %get-tuple-element.22), kind=kOutput, calls=%fused_computation.9 | convolution fusion | flops 1623195648 | bytes 29376512 | tf_op jit(solution)/shard_map/kgac,akgd->ckd/dot_general | solution.py:80
  255.7 35.6 %collective-permute-done.2 = bf16[2,512,512]{1,2,0:T(8,128)(2,1)S(1)} collective-permute-done((bf16[2,512,512]{1,2,0:T(8,128)(2,1)S(1)}, bf16[2,512,512]{1,2,0:T(8,128)(2,1)S(1)}, u32[]{:S(2)}, u32[]{:S(2)}) %collective-permute-start.2) | collective-permute-done | bytes 1048608 | tf_op jit(solution)/shard_map/ppermute | solution.py:20
  293.8 18.9 %collective-permute-done.3 = bf16[2,512,512]{1,2,0:T(8,128)(2,1)S(1)} collective-permute-done((bf16[2,512,512]{1,2,0:T(8,128)(2,1)S(1)}, bf16[2,512,512]{1,2,0:T(8,128)(2,1)S(1)}, u32[]{:S(2)}, u32[]{:S(2)}) %collective-permute-start.3) | collective-permute-done | bytes 1048608 | tf_op jit(solution)/shard_map/ppermute | solution.py:20
  313.1 8.9 %convolution_convert_fusion = bf16[1024,5376]{0,1:T(8,128)(2,1)} fusion(bf16[512,5376]{0,1:T(8,128)(2,1)S(1)} %bitcast.92, bf16[512,512]{0,1:T(8,128)(2,1)S(1)} %get-tuple-element.21, bf16[512,512]{0,1:T(8,128)(2,1)S(1)} %get-tuple-element.20), kind=kOutput, calls=%fused_computation.15 | convolution fusion | flops 5644746752 | bytes 17563648 | tf_op jit(solution)/shard_map/dot_general | solution.py:30
  323.2 12.9 %fusion.39 = f32[512,5376]{0,1:T(8,128)} fusion(bf16[5376,1024]{1,0:T(8,128)(2,1)} %param.7, bf16[512,1024]{0,1:T(8,128)(2,1)S(1)} %bitcast.90), kind=kOutput, calls=%fused_computation.76 | convolution fusion | flops 5637144576 | bytes 23068672 | tf_op jit(solution)/shard_map/dot_general | solution.py:24
  336.1 7.0 %fusion.36 = f32[512,5376]{0,1:T(8,128)} fusion(bf16[5376,512]{1,0:T(8,128)(2,1)S(1)} %bitcast.82, bf16[2,512,512]{1,2,0:T(8,128)(2,1)S(1)} %fusion.21), kind=kOutput, calls=%fused_computation.73 | convolution fusion | flops 2818572288 | bytes 17039360 | tf_op jit(solution)/shard_map/dot_general | solution.py:24
  343.1 21.5 %add_add_fusion = f32[512,5376]{0,1:T(8,128)S(1)} fusion(f32[512,5376]{0,1:T(8,128)} %fusion.39, f32[512,5376]{0,1:T(8,128)} %fusion.36, bf16[5376,512]{1,0:T(8,128)(2,1)} %param.9, bf16[2,512,512]{1,2,0:T(8,128)(2,1)S(1)} %fusion.21), kind=kOutput, calls=%fused_computation.17 | convolution fusion | flops 2824077312 | bytes 39059456 | tf_op jit(solution)/shard_map/dot_general | solution.py:24
  364.6 4.2 copy-done
  372.2 29.5 %collective-permute-done.4 = bf16[512,1344]{0,1:T(8,128)(2,1)} collective-permute-done((bf16[512,1344]{0,1:T(8,128)(2,1)S(1)}, bf16[512,1344]{0,1:T(8,128)(2,1)}, u32[]{:S(2)}, u32[]{:S(2)}) %collective-permute-start.4) | collective-permute-done | bytes 1376288 | tf_op jit(solution)/shard_map/ppermute | solution.py:151
  406.3 30.8 %collective-permute-done.5 = bf16[512,1344]{0,1:T(8,128)(2,1)} collective-permute-done((bf16[512,1344]{0,1:T(8,128)(2,1)S(1)}, bf16[512,1344]{0,1:T(8,128)(2,1)}, u32[]{:S(2)}, u32[]{:S(2)}) %collective-permute-start.5) | collective-permute-done | bytes 1376288 | tf_op jit(solution)/shard_map/ppermute | solution.py:151
  437.1 5.8 %add_convert_fusion.3 = (bf16[512,1344]{0,1:T(8,128)(2,1)}, bf16[512,1344]{0,1:T(8,128)(2,1)}) fusion(bf16[512,1344]{0,1:T(8,128)(2,1)} %collective-permute-done.5, f32[512,5376]{0,1:T(8,128)} %copy-done, s32[]{:T(128)S(6)} %select_n.39, bf16[512,1344]{0,1:T(8,128)(2,1)} %collective-permute-done.7, s32[]{:T(128)S(6)} %select_n.43), kind=kLoop, calls=%fused_computation.36 | loop fusion | flops 4128768 | bytes 11010056 | tf_op jit(solution)/shard_map/convert_element_type | solution.py:151
  448.2 28.9 %collective-permute-done.8 = bf16[512,1344]{0,1:T(8,128)(2,1)S(1)} collective-permute-done((bf16[512,1344]{0,1:T(8,128)(2,1)}, bf16[512,1344]{0,1:T(8,128)(2,1)S(1)}, u32[]{:S(2)}, u32[]{:S(2)}) %collective-permute-start.8) | collective-permute-done | bytes 1376288 | tf_op jit(solution)/shard_map/ppermute | solution.py:156
  482.4 31.6 %collective-permute-done.9 = bf16[512,1344]{0,1:T(8,128)(2,1)S(1)} collective-permute-done((bf16[512,1344]{0,1:T(8,128)(2,1)}, bf16[512,1344]{0,1:T(8,128)(2,1)S(1)}, u32[]{:S(2)}, u32[]{:S(2)}) %collective-permute-start.9) | collective-permute-done | bytes 1376288 | tf_op jit(solution)/shard_map/ppermute | solution.py:156
  (73 shorter events, 57.6 us)
Async XLA Ops:
  7.2 103.3 %all-gather.2.cloned.1.call-start = ((), (), s32[]{:S(2)}) async-start(), calls=%async_computation.2 | async-start | bytes 6881280 | tf_op jit(solution)/shard_map/all_gather | solution.py:90
  7.9 509.5 %reduce-scatter.3.cloned.1.call-start = ((), (), s32[]{:S(2)}) async-start(), calls=%async_computation.3 | async-start | bytes 12386304 | tf_op jit(solution)/shard_map/reduce_scatter | solution.py:129
  110.5 7.4 %copy-start.9 = (bf16[512,5376]{0,1:T(8,128)(2,1)S(1)}, bf16[512,5376]{0,1:T(8,128)(2,1)}, u32[]{:S(2)}) copy-start(bf16[512,5376]{0,1:T(8,128)(2,1)} %all-gather.2.cloned.1.call-done) | copy-start | bytes 16515076
  117.9 9.5 %copy-start.3 = (bf16[512,1024]{1,0:T(8,128)(2,1)S(1)}, bf16[512,1024]{1,0:T(8,128)(2,1)}, u32[]{:S(2)}) copy-start(bf16[512,1024]{1,0:T(8,128)(2,1)} %param.10) | copy-start | bytes 3145732
  123.6 5.1 copy-start.8
  123.7 15.4 %collective-permute-start = (bf16[2,512,512]{2,1,0:T(8,128)(2,1)S(1)}, bf16[2,512,512]{2,1,0:T(8,128)(2,1)}, u32[]{:S(2)}, u32[]{:S(2)}) collective-permute-start(bf16[2,512,512]{2,1,0:T(8,128)(2,1)S(1)} %pad_maximum_fusion.1), channel_id=1, source_target_pairs={{0,4},{4,8},{8,12},{12,16},{16,20},{20,24},{24,28},{1,5},{5,9},{9,... | collective-permute-start | bytes 3145736 | tf_op jit(solution)/shard_map/ppermute | solution.py:20
  139.1 17.4 %collective-permute-start.1 = (bf16[2,512,512]{2,1,0:T(8,128)(2,1)}, bf16[2,512,512]{2,1,0:T(8,128)(2,1)S(1)}, u32[]{:S(2)}, u32[]{:S(2)}) collective-permute-start(bf16[2,512,512]{2,1,0:T(8,128)(2,1)} %collective-permute-done), channel_id=1, source_target_pairs={{0,4},{4,8},{8,12},{12,16},{16,20},{20,24},{24,28},{1,5},{5,9},{9,... | collective-permute-start | bytes 3145736 | tf_op jit(solution)/shard_map/ppermute | solution.py:20
  160.7 3.7 copy-start.2
  212.5 4.6 copy-start.1
  229.4 8.8 %copy-start.4 = (bf16[512,1024]{0,1:T(8,128)(2,1)S(1)}, bf16[512,1024]{0,1:T(8,128)(2,1)}, u32[]{:S(2)}) copy-start(bf16[512,1024]{0,1:T(8,128)(2,1)} %copy.75) | copy-start | bytes 3145732
  229.5 290.7 %reduce-scatter.5.cloned.1.call-start = ((), (), s32[]{:S(2)}) async-start(), calls=%async_computation.4 | async-start | bytes 12386304 | tf_op jit(solution)/shard_map/reduce_scatter | solution.py:133
  253.3 37.9 %collective-permute-start.2 = (bf16[2,512,512]{1,2,0:T(8,128)(2,1)S(1)}, bf16[2,512,512]{1,2,0:T(8,128)(2,1)S(1)}, u32[]{:S(2)}, u32[]{:S(2)}) collective-permute-start(bf16[2,512,512]{1,2,0:T(8,128)(2,1)S(1)} %fusion.22), channel_id=1, source_target_pairs={{4,0},{8,4},{12,8},{16,12},{20,16},{24,20},{28,24},{5,1},{9,5},{13... | collective-permute-start | bytes 3145736 | tf_op jit(solution)/shard_map/ppermute | solution.py:20
  291.2 21.8 %slice-start.2 = ((s8[5505024]{0:T(1024)(128)(4,1)}), s8[4194304]{0:T(1024)(128)(4,1)S(1)}, s32[]{:S(2)}) async-start(s8[5505024]{0:T(1024)(128)(4,1)} %bitcast.91), calls=%async_computation.7 | async-start | bytes 8388608
  291.6 21.5 %slice-start.3 = ((s8[5505024]{0:T(1024)(128)(4,1)}), s8[1310720]{0:T(1024)(128)(4,1)S(1)}, s32[]{:S(2)}) async-start(s8[5505024]{0:T(1024)(128)(4,1)} %bitcast.91), calls=%async_computation.8 | async-start | bytes 2621440
  291.6 21.0 %collective-permute-start.3 = (bf16[2,512,512]{1,2,0:T(8,128)(2,1)S(1)}, bf16[2,512,512]{1,2,0:T(8,128)(2,1)S(1)}, u32[]{:S(2)}, u32[]{:S(2)}) collective-permute-start(bf16[2,512,512]{1,2,0:T(8,128)(2,1)S(1)} %fusion.18), channel_id=1, source_target_pairs={{4,0},{8,4},{12,8},{16,12},{20,16},{24,20},{28,24},{5,1},{9,5},{13... | collective-permute-start | bytes 3145736 | tf_op jit(solution)/shard_map/ppermute | solution.py:20
  322.0 14.1 %slice-start = ((s8[5505024]{0:T(1024)(128)(4,1)}), s8[1310720]{0:T(1024)(128)(4,1)S(1)}, s32[]{:S(2)}) async-start(s8[5505024]{0:T(1024)(128)(4,1)} %bitcast.81), calls=%async_computation.5 | async-start | bytes 2621440
  323.2 12.9 %slice-start.1 = ((s8[5505024]{0:T(1024)(128)(4,1)}), s8[4194304]{0:T(1024)(128)(4,1)S(1)}, s32[]{:S(2)}) async-start(s8[5505024]{0:T(1024)(128)(4,1)} %bitcast.81), calls=%async_computation.6 | async-start | bytes 8388608
  364.6 4.2 copy-start
  369.1 32.6 %collective-permute-start.4 = (bf16[512,1344]{0,1:T(8,128)(2,1)S(1)}, bf16[512,1344]{0,1:T(8,128)(2,1)}, u32[]{:S(2)}, u32[]{:S(2)}) collective-permute-start(bf16[512,1344]{0,1:T(8,128)(2,1)S(1)} %get-tuple-element.14), channel_id=1, source_target_pairs={{0,1},{4,5},{8,9},{12,13},{16,17},{20,21},{24,25},{28,29}} | collective-permute-start | bytes 4128776 | tf_op jit(solution)/shard_map/ppermute | solution.py:151
  370.4 35.9 %collective-permute-start.7 = (bf16[512,1344]{0,1:T(8,128)(2,1)S(1)}, bf16[512,1344]{0,1:T(8,128)(2,1)}, u32[]{:S(2)}, u32[]{:S(2)}) collective-permute-start(bf16[512,1344]{0,1:T(8,128)(2,1)S(1)} %get-tuple-element.15), channel_id=1, source_target_pairs={{3,2},{7,6},{11,10},{15,14},{19,18},{23,22},{27,26},{31,30}} | collective-permute-start | bytes 4128776 | tf_op jit(solution)/shard_map/ppermute | solution.py:156
  404.4 32.7 %collective-permute-start.5 = (bf16[512,1344]{0,1:T(8,128)(2,1)S(1)}, bf16[512,1344]{0,1:T(8,128)(2,1)}, u32[]{:S(2)}, u32[]{:S(2)}) collective-permute-start(bf16[512,1344]{0,1:T(8,128)(2,1)S(1)} %add_convert_fusion.4), channel_id=1, source_target_pairs={{0,1},{1,2},{4,5},{5,6},{8,9},{9,10},{12,13},{13,14},{16,17},{17,1... | collective-permute-start | bytes 4128776 | tf_op jit(solution)/shard_map/ppermute | solution.py:151
  442.9 34.2 %collective-permute-start.8 = (bf16[512,1344]{0,1:T(8,128)(2,1)}, bf16[512,1344]{0,1:T(8,128)(2,1)S(1)}, u32[]{:S(2)}, u32[]{:S(2)}) collective-permute-start(bf16[512,1344]{0,1:T(8,128)(2,1)} %get-tuple-element.13), channel_id=1, source_target_pairs={{2,1},{3,2},{6,5},{7,6},{10,9},{11,10},{14,13},{15,14},{18,17},{19... | collective-permute-start | bytes 4128776 | tf_op jit(solution)/shard_map/ppermute | solution.py:156
  444.2 38.1 %collective-permute-start.6 = (bf16[512,1344]{0,1:T(8,128)(2,1)}, bf16[512,1344]{0,1:T(8,128)(2,1)S(1)}, u32[]{:S(2)}, u32[]{:S(2)}) collective-permute-start(bf16[512,1344]{0,1:T(8,128)(2,1)} %get-tuple-element.12), channel_id=1, source_target_pairs={{0,1},{1,2},{2,3},{4,5},{5,6},{6,7},{8,9},{9,10},{10,11},{12,13},{... | collective-permute-start | bytes 4128776 | tf_op jit(solution)/shard_map/ppermute | solution.py:151
  480.4 33.6 %collective-permute-start.9 = (bf16[512,1344]{0,1:T(8,128)(2,1)}, bf16[512,1344]{0,1:T(8,128)(2,1)S(1)}, u32[]{:S(2)}, u32[]{:S(2)}) collective-permute-start(bf16[512,1344]{0,1:T(8,128)(2,1)} %add_convert_fusion.1), channel_id=1, source_target_pairs={{1,0},{2,1},{3,2},{5,4},{6,5},{7,6},{9,8},{10,9},{11,10},{13,12},{... | collective-permute-start | bytes 4128776 | tf_op jit(solution)/shard_map/ppermute | solution.py:156
  (3 other events, 5.8 us)
Sparse Core Ops, SparseCore 0:
  9.6 100.8 all-gather.1
  229.6 98.2 reduce-scatter.2
  331.4 83.6 reduce-scatter.4

commit v9 on v6

--- a/solution.py
+++ b/solution.py
@@ -132,24 +132,29 @@
         return part.astype(jnp.bfloat16)
 
     token_sum = None
+    outgoing = []
     for shift in range(n_head - 1, 0, -1):
         sent = term((me + shift) % n_head)
+        outgoing.append(sent)
         pairs = [(i, (i + shift) % n_head) for i in range(n_head)]
         got = lax.ppermute(sent, "head", pairs).astype(jnp.float32)
         token_sum = got if token_sum is None else token_sum + got
     own = term(me).astype(jnp.float32)
     token_grad = (own if token_sum is None else token_sum + own).astype(jnp.bfloat16)
     proj_grads = jnp.concatenate([query_grad, key_grad, value_grad], axis=1)
+    proj_grads, _ = lax.optimization_barrier((proj_grads, outgoing))
     n_hi = lax.axis_size("seq_hi")
     core = lax.axis_index("core")
     swap = [(0, 1), (1, 0)]
     halves = gathered.reshape(tok_rows, n_hi, 2, -1)
     own_cols = lax.dynamic_index_in_dim(halves, core, 2, keepdims=False).reshape(tok_rows, -1)
     partner_cols = lax.dynamic_index_in_dim(halves, 1 - core, 2, keepdims=False).reshape(tok_rows, -1)
-    partner_tokens = lax.ppermute(partner_cols, "core", swap)
-    partner_grads = lax.ppermute(proj_grads, "core", swap)
-    pair_tokens = jnp.concatenate([own_cols, partner_tokens], axis=0)
-    pair_grads = jnp.concatenate([proj_grads, partner_grads], axis=0)
+    both_halves = lax.all_gather(partner_cols, "core", axis=0, tiled=True)
+    partner_tokens = lax.dynamic_slice_in_dim(both_halves, (1 - core) * tok_rows, tok_rows, 0)
+    first = jnp.where(core == 0, own_cols, partner_tokens)
+    second = jnp.where(core == 0, partner_tokens, own_cols)
+    pair_tokens = jnp.concatenate([first, second], axis=0)
+    pair_grads = lax.all_gather(proj_grads, "core", axis=0, tiled=True)
     pair_sum = contract_first(pair_grads, pair_tokens).astype(jnp.bfloat16)
     summed = lax.psum_scatter(pair_sum, "seq_hi", scatter_dimension=1, tiled=True)
     summed = summed.astype(jnp.float32)

time: 456 us -> 467 us (1.024)
  other arithmetic: 27.8 us -> 35.3 us
  matrix products: 116 us -> 123 us
    ppermute x4, waiting for transfers between devices: 44.2 us -> 35.2 us  [passed_along(): return lax.ppermute(x, axis, pairs)]
    all_gather x0 -> x2, waiting for transfers between devices: none -> 7.73 us  [the longest x1 7.71 us: per_device(): pair_grads = lax.all_gather(proj_grads, 'core', axis=0, tiled=True)]
    select_n x0 -> x1, other arithmetic: none -> 6.1 us  [per_device(): first = jnp.where(core == 0, own_cols, partner_tokens)]
    dot_general x12, matrix products: 29.6 us -> 35.1 us  [contract_last(): lax.dot_general(left, right, (((1,), (1,)), ((), ())), preferred_element_...]
  transfers between devices with their start and end apart: 11 -> 11, of which waited for: 9 -> 9; matrix products, arithmetic and copies ran while one was open for 29% -> 31% of each run, Pallas kernels for 0% -> 0%
where the time goes in v9:
time: 467 us; the launch traced here: 460 us
  waiting for transfers between devices  253 us (54%)
  matrix products  123 us (26%)
  other arithmetic  35.3 us (8%)
  local copies, waits for them, and re-layouts  18.5 us (4%)
  starting transfers between devices  15.4 us (3%)
  between operations  14.7 us (3%)
    ppermute x3, waiting for transfers between devices, per_device(): got = lax.ppermute(sent, 'head', pairs).astype(jnp.float32)  112 us
    all_gather x1, waiting for transfers between devices, per_device(): gathered = lax.all_gather(tokens, 'head', axis=1, tiled=True)  97.4 us
    ppermute x4, waiting for transfers between devices, passed_along(): return lax.ppermute(x, axis, pairs)  35.2 us
    dot_general x12, matrix products, contract_last(): lax.dot_general(left, right, (((1,), (1,)), ((), ())), preferred_element_...  35.1 us
    dot_general x1, matrix products, contract_first(): lax.dot_general(left, right, (((0,), (0,)), ((), ())), preferred_element_...  17.3 us
    convert_element_type x1, other arithmetic, attend(): dscores = (probs * (dprobs - center)).astype(jnp.bfloat16)  16.8 us
    dot_general x1, matrix products, attend(): jnp.einsum('akgd,ckd->kgac', grad_four, value_three, preferred_element_ty...  16.4 us
    sub x1, matrix products, attend(): expo = jnp.where(allowed, jnp.exp(masked - row_max), 0.0)  13.6 us
  transfers between devices with their start and end apart: 11, of which 9 were waited for; matrix products, arithmetic and copies ran while one was open for 31% of the time, Pallas kernels for 0%

profile of v9, /device:TPU:11, one launch (start us, length us, event | category | flops | bytes accessed | tf_op | source)
XLA Modules:
  0.0 460.1 jit_solution(5419028488961634931)
XLA Ops:
  13.1 97.4 %all-gather.4.cloned.1.call-done = bf16[512,5376]{0,1:T(8,128)(2,1)} async-done(((bf16[512,1344]{0,1:T(8,128)(2,1)}), bf16[512,5376]{0,1:T(8,128)(2,1)}) %all-gather.4.cloned.1.call-update) | async-done | bytes 5505040 | tf_op jit(solution)/shard_map/all_gather | solution.py:91
  110.5 7.3 %fusion.51 = bf16[1,512,512]{2,1,0:T(8,128)(2,1)S(1)} fusion(bf16[512,5376]{0,1:T(8,128)(2,1)} %all-gather.4.cloned.1.call-done, bf16[5376,512]{1,0:T(8,128)(2,1)} %param.9), kind=kOutput, calls=%fused_computation.78 | convolution fusion | flops 2818834432 | bytes 11534336 | tf_op jit(solution)/shard_map/dot_general | solution.py:98
  117.9 5.8 %fusion.50 = bf16[1,512,512]{2,1,0:T(8,128)(2,1)S(1)} fusion(bf16[512,5376]{0,1:T(8,128)(2,1)S(1)} %copy-done.4, bf16[5376,512]{1,0:T(8,128)(2,1)} %param.8), kind=kOutput, calls=%fused_computation.77 | convolution fusion | flops 2818834432 | bytes 11534336 | tf_op jit(solution)/shard_map/dot_general | solution.py:95
  123.7 3.7 collective-permute-start.1
  130.6 5.9 %convolution_convert_fusion.1 = bf16[512,1024]{1,0:T(8,128)(2,1)S(1)} fusion(bf16[512,5376]{0,1:T(8,128)(2,1)S(1)} %copy-done.4, bf16[5376,1024]{1,0:T(8,128)(2,1)S(1)} %bitcast.100), kind=kOutput, calls=%fused_computation.66 | convolution fusion | flops 5637668864 | bytes 17563648 | tf_op jit(solution)/shard_map/dot_general | solution.py:92
  137.8 5.3 %constant_dynamic-slice_fusion = (bf16[512,4,1,672]{0,3,2,1:T(8,128)(2,1)}, bf16[512,4,1,672]{0,3,2,1:T(8,128)(2,1)}) fusion(bf16[512,4,2,672]{0,3,2,1:T(8,128)(2,1)} %bitcast.88, s32[]{:T(128)S(6)} %select_n.83, s32[]{:T(128)S(6)} %select_n.82), kind=kLoop, calls=%fused_computation.85 | loop fusion | bytes 11010056 | tf_op jit(solution)/shard_map/jit(dynamic_index_in_dim)/dynamic_slice | solution.py:151
  143.3 4.5 collective-permute-done.1
  147.8 14.6 %collective-permute-done = bf16[2,512,512]{2,1,0:T(8,128)(2,1)} collective-permute-done((bf16[2,512,512]{2,1,0:T(8,128)(2,1)S(1)}, bf16[2,512,512]{2,1,0:T(8,128)(2,1)}, u32[]{:S(2)}, u32[]{:S(2)}) %collective-permute-start) | collective-permute-done | bytes 1048608 | tf_op jit(solution)/shard_map/ppermute | solution.py:21
  166.9 4.0 reshape_squeeze.7
  171.0 13.6 %fusion.70 = (f32[4,2,512]{2,1,0:T(2,128)S(1)}, f32[4,2,512,1536]{2,3,1,0:T(8,128)}) fusion(pred[512,1536]{0,1:T(8,128)(4,1)S(1)} %copy-done.12, bf16[1536,4,128,1]{0,2,3,1:T(8,128)(2,1)S(1)} %copy.22, bf16[512,4,2,128]{0,3,2,1:T(8,128)(2,1)S(1)} %bitcast.90), kind=kOutput, calls=%fused_computation.106 | convolution fusion | flops 1642071552 | bytes 28590080 | tf_op jit(solution)/shard_map/sub | solution.py:61
  184.6 12.6 %fusion.5 = f32[4,1536,128,1]{1,2,3,0:T(8,128)} fusion(bf16[512,4,2,128]{0,3,2,1:T(8,128)(2,1)} %bitcast.97, f32[4,2,512,1536]{2,3,1,0:T(8,128)} %get-tuple-element.19, f32[4,2,512]{2,1,0:T(2,128)S(1)} %get-tuple-element.18), kind=kOutput, calls=%fused_computation.9 | convolution fusion | flops 1623195648 | bytes 29376512 | tf_op jit(solution)/shard_map/kgac,akgd->ckd/dot_general | solution.py:81
  197.2 16.4 %fusion.1 = (f32[4,2,512]{2,1,0:T(2,128)S(1)}, f32[4,1536,512,2]{2,1,3,0:T(8,128)}) fusion(f32[4,2,512,1536]{2,3,1,0:T(8,128)} %get-tuple-element.19, f32[4,2,512]{2,1,0:T(2,128)S(1)} %get-tuple-element.18, bf16[512,4,2,128]{0,3,2,1:T(8,128)(2,1)S(1)} %bitcast.98, bf16[1536,4,128,1]{2,1,0,3:T(4,128)(2,1)S(1)} %bitcast.96), kind=kOutput, calls=%fused_computation.3 | convolution fusion | flops 1629483008 | bytes 52985856 | tf_op jit(solution)/shard_map/akgd,ckd->kgac/dot_general | solution.py:63
  213.6 16.8 %fusion.3 = bf16[4,2,512,1536]{2,3,1,0:T(8,128)(2,1)S(1)} fusion(f32[4,1536,512,2]{2,1,3,0:T(8,128)} %get-tuple-element.21, f32[4,2,512]{2,1,0:T(2,128)S(1)} %get-tuple-element.20, f32[4,2,512,1536]{2,3,1,0:T(8,128)} %get-tuple-element.19, f32[4,2,512]{2,1,0:T(2,128)S(1)} %get-tuple-element.18), kind=kLoop, calls=%fused_computation.5 | loop fusion | flops 25165824 | bytes 62947328 | tf_op jit(solution)/shard_map/convert_element_type | solution.py:67
  230.4 7.0 %fusion.16 = f32[4,128,1536]{2,1,0:T(8,128)} fusion(bf16[512,4,2,128]{0,3,2,1:T(8,128)(2,1)} %bitcast.89, bf16[4,2,512,1536]{2,3,1,0:T(8,128)(2,1)S(1)} %fusion.3), kind=kOutput, calls=%fused_computation.36 | convolution fusion | flops 1611399168 | bytes 16777216 | tf_op jit(solution)/shard_map/kgac,akgd->ckd/dot_general | solution.py:78
  237.4 3.6 fusion.10
  257.0 12.2 %collective-permute-done.3 = bf16[2,512,512]{1,2,0:T(8,128)(2,1)S(1)} collective-permute-done((bf16[2,512,512]{1,2,0:T(8,128)(2,1)S(1)}, bf16[2,512,512]{1,2,0:T(8,128)(2,1)S(1)}, u32[]{:S(2)}, u32[]{:S(2)}) %collective-permute-start.3) | collective-permute-done | bytes 1048608 | tf_op jit(solution)/shard_map/ppermute | solution.py:21
  269.2 3.9 collective-permute-done.2
  278.4 3.5 fusion.22
  290.7 6.1 %bitcast_select_fusion.3 = (bf16[512,2688]{0,1:T(8,128)(2,1)}, bf16[512,2688]{0,1:T(8,128)(2,1)}) fusion(bf16[512,4,1,672]{0,3,2,1:T(8,128)(2,1)} %get-tuple-element.9, pred[]{:T(512)S(6)} %eq.24, bf16[1024,2688]{0,1:T(8,128)(2,1)} %all-gather.8.cloned.1.call-done, s32[]{:T(128)S(6)} %select_n.84), kind=kLoop, calls=%fused_computation.48 | loop fusion | flops 2752512 | bytes 11010053 | tf_op jit(solution)/shard_map/jit(_where)/select_n | solution.py:154
  296.8 7.7 %all-gather.6.cloned.1.call-done = bf16[1024,2048]{0,1:T(8,128)(2,1)} async-done(((bf16[512,2048]{0,1:T(8,128)(2,1)}), bf16[1024,2048]{0,1:T(8,128)(2,1)}) %all-gather.6.cloned.1.call-update) | async-done | bytes 4194320 | tf_op jit(solution)/shard_map/all_gather | solution.py:157
  304.5 17.3 %convolution_convert_fusion = bf16[2048,2688]{0,1:T(8,128)(2,1)} fusion(bf16[1024,2048]{0,1:T(8,128)(2,1)} %all-gather.6.cloned.1.call-done, bf16[512,2688]{0,1:T(8,128)(2,1)} %get-tuple-element.7, bf16[512,2688]{0,1:T(8,128)(2,1)} %get-tuple-element.6), kind=kOutput, calls=%fused_computation.15 | convolution fusion | flops 11290804224 | bytes 20709376 | tf_op jit(solution)/shard_map/dot_general | solution.py:31
  331.6 22.2 %collective-permute-done.6 = bf16[512,1344]{0,1:T(8,128)(2,1)S(1)} collective-permute-done((bf16[512,1344]{0,1:T(8,128)(2,1)}, bf16[512,1344]{0,1:T(8,128)(2,1)S(1)}, u32[]{:S(2)}, u32[]{:S(2)}) %collective-permute-start.6) | collective-permute-done | bytes 1376288 | tf_op jit(solution)/shard_map/ppermute | solution.py:140
  353.8 87.5 %collective-permute-done.5 = bf16[512,1344]{0,1:T(8,128)(2,1)} collective-permute-done((bf16[512,1344]{0,1:T(8,128)(2,1)}, bf16[512,1344]{0,1:T(8,128)(2,1)}, u32[]{:S(2)}, u32[]{:S(2)}) %collective-permute-start.5) | collective-permute-done | bytes 1376288 | tf_op jit(solution)/shard_map/ppermute | solution.py:140
  443.7 4.5 add_convert_fusion
  (94 shorter events, 61.9 us)
Async XLA Ops:
  7.2 103.3 %all-gather.4.cloned.1.call-start = ((), (), s32[]{:S(2)}) async-start(), calls=%async_computation.1 | async-start | bytes 6881280 | tf_op jit(solution)/shard_map/all_gather | solution.py:91
  7.9 282.8 %all-gather.8.cloned.1.call-start = ((), (), s32[]{:S(2)}) async-start(), calls=%async_computation.3 | async-start | bytes 8257536 | tf_op jit(solution)/shard_map/all_gather | solution.py:152
  110.5 7.4 %copy-start.4 = (bf16[512,5376]{0,1:T(8,128)(2,1)S(1)}, bf16[512,5376]{0,1:T(8,128)(2,1)}, u32[]{:S(2)}) copy-start(bf16[512,5376]{0,1:T(8,128)(2,1)} %all-gather.4.cloned.1.call-done) | copy-start | bytes 16515076
  110.5 20.0 %slice-start.2 = ((s8[11010048]{0:T(1024)(128)(4,1)}), s8[4194304]{0:T(1024)(128)(4,1)S(1)}, s32[]{:S(2)}) async-start(s8[11010048]{0:T(1024)(128)(4,1)} %bitcast.99), calls=%async_computation.7 | async-start | bytes 8388608
  110.5 20.0 %slice-start.3 = ((s8[11010048]{0:T(1024)(128)(4,1)}), s8[4194304]{0:T(1024)(128)(4,1)S(1)}, s32[]{:S(2)}) async-start(s8[11010048]{0:T(1024)(128)(4,1)} %bitcast.99), calls=%async_computation.8 | async-start | bytes 8388608
  117.9 12.7 %slice-start.4 = ((s8[11010048]{0:T(1024)(128)(4,1)}), s8[2621440]{0:T(1024)(128)(4,1)S(1)}, s32[]{:S(2)}) async-start(s8[11010048]{0:T(1024)(128)(4,1)} %bitcast.99), calls=%async_computation.9 | async-start | bytes 5242880
  123.7 24.0 %collective-permute-start.1 = (bf16[2,512,512]{2,1,0:T(8,128)(2,1)S(1)}, bf16[2,512,512]{2,1,0:T(8,128)(2,1)}, u32[]{:S(2)}, u32[]{:S(2)}) collective-permute-start(bf16[2,512,512]{2,1,0:T(8,128)(2,1)S(1)} %pad_maximum_fusion.2), channel_id=1, source_target_pairs={{0,4},{4,8},{8,12},{12,16},{16,20},{20,24},{24,28},{1,5},{5,9},{9,... | collective-permute-start | bytes 3145736 | tf_op jit(solution)/shard_map/ppermute | solution.py:21
  127.4 35.0 %collective-permute-start = (bf16[2,512,512]{2,1,0:T(8,128)(2,1)S(1)}, bf16[2,512,512]{2,1,0:T(8,128)(2,1)}, u32[]{:S(2)}, u32[]{:S(2)}) collective-permute-start(bf16[2,512,512]{2,1,0:T(8,128)(2,1)S(1)} %pad_maximum_fusion.2), channel_id=1, source_target_pairs={{0,8},{4,12},{8,16},{12,20},{16,24},{20,28},{1,9},{5,13},{9,17},{1... | collective-permute-start | bytes 3145736 | tf_op jit(solution)/shard_map/ppermute | solution.py:21
  143.1 161.4 %all-gather.6.cloned.1.call-start = ((), (), s32[]{:S(2)}) async-start(), calls=%async_computation.2 | async-start | bytes 6291456 | tf_op jit(solution)/shard_map/all_gather | solution.py:157
  166.9 17.7 %copy-start.2 = (bf16[1536,4,128,1]{0,2,3,1:T(8,128)(2,1)}, bf16[1536,4,128,1]{0,2,3,1:T(8,128)(2,1)S(1)}, u32[]{:S(2)}) copy-start(bf16[1536,4,128,1]{0,2,3,1:T(8,128)(2,1)S(1)} %copy.22) | copy-start | bytes 4718596
  184.5 12.7 %copy-start.10 = (bf16[1536,4,128]{2,1,0:T(4,128)(2,1)S(1)}, bf16[1536,4,128]{2,1,0:T(4,128)(2,1)}, u32[]{:S(2)}) copy-start(bf16[1536,4,128]{2,1,0:T(4,128)(2,1)} %reshape_squeeze.7) | copy-start | bytes 4718596
  184.5 12.6 %copy-start.11 = (bf16[512,1024]{0,1:T(8,128)(2,1)S(1)}, bf16[512,1024]{0,1:T(8,128)(2,1)}, u32[]{:S(2)}) copy-start(bf16[512,1024]{0,1:T(8,128)(2,1)} %copy.35) | copy-start | bytes 3145732
  237.4 10.1 %slice-start.5 = ((s8[11010048]{0:T(1024)(128)(4,1)}), s8[4194304]{0:T(1024)(128)(4,1)S(1)}, s32[]{:S(2)}) async-start(s8[11010048]{0:T(1024)(128)(4,1)} %bitcast.101), calls=%async_computation.10 | async-start | bytes 8388608
  241.0 6.5 %slice-start.6 = ((s8[11010048]{0:T(1024)(128)(4,1)}), s8[4194304]{0:T(1024)(128)(4,1)S(1)}, s32[]{:S(2)}) async-start(s8[11010048]{0:T(1024)(128)(4,1)} %bitcast.101), calls=%async_computation.11 | async-start | bytes 8388608
  241.2 28.0 %collective-permute-start.3 = (bf16[2,512,512]{1,2,0:T(8,128)(2,1)S(1)}, bf16[2,512,512]{1,2,0:T(8,128)(2,1)S(1)}, u32[]{:S(2)}, u32[]{:S(2)}) collective-permute-start(bf16[2,512,512]{1,2,0:T(8,128)(2,1)S(1)} %get-tuple-element.11), channel_id=1, source_target_pairs={{8,0},{12,4},{16,8},{20,12},{24,16},{28,20},{9,1},{13,5},{17,9},{2... | collective-permute-start | bytes 3145736 | tf_op jit(solution)/shard_map/ppermute | solution.py:21
  243.4 29.7 %collective-permute-start.2 = (bf16[2,512,512]{1,2,0:T(8,128)(2,1)S(1)}, bf16[2,512,512]{1,2,0:T(8,128)(2,1)S(1)}, u32[]{:S(2)}, u32[]{:S(2)}) collective-permute-start(bf16[2,512,512]{1,2,0:T(8,128)(2,1)S(1)} %get-tuple-element.10), channel_id=1, source_target_pairs={{4,0},{8,4},{12,8},{16,12},{20,16},{24,20},{28,24},{5,1},{9,5},{13... | collective-permute-start | bytes 3145736 | tf_op jit(solution)/shard_map/ppermute | solution.py:21
  247.5 26.2 %copy-start.6 = (bf16[4,128,2,512]{3,1,2,0:T(8,128)(2,1)}, bf16[4,128,2,512]{3,1,2,0:T(8,128)(2,1)S(1)}, u32[]{:S(2)}) copy-start(bf16[4,128,2,512]{3,1,2,0:T(8,128)(2,1)S(1)} %multiply_convert_fusion.1) | copy-start | bytes 3145732
  253.9 19.2 %copy-start = (f32[4,128,1536]{2,1,0:T(8,128)S(1)}, f32[4,128,1536]{2,1,0:T(8,128)}, u32[]{:S(2)}) copy-start(f32[4,128,1536]{2,1,0:T(8,128)} %fusion.16) | copy-start | bytes 9437188
  253.9 19.2 %copy-start.1 = (f32[4,1536,128,1]{1,2,3,0:T(8,128)S(1)}, f32[4,1536,128,1]{1,2,3,0:T(8,128)}, u32[]{:S(2)}) copy-start(f32[4,1536,128,1]{1,2,3,0:T(8,128)} %fusion.5) | copy-start | bytes 9437188
  275.2 9.0 %slice-start = ((s8[5505024]{0:T(1024)(128)(4,1)}), s8[4194304]{0:T(1024)(128)(4,1)S(1)}, s32[]{:S(2)}) async-start(s8[5505024]{0:T(1024)(128)(4,1)} %bitcast.86), calls=%async_computation.5 | async-start | bytes 8388608
  290.4 157.9 %reduce-scatter.2.cloned.1.call-start = ((), (), s32[]{:S(2)}) async-start(), calls=%async_computation.4 | async-start | bytes 13762560 | tf_op jit(solution)/shard_map/reduce_scatter | solution.py:159
  321.9 31.9 %collective-permute-start.6 = (bf16[512,1344]{0,1:T(8,128)(2,1)}, bf16[512,1344]{0,1:T(8,128)(2,1)S(1)}, u32[]{:S(2)}, u32[]{:S(2)}) collective-permute-start(bf16[512,1344]{0,1:T(8,128)(2,1)} %fusion.22), channel_id=1, source_target_pairs={{0,1},{1,2},{2,3},{3,0},{4,5},{5,6},{6,7},{7,4},{8,9},{9,10},{10,1... | collective-permute-start | bytes 4128776 | tf_op jit(solution)/shard_map/ppermute | solution.py:140
  323.1 118.2 %collective-permute-start.5 = (bf16[512,1344]{0,1:T(8,128)(2,1)}, bf16[512,1344]{0,1:T(8,128)(2,1)}, u32[]{:S(2)}, u32[]{:S(2)}) collective-permute-start(bf16[512,1344]{0,1:T(8,128)(2,1)} %fusion.21), channel_id=1, source_target_pairs={{0,2},{1,3},{2,0},{3,1},{4,6},{5,7},{6,4},{7,5},{8,10},{9,11},{10,... | collective-permute-start | bytes 4128776 | tf_op jit(solution)/shard_map/ppermute | solution.py:140
  324.3 119.5 %collective-permute-start.4 = (bf16[512,1344]{0,1:T(8,128)(2,1)}, bf16[512,1344]{0,1:T(8,128)(2,1)}, u32[]{:S(2)}, u32[]{:S(2)}) collective-permute-start(bf16[512,1344]{0,1:T(8,128)(2,1)} %fusion.20), channel_id=1, source_target_pairs={{0,3},{1,0},{2,1},{3,2},{4,7},{5,4},{6,5},{7,6},{8,11},{9,8},{10,9... | collective-permute-start | bytes 4128776 | tf_op jit(solution)/shard_map/ppermute | solution.py:140
  (9 other events, 35.0 us)
Sparse Core Ops, SparseCore 0:
  9.6 100.8 all-gather.3
  143.2 15.9 all-gather.7
  290.5 13.9 all-gather.5
  322.0 108.1 reduce-scatter.1

commit v10 on v1

--- a/solution.py
+++ b/solution.py
@@ -1,6 +1,8 @@
 import jax
 import jax.numpy as jnp
 from jax import lax
+from jax.experimental import pallas as pl
+from jax.experimental.pallas import tpu as pltpu
 from jax.sharding import PartitionSpec as P
 
 D = 5376
@@ -32,16 +34,41 @@
     )
 
 
+def attention_kernel(mask_ref, q_ref, k_ref, v_ref, g_ref, qg_ref, kg_ref, vg_ref):
+    score_scale = (D / HEADS) ** (-0.5)
+    rows = mask_ref.shape[0]
+    groups = q_ref.shape[1] // rows
+    allowed = mask_ref[...] > 0.5
+    keys = k_ref[0]
+    values = v_ref[0]
+    key_acc = jnp.zeros(kg_ref.shape[1:], jnp.float32)
+    value_acc = jnp.zeros(vg_ref.shape[1:], jnp.float32)
+    for group in range(groups):
+        rows_of = slice(group * rows, (group + 1) * rows)
+        queries = q_ref[0, rows_of, :]
+        grads = g_ref[0, rows_of, :]
+        scores = contract_last(queries, keys) * score_scale
+        masked = jnp.where(allowed, scores, neg_large)
+        row_max = jnp.max(masked, axis=-1, keepdims=True)
+        expo = jnp.where(allowed, jnp.exp(masked - row_max), 0.0)
+        probs = expo / jnp.sum(expo, axis=-1, keepdims=True)
+        dprobs = contract_last(grads, values)
+        center = jnp.sum(probs * dprobs, axis=-1, keepdims=True)
+        dscores = (probs * (dprobs - center)).astype(jnp.bfloat16)
+        probs_low = probs.astype(jnp.bfloat16)
+        query_grad = jnp.dot(dscores, keys, preferred_element_type=jnp.float32) * score_scale
+        qg_ref[0, rows_of, :] = query_grad.astype(jnp.bfloat16)
+        key_acc = key_acc + contract_first(dscores, queries)
+        value_acc = value_acc + contract_first(probs_low, grads)
+    kg_ref[0] = key_acc * score_scale
+    vg_ref[0] = value_acc
+
+
 def attend(queries, key_value, grads, query_first, key_first, seg_query, seg_key):
     tok_rows = queries.shape[0]
     key_rows = key_value.shape[1]
     groups = HEADS // KV_HEADS
     kv_local = key_value.shape[2] // HEAD_DIM
-    score_scale = (D / HEADS) ** (-0.5)
-    query_four = queries.reshape(tok_rows, kv_local, groups, HEAD_DIM)
-    grad_four = grads.reshape(tok_rows, kv_local, groups, HEAD_DIM)
-    key_three = key_value[0].reshape(key_rows, kv_local, HEAD_DIM)
-    value_three = key_value[1].reshape(key_rows, kv_local, HEAD_DIM)
     query_pos = query_first + jnp.arange(tok_rows, dtype=jnp.int32)
     key_pos = key_first + jnp.arange(key_rows, dtype=jnp.int32)
     spacing = query_pos[:, None] - key_pos[None, :]
@@ -51,36 +78,45 @@
         & (spacing < WINDOW)
         & (seg_query[:, None] == seg_key[None, :])
     )
-    scores = (
-        jnp.einsum("akgd,ckd->kgac", query_four, key_three, preferred_element_type=jnp.float32)
-        * score_scale
-    )
-    masked = jnp.where(allowed, scores, neg_large)
-    row_max = jnp.max(masked, axis=-1, keepdims=True)
-    expo = jnp.where(allowed, jnp.exp(masked - row_max), 0.0)
-    probs = expo / jnp.sum(expo, axis=-1, keepdims=True)
-    dprobs = jnp.einsum(
-        "akgd,ckd->kgac", grad_four, value_three, preferred_element_type=jnp.float32
-    )
-    center = jnp.sum(probs * dprobs, axis=-1, keepdims=True)
-    dscores = (probs * (dprobs - center)).astype(jnp.bfloat16)
-    probs_low = probs.astype(jnp.bfloat16)
+    mask = allowed.astype(jnp.float32)
+
+    def by_head(x, rows):
+        return x.reshape(rows, kv_local, -1, HEAD_DIM).transpose(1, 2, 0, 3).reshape(kv_local, -1, HEAD_DIM)
+
+    q_heads = by_head(queries, tok_rows)
+    g_heads = by_head(grads, tok_rows)
+    k_heads = by_head(key_value[0], key_rows)
+    v_heads = by_head(key_value[1], key_rows)
+    q_spec = pl.BlockSpec((1, groups * tok_rows, HEAD_DIM), lambda h: (h, 0, 0))
+    k_spec = pl.BlockSpec((1, key_rows, HEAD_DIM), lambda h: (h, 0, 0))
+    q_grad, k_grad, v_grad = pl.pallas_call(
+        attention_kernel,
+        grid=(kv_local,),
+        in_specs=[
+            pl.BlockSpec((tok_rows, key_rows), lambda h: (0, 0)),
+            q_spec,
+            k_spec,
+            k_spec,
+            q_spec,
+        ],
+        out_specs=[q_spec, k_spec, k_spec],
+        out_shape=[
+            jax.ShapeDtypeStruct(q_heads.shape, jnp.bfloat16),
+            jax.ShapeDtypeStruct(k_heads.shape, jnp.float32),
+            jax.ShapeDtypeStruct(k_heads.shape, jnp.float32),
+        ],
+        compiler_params=pltpu.CompilerParams(vmem_limit_bytes=56 * 1024 * 1024),
+    )(mask, q_heads, k_heads, v_heads, g_heads)
     query_grad = (
-        (
-            jnp.einsum("kgac,ckd->akgd", dscores, key_three, preferred_element_type=jnp.float32)
-            * score_scale
-        )
+        q_grad.reshape(kv_local, groups, tok_rows, HEAD_DIM)
+        .transpose(2, 0, 1, 3)
         .reshape(tok_rows, -1)
-        .astype(jnp.bfloat16)
-    )
-    key_grad = (
-        jnp.einsum("kgac,akgd->ckd", dscores, query_four, preferred_element_type=jnp.float32)
-        * score_scale
-    ).reshape(key_rows, -1)
-    value_grad = jnp.einsum(
-        "kgac,akgd->ckd", probs_low, grad_four, preferred_element_type=jnp.float32
-    ).reshape(key_rows, -1)
-    return (query_grad, jnp.stack([key_grad, value_grad]))
+    )
+
+    def by_row(x):
+        return x.transpose(1, 0, 2).reshape(key_rows, -1)
+
+    return (query_grad, jnp.stack([by_row(k_grad), by_row(v_grad)]))
 
 
 def per_device(tokens, query_weight, key_weight, value_weight, output_grad, segments):

time: 443 us -> 415 us (0.937)
  matrix products: 127 us -> 74.1 us
  Pallas kernels: 0 us -> 29.4 us
  other arithmetic: 26.2 us -> 12.8 us
  local copies, waits for them, and re-layouts: 12.1 us -> 23.6 us
    dot_general x4 -> x0, matrix products: 38.7 us -> none  [the longest x1 16.4 us: attend(): jnp.einsum('akgd,ckd->kgac', grad_four, value_three, preferred_element_ty...]
    pallas_call x0 -> x1, Pallas kernels: none -> 29.4 us  [attend(): pl.pallas_call(attention_kernel, grid=(kv_local,), in_specs=[pl.BlockSpec...]
    convert_element_type x1, other arithmetic: 17 us -> 2.82 us  [attend(): mask = allowed.astype(jnp.float32)]
    sub x1 -> x0, matrix products: 13.6 us -> none  [attend(): expo = jnp.where(allowed, jnp.exp(masked - row_max), 0.0)]
    transpose x0 -> x2, local copies, waits for them, and re-layouts: none -> 5.89 us  [by_row(): return x.transpose(1, 0, 2).reshape(key_rows, -1)]
  transfers between devices with their start and end apart: 9 -> 9, of which waited for: 9 -> 7; matrix products, arithmetic and copies ran while one was open for 11% -> 13% of each run, Pallas kernels for 0% -> 0%
where the time goes in v10:
time: 415 us; the launch traced here: 412 us
  waiting for transfers between devices  240 us (58%)
  matrix products  74.1 us (18%)
  Pallas kernels  29.4 us (7%)
  local copies, waits for them, and re-layouts  23.6 us (6%)
  starting transfers between devices  17.6 us (4%)
  between operations  14.4 us (3%)
  other arithmetic  12.8 us (3%)
    all_gather x1, waiting for transfers between devices, per_device(): gathered = lax.all_gather(tokens, 'head', axis=1, tiled=True)  103 us
    ppermute x3, waiting for transfers between devices, per_device(): got = lax.ppermute(sent, 'head', pairs).astype(jnp.float32)  100 us
    ppermute x4, waiting for transfers between devices, passed_along(): return lax.ppermute(x, axis, pairs)  35.4 us
    dot_general x12, matrix products, contract_last(): lax.dot_general(left, right, (((1,), (1,)), ((), ())), preferred_element_...  32.7 us
    pallas_call x1, Pallas kernels, attend(): pl.pallas_call(attention_kernel, grid=(kv_local,), in_specs=[pl.BlockSpec...  29.4 us
    dot_general x1, matrix products, contract_first(): lax.dot_general(left, right, (((0,), (0,)), ((), ())), preferred_element_...  18 us
    ppermute x4, starting transfers between devices, passed_along(): return lax.ppermute(x, axis, pairs)  13.2 us
    dot_general x1, matrix products, per_device(): jnp.dot(gathered, query_weight, preferred_element_type=jnp.float32)  10.5 us
  transfers between devices with their start and end apart: 9, of which 7 were waited for; matrix products, arithmetic and copies ran while one was open for 13% of the time, Pallas kernels for 0%

profile of v10, /device:TPU:11, one launch (start us, length us, event | category | flops | bytes accessed | tf_op | source)
XLA Modules:
  0.0 412.4 jit_solution(49399940664665000)
XLA Ops:
  7.9 102.5 %all-gather.2.cloned.1.call-done = bf16[512,5376]{0,1:T(8,128)(2,1)} async-done(((bf16[512,1344]{0,1:T(8,128)(2,1)}), bf16[512,5376]{0,1:T(8,128)(2,1)}) %all-gather.2.cloned.1.call-update) | async-done | bytes 5505040 | tf_op jit(solution)/shard_map/all_gather | solution.py:126
  110.5 7.3 %fusion.40 = bf16[1,512,512]{2,1,0:T(8,128)(2,1)S(1)} fusion(bf16[512,5376]{0,1:T(8,128)(2,1)} %all-gather.2.cloned.1.call-done, bf16[5376,512]{1,0:T(8,128)(2,1)} %param.8), kind=kOutput, calls=%fused_computation.60 | convolution fusion | flops 2818834432 | bytes 11534336 | tf_op jit(solution)/shard_map/dot_general | solution.py:130
  117.9 5.6 %fusion.41 = bf16[1,512,512]{2,1,0:T(8,128)(2,1)S(1)} fusion(bf16[512,5376]{0,1:T(8,128)(2,1)S(1)} %copy-done.6, bf16[5376,512]{1,0:T(8,128)(2,1)} %param.9), kind=kOutput, calls=%fused_computation.61 | convolution fusion | flops 2818834432 | bytes 11534336 | tf_op jit(solution)/shard_map/dot_general | solution.py:133
  124.5 3.6 collective-permute-start
  130.3 2.8 fusion.3.mask_ref
  133.1 7.1 %collective-permute-done = bf16[2,512,512]{2,1,0:T(8,128)(2,1)} collective-permute-done((bf16[2,512,512]{2,1,0:T(8,128)(2,1)}, bf16[2,512,512]{2,1,0:T(8,128)(2,1)}, u32[]{:S(2)}, u32[]{:S(2)}) %collective-permute-start) | collective-permute-done | bytes 1048608 | tf_op jit(solution)/shard_map/ppermute | solution.py:22
  140.2 5.5 %collective-permute-start.1 = (bf16[2,512,512]{2,1,0:T(8,128)(2,1)}, bf16[2,512,512]{2,1,0:T(8,128)(2,1)}, u32[]{:S(2)}, u32[]{:S(2)}) collective-permute-start(bf16[2,512,512]{2,1,0:T(8,128)(2,1)} %collective-permute-done), channel_id=1, source_target_pairs={{0,4},{4,8},{8,12},{12,16},{16,20},{20,24},{24,28},{1,5},{5,9},{9,... | collective-permute-start | bytes 3145736 | tf_op jit(solution)/shard_map/ppermute | solution.py:22
  145.7 10.5 %convolution_convert_fusion.1 = bf16[512,1024]{1,0:T(8,128)(2,1)S(1)} fusion(bf16[512,5376]{0,1:T(8,128)(2,1)} %all-gather.2.cloned.1.call-done, bf16[5376,1024]{1,0:T(8,128)(2,1)} %param.7), kind=kOutput, calls=%fused_computation.49 | convolution fusion | flops 5637668864 | bytes 17563648 | tf_op jit(solution)/shard_map/dot_general | solution.py:127
  166.8 29.4 %shard_map.93 = (bf16[4,1024,128]{2,1,0:T(8,128)(2,1)}, f32[4,1536,128]{2,1,0:T(8,128)}, f32[4,1536,128]{2,1,0:T(8,128)}) custom-call(f32[512,1536]{1,0:T(8,128)} %fusion.3.mask_ref, bf16[4,1024,128]{2,1,0:T(8,128)(2,1)} %bitcast.66, bf16[4,1536,128]{2,1,0:T(8,128)(2,1)} %bitcast.57, bf16[4,1536,128]{2,1,0:T(8,128)(2,1)} %bitcast.58, ...), custom_call_target="tpu_custom_call" | custom-call | tf_op jit(solution)/shard_map/pallas_call | solution.py:92
  196.2 2.4 copy.19
  198.5 3.5 copy.20
  205.7 15.1 %collective-permute-done.2 = bf16[2,512,512]{1,2,0:T(8,128)(2,1)S(1)} collective-permute-done((bf16[2,512,512]{1,2,0:T(8,128)(2,1)S(1)}, bf16[2,512,512]{1,2,0:T(8,128)(2,1)S(1)}, u32[]{:S(2)}, u32[]{:S(2)}) %collective-permute-start.2) | collective-permute-done | bytes 1048608 | tf_op jit(solution)/shard_map/ppermute | solution.py:22
  226.3 13.1 %collective-permute-done.3 = bf16[2,512,512]{1,2,0:T(8,128)(2,1)} collective-permute-done((bf16[2,512,512]{1,2,0:T(8,128)(2,1)}, bf16[2,512,512]{1,2,0:T(8,128)(2,1)}, u32[]{:S(2)}, u32[]{:S(2)}) %collective-permute-start.3) | collective-permute-done | bytes 1048608 | tf_op jit(solution)/shard_map/ppermute | solution.py:22
  242.4 18.0 %convolution_convert_fusion = bf16[2048,5376]{0,1:T(8,128)(2,1)} fusion(bf16[512,5376]{0,1:T(8,128)(2,1)} %all-gather.2.cloned.1.call-done, bf16[512,512]{0,1:T(8,128)(2,1)S(1)} %get-tuple-element.15, bf16[512,512]{0,1:T(8,128)(2,1)S(1)} %get-tuple-element.14, bf16[512,1024]{0,1:T(8,128)(2,1)} %bitcast.69), kind=kOutput, calls=%fused_computation | convolution fusion | flops 11291590656 | bytes 29622272 | tf_op jit(solution)/shard_map/dot_general | solution.py:32
  261.6 3.4 fusion.16
  265.0 4.3 %fusion.14 = f32[512,1344]{0,1:T(8,128)S(1)} fusion(bf16[512,1024]{0,1:T(8,128)(2,1)S(1)} %bitcast.71, bf16[5376,1024]{1,0:T(8,128)(2,1)} %param.7, s32[]{:T(128)S(6)} %select_n.46), kind=kOutput, calls=%fused_computation.32 | convolution fusion | flops 1409286144 | bytes 6553604 | tf_op jit(solution)/shard_map/dot_general | solution.py:26
  269.3 5.7 %fusion.12 = f32[512,1344]{0,1:T(8,128)S(1)} fusion(bf16[512,1024]{0,1:T(8,128)(2,1)S(1)} %bitcast.72, bf16[5376,1024]{1,0:T(8,128)(2,1)} %param.7, s32[]{:T(128)S(6)} %select_n.48), kind=kOutput, calls=%fused_computation.30 | convolution fusion | flops 1409286144 | bytes 6553604 | tf_op jit(solution)/shard_map/dot_general | solution.py:26
  277.9 3.0 collective-permute-start.4
  288.0 4.0 fusion.10
  292.1 2.3 convolution_add_fusion.1
  294.4 75.4 %collective-permute-done.4 = bf16[512,1344]{0,1:T(8,128)(2,1)S(1)} collective-permute-done((bf16[512,1344]{0,1:T(8,128)(2,1)}, bf16[512,1344]{0,1:T(8,128)(2,1)S(1)}, u32[]{:S(2)}, u32[]{:S(2)}) %collective-permute-start.4) | collective-permute-done | bytes 1376288 | tf_op jit(solution)/shard_map/ppermute | solution.py:176
  369.8 24.5 %collective-permute-done.6 = bf16[512,1344]{0,1:T(8,128)(2,1)} collective-permute-done((bf16[512,1344]{0,1:T(8,128)(2,1)}, bf16[512,1344]{0,1:T(8,128)(2,1)}, u32[]{:S(2)}, u32[]{:S(2)}) %collective-permute-start.6) | collective-permute-done | bytes 1376288 | tf_op jit(solution)/shard_map/ppermute | solution.py:176
  394.3 4.5 %add_convert_fusion = bf16[512,1344]{0,1:T(8,128)(2,1)} fusion(bf16[512,1344]{0,1:T(8,128)(2,1)} %collective-permute-done.6, bf16[512,1344]{0,1:T(8,128)(2,1)} %collective-permute-done.5, bf16[512,1344]{0,1:T(8,128)(2,1)S(1)} %collective-permute-done.4, f32[512,1344]{0,1:T(8,128)S(1)} %convolution_add_fusion.1, bf16[5376,512]{1,0:T(8,128)(2,1)} %param.9, ...), kind=kOutput, calls=%fused_computation.27 | convolution fusion | flops 711524352 | bytes 10158084 | tf_op jit(solution)/shard_map/dot_general | solution.py:26
  400.7 2.4 fusion.9
  (63 shorter events, 41.9 us)
Async XLA Ops:
  7.2 103.3 %all-gather.2.cloned.1.call-start = ((), (), s32[]{:S(2)}) async-start(), calls=%async_computation.1 | async-start | bytes 6881280 | tf_op jit(solution)/shard_map/all_gather | solution.py:126
  7.9 392.8 %reduce-scatter.2.cloned.1.call-start = ((), (), s32[]{:S(2)}) async-start(), calls=%async_computation.2 | async-start | bytes 24772608 | tf_op jit(solution)/shard_map/reduce_scatter | solution.py:181
  110.5 7.4 %copy-start.6 = (bf16[512,5376]{0,1:T(8,128)(2,1)S(1)}, bf16[512,5376]{0,1:T(8,128)(2,1)}, u32[]{:S(2)}) copy-start(bf16[512,5376]{0,1:T(8,128)(2,1)} %all-gather.2.cloned.1.call-done) | copy-start | bytes 16515076
  123.5 4.7 %copy-start.3 = (bf16[512,1024]{1,0:T(8,128)(2,1)S(1)}, bf16[512,1024]{1,0:T(8,128)(2,1)}, u32[]{:S(2)}) copy-start(bf16[512,1024]{1,0:T(8,128)(2,1)} %param.10) | copy-start | bytes 3145732
  123.5 6.6 %copy-start.5 = (s32[4096]{0:T(1024)S(1)}, s32[4096]{0:T(1024)}, u32[]{:S(2)}) copy-start(s32[4096]{0:T(1024)} %param.11) | copy-start | bytes 49156
  124.5 15.7 %collective-permute-start = (bf16[2,512,512]{2,1,0:T(8,128)(2,1)}, bf16[2,512,512]{2,1,0:T(8,128)(2,1)}, u32[]{:S(2)}, u32[]{:S(2)}) collective-permute-start(bf16[2,512,512]{2,1,0:T(8,128)(2,1)} %pad_maximum_fusion.1), channel_id=1, source_target_pairs={{0,4},{4,8},{8,12},{12,16},{16,20},{20,24},{24,28},{1,5},{5,9},{9,... | collective-permute-start | bytes 3145736 | tf_op jit(solution)/shard_map/ppermute | solution.py:22
  140.2 17.8 %collective-permute-start.1 = (bf16[2,512,512]{2,1,0:T(8,128)(2,1)}, bf16[2,512,512]{2,1,0:T(8,128)(2,1)}, u32[]{:S(2)}, u32[]{:S(2)}) collective-permute-start(bf16[2,512,512]{2,1,0:T(8,128)(2,1)} %collective-permute-done), channel_id=1, source_target_pairs={{0,4},{4,8},{8,12},{12,16},{16,20},{20,24},{24,28},{1,5},{5,9},{9,... | collective-permute-start | bytes 3145736 | tf_op jit(solution)/shard_map/ppermute | solution.py:22
  202.1 18.8 %copy-start = (f32[1536,4,128]{0,2,1:T(8,128)S(1)}, f32[1536,4,128]{0,2,1:T(8,128)}, u32[]{:S(2)}) copy-start(f32[1536,4,128]{0,2,1:T(8,128)} %copy.20) | copy-start | bytes 9437188
  203.6 17.3 %collective-permute-start.2 = (bf16[2,512,512]{1,2,0:T(8,128)(2,1)S(1)}, bf16[2,512,512]{1,2,0:T(8,128)(2,1)S(1)}, u32[]{:S(2)}, u32[]{:S(2)}) collective-permute-start(bf16[2,512,512]{1,2,0:T(8,128)(2,1)S(1)} %fusion.24), channel_id=1, source_target_pairs={{4,0},{8,4},{12,8},{16,12},{20,16},{24,20},{28,24},{5,1},{9,5},{13... | collective-permute-start | bytes 3145736 | tf_op jit(solution)/shard_map/ppermute | solution.py:22
  222.2 17.3 %collective-permute-start.3 = (bf16[2,512,512]{1,2,0:T(8,128)(2,1)}, bf16[2,512,512]{1,2,0:T(8,128)(2,1)}, u32[]{:S(2)}, u32[]{:S(2)}) collective-permute-start(bf16[2,512,512]{1,2,0:T(8,128)(2,1)} %fusion.20), channel_id=1, source_target_pairs={{4,0},{8,4},{12,8},{16,12},{20,16},{24,20},{28,24},{5,1},{9,5},{13... | collective-permute-start | bytes 3145736 | tf_op jit(solution)/shard_map/ppermute | solution.py:22
  241.4 1.0 copy-start.1
  260.4 1.2 copy-start.4
  265.0 10.0 %slice-start.2 = ((s8[5505024]{0:T(1024)(128)(4,1)}), s8[4194304]{0:T(1024)(128)(4,1)S(1)}, s32[]{:S(2)}) async-start(s8[5505024]{0:T(1024)(128)(4,1)} %bitcast.63), calls=%async_computation.5 | async-start | bytes 8388608
  265.0 10.9 %slice-start = ((s8[5505024]{0:T(1024)(128)(4,1)}), s8[4194304]{0:T(1024)(128)(4,1)S(1)}, s32[]{:S(2)}) async-start(s8[5505024]{0:T(1024)(128)(4,1)} %bitcast.61), calls=%async_computation.3 | async-start | bytes 8388608
  269.3 5.7 %copy-start.2 = (bf16[2,512,512]{1,2,0:T(8,128)(2,1)S(1)}, bf16[2,512,512]{1,2,0:T(8,128)(2,1)}, u32[]{:S(2)}) copy-start(bf16[2,512,512]{1,2,0:T(8,128)(2,1)} %copy-done.1) | copy-start | bytes 3145732
  269.3 5.7 %slice-start.3 = ((s8[5505024]{0:T(1024)(128)(4,1)}), s8[1310720]{0:T(1024)(128)(4,1)S(1)}, s32[]{:S(2)}) async-start(s8[5505024]{0:T(1024)(128)(4,1)} %bitcast.63), calls=%async_computation.6 | async-start | bytes 2621440
  269.3 6.6 %slice-start.1 = ((s8[5505024]{0:T(1024)(128)(4,1)}), s8[1310720]{0:T(1024)(128)(4,1)S(1)}, s32[]{:S(2)}) async-start(s8[5505024]{0:T(1024)(128)(4,1)} %bitcast.61), calls=%async_computation.4 | async-start | bytes 2621440
  277.9 91.9 %collective-permute-start.4 = (bf16[512,1344]{0,1:T(8,128)(2,1)}, bf16[512,1344]{0,1:T(8,128)(2,1)S(1)}, u32[]{:S(2)}, u32[]{:S(2)}) collective-permute-start(bf16[512,1344]{0,1:T(8,128)(2,1)} %fusion.4), channel_id=1, source_target_pairs={{0,3},{1,0},{2,1},{3,2},{4,7},{5,4},{6,5},{7,6},{8,11},{9,8},{10,9... | collective-permute-start | bytes 4128776 | tf_op jit(solution)/shard_map/ppermute | solution.py:176
  283.8 86.0 %collective-permute-start.5 = (bf16[512,1344]{0,1:T(8,128)(2,1)}, bf16[512,1344]{0,1:T(8,128)(2,1)}, u32[]{:S(2)}, u32[]{:S(2)}) collective-permute-start(bf16[512,1344]{0,1:T(8,128)(2,1)} %fusion.5), channel_id=1, source_target_pairs={{0,2},{1,3},{2,0},{3,1},{4,6},{5,7},{6,4},{7,5},{8,10},{9,11},{10,... | collective-permute-start | bytes 4128776 | tf_op jit(solution)/shard_map/ppermute | solution.py:176
  286.6 107.7 %collective-permute-start.6 = (bf16[512,1344]{0,1:T(8,128)(2,1)}, bf16[512,1344]{0,1:T(8,128)(2,1)}, u32[]{:S(2)}, u32[]{:S(2)}) collective-permute-start(bf16[512,1344]{0,1:T(8,128)(2,1)} %fusion.6), channel_id=1, source_target_pairs={{0,1},{1,2},{2,3},{3,0},{4,5},{5,6},{6,7},{7,4},{8,9},{9,10},{10,1... | collective-permute-start | bytes 4128776 | tf_op jit(solution)/shard_map/ppermute | solution.py:176
Sparse Core Ops, SparseCore 0:
  9.6 100.8 all-gather.1
  260.6 140.0 reduce-scatter.1

commit v11 on v10

--- a/solution.py
+++ b/solution.py
@@ -36,17 +36,16 @@
 
 def attention_kernel(mask_ref, q_ref, k_ref, v_ref, g_ref, qg_ref, kg_ref, vg_ref):
     score_scale = (D / HEADS) ** (-0.5)
-    rows = mask_ref.shape[0]
-    groups = q_ref.shape[1] // rows
+    groups = q_ref.shape[1] // HEAD_DIM
     allowed = mask_ref[...] > 0.5
     keys = k_ref[0]
     values = v_ref[0]
-    key_acc = jnp.zeros(kg_ref.shape[1:], jnp.float32)
-    value_acc = jnp.zeros(vg_ref.shape[1:], jnp.float32)
+    key_acc = jnp.zeros(kg_ref.shape, jnp.float32)
+    value_acc = jnp.zeros(vg_ref.shape, jnp.float32)
     for group in range(groups):
-        rows_of = slice(group * rows, (group + 1) * rows)
-        queries = q_ref[0, rows_of, :]
-        grads = g_ref[0, rows_of, :]
+        cols = slice(group * HEAD_DIM, (group + 1) * HEAD_DIM)
+        queries = q_ref[:, cols]
+        grads = g_ref[:, cols]
         scores = contract_last(queries, keys) * score_scale
         masked = jnp.where(allowed, scores, neg_large)
         row_max = jnp.max(masked, axis=-1, keepdims=True)
@@ -57,11 +56,11 @@
         dscores = (probs * (dprobs - center)).astype(jnp.bfloat16)
         probs_low = probs.astype(jnp.bfloat16)
         query_grad = jnp.dot(dscores, keys, preferred_element_type=jnp.float32) * score_scale
-        qg_ref[0, rows_of, :] = query_grad.astype(jnp.bfloat16)
+        qg_ref[:, cols] = query_grad.astype(jnp.bfloat16)
         key_acc = key_acc + contract_first(dscores, queries)
         value_acc = value_acc + contract_first(probs_low, grads)
-    kg_ref[0] = key_acc * score_scale
-    vg_ref[0] = value_acc
+    kg_ref[...] = key_acc * score_scale
+    vg_ref[...] = value_acc
 
 
 def attend(queries, key_value, grads, query_first, key_first, seg_query, seg_key):
@@ -79,44 +78,27 @@
         & (seg_query[:, None] == seg_key[None, :])
     )
     mask = allowed.astype(jnp.float32)
-
-    def by_head(x, rows):
-        return x.reshape(rows, kv_local, -1, HEAD_DIM).transpose(1, 2, 0, 3).reshape(kv_local, -1, HEAD_DIM)
-
-    q_heads = by_head(queries, tok_rows)
-    g_heads = by_head(grads, tok_rows)
-    k_heads = by_head(key_value[0], key_rows)
-    v_heads = by_head(key_value[1], key_rows)
-    q_spec = pl.BlockSpec((1, groups * tok_rows, HEAD_DIM), lambda h: (h, 0, 0))
-    k_spec = pl.BlockSpec((1, key_rows, HEAD_DIM), lambda h: (h, 0, 0))
-    q_grad, k_grad, v_grad = pl.pallas_call(
+    q_spec = pl.BlockSpec((tok_rows, groups * HEAD_DIM), lambda h: (0, h))
+    kv_out_spec = pl.BlockSpec((key_rows, HEAD_DIM), lambda h: (0, h))
+    query_grad, key_grad, value_grad = pl.pallas_call(
         attention_kernel,
         grid=(kv_local,),
         in_specs=[
             pl.BlockSpec((tok_rows, key_rows), lambda h: (0, 0)),
             q_spec,
-            k_spec,
-            k_spec,
+            pl.BlockSpec((1, key_rows, HEAD_DIM), lambda h: (0, 0, h)),
+            pl.BlockSpec((1, key_rows, HEAD_DIM), lambda h: (1, 0, h)),
             q_spec,
         ],
-        out_specs=[q_spec, k_spec, k_spec],
+        out_specs=[q_spec, kv_out_spec, kv_out_spec],
         out_shape=[
-            jax.ShapeDtypeStruct(q_heads.shape, jnp.bfloat16),
-            jax.ShapeDtypeStruct(k_heads.shape, jnp.float32),
-            jax.ShapeDtypeStruct(k_heads.shape, jnp.float32),
+            jax.ShapeDtypeStruct(queries.shape, jnp.bfloat16),
+            jax.ShapeDtypeStruct(key_value.shape[1:], jnp.float32),
+            jax.ShapeDtypeStruct(key_value.shape[1:], jnp.float32),
         ],
         compiler_params=pltpu.CompilerParams(vmem_limit_bytes=56 * 1024 * 1024),
-    )(mask, q_heads, k_heads, v_heads, g_heads)
-    query_grad = (
-        q_grad.reshape(kv_local, groups, tok_rows, HEAD_DIM)
-        .transpose(2, 0, 1, 3)
-        .reshape(tok_rows, -1)
-    )
-
-    def by_row(x):
-        return x.transpose(1, 0, 2).reshape(key_rows, -1)
-
-    return (query_grad, jnp.stack([by_row(k_grad), by_row(v_grad)]))
+    )(mask, queries, key_value, key_value, grads)
+    return (query_grad, jnp.stack([key_grad, value_grad]))
 
 
 def per_device(tokens, query_weight, key_weight, value_weight, output_grad, segments):

time: 415 us -> 397 us (0.957)
  local copies, waits for them, and re-layouts: 23.6 us -> 2.63 us
  waiting for transfers between devices: 240 us -> 246 us
    reshape x5 -> x0, local copies, waits for them, and re-layouts: 6.01 us -> none  [the longest x4 3.74 us: by_head(): x.reshape(rows, kv_local, -1, HEAD_DIM).transpose(1, 2, 0, 3)]
    transpose x2 -> x0, local copies, waits for them, and re-layouts: 5.89 us -> none  [by_row(): return x.transpose(1, 0, 2).reshape(key_rows, -1)]
  transfers between devices with their start and end apart: 9 -> 9, of which waited for: 7 -> 8; matrix products, arithmetic and copies ran while one was open for 13% -> 11% of each run, Pallas kernels for 0% -> 0%
where the time goes in v11:
time: 397 us; the launch traced here: 395 us
  waiting for transfers between devices  246 us (62%)
  matrix products  72.9 us (18%)
  Pallas kernels  29.8 us (8%)
  starting transfers between devices  19 us (5%)
  between operations  14.4 us (4%)
  other arithmetic  9.76 us (2%)
    all_gather x1, waiting for transfers between devices, per_device(): gathered = lax.all_gather(tokens, 'head', axis=1, tiled=True)  103 us
    ppermute x3, waiting for transfers between devices, per_device(): got = lax.ppermute(sent, 'head', pairs).astype(jnp.float32)  99.8 us
    ppermute x4, waiting for transfers between devices, passed_along(): return lax.ppermute(x, axis, pairs)  39.2 us
    dot_general x12, matrix products, contract_last(): lax.dot_general(left, right, (((1,), (1,)), ((), ())), preferred_element_...  31 us
    pallas_call x1, Pallas kernels, attend(): pl.pallas_call(attention_kernel, grid=(kv_local,), in_specs=[pl.BlockSpec...  29.8 us
    dot_general x1, matrix products, contract_first(): lax.dot_general(left, right, (((0,), (0,)), ((), ())), preferred_element_...  17.7 us
    ppermute x4, starting transfers between devices, passed_along(): return lax.ppermute(x, axis, pairs)  13.9 us
    dot_general x1, matrix products, per_device(): jnp.dot(gathered, query_weight, preferred_element_type=jnp.float32)  11.2 us
  transfers between devices with their start and end apart: 9, of which 8 were waited for; matrix products, arithmetic and copies ran while one was open for 11% of the time, Pallas kernels for 0%

profile of v11, /device:TPU:11, one launch (start us, length us, event | category | flops | bytes accessed | tf_op | source)
XLA Modules:
  0.0 394.9 jit_solution(6433835051787524635)
XLA Ops:
  7.9 102.5 %all-gather.2.cloned.1.call-done = bf16[512,5376]{0,1:T(8,128)(2,1)} async-done(((bf16[512,1344]{0,1:T(8,128)(2,1)}), bf16[512,5376]{0,1:T(8,128)(2,1)}) %all-gather.2.cloned.1.call-update) | async-done | bytes 5505040 | tf_op jit(solution)/shard_map/all_gather | solution.py:108
  110.5 7.4 %fusion.40 = bf16[1,512,512]{2,1,0:T(8,128)(2,1)S(1)} fusion(bf16[512,5376]{0,1:T(8,128)(2,1)} %all-gather.2.cloned.1.call-done, bf16[5376,512]{1,0:T(8,128)(2,1)} %param.8), kind=kOutput, calls=%fused_computation.60 | convolution fusion | flops 2818834432 | bytes 11534336 | tf_op jit(solution)/shard_map/dot_general | solution.py:112
  117.9 5.6 %fusion.41 = bf16[1,512,512]{2,1,0:T(8,128)(2,1)S(1)} fusion(bf16[512,5376]{0,1:T(8,128)(2,1)S(1)} %copy-done.3, bf16[5376,512]{1,0:T(8,128)(2,1)} %param.9), kind=kOutput, calls=%fused_computation.61 | convolution fusion | flops 2818834432 | bytes 11534336 | tf_op jit(solution)/shard_map/dot_general | solution.py:115
  123.6 3.6 collective-permute-start
  127.4 2.8 fusion.3.mask_ref
  130.3 8.7 %collective-permute-done = bf16[2,512,512]{2,1,0:T(8,128)(2,1)S(1)} collective-permute-done((bf16[2,512,512]{2,1,0:T(8,128)(2,1)S(1)}, bf16[2,512,512]{2,1,0:T(8,128)(2,1)S(1)}, u32[]{:S(2)}, u32[]{:S(2)}) %collective-permute-start) | collective-permute-done | bytes 1048608 | tf_op jit(solution)/shard_map/ppermute | solution.py:22
  139.0 5.5 %collective-permute-start.1 = (bf16[2,512,512]{2,1,0:T(8,128)(2,1)S(1)}, bf16[2,512,512]{2,1,0:T(8,128)(2,1)S(1)}, u32[]{:S(2)}, u32[]{:S(2)}) collective-permute-start(bf16[2,512,512]{2,1,0:T(8,128)(2,1)S(1)} %collective-permute-done), channel_id=1, source_target_pairs={{0,4},{4,8},{8,12},{12,16},{16,20},{20,24},{24,28},{1,5},{5,9},{9,... | collective-permute-start | bytes 3145736 | tf_op jit(solution)/shard_map/ppermute | solution.py:22
  144.4 11.2 %convolution_convert_fusion.1.q_ref = bf16[512,1024]{1,0:T(8,128)(2,1)} fusion(bf16[512,5376]{0,1:T(8,128)(2,1)} %all-gather.2.cloned.1.call-done, bf16[5376,1024]{1,0:T(8,128)(2,1)} %param.7), kind=kOutput, calls=%fused_computation.49 | convolution fusion | flops 5637668864 | bytes 17563648 | tf_op jit(solution)/shard_map/dot_general | solution.py:109
  157.8 29.8 %shard_map.93 = (bf16[512,1024]{1,0:T(8,128)(2,1)}, f32[1536,512]{1,0:T(8,128)}, f32[1536,512]{1,0:T(8,128)}) custom-call(f32[512,1536]{1,0:T(8,128)} %fusion.3.mask_ref, bf16[512,1024]{1,0:T(8,128)(2,1)} %convolution_convert_fusion.1.q_ref, bf16[2,1536,512]{2,1,0:T(8,128)(2,1)} %maximum_maximum_fusion.k_ref.v_ref, ...), custom_call_target="tpu_custom_call" | custom-call | tf_op jit(solution)/shard_map/pallas_call | solution.py:83
  189.4 2.5 collective-permute-start.2
  191.9 15.3 %collective-permute-done.2 = bf16[2,512,512]{2,1,0:T(8,128)(2,1)S(1)} collective-permute-done((bf16[2,512,512]{2,1,0:T(8,128)(2,1)S(1)}, bf16[2,512,512]{2,1,0:T(8,128)(2,1)S(1)}, u32[]{:S(2)}, u32[]{:S(2)}) %collective-permute-start.2) | collective-permute-done | bytes 1048608 | tf_op jit(solution)/shard_map/ppermute | solution.py:22
  209.9 14.9 %collective-permute-done.3 = bf16[2,512,512]{2,1,0:T(8,128)(2,1)S(1)} collective-permute-done((bf16[2,512,512]{2,1,0:T(8,128)(2,1)S(1)}, bf16[2,512,512]{2,1,0:T(8,128)(2,1)S(1)}, u32[]{:S(2)}, u32[]{:S(2)}) %collective-permute-start.3) | collective-permute-done | bytes 1048608 | tf_op jit(solution)/shard_map/ppermute | solution.py:22
  225.3 17.7 %convolution_convert_fusion = bf16[2048,5376]{0,1:T(8,128)(2,1)} fusion(bf16[512,5376]{0,1:T(8,128)(2,1)} %all-gather.2.cloned.1.call-done, bf16[512,512]{1,0:T(8,128)(2,1)S(1)} %get-tuple-element.13, bf16[512,512]{1,0:T(8,128)(2,1)S(1)} %get-tuple-element.12, bf16[512,1024]{1,0:T(8,128)(2,1)S(1)} %copy-done.4), kind=kOutput, calls=%fused_computation | convolution fusion | flops 11291590656 | bytes 29622272 | tf_op jit(solution)/shard_map/dot_general | solution.py:32
  243.0 3.4 fusion.16
  246.5 3.6 fusion.14
  250.1 5.0 %fusion.12 = f32[512,1344]{0,1:T(8,128)S(1)} fusion(bf16[512,1024]{1,0:T(8,128)(2,1)S(1)} %copy-done.4, bf16[5376,1024]{1,0:T(8,128)(2,1)} %param.7, s32[]{:T(128)S(6)} %select_n.48), kind=kOutput, calls=%fused_computation.30 | convolution fusion | flops 1409286144 | bytes 6553604 | tf_op jit(solution)/shard_map/dot_general | solution.py:26
  257.0 3.8 collective-permute-start.4
  267.9 4.0 %fusion.10 = f32[512,1344]{0,1:T(8,128)S(1)} fusion(bf16[512,1024]{1,0:T(8,128)(2,1)S(1)} %copy-done.4, bf16[5376,1024]{1,0:T(8,128)(2,1)} %param.7, s32[]{:T(128)S(6)} %select_n.49), kind=kOutput, calls=%fused_computation.28 | convolution fusion | flops 1409286144 | bytes 6553604 | tf_op jit(solution)/shard_map/dot_general | solution.py:26
  271.9 2.4 convolution_add_fusion.1
  274.3 75.7 %collective-permute-done.4 = bf16[512,1344]{0,1:T(8,128)(2,1)} collective-permute-done((bf16[512,1344]{0,1:T(8,128)(2,1)S(1)}, bf16[512,1344]{0,1:T(8,128)(2,1)}, u32[]{:S(2)}, u32[]{:S(2)}) %collective-permute-start.4) | collective-permute-done | bytes 1376288 | tf_op jit(solution)/shard_map/ppermute | solution.py:158
  349.9 24.1 %collective-permute-done.6 = bf16[512,1344]{0,1:T(8,128)(2,1)} collective-permute-done((bf16[512,1344]{0,1:T(8,128)(2,1)}, bf16[512,1344]{0,1:T(8,128)(2,1)}, u32[]{:S(2)}, u32[]{:S(2)}) %collective-permute-start.6) | collective-permute-done | bytes 1376288 | tf_op jit(solution)/shard_map/ppermute | solution.py:158
  374.0 5.0 %add_convert_fusion = bf16[512,1344]{0,1:T(8,128)(2,1)} fusion(bf16[512,1344]{0,1:T(8,128)(2,1)} %collective-permute-done.6, bf16[512,1344]{0,1:T(8,128)(2,1)} %collective-permute-done.5, bf16[512,1344]{0,1:T(8,128)(2,1)} %collective-permute-done.4, f32[512,1344]{0,1:T(8,128)S(1)} %convolution_add_fusion.1, bf16[5376,512]{1,0:T(8,128)(2,1)} %param.9, ...), kind=kOutput, calls=%fused_computation.27 | convolution fusion | flops 711524352 | bytes 10158084 | tf_op jit(solution)/shard_map/dot_general | solution.py:26
  379.0 4.2 %reduce-scatter.2.cloned.1.call-done = bf16[2048,672]{0,1:T(8,128)(2,1)} async-done(((bf16[2048,5376]{0,1:T(8,128)(2,1)}), bf16[2048,672]{0,1:T(8,128)(2,1)}) %reduce-scatter.2.cloned.1.call-update) | async-done | bytes 2752528 | tf_op jit(solution)/shard_map/reduce_scatter | solution.py:163
  383.2 2.4 fusion.9
  (47 shorter events, 19.4 us)
Async XLA Ops:
  7.2 103.3 %all-gather.2.cloned.1.call-start = ((), (), s32[]{:S(2)}) async-start(), calls=%async_computation.1 | async-start | bytes 6881280 | tf_op jit(solution)/shard_map/all_gather | solution.py:108
  7.9 375.3 %reduce-scatter.2.cloned.1.call-start = ((), (), s32[]{:S(2)}) async-start(), calls=%async_computation.2 | async-start | bytes 24772608 | tf_op jit(solution)/shard_map/reduce_scatter | solution.py:163
  110.5 7.4 %copy-start.3 = (bf16[512,5376]{0,1:T(8,128)(2,1)S(1)}, bf16[512,5376]{0,1:T(8,128)(2,1)}, u32[]{:S(2)}) copy-start(bf16[512,5376]{0,1:T(8,128)(2,1)} %all-gather.2.cloned.1.call-done) | copy-start | bytes 16515076
  117.9 9.4 %copy-start.2 = (s32[4096]{0:T(1024)S(1)}, s32[4096]{0:T(1024)}, u32[]{:S(2)}) copy-start(s32[4096]{0:T(1024)} %param.11) | copy-start | bytes 49156
  123.6 15.4 %collective-permute-start = (bf16[2,512,512]{2,1,0:T(8,128)(2,1)S(1)}, bf16[2,512,512]{2,1,0:T(8,128)(2,1)S(1)}, u32[]{:S(2)}, u32[]{:S(2)}) collective-permute-start(bf16[2,512,512]{2,1,0:T(8,128)(2,1)S(1)} %pad_maximum_fusion.1), channel_id=1, source_target_pairs={{0,4},{4,8},{8,12},{12,16},{16,20},{20,24},{24,28},{1,5},{5,9},{9,... | collective-permute-start | bytes 3145736 | tf_op jit(solution)/shard_map/ppermute | solution.py:22
  139.0 17.0 %collective-permute-start.1 = (bf16[2,512,512]{2,1,0:T(8,128)(2,1)S(1)}, bf16[2,512,512]{2,1,0:T(8,128)(2,1)S(1)}, u32[]{:S(2)}, u32[]{:S(2)}) collective-permute-start(bf16[2,512,512]{2,1,0:T(8,128)(2,1)S(1)} %collective-permute-done), channel_id=1, source_target_pairs={{0,4},{4,8},{8,12},{12,16},{16,20},{20,24},{24,28},{1,5},{5,9},{9,... | collective-permute-start | bytes 3145736 | tf_op jit(solution)/shard_map/ppermute | solution.py:22
  187.5 19.7 %copy-start = (f32[1536,512]{1,0:T(8,128)S(1)}, f32[1536,512]{1,0:T(8,128)}, u32[]{:S(2)}) copy-start(f32[1536,512]{1,0:T(8,128)} %get-tuple-element.8) | copy-start | bytes 9437188
  187.5 19.7 %copy-start.1 = (f32[1536,512]{1,0:T(8,128)S(1)}, f32[1536,512]{1,0:T(8,128)}, u32[]{:S(2)}) copy-start(f32[1536,512]{1,0:T(8,128)} %get-tuple-element.9) | copy-start | bytes 9437188
  189.4 17.9 %collective-permute-start.2 = (bf16[2,512,512]{2,1,0:T(8,128)(2,1)S(1)}, bf16[2,512,512]{2,1,0:T(8,128)(2,1)S(1)}, u32[]{:S(2)}, u32[]{:S(2)}) collective-permute-start(bf16[2,512,512]{2,1,0:T(8,128)(2,1)S(1)} %fusion.24), channel_id=1, source_target_pairs={{4,0},{8,4},{12,8},{16,12},{20,16},{24,20},{28,24},{5,1},{9,5},{13... | collective-permute-start | bytes 3145736 | tf_op jit(solution)/shard_map/ppermute | solution.py:22
  207.7 17.6 %copy-start.4 = (bf16[512,1024]{1,0:T(8,128)(2,1)S(1)}, bf16[512,1024]{1,0:T(8,128)(2,1)}, u32[]{:S(2)}) copy-start(bf16[512,1024]{1,0:T(8,128)(2,1)} %get-tuple-element.7) | copy-start | bytes 3145732
  207.7 17.1 %collective-permute-start.3 = (bf16[2,512,512]{2,1,0:T(8,128)(2,1)S(1)}, bf16[2,512,512]{2,1,0:T(8,128)(2,1)S(1)}, u32[]{:S(2)}, u32[]{:S(2)}) collective-permute-start(bf16[2,512,512]{2,1,0:T(8,128)(2,1)S(1)} %fusion.20), channel_id=1, source_target_pairs={{4,0},{8,4},{12,8},{16,12},{20,16},{24,20},{28,24},{5,1},{9,5},{13... | collective-permute-start | bytes 3145736 | tf_op jit(solution)/shard_map/ppermute | solution.py:22
  246.4 8.6 %slice-start = ((s8[5505024]{0:T(1024)(128)(4,1)}), s8[4194304]{0:T(1024)(128)(4,1)S(1)}, s32[]{:S(2)}) async-start(s8[5505024]{0:T(1024)(128)(4,1)} %bitcast.37), calls=%async_computation.3 | async-start | bytes 8388608
  246.5 9.5 %slice-start.2 = ((s8[5505024]{0:T(1024)(128)(4,1)}), s8[4194304]{0:T(1024)(128)(4,1)S(1)}, s32[]{:S(2)}) async-start(s8[5505024]{0:T(1024)(128)(4,1)} %bitcast.39), calls=%async_computation.5 | async-start | bytes 8388608
  250.0 5.0 %slice-start.1 = ((s8[5505024]{0:T(1024)(128)(4,1)}), s8[1310720]{0:T(1024)(128)(4,1)S(1)}, s32[]{:S(2)}) async-start(s8[5505024]{0:T(1024)(128)(4,1)} %bitcast.37), calls=%async_computation.4 | async-start | bytes 2621440
  250.1 5.9 %slice-start.3 = ((s8[5505024]{0:T(1024)(128)(4,1)}), s8[1310720]{0:T(1024)(128)(4,1)S(1)}, s32[]{:S(2)}) async-start(s8[5505024]{0:T(1024)(128)(4,1)} %bitcast.39), calls=%async_computation.6 | async-start | bytes 2621440
  257.0 93.0 %collective-permute-start.4 = (bf16[512,1344]{0,1:T(8,128)(2,1)S(1)}, bf16[512,1344]{0,1:T(8,128)(2,1)}, u32[]{:S(2)}, u32[]{:S(2)}) collective-permute-start(bf16[512,1344]{0,1:T(8,128)(2,1)S(1)} %fusion.4), channel_id=1, source_target_pairs={{0,3},{1,0},{2,1},{3,2},{4,7},{5,4},{6,5},{7,6},{8,11},{9,8},{10,9... | collective-permute-start | bytes 4128776 | tf_op jit(solution)/shard_map/ppermute | solution.py:158
  263.7 86.2 %collective-permute-start.5 = (bf16[512,1344]{0,1:T(8,128)(2,1)}, bf16[512,1344]{0,1:T(8,128)(2,1)}, u32[]{:S(2)}, u32[]{:S(2)}) collective-permute-start(bf16[512,1344]{0,1:T(8,128)(2,1)} %fusion.5), channel_id=1, source_target_pairs={{0,2},{1,3},{2,0},{3,1},{4,6},{5,7},{6,4},{7,5},{8,10},{9,11},{10,... | collective-permute-start | bytes 4128776 | tf_op jit(solution)/shard_map/ppermute | solution.py:158
  267.4 106.7 %collective-permute-start.6 = (bf16[512,1344]{0,1:T(8,128)(2,1)}, bf16[512,1344]{0,1:T(8,128)(2,1)}, u32[]{:S(2)}, u32[]{:S(2)}) collective-permute-start(bf16[512,1344]{0,1:T(8,128)(2,1)} %fusion.6), channel_id=1, source_target_pairs={{0,1},{1,2},{2,3},{3,0},{4,5},{5,6},{6,7},{7,4},{8,9},{9,10},{10,1... | collective-permute-start | bytes 4128776 | tf_op jit(solution)/shard_map/ppermute | solution.py:158
Sparse Core Ops, SparseCore 0:
  9.6 100.8 all-gather.1
  243.1 140.0 reduce-scatter.1

commit v12 on v11

--- a/solution.py
+++ b/solution.py
@@ -117,10 +117,8 @@
     )
     key_value = jnp.stack([keys_own, values_own])
     blocks = [key_value] * (hop_count + 1)
-    moving = key_value
     for distance in range(1, hop_count + 1):
-        moving = passed_along(moving, "seq", 1)
-        blocks[hop_count - distance] = moving
+        blocks[hop_count - distance] = passed_along(key_value, "seq", distance)
     keys_all = jnp.concatenate(blocks, axis=1)
     position = lax.axis_index("seq")
     query_first = position * tok_rows
@@ -133,11 +131,10 @@
     pieces = [
         kv_grad[:, block * tok_rows : (block + 1) * tok_rows] for block in range(hop_count + 1)
     ]
-    carried = pieces[0]
+    carried = pieces[hop_count]
     for distance in range(1, hop_count + 1):
-        carried = pieces[distance] + passed_along(carried.astype(jnp.bfloat16), "seq", -1).astype(
-            carried.dtype
-        )
+        back = passed_along(pieces[hop_count - distance].astype(jnp.bfloat16), "seq", -distance)
+        carried = carried + back.astype(jnp.float32)
     key_grad = carried[0].astype(jnp.bfloat16)
     value_grad = carried[1].astype(jnp.bfloat16)
     n_head = lax.axis_size("head")

time: 397 us -> 410 us (1.033)
  waiting for transfers between devices: 246 us -> 263 us
  matrix products: 72.9 us -> 67.3 us
    ppermute x4, waiting for transfers between devices: 39.2 us -> 49.1 us  [passed_along(): return lax.ppermute(x, axis, pairs)]
    reduce_scatter x1, waiting for transfers between devices: 4.24 us -> 10.1 us  [per_device(): lax.psum_scatter(contract_first(proj_grads, gathered).astype(jnp.bfloat16...]
    ppermute x3, waiting for transfers between devices: 99.8 us -> 105 us  [per_device(): got = lax.ppermute(sent, 'head', pairs).astype(jnp.float32)]
    all_gather x1, waiting for transfers between devices: 103 us -> 98.1 us  [per_device(): gathered = lax.all_gather(tokens, 'head', axis=1, tiled=True)]
    dot_general x1, matrix products: 11.2 us -> 6.85 us  [per_device(): jnp.dot(gathered, query_weight, preferred_element_type=jnp.float32)]
  transfers between devices with their start and end apart: 9 -> 9, of which waited for: 8 -> 9; matrix products, arithmetic and copies ran while one was open for 11% -> 10% of each run, Pallas kernels for 0% -> 0%
where the time goes in v12:
time: 410 us; the launch traced here: 408 us
  waiting for transfers between devices  263 us (64%)
  matrix products  67.3 us (16%)
  Pallas kernels  29.8 us (7%)
  starting transfers between devices  18 us (4%)
  between operations  14.4 us (4%)
  other arithmetic  11.9 us (3%)
    ppermute x3, waiting for transfers between devices, per_device(): got = lax.ppermute(sent, 'head', pairs).astype(jnp.float32)  105 us
    all_gather x1, waiting for transfers between devices, per_device(): gathered = lax.all_gather(tokens, 'head', axis=1, tiled=True)  98.1 us
    ppermute x4, waiting for transfers between devices, passed_along(): return lax.ppermute(x, axis, pairs)  49.1 us
    pallas_call x1, Pallas kernels, attend(): pl.pallas_call(attention_kernel, grid=(kv_local,), in_specs=[pl.BlockSpec...  29.8 us
    dot_general x12, matrix products, contract_last(): lax.dot_general(left, right, (((1,), (1,)), ((), ())), preferred_element_...  29.6 us
    dot_general x1, matrix products, contract_first(): lax.dot_general(left, right, (((0,), (0,)), ((), ())), preferred_element_...  17.7 us
    ppermute x4, starting transfers between devices, passed_along(): return lax.ppermute(x, axis, pairs)  12.9 us
    reduce_scatter x1, waiting for transfers between devices, per_device(): lax.psum_scatter(contract_first(proj_grads, gathered).astype(jnp.bfloat16...  10.1 us
  transfers between devices with their start and end apart: 9, of which 9 were waited for; matrix products, arithmetic and copies ran while one was open for 10% of the time, Pallas kernels for 0%

profile of v12, /device:TPU:11, one launch (start us, length us, event | category | flops | bytes accessed | tf_op | source)
XLA Modules:
  0.0 407.6 jit_solution(4736542536749462524)
XLA Ops:
  12.3 98.1 %all-gather.2.cloned.1.call-done = bf16[512,5376]{0,1:T(8,128)(2,1)} async-done(((bf16[512,1344]{0,1:T(8,128)(2,1)}), bf16[512,5376]{0,1:T(8,128)(2,1)}) %all-gather.2.cloned.1.call-update) | async-done | bytes 5505040 | tf_op jit(solution)/shard_map/all_gather | solution.py:108
  110.5 7.4 %fusion.38 = bf16[1,512,512]{2,1,0:T(8,128)(2,1)S(1)} fusion(bf16[512,5376]{0,1:T(8,128)(2,1)} %all-gather.2.cloned.1.call-done, bf16[5376,512]{1,0:T(8,128)(2,1)} %param.8), kind=kOutput, calls=%fused_computation.56 | convolution fusion | flops 2818834432 | bytes 11534336 | tf_op jit(solution)/shard_map/dot_general | solution.py:112
  117.9 5.7 %fusion.39 = bf16[1,512,512]{2,1,0:T(8,128)(2,1)S(1)} fusion(bf16[512,5376]{0,1:T(8,128)(2,1)S(1)} %copy-done.2, bf16[5376,512]{1,0:T(8,128)(2,1)} %param.9), kind=kOutput, calls=%fused_computation.57 | convolution fusion | flops 2818834432 | bytes 11534336 | tf_op jit(solution)/shard_map/dot_general | solution.py:115
  123.7 3.1 collective-permute-start
  126.8 4.1 %collective-permute-start.1 = (bf16[2,512,512]{2,1,0:T(8,128)(2,1)S(1)}, bf16[2,512,512]{2,1,0:T(8,128)(2,1)S(1)}, u32[]{:S(2)}, u32[]{:S(2)}) collective-permute-start(bf16[2,512,512]{2,1,0:T(8,128)(2,1)S(1)} %pad_maximum_fusion.1), channel_id=1, source_target_pairs={{0,4},{4,8},{8,12},{12,16},{16,20},{20,24},{24,28},{1,5},{5,9},{9,... | collective-permute-start | bytes 3145736 | tf_op jit(solution)/shard_map/ppermute | solution.py:22
  131.0 6.8 %convolution_convert_fusion.1.q_ref = bf16[512,1024]{1,0:T(8,128)(2,1)} fusion(bf16[512,5376]{0,1:T(8,128)(2,1)S(1)} %copy-done.2, bf16[5376,1024]{1,0:T(8,128)(2,1)S(1)} %bitcast.40), kind=kOutput, calls=%fused_computation.45 | convolution fusion | flops 5637668864 | bytes 17563648 | tf_op jit(solution)/shard_map/dot_general | solution.py:109
  137.9 11.8 %collective-permute-done = bf16[2,512,512]{2,1,0:T(8,128)(2,1)S(1)} collective-permute-done((bf16[2,512,512]{2,1,0:T(8,128)(2,1)S(1)}, bf16[2,512,512]{2,1,0:T(8,128)(2,1)S(1)}, u32[]{:S(2)}, u32[]{:S(2)}) %collective-permute-start) | collective-permute-done | bytes 1048608 | tf_op jit(solution)/shard_map/ppermute | solution.py:22
  149.7 11.4 %collective-permute-done.1 = bf16[2,512,512]{2,1,0:T(8,128)(2,1)S(1)} collective-permute-done((bf16[2,512,512]{2,1,0:T(8,128)(2,1)S(1)}, bf16[2,512,512]{2,1,0:T(8,128)(2,1)S(1)}, u32[]{:S(2)}, u32[]{:S(2)}) %collective-permute-start.1) | collective-permute-done | bytes 1048608 | tf_op jit(solution)/shard_map/ppermute | solution.py:22
  162.8 29.8 %shard_map.93 = (bf16[512,1024]{1,0:T(8,128)(2,1)}, f32[1536,512]{1,0:T(8,128)}, f32[1536,512]{1,0:T(8,128)}) custom-call(f32[512,1536]{1,0:T(8,128)} %fusion.4.mask_ref, bf16[512,1024]{1,0:T(8,128)(2,1)} %convolution_convert_fusion.1.q_ref, bf16[2,1536,512]{2,1,0:T(8,128)(2,1)} %maximum_maximum_fusion.k_ref.v_ref, ...), custom_call_target="tpu_custom_call" | custom-call | tf_op jit(solution)/shard_map/pallas_call | solution.py:83
  192.6 3.6 fusion
  196.4 3.4 collective-permute-start.2
  202.1 21.2 %collective-permute-done.2 = bf16[2,512,512]{2,1,0:T(8,128)(2,1)S(1)} collective-permute-done((bf16[2,512,512]{2,1,0:T(8,128)(2,1)S(1)}, bf16[2,512,512]{2,1,0:T(8,128)(2,1)S(1)}, u32[]{:S(2)}, u32[]{:S(2)}) %collective-permute-start.2) | collective-permute-done | bytes 1048608 | tf_op jit(solution)/shard_map/ppermute | solution.py:22
  223.3 4.7 %collective-permute-done.3 = bf16[2,512,512]{2,1,0:T(8,128)(2,1)S(1)} collective-permute-done((bf16[2,512,512]{2,1,0:T(8,128)(2,1)S(1)}, bf16[2,512,512]{2,1,0:T(8,128)(2,1)S(1)}, u32[]{:S(2)}, u32[]{:S(2)}) %collective-permute-start.3) | collective-permute-done | bytes 1048608 | tf_op jit(solution)/shard_map/ppermute | solution.py:22
  228.6 17.7 %convolution_convert_fusion = bf16[2048,5376]{0,1:T(8,128)(2,1)} fusion(bf16[512,5376]{0,1:T(8,128)(2,1)} %all-gather.2.cloned.1.call-done, bf16[512,512]{1,0:T(8,128)(2,1)S(1)} %get-tuple-element.15, bf16[512,512]{1,0:T(8,128)(2,1)S(1)} %get-tuple-element.14, bf16[512,1024]{1,0:T(8,128)(2,1)S(1)} %copy-done.3), kind=kOutput, calls=%fused_computation | convolution fusion | flops 11291590656 | bytes 29622272 | tf_op jit(solution)/shard_map/dot_general | solution.py:32
  246.3 3.4 fusion.17
  249.8 3.6 fusion.15
  253.4 3.6 fusion.13
  258.9 3.4 collective-permute-start.4
  269.7 3.9 fusion.11
  276.2 4.5 %collective-permute-done.4 = bf16[512,1344]{0,1:T(8,128)(2,1)} collective-permute-done((bf16[512,1344]{0,1:T(8,128)(2,1)S(1)}, bf16[512,1344]{0,1:T(8,128)(2,1)}, u32[]{:S(2)}, u32[]{:S(2)}) %collective-permute-start.4) | collective-permute-done | bytes 1376288 | tf_op jit(solution)/shard_map/ppermute | solution.py:155
  280.7 70.7 %collective-permute-done.5 = bf16[512,1344]{0,1:T(8,128)(2,1)} collective-permute-done((bf16[512,1344]{0,1:T(8,128)(2,1)}, bf16[512,1344]{0,1:T(8,128)(2,1)}, u32[]{:S(2)}, u32[]{:S(2)}) %collective-permute-start.5) | collective-permute-done | bytes 1376288 | tf_op jit(solution)/shard_map/ppermute | solution.py:155
  351.4 29.5 %collective-permute-done.6 = bf16[512,1344]{0,1:T(8,128)(2,1)} collective-permute-done((bf16[512,1344]{0,1:T(8,128)(2,1)}, bf16[512,1344]{0,1:T(8,128)(2,1)}, u32[]{:S(2)}, u32[]{:S(2)}) %collective-permute-start.6) | collective-permute-done | bytes 1376288 | tf_op jit(solution)/shard_map/ppermute | solution.py:155
  380.9 4.9 %add_convert_fusion = bf16[512,1344]{0,1:T(8,128)(2,1)} fusion(bf16[512,1344]{0,1:T(8,128)(2,1)} %collective-permute-done.6, bf16[512,1344]{0,1:T(8,128)(2,1)} %collective-permute-done.5, bf16[512,1344]{0,1:T(8,128)(2,1)} %collective-permute-done.4, f32[512,1344]{0,1:T(8,128)S(1)} %convolution_add_fusion.1, bf16[5376,512]{1,0:T(8,128)(2,1)} %param.9, ...), kind=kOutput, calls=%fused_computation.27 | convolution fusion | flops 711524352 | bytes 10158084 | tf_op jit(solution)/shard_map/dot_general | solution.py:26
  385.8 10.1 %reduce-scatter.2.cloned.1.call-done = bf16[2048,672]{0,1:T(8,128)(2,1)} async-done(((bf16[2048,5376]{0,1:T(8,128)(2,1)}), bf16[2048,672]{0,1:T(8,128)(2,1)}) %reduce-scatter.2.cloned.1.call-update) | async-done | bytes 2752528 | tf_op jit(solution)/shard_map/reduce_scatter | solution.py:160
  (52 shorter events, 26.7 us)
Async XLA Ops:
  7.2 103.3 %all-gather.2.cloned.1.call-start = ((), (), s32[]{:S(2)}) async-start(), calls=%async_computation.1 | async-start | bytes 6881280 | tf_op jit(solution)/shard_map/all_gather | solution.py:108
  7.9 388.0 %reduce-scatter.2.cloned.1.call-start = ((), (), s32[]{:S(2)}) async-start(), calls=%async_computation.2 | async-start | bytes 24772608 | tf_op jit(solution)/shard_map/reduce_scatter | solution.py:160
  110.5 7.4 %copy-start.2 = (bf16[512,5376]{0,1:T(8,128)(2,1)S(1)}, bf16[512,5376]{0,1:T(8,128)(2,1)}, u32[]{:S(2)}) copy-start(bf16[512,5376]{0,1:T(8,128)(2,1)} %all-gather.2.cloned.1.call-done) | copy-start | bytes 16515076
  110.5 20.5 %slice-start.4 = ((s8[11010048]{0:T(1024)(128)(4,1)}), s8[4194304]{0:T(1024)(128)(4,1)S(1)}, s32[]{:S(2)}) async-start(s8[11010048]{0:T(1024)(128)(4,1)} %bitcast.39), calls=%async_computation.7 | async-start | bytes 8388608
  110.5 20.5 %slice-start.5 = ((s8[11010048]{0:T(1024)(128)(4,1)}), s8[4194304]{0:T(1024)(128)(4,1)S(1)}, s32[]{:S(2)}) async-start(s8[11010048]{0:T(1024)(128)(4,1)} %bitcast.39), calls=%async_computation.8 | async-start | bytes 8388608
  117.9 13.1 %slice-start.6 = ((s8[11010048]{0:T(1024)(128)(4,1)}), s8[2621440]{0:T(1024)(128)(4,1)S(1)}, s32[]{:S(2)}) async-start(s8[11010048]{0:T(1024)(128)(4,1)} %bitcast.39), calls=%async_computation.9 | async-start | bytes 5242880
  123.7 25.9 %collective-permute-start = (bf16[2,512,512]{2,1,0:T(8,128)(2,1)S(1)}, bf16[2,512,512]{2,1,0:T(8,128)(2,1)S(1)}, u32[]{:S(2)}, u32[]{:S(2)}) collective-permute-start(bf16[2,512,512]{2,1,0:T(8,128)(2,1)S(1)} %pad_maximum_fusion.1), channel_id=1, source_target_pairs={{0,8},{4,12},{8,16},{12,20},{16,24},{20,28},{1,9},{5,13},{9,17},{1... | collective-permute-start | bytes 3145736 | tf_op jit(solution)/shard_map/ppermute | solution.py:22
  126.8 34.2 %collective-permute-start.1 = (bf16[2,512,512]{2,1,0:T(8,128)(2,1)S(1)}, bf16[2,512,512]{2,1,0:T(8,128)(2,1)S(1)}, u32[]{:S(2)}, u32[]{:S(2)}) collective-permute-start(bf16[2,512,512]{2,1,0:T(8,128)(2,1)S(1)} %pad_maximum_fusion.1), channel_id=1, source_target_pairs={{0,4},{4,8},{8,12},{12,16},{16,20},{20,24},{24,28},{1,5},{5,9},{9,... | collective-permute-start | bytes 3145736 | tf_op jit(solution)/shard_map/ppermute | solution.py:22
  192.6 35.4 %copy-start.1 = (f32[1536,512]{1,0:T(8,128)S(1)}, f32[1536,512]{1,0:T(8,128)}, u32[]{:S(2)}) copy-start(f32[1536,512]{1,0:T(8,128)} %get-tuple-element.9) | copy-start | bytes 9437188
  196.2 31.8 %copy-start = (f32[1536,512]{1,0:T(8,128)S(1)}, f32[1536,512]{1,0:T(8,128)}, u32[]{:S(2)}) copy-start(f32[1536,512]{1,0:T(8,128)} %get-tuple-element.8) | copy-start | bytes 9437188
  196.4 26.9 %collective-permute-start.2 = (bf16[2,512,512]{2,1,0:T(8,128)(2,1)S(1)}, bf16[2,512,512]{2,1,0:T(8,128)(2,1)S(1)}, u32[]{:S(2)}, u32[]{:S(2)}) collective-permute-start(bf16[2,512,512]{2,1,0:T(8,128)(2,1)S(1)} %get-tuple-element.10), channel_id=1, source_target_pairs={{4,0},{8,4},{12,8},{16,12},{20,16},{24,20},{28,24},{5,1},{9,5},{13... | collective-permute-start | bytes 3145736 | tf_op jit(solution)/shard_map/ppermute | solution.py:22
  199.8 28.7 %copy-start.3 = (bf16[512,1024]{1,0:T(8,128)(2,1)S(1)}, bf16[512,1024]{1,0:T(8,128)(2,1)}, u32[]{:S(2)}) copy-start(bf16[512,1024]{1,0:T(8,128)(2,1)} %get-tuple-element.7) | copy-start | bytes 3145732
  199.8 28.2 %collective-permute-start.3 = (bf16[2,512,512]{2,1,0:T(8,128)(2,1)S(1)}, bf16[2,512,512]{2,1,0:T(8,128)(2,1)S(1)}, u32[]{:S(2)}, u32[]{:S(2)}) collective-permute-start(bf16[2,512,512]{2,1,0:T(8,128)(2,1)S(1)} %get-tuple-element.11), channel_id=1, source_target_pairs={{8,0},{12,4},{16,8},{20,12},{24,16},{28,20},{9,1},{13,5},{17,9},{2... | collective-permute-start | bytes 3145736 | tf_op jit(solution)/shard_map/ppermute | solution.py:22
  249.7 7.2 %slice-start = ((s8[5505024]{0:T(1024)(128)(4,1)}), s8[4194304]{0:T(1024)(128)(4,1)S(1)}, s32[]{:S(2)}) async-start(s8[5505024]{0:T(1024)(128)(4,1)} %bitcast.35), calls=%async_computation.3 | async-start | bytes 8388608
  249.8 8.1 %slice-start.2 = ((s8[5505024]{0:T(1024)(128)(4,1)}), s8[4194304]{0:T(1024)(128)(4,1)S(1)}, s32[]{:S(2)}) async-start(s8[5505024]{0:T(1024)(128)(4,1)} %bitcast.37), calls=%async_computation.5 | async-start | bytes 8388608
  253.3 3.6 slice-start.1
  253.3 4.5 %slice-start.3 = ((s8[5505024]{0:T(1024)(128)(4,1)}), s8[1310720]{0:T(1024)(128)(4,1)S(1)}, s32[]{:S(2)}) async-start(s8[5505024]{0:T(1024)(128)(4,1)} %bitcast.37), calls=%async_computation.6 | async-start | bytes 2621440
  258.9 21.8 %collective-permute-start.4 = (bf16[512,1344]{0,1:T(8,128)(2,1)S(1)}, bf16[512,1344]{0,1:T(8,128)(2,1)}, u32[]{:S(2)}, u32[]{:S(2)}) collective-permute-start(bf16[512,1344]{0,1:T(8,128)(2,1)S(1)} %fusion.5), channel_id=1, source_target_pairs={{0,3},{1,0},{2,1},{3,2},{4,7},{5,4},{6,5},{7,6},{8,11},{9,8},{10,9... | collective-permute-start | bytes 4128776 | tf_op jit(solution)/shard_map/ppermute | solution.py:155
  265.2 86.2 %collective-permute-start.5 = (bf16[512,1344]{0,1:T(8,128)(2,1)}, bf16[512,1344]{0,1:T(8,128)(2,1)}, u32[]{:S(2)}, u32[]{:S(2)}) collective-permute-start(bf16[512,1344]{0,1:T(8,128)(2,1)} %fusion.6), channel_id=1, source_target_pairs={{0,2},{1,3},{2,0},{3,1},{4,6},{5,7},{6,4},{7,5},{8,10},{9,11},{10,... | collective-permute-start | bytes 4128776 | tf_op jit(solution)/shard_map/ppermute | solution.py:155
  268.4 112.5 %collective-permute-start.6 = (bf16[512,1344]{0,1:T(8,128)(2,1)}, bf16[512,1344]{0,1:T(8,128)(2,1)}, u32[]{:S(2)}, u32[]{:S(2)}) collective-permute-start(bf16[512,1344]{0,1:T(8,128)(2,1)} %fusion.7), channel_id=1, source_target_pairs={{0,1},{1,2},{2,3},{3,0},{4,5},{5,6},{6,7},{7,4},{8,9},{9,10},{10,1... | collective-permute-start | bytes 4128776 | tf_op jit(solution)/shard_map/ppermute | solution.py:155
Sparse Core Ops, SparseCore 0:
  9.6 100.8 all-gather.1
  246.4 149.4 reduce-scatter.1

commit v13 on v11

--- a/solution.py
+++ b/solution.py
@@ -37,30 +37,38 @@
 def attention_kernel(mask_ref, q_ref, k_ref, v_ref, g_ref, qg_ref, kg_ref, vg_ref):
     score_scale = (D / HEADS) ** (-0.5)
     groups = q_ref.shape[1] // HEAD_DIM
-    allowed = mask_ref[...] > 0.5
-    keys = k_ref[0]
-    values = v_ref[0]
-    key_acc = jnp.zeros(kg_ref.shape, jnp.float32)
-    value_acc = jnp.zeros(vg_ref.shape, jnp.float32)
-    for group in range(groups):
-        cols = slice(group * HEAD_DIM, (group + 1) * HEAD_DIM)
-        queries = q_ref[:, cols]
-        grads = g_ref[:, cols]
-        scores = contract_last(queries, keys) * score_scale
-        masked = jnp.where(allowed, scores, neg_large)
-        row_max = jnp.max(masked, axis=-1, keepdims=True)
-        expo = jnp.where(allowed, jnp.exp(masked - row_max), 0.0)
-        probs = expo / jnp.sum(expo, axis=-1, keepdims=True)
-        dprobs = contract_last(grads, values)
-        center = jnp.sum(probs * dprobs, axis=-1, keepdims=True)
-        dscores = (probs * (dprobs - center)).astype(jnp.bfloat16)
-        probs_low = probs.astype(jnp.bfloat16)
-        query_grad = jnp.dot(dscores, keys, preferred_element_type=jnp.float32) * score_scale
-        qg_ref[:, cols] = query_grad.astype(jnp.bfloat16)
-        key_acc = key_acc + contract_first(dscores, queries)
-        value_acc = value_acc + contract_first(probs_low, grads)
-    kg_ref[...] = key_acc * score_scale
-    vg_ref[...] = value_acc
+    tok_rows = q_ref.shape[0]
+    half = tok_rows // 2
+    span = WINDOW + half
+    kg_ref[...] = jnp.zeros(kg_ref.shape, jnp.float32)
+    vg_ref[...] = jnp.zeros(vg_ref.shape, jnp.float32)
+    for piece in range(2):
+        rows = slice(piece * half, (piece + 1) * half)
+        reach = slice(piece * half, piece * half + span)
+        allowed = mask_ref[rows, reach] > 0.5
+        keys = k_ref[0, reach, :]
+        values = v_ref[0, reach, :]
+        key_acc = jnp.zeros((span, HEAD_DIM), jnp.float32)
+        value_acc = jnp.zeros((span, HEAD_DIM), jnp.float32)
+        for group in range(groups):
+            cols = slice(group * HEAD_DIM, (group + 1) * HEAD_DIM)
+            queries = q_ref[rows, cols]
+            grads = g_ref[rows, cols]
+            scores = contract_last(queries, keys) * score_scale
+            masked = jnp.where(allowed, scores, neg_large)
+            row_max = jnp.max(masked, axis=-1, keepdims=True)
+            expo = jnp.where(allowed, jnp.exp(masked - row_max), 0.0)
+            probs = expo / jnp.sum(expo, axis=-1, keepdims=True)
+            dprobs = contract_last(grads, values)
+            center = jnp.sum(probs * dprobs, axis=-1, keepdims=True)
+            dscores = (probs * (dprobs - center)).astype(jnp.bfloat16)
+            probs_low = probs.astype(jnp.bfloat16)
+            query_grad = jnp.dot(dscores, keys, preferred_element_type=jnp.float32) * score_scale
+            qg_ref[rows, cols] = query_grad.astype(jnp.bfloat16)
+            key_acc = key_acc + contract_first(dscores, queries)
+            value_acc = value_acc + contract_first(probs_low, grads)
+        kg_ref[reach, :] = kg_ref[reach, :] + key_acc * score_scale
+        vg_ref[reach, :] = vg_ref[reach, :] + value_acc
 
 
 def attend(queries, key_value, grads, query_first, key_first, seg_query, seg_key):
@@ -77,6 +85,7 @@
         & (spacing < WINDOW)
         & (seg_query[:, None] == seg_key[None, :])
     )
+    assert key_rows == WINDOW + tok_rows and tok_rows % 256 == 0
     mask = allowed.astype(jnp.float32)
     q_spec = pl.BlockSpec((tok_rows, groups * HEAD_DIM), lambda h: (0, h))
     kv_out_spec = pl.BlockSpec((key_rows, HEAD_DIM), lambda h: (0, h))

time: 397 us -> 395 us (level)
  transfers between devices with their start and end apart: 9 -> 9, of which waited for: 8 -> 8; matrix products, arithmetic and copies ran while one was open for 11% -> 12% of each run, Pallas kernels for 0% -> 0%
where the time goes in v13:
time: 395 us; the launch traced here: 392 us
  waiting for transfers between devices  246 us (62%)
  matrix products  72.9 us (18%)
  Pallas kernels  27.3 us (7%)
  starting transfers between devices  19 us (5%)
  between operations  14.4 us (4%)
  other arithmetic  9.76 us (2%)
    all_gather x1, waiting for transfers between devices, per_device(): gathered = lax.all_gather(tokens, 'head', axis=1, tiled=True)  103 us
    ppermute x3, waiting for transfers between devices, per_device(): got = lax.ppermute(sent, 'head', pairs).astype(jnp.float32)  99.8 us
    ppermute x4, waiting for transfers between devices, passed_along(): return lax.ppermute(x, axis, pairs)  39.2 us
    dot_general x12, matrix products, contract_last(): lax.dot_general(left, right, (((1,), (1,)), ((), ())), preferred_element_...  31 us
    pallas_call x1, Pallas kernels, attend(): pl.pallas_call(attention_kernel, grid=(kv_local,), in_specs=[pl.BlockSpec...  27.3 us
    dot_general x1, matrix products, contract_first(): lax.dot_general(left, right, (((0,), (0,)), ((), ())), preferred_element_...  17.7 us
    ppermute x4, starting transfers between devices, passed_along(): return lax.ppermute(x, axis, pairs)  13.9 us
    dot_general x1, matrix products, per_device(): jnp.dot(gathered, query_weight, preferred_element_type=jnp.float32)  11.2 us
  transfers between devices with their start and end apart: 9, of which 8 were waited for; matrix products, arithmetic and copies ran while one was open for 12% of the time, Pallas kernels for 0%

profile of v13, /device:TPU:11, one launch (start us, length us, event | category | flops | bytes accessed | tf_op | source)
XLA Modules:
  0.0 392.5 jit_solution(3485833006367121328)
XLA Ops:
  7.9 102.5 %all-gather.2.cloned.1.call-done = bf16[512,5376]{0,1:T(8,128)(2,1)} async-done(((bf16[512,1344]{0,1:T(8,128)(2,1)}), bf16[512,5376]{0,1:T(8,128)(2,1)}) %all-gather.2.cloned.1.call-update) | async-done | bytes 5505040 | tf_op jit(solution)/shard_map/all_gather | solution.py:117
  110.5 7.4 %fusion.40 = bf16[1,512,512]{2,1,0:T(8,128)(2,1)S(1)} fusion(bf16[512,5376]{0,1:T(8,128)(2,1)} %all-gather.2.cloned.1.call-done, bf16[5376,512]{1,0:T(8,128)(2,1)} %param.8), kind=kOutput, calls=%fused_computation.60 | convolution fusion | flops 2818834432 | bytes 11534336 | tf_op jit(solution)/shard_map/dot_general | solution.py:121
  117.9 5.6 %fusion.41 = bf16[1,512,512]{2,1,0:T(8,128)(2,1)S(1)} fusion(bf16[512,5376]{0,1:T(8,128)(2,1)S(1)} %copy-done.3, bf16[5376,512]{1,0:T(8,128)(2,1)} %param.9), kind=kOutput, calls=%fused_computation.61 | convolution fusion | flops 2818834432 | bytes 11534336 | tf_op jit(solution)/shard_map/dot_general | solution.py:124
  123.6 3.6 collective-permute-start
  127.4 2.8 fusion.3.mask_ref
  130.3 8.7 %collective-permute-done = bf16[2,512,512]{2,1,0:T(8,128)(2,1)S(1)} collective-permute-done((bf16[2,512,512]{2,1,0:T(8,128)(2,1)S(1)}, bf16[2,512,512]{2,1,0:T(8,128)(2,1)S(1)}, u32[]{:S(2)}, u32[]{:S(2)}) %collective-permute-start) | collective-permute-done | bytes 1048608 | tf_op jit(solution)/shard_map/ppermute | solution.py:22
  139.0 5.5 %collective-permute-start.1 = (bf16[2,512,512]{2,1,0:T(8,128)(2,1)S(1)}, bf16[2,512,512]{2,1,0:T(8,128)(2,1)S(1)}, u32[]{:S(2)}, u32[]{:S(2)}) collective-permute-start(bf16[2,512,512]{2,1,0:T(8,128)(2,1)S(1)} %collective-permute-done), channel_id=1, source_target_pairs={{0,4},{4,8},{8,12},{12,16},{16,20},{20,24},{24,28},{1,5},{5,9},{9,... | collective-permute-start | bytes 3145736 | tf_op jit(solution)/shard_map/ppermute | solution.py:22
  144.4 11.2 %convolution_convert_fusion.1.q_ref = bf16[512,1024]{1,0:T(8,128)(2,1)} fusion(bf16[512,5376]{0,1:T(8,128)(2,1)} %all-gather.2.cloned.1.call-done, bf16[5376,1024]{1,0:T(8,128)(2,1)} %param.7), kind=kOutput, calls=%fused_computation.49 | convolution fusion | flops 5637668864 | bytes 17563648 | tf_op jit(solution)/shard_map/dot_general | solution.py:118
  157.8 27.3 %shard_map.93 = (bf16[512,1024]{1,0:T(8,128)(2,1)}, f32[1536,512]{1,0:T(8,128)}, f32[1536,512]{1,0:T(8,128)}) custom-call(f32[512,1536]{1,0:T(8,128)} %fusion.3.mask_ref, bf16[512,1024]{1,0:T(8,128)(2,1)} %convolution_convert_fusion.1.q_ref, bf16[2,1536,512]{2,1,0:T(8,128)(2,1)} %maximum_maximum_fusion.k_ref.v_ref, ...), custom_call_target="tpu_custom_call" | custom-call | tf_op jit(solution)/shard_map/pallas_call | solution.py:92
  186.9 2.5 collective-permute-start.2
  189.5 15.3 %collective-permute-done.2 = bf16[2,512,512]{2,1,0:T(8,128)(2,1)S(1)} collective-permute-done((bf16[2,512,512]{2,1,0:T(8,128)(2,1)S(1)}, bf16[2,512,512]{2,1,0:T(8,128)(2,1)S(1)}, u32[]{:S(2)}, u32[]{:S(2)}) %collective-permute-start.2) | collective-permute-done | bytes 1048608 | tf_op jit(solution)/shard_map/ppermute | solution.py:22
  207.5 14.9 %collective-permute-done.3 = bf16[2,512,512]{2,1,0:T(8,128)(2,1)S(1)} collective-permute-done((bf16[2,512,512]{2,1,0:T(8,128)(2,1)S(1)}, bf16[2,512,512]{2,1,0:T(8,128)(2,1)S(1)}, u32[]{:S(2)}, u32[]{:S(2)}) %collective-permute-start.3) | collective-permute-done | bytes 1048608 | tf_op jit(solution)/shard_map/ppermute | solution.py:22
  222.8 17.7 %convolution_convert_fusion = bf16[2048,5376]{0,1:T(8,128)(2,1)} fusion(bf16[512,5376]{0,1:T(8,128)(2,1)} %all-gather.2.cloned.1.call-done, bf16[512,512]{1,0:T(8,128)(2,1)S(1)} %get-tuple-element.13, bf16[512,512]{1,0:T(8,128)(2,1)S(1)} %get-tuple-element.12, bf16[512,1024]{1,0:T(8,128)(2,1)S(1)} %copy-done.4), kind=kOutput, calls=%fused_computation | convolution fusion | flops 11291590656 | bytes 29622272 | tf_op jit(solution)/shard_map/dot_general | solution.py:32
  240.6 3.4 fusion.16
  244.0 3.6 fusion.14
  247.6 5.0 %fusion.12 = f32[512,1344]{0,1:T(8,128)S(1)} fusion(bf16[512,1024]{1,0:T(8,128)(2,1)S(1)} %copy-done.4, bf16[5376,1024]{1,0:T(8,128)(2,1)} %param.7, s32[]{:T(128)S(6)} %select_n.48), kind=kOutput, calls=%fused_computation.30 | convolution fusion | flops 1409286144 | bytes 6553604 | tf_op jit(solution)/shard_map/dot_general | solution.py:26
  254.5 3.8 collective-permute-start.4
  265.4 4.0 %fusion.10 = f32[512,1344]{0,1:T(8,128)S(1)} fusion(bf16[512,1024]{1,0:T(8,128)(2,1)S(1)} %copy-done.4, bf16[5376,1024]{1,0:T(8,128)(2,1)} %param.7, s32[]{:T(128)S(6)} %select_n.49), kind=kOutput, calls=%fused_computation.28 | convolution fusion | flops 1409286144 | bytes 6553604 | tf_op jit(solution)/shard_map/dot_general | solution.py:26
  269.4 2.4 convolution_add_fusion.1
  271.8 75.7 %collective-permute-done.4 = bf16[512,1344]{0,1:T(8,128)(2,1)} collective-permute-done((bf16[512,1344]{0,1:T(8,128)(2,1)S(1)}, bf16[512,1344]{0,1:T(8,128)(2,1)}, u32[]{:S(2)}, u32[]{:S(2)}) %collective-permute-start.4) | collective-permute-done | bytes 1376288 | tf_op jit(solution)/shard_map/ppermute | solution.py:167
  347.5 24.1 %collective-permute-done.6 = bf16[512,1344]{0,1:T(8,128)(2,1)} collective-permute-done((bf16[512,1344]{0,1:T(8,128)(2,1)}, bf16[512,1344]{0,1:T(8,128)(2,1)}, u32[]{:S(2)}, u32[]{:S(2)}) %collective-permute-start.6) | collective-permute-done | bytes 1376288 | tf_op jit(solution)/shard_map/ppermute | solution.py:167
  371.6 5.0 %add_convert_fusion = bf16[512,1344]{0,1:T(8,128)(2,1)} fusion(bf16[512,1344]{0,1:T(8,128)(2,1)} %collective-permute-done.6, bf16[512,1344]{0,1:T(8,128)(2,1)} %collective-permute-done.5, bf16[512,1344]{0,1:T(8,128)(2,1)} %collective-permute-done.4, f32[512,1344]{0,1:T(8,128)S(1)} %convolution_add_fusion.1, bf16[5376,512]{1,0:T(8,128)(2,1)} %param.9, ...), kind=kOutput, calls=%fused_computation.27 | convolution fusion | flops 711524352 | bytes 10158084 | tf_op jit(solution)/shard_map/dot_general | solution.py:26
  376.6 4.2 %reduce-scatter.2.cloned.1.call-done = bf16[2048,672]{0,1:T(8,128)(2,1)} async-done(((bf16[2048,5376]{0,1:T(8,128)(2,1)}), bf16[2048,672]{0,1:T(8,128)(2,1)}) %reduce-scatter.2.cloned.1.call-update) | async-done | bytes 2752528 | tf_op jit(solution)/shard_map/reduce_scatter | solution.py:172
  380.8 2.4 fusion.9
  (47 shorter events, 19.4 us)
Async XLA Ops:
  7.2 103.3 %all-gather.2.cloned.1.call-start = ((), (), s32[]{:S(2)}) async-start(), calls=%async_computation.1 | async-start | bytes 6881280 | tf_op jit(solution)/shard_map/all_gather | solution.py:117
  7.9 372.9 %reduce-scatter.2.cloned.1.call-start = ((), (), s32[]{:S(2)}) async-start(), calls=%async_computation.2 | async-start | bytes 24772608 | tf_op jit(solution)/shard_map/reduce_scatter | solution.py:172
  110.5 7.4 %copy-start.3 = (bf16[512,5376]{0,1:T(8,128)(2,1)S(1)}, bf16[512,5376]{0,1:T(8,128)(2,1)}, u32[]{:S(2)}) copy-start(bf16[512,5376]{0,1:T(8,128)(2,1)} %all-gather.2.cloned.1.call-done) | copy-start | bytes 16515076
  117.9 9.4 %copy-start.2 = (s32[4096]{0:T(1024)S(1)}, s32[4096]{0:T(1024)}, u32[]{:S(2)}) copy-start(s32[4096]{0:T(1024)} %param.11) | copy-start | bytes 49156
  123.6 15.4 %collective-permute-start = (bf16[2,512,512]{2,1,0:T(8,128)(2,1)S(1)}, bf16[2,512,512]{2,1,0:T(8,128)(2,1)S(1)}, u32[]{:S(2)}, u32[]{:S(2)}) collective-permute-start(bf16[2,512,512]{2,1,0:T(8,128)(2,1)S(1)} %pad_maximum_fusion.1), channel_id=1, source_target_pairs={{0,4},{4,8},{8,12},{12,16},{16,20},{20,24},{24,28},{1,5},{5,9},{9,... | collective-permute-start | bytes 3145736 | tf_op jit(solution)/shard_map/ppermute | solution.py:22
  139.0 17.0 %collective-permute-start.1 = (bf16[2,512,512]{2,1,0:T(8,128)(2,1)S(1)}, bf16[2,512,512]{2,1,0:T(8,128)(2,1)S(1)}, u32[]{:S(2)}, u32[]{:S(2)}) collective-permute-start(bf16[2,512,512]{2,1,0:T(8,128)(2,1)S(1)} %collective-permute-done), channel_id=1, source_target_pairs={{0,4},{4,8},{8,12},{12,16},{16,20},{20,24},{24,28},{1,5},{5,9},{9,... | collective-permute-start | bytes 3145736 | tf_op jit(solution)/shard_map/ppermute | solution.py:22
  185.1 19.7 %copy-start = (f32[1536,512]{1,0:T(8,128)S(1)}, f32[1536,512]{1,0:T(8,128)}, u32[]{:S(2)}) copy-start(f32[1536,512]{1,0:T(8,128)} %get-tuple-element.8) | copy-start | bytes 9437188
  185.1 19.7 %copy-start.1 = (f32[1536,512]{1,0:T(8,128)S(1)}, f32[1536,512]{1,0:T(8,128)}, u32[]{:S(2)}) copy-start(f32[1536,512]{1,0:T(8,128)} %get-tuple-element.9) | copy-start | bytes 9437188
  186.9 17.9 %collective-permute-start.2 = (bf16[2,512,512]{2,1,0:T(8,128)(2,1)S(1)}, bf16[2,512,512]{2,1,0:T(8,128)(2,1)S(1)}, u32[]{:S(2)}, u32[]{:S(2)}) collective-permute-start(bf16[2,512,512]{2,1,0:T(8,128)(2,1)S(1)} %fusion.24), channel_id=1, source_target_pairs={{4,0},{8,4},{12,8},{16,12},{20,16},{24,20},{28,24},{5,1},{9,5},{13... | collective-permute-start | bytes 3145736 | tf_op jit(solution)/shard_map/ppermute | solution.py:22
  205.2 17.6 %copy-start.4 = (bf16[512,1024]{1,0:T(8,128)(2,1)S(1)}, bf16[512,1024]{1,0:T(8,128)(2,1)}, u32[]{:S(2)}) copy-start(bf16[512,1024]{1,0:T(8,128)(2,1)} %get-tuple-element.7) | copy-start | bytes 3145732
  205.2 17.1 %collective-permute-start.3 = (bf16[2,512,512]{2,1,0:T(8,128)(2,1)S(1)}, bf16[2,512,512]{2,1,0:T(8,128)(2,1)S(1)}, u32[]{:S(2)}, u32[]{:S(2)}) collective-permute-start(bf16[2,512,512]{2,1,0:T(8,128)(2,1)S(1)} %fusion.20), channel_id=1, source_target_pairs={{4,0},{8,4},{12,8},{16,12},{20,16},{24,20},{28,24},{5,1},{9,5},{13... | collective-permute-start | bytes 3145736 | tf_op jit(solution)/shard_map/ppermute | solution.py:22
  244.0 8.6 %slice-start = ((s8[5505024]{0:T(1024)(128)(4,1)}), s8[4194304]{0:T(1024)(128)(4,1)S(1)}, s32[]{:S(2)}) async-start(s8[5505024]{0:T(1024)(128)(4,1)} %bitcast.37), calls=%async_computation.3 | async-start | bytes 8388608
  244.0 9.5 %slice-start.2 = ((s8[5505024]{0:T(1024)(128)(4,1)}), s8[4194304]{0:T(1024)(128)(4,1)S(1)}, s32[]{:S(2)}) async-start(s8[5505024]{0:T(1024)(128)(4,1)} %bitcast.39), calls=%async_computation.5 | async-start | bytes 8388608
  247.6 5.0 %slice-start.1 = ((s8[5505024]{0:T(1024)(128)(4,1)}), s8[1310720]{0:T(1024)(128)(4,1)S(1)}, s32[]{:S(2)}) async-start(s8[5505024]{0:T(1024)(128)(4,1)} %bitcast.37), calls=%async_computation.4 | async-start | bytes 2621440
  247.6 5.9 %slice-start.3 = ((s8[5505024]{0:T(1024)(128)(4,1)}), s8[1310720]{0:T(1024)(128)(4,1)S(1)}, s32[]{:S(2)}) async-start(s8[5505024]{0:T(1024)(128)(4,1)} %bitcast.39), calls=%async_computation.6 | async-start | bytes 2621440
  254.5 93.0 %collective-permute-start.4 = (bf16[512,1344]{0,1:T(8,128)(2,1)S(1)}, bf16[512,1344]{0,1:T(8,128)(2,1)}, u32[]{:S(2)}, u32[]{:S(2)}) collective-permute-start(bf16[512,1344]{0,1:T(8,128)(2,1)S(1)} %fusion.4), channel_id=1, source_target_pairs={{0,3},{1,0},{2,1},{3,2},{4,7},{5,4},{6,5},{7,6},{8,11},{9,8},{10,9... | collective-permute-start | bytes 4128776 | tf_op jit(solution)/shard_map/ppermute | solution.py:167
  261.3 86.2 %collective-permute-start.5 = (bf16[512,1344]{0,1:T(8,128)(2,1)}, bf16[512,1344]{0,1:T(8,128)(2,1)}, u32[]{:S(2)}, u32[]{:S(2)}) collective-permute-start(bf16[512,1344]{0,1:T(8,128)(2,1)} %fusion.5), channel_id=1, source_target_pairs={{0,2},{1,3},{2,0},{3,1},{4,6},{5,7},{6,4},{7,5},{8,10},{9,11},{10,... | collective-permute-start | bytes 4128776 | tf_op jit(solution)/shard_map/ppermute | solution.py:167
  265.0 106.6 %collective-permute-start.6 = (bf16[512,1344]{0,1:T(8,128)(2,1)}, bf16[512,1344]{0,1:T(8,128)(2,1)}, u32[]{:S(2)}, u32[]{:S(2)}) collective-permute-start(bf16[512,1344]{0,1:T(8,128)(2,1)} %fusion.6), channel_id=1, source_target_pairs={{0,1},{1,2},{2,3},{3,0},{4,5},{5,6},{6,7},{7,4},{8,9},{9,10},{10,1... | collective-permute-start | bytes 4128776 | tf_op jit(solution)/shard_map/ppermute | solution.py:167
Sparse Core Ops, SparseCore 0:
  9.6 100.8 all-gather.1
  240.7 140.0 reduce-scatter.1

commit v14 on v11

--- a/solution.py
+++ b/solution.py
@@ -37,15 +37,21 @@
 def attention_kernel(mask_ref, q_ref, k_ref, v_ref, g_ref, qg_ref, kg_ref, vg_ref):
     score_scale = (D / HEADS) ** (-0.5)
     groups = q_ref.shape[1] // HEAD_DIM
-    allowed = mask_ref[...] > 0.5
-    keys = k_ref[0]
-    values = v_ref[0]
-    key_acc = jnp.zeros(kg_ref.shape, jnp.float32)
-    value_acc = jnp.zeros(vg_ref.shape, jnp.float32)
-    for group in range(groups):
-        cols = slice(group * HEAD_DIM, (group + 1) * HEAD_DIM)
-        queries = q_ref[:, cols]
-        grads = g_ref[:, cols]
+    tok_rows = q_ref.shape[0]
+    half = tok_rows // 2
+    span = WINDOW + half
+    kg_ref[...] = jnp.zeros(kg_ref.shape, jnp.float32)
+    vg_ref[...] = jnp.zeros(vg_ref.shape, jnp.float32)
+    for piece in range(2):
+        rows = slice(piece * half, (piece + 1) * half)
+        reach = slice(piece * half, piece * half + span)
+        allowed_one = mask_ref[rows, reach] > 0.5
+        allowed = jnp.concatenate([allowed_one] * groups, axis=0)
+        keys = k_ref[0, reach, :]
+        values = v_ref[0, reach, :]
+        col = [slice(group * HEAD_DIM, (group + 1) * HEAD_DIM) for group in range(groups)]
+        queries = jnp.concatenate([q_ref[rows, c] for c in col], axis=0)
+        grads = jnp.concatenate([g_ref[rows, c] for c in col], axis=0)
         scores = contract_last(queries, keys) * score_scale
         masked = jnp.where(allowed, scores, neg_large)
         row_max = jnp.max(masked, axis=-1, keepdims=True)
@@ -56,11 +62,11 @@
         dscores = (probs * (dprobs - center)).astype(jnp.bfloat16)
         probs_low = probs.astype(jnp.bfloat16)
         query_grad = jnp.dot(dscores, keys, preferred_element_type=jnp.float32) * score_scale
-        qg_ref[:, cols] = query_grad.astype(jnp.bfloat16)
-        key_acc = key_acc + contract_first(dscores, queries)
-        value_acc = value_acc + contract_first(probs_low, grads)
-    kg_ref[...] = key_acc * score_scale
-    vg_ref[...] = value_acc
+        query_grad = query_grad.astype(jnp.bfloat16)
+        for group in range(groups):
+            qg_ref[rows, col[group]] = query_grad[group * half : (group + 1) * half]
+        kg_ref[reach, :] = kg_ref[reach, :] + contract_first(dscores, queries) * score_scale
+        vg_ref[reach, :] = vg_ref[reach, :] + contract_first(probs_low, grads)
 
 
 def attend(queries, key_value, grads, query_first, key_first, seg_query, seg_key):
@@ -77,6 +83,7 @@
         & (spacing < WINDOW)
         & (seg_query[:, None] == seg_key[None, :])
     )
+    assert key_rows == WINDOW + tok_rows and tok_rows % 256 == 0
     mask = allowed.astype(jnp.float32)
     q_spec = pl.BlockSpec((tok_rows, groups * HEAD_DIM), lambda h: (0, h))
     kv_out_spec = pl.BlockSpec((key_rows, HEAD_DIM), lambda h: (0, h))

time: 397 us -> 395 us (level)
  no operation moved by 1% of the time
where the time goes in v14:
time: 395 us; the launch traced here: 393 us
  waiting for transfers between devices  247 us (63%)
  matrix products  72.8 us (18%)
  Pallas kernels  28.2 us (7%)
  starting transfers between devices  19 us (5%)
  between operations  14.4 us (4%)
  other arithmetic  9.76 us (2%)
    all_gather x1, waiting for transfers between devices, per_device(): gathered = lax.all_gather(tokens, 'head', axis=1, tiled=True)  103 us
    ppermute x3, waiting for transfers between devices, per_device(): got = lax.ppermute(sent, 'head', pairs).astype(jnp.float32)  99.8 us
    ppermute x4, waiting for transfers between devices, passed_along(): return lax.ppermute(x, axis, pairs)  39.2 us
    dot_general x12, matrix products, contract_last(): lax.dot_general(left, right, (((1,), (1,)), ((), ())), preferred_element_...  31 us
    pallas_call x1, Pallas kernels, attend(): pl.pallas_call(attention_kernel, grid=(kv_local,), in_specs=[pl.BlockSpec...  28.2 us
    dot_general x1, matrix products, contract_first(): lax.dot_general(left, right, (((0,), (0,)), ((), ())), preferred_element_...  17.7 us
    ppermute x4, starting transfers between devices, passed_along(): return lax.ppermute(x, axis, pairs)  13.9 us
    dot_general x1, matrix products, per_device(): jnp.dot(gathered, query_weight, preferred_element_type=jnp.float32)  11.2 us
  transfers between devices with their start and end apart: 9, of which 8 were waited for; matrix products, arithmetic and copies ran while one was open for 11% of the time, Pallas kernels for 0%

profile of v14, /device:TPU:11, one launch (start us, length us, event | category | flops | bytes accessed | tf_op | source)
XLA Modules:
  0.0 393.3 jit_solution(12958400840954422937)
XLA Ops:
  7.9 102.5 %all-gather.2.cloned.1.call-done = bf16[512,5376]{0,1:T(8,128)(2,1)} async-done(((bf16[512,1344]{0,1:T(8,128)(2,1)}), bf16[512,5376]{0,1:T(8,128)(2,1)}) %all-gather.2.cloned.1.call-update) | async-done | bytes 5505040 | tf_op jit(solution)/shard_map/all_gather | solution.py:115
  110.5 7.4 %fusion.40 = bf16[1,512,512]{2,1,0:T(8,128)(2,1)S(1)} fusion(bf16[512,5376]{0,1:T(8,128)(2,1)} %all-gather.2.cloned.1.call-done, bf16[5376,512]{1,0:T(8,128)(2,1)} %param.8), kind=kOutput, calls=%fused_computation.60 | convolution fusion | flops 2818834432 | bytes 11534336 | tf_op jit(solution)/shard_map/dot_general | solution.py:119
  117.9 5.6 %fusion.41 = bf16[1,512,512]{2,1,0:T(8,128)(2,1)S(1)} fusion(bf16[512,5376]{0,1:T(8,128)(2,1)S(1)} %copy-done.3, bf16[5376,512]{1,0:T(8,128)(2,1)} %param.9), kind=kOutput, calls=%fused_computation.61 | convolution fusion | flops 2818834432 | bytes 11534336 | tf_op jit(solution)/shard_map/dot_general | solution.py:122
  123.6 3.6 collective-permute-start
  127.4 2.8 fusion.3.mask_ref
  130.3 8.7 %collective-permute-done = bf16[2,512,512]{2,1,0:T(8,128)(2,1)S(1)} collective-permute-done((bf16[2,512,512]{2,1,0:T(8,128)(2,1)S(1)}, bf16[2,512,512]{2,1,0:T(8,128)(2,1)S(1)}, u32[]{:S(2)}, u32[]{:S(2)}) %collective-permute-start) | collective-permute-done | bytes 1048608 | tf_op jit(solution)/shard_map/ppermute | solution.py:22
  139.0 5.5 %collective-permute-start.1 = (bf16[2,512,512]{2,1,0:T(8,128)(2,1)S(1)}, bf16[2,512,512]{2,1,0:T(8,128)(2,1)S(1)}, u32[]{:S(2)}, u32[]{:S(2)}) collective-permute-start(bf16[2,512,512]{2,1,0:T(8,128)(2,1)S(1)} %collective-permute-done), channel_id=1, source_target_pairs={{0,4},{4,8},{8,12},{12,16},{16,20},{20,24},{24,28},{1,5},{5,9},{9,... | collective-permute-start | bytes 3145736 | tf_op jit(solution)/shard_map/ppermute | solution.py:22
  144.4 11.2 %convolution_convert_fusion.1.q_ref = bf16[512,1024]{1,0:T(8,128)(2,1)} fusion(bf16[512,5376]{0,1:T(8,128)(2,1)} %all-gather.2.cloned.1.call-done, bf16[5376,1024]{1,0:T(8,128)(2,1)} %param.7), kind=kOutput, calls=%fused_computation.49 | convolution fusion | flops 5637668864 | bytes 17563648 | tf_op jit(solution)/shard_map/dot_general | solution.py:116
  157.8 28.2 %shard_map.93 = (bf16[512,1024]{1,0:T(8,128)(2,1)}, f32[1536,512]{1,0:T(8,128)}, f32[1536,512]{1,0:T(8,128)}) custom-call(f32[512,1536]{1,0:T(8,128)} %fusion.3.mask_ref, bf16[512,1024]{1,0:T(8,128)(2,1)} %convolution_convert_fusion.1.q_ref, bf16[2,1536,512]{2,1,0:T(8,128)(2,1)} %maximum_maximum_fusion.k_ref.v_ref, ...), custom_call_target="tpu_custom_call" | custom-call | tf_op jit(solution)/shard_map/pallas_call | solution.py:90
  187.8 2.5 collective-permute-start.2
  190.4 15.3 %collective-permute-done.2 = bf16[2,512,512]{2,1,0:T(8,128)(2,1)S(1)} collective-permute-done((bf16[2,512,512]{2,1,0:T(8,128)(2,1)S(1)}, bf16[2,512,512]{2,1,0:T(8,128)(2,1)S(1)}, u32[]{:S(2)}, u32[]{:S(2)}) %collective-permute-start.2) | collective-permute-done | bytes 1048608 | tf_op jit(solution)/shard_map/ppermute | solution.py:22
  208.4 14.9 %collective-permute-done.3 = bf16[2,512,512]{2,1,0:T(8,128)(2,1)S(1)} collective-permute-done((bf16[2,512,512]{2,1,0:T(8,128)(2,1)S(1)}, bf16[2,512,512]{2,1,0:T(8,128)(2,1)S(1)}, u32[]{:S(2)}, u32[]{:S(2)}) %collective-permute-start.3) | collective-permute-done | bytes 1048608 | tf_op jit(solution)/shard_map/ppermute | solution.py:22
  223.7 17.7 %convolution_convert_fusion = bf16[2048,5376]{0,1:T(8,128)(2,1)} fusion(bf16[512,5376]{0,1:T(8,128)(2,1)} %all-gather.2.cloned.1.call-done, bf16[512,512]{1,0:T(8,128)(2,1)S(1)} %get-tuple-element.13, bf16[512,512]{1,0:T(8,128)(2,1)S(1)} %get-tuple-element.12, bf16[512,1024]{1,0:T(8,128)(2,1)S(1)} %copy-done.4), kind=kOutput, calls=%fused_computation | convolution fusion | flops 11291590656 | bytes 29622272 | tf_op jit(solution)/shard_map/dot_general | solution.py:32
  241.5 3.4 fusion.16
  244.9 3.6 fusion.14
  248.5 5.0 %fusion.12 = f32[512,1344]{0,1:T(8,128)S(1)} fusion(bf16[512,1024]{1,0:T(8,128)(2,1)S(1)} %copy-done.4, bf16[5376,1024]{1,0:T(8,128)(2,1)} %param.7, s32[]{:T(128)S(6)} %select_n.48), kind=kOutput, calls=%fused_computation.30 | convolution fusion | flops 1409286144 | bytes 6553604 | tf_op jit(solution)/shard_map/dot_general | solution.py:26
  255.4 3.8 collective-permute-start.4
  266.3 4.0 %fusion.10 = f32[512,1344]{0,1:T(8,128)S(1)} fusion(bf16[512,1024]{1,0:T(8,128)(2,1)S(1)} %copy-done.4, bf16[5376,1024]{1,0:T(8,128)(2,1)} %param.7, s32[]{:T(128)S(6)} %select_n.49), kind=kOutput, calls=%fused_computation.28 | convolution fusion | flops 1409286144 | bytes 6553604 | tf_op jit(solution)/shard_map/dot_general | solution.py:26
  270.3 2.4 convolution_add_fusion.1
  272.7 75.7 %collective-permute-done.4 = bf16[512,1344]{0,1:T(8,128)(2,1)} collective-permute-done((bf16[512,1344]{0,1:T(8,128)(2,1)S(1)}, bf16[512,1344]{0,1:T(8,128)(2,1)}, u32[]{:S(2)}, u32[]{:S(2)}) %collective-permute-start.4) | collective-permute-done | bytes 1376288 | tf_op jit(solution)/shard_map/ppermute | solution.py:165
  348.4 24.1 %collective-permute-done.6 = bf16[512,1344]{0,1:T(8,128)(2,1)} collective-permute-done((bf16[512,1344]{0,1:T(8,128)(2,1)}, bf16[512,1344]{0,1:T(8,128)(2,1)}, u32[]{:S(2)}, u32[]{:S(2)}) %collective-permute-start.6) | collective-permute-done | bytes 1376288 | tf_op jit(solution)/shard_map/ppermute | solution.py:165
  372.5 5.0 %add_convert_fusion = bf16[512,1344]{0,1:T(8,128)(2,1)} fusion(bf16[512,1344]{0,1:T(8,128)(2,1)} %collective-permute-done.6, bf16[512,1344]{0,1:T(8,128)(2,1)} %collective-permute-done.5, bf16[512,1344]{0,1:T(8,128)(2,1)} %collective-permute-done.4, f32[512,1344]{0,1:T(8,128)S(1)} %convolution_add_fusion.1, bf16[5376,512]{1,0:T(8,128)(2,1)} %param.9, ...), kind=kOutput, calls=%fused_computation.27 | convolution fusion | flops 711524352 | bytes 10158084 | tf_op jit(solution)/shard_map/dot_general | solution.py:26
  377.4 4.2 %reduce-scatter.2.cloned.1.call-done = bf16[2048,672]{0,1:T(8,128)(2,1)} async-done(((bf16[2048,5376]{0,1:T(8,128)(2,1)}), bf16[2048,672]{0,1:T(8,128)(2,1)}) %reduce-scatter.2.cloned.1.call-update) | async-done | bytes 2752528 | tf_op jit(solution)/shard_map/reduce_scatter | solution.py:170
  381.6 2.4 fusion.9
  (47 shorter events, 19.4 us)
Async XLA Ops:
  7.2 103.3 %all-gather.2.cloned.1.call-start = ((), (), s32[]{:S(2)}) async-start(), calls=%async_computation.1 | async-start | bytes 6881280 | tf_op jit(solution)/shard_map/all_gather | solution.py:115
  7.9 373.7 %reduce-scatter.2.cloned.1.call-start = ((), (), s32[]{:S(2)}) async-start(), calls=%async_computation.2 | async-start | bytes 24772608 | tf_op jit(solution)/shard_map/reduce_scatter | solution.py:170
  110.5 7.4 %copy-start.3 = (bf16[512,5376]{0,1:T(8,128)(2,1)S(1)}, bf16[512,5376]{0,1:T(8,128)(2,1)}, u32[]{:S(2)}) copy-start(bf16[512,5376]{0,1:T(8,128)(2,1)} %all-gather.2.cloned.1.call-done) | copy-start | bytes 16515076
  117.9 9.4 %copy-start.2 = (s32[4096]{0:T(1024)S(1)}, s32[4096]{0:T(1024)}, u32[]{:S(2)}) copy-start(s32[4096]{0:T(1024)} %param.11) | copy-start | bytes 49156
  123.6 15.4 %collective-permute-start = (bf16[2,512,512]{2,1,0:T(8,128)(2,1)S(1)}, bf16[2,512,512]{2,1,0:T(8,128)(2,1)S(1)}, u32[]{:S(2)}, u32[]{:S(2)}) collective-permute-start(bf16[2,512,512]{2,1,0:T(8,128)(2,1)S(1)} %pad_maximum_fusion.1), channel_id=1, source_target_pairs={{0,4},{4,8},{8,12},{12,16},{16,20},{20,24},{24,28},{1,5},{5,9},{9,... | collective-permute-start | bytes 3145736 | tf_op jit(solution)/shard_map/ppermute | solution.py:22
  139.0 17.0 %collective-permute-start.1 = (bf16[2,512,512]{2,1,0:T(8,128)(2,1)S(1)}, bf16[2,512,512]{2,1,0:T(8,128)(2,1)S(1)}, u32[]{:S(2)}, u32[]{:S(2)}) collective-permute-start(bf16[2,512,512]{2,1,0:T(8,128)(2,1)S(1)} %collective-permute-done), channel_id=1, source_target_pairs={{0,4},{4,8},{8,12},{12,16},{16,20},{20,24},{24,28},{1,5},{5,9},{9,... | collective-permute-start | bytes 3145736 | tf_op jit(solution)/shard_map/ppermute | solution.py:22
  186.0 19.7 %copy-start = (f32[1536,512]{1,0:T(8,128)S(1)}, f32[1536,512]{1,0:T(8,128)}, u32[]{:S(2)}) copy-start(f32[1536,512]{1,0:T(8,128)} %get-tuple-element.8) | copy-start | bytes 9437188
  186.0 19.7 %copy-start.1 = (f32[1536,512]{1,0:T(8,128)S(1)}, f32[1536,512]{1,0:T(8,128)}, u32[]{:S(2)}) copy-start(f32[1536,512]{1,0:T(8,128)} %get-tuple-element.9) | copy-start | bytes 9437188
  187.8 17.9 %collective-permute-start.2 = (bf16[2,512,512]{2,1,0:T(8,128)(2,1)S(1)}, bf16[2,512,512]{2,1,0:T(8,128)(2,1)S(1)}, u32[]{:S(2)}, u32[]{:S(2)}) collective-permute-start(bf16[2,512,512]{2,1,0:T(8,128)(2,1)S(1)} %fusion.24), channel_id=1, source_target_pairs={{4,0},{8,4},{12,8},{16,12},{20,16},{24,20},{28,24},{5,1},{9,5},{13... | collective-permute-start | bytes 3145736 | tf_op jit(solution)/shard_map/ppermute | solution.py:22
  206.1 17.6 %copy-start.4 = (bf16[512,1024]{1,0:T(8,128)(2,1)S(1)}, bf16[512,1024]{1,0:T(8,128)(2,1)}, u32[]{:S(2)}) copy-start(bf16[512,1024]{1,0:T(8,128)(2,1)} %get-tuple-element.7) | copy-start | bytes 3145732
  206.1 17.1 %collective-permute-start.3 = (bf16[2,512,512]{2,1,0:T(8,128)(2,1)S(1)}, bf16[2,512,512]{2,1,0:T(8,128)(2,1)S(1)}, u32[]{:S(2)}, u32[]{:S(2)}) collective-permute-start(bf16[2,512,512]{2,1,0:T(8,128)(2,1)S(1)} %fusion.20), channel_id=1, source_target_pairs={{4,0},{8,4},{12,8},{16,12},{20,16},{24,20},{28,24},{5,1},{9,5},{13... | collective-permute-start | bytes 3145736 | tf_op jit(solution)/shard_map/ppermute | solution.py:22
  244.9 8.6 %slice-start = ((s8[5505024]{0:T(1024)(128)(4,1)}), s8[4194304]{0:T(1024)(128)(4,1)S(1)}, s32[]{:S(2)}) async-start(s8[5505024]{0:T(1024)(128)(4,1)} %bitcast.37), calls=%async_computation.3 | async-start | bytes 8388608
  244.9 9.5 %slice-start.2 = ((s8[5505024]{0:T(1024)(128)(4,1)}), s8[4194304]{0:T(1024)(128)(4,1)S(1)}, s32[]{:S(2)}) async-start(s8[5505024]{0:T(1024)(128)(4,1)} %bitcast.39), calls=%async_computation.5 | async-start | bytes 8388608
  248.5 5.0 %slice-start.1 = ((s8[5505024]{0:T(1024)(128)(4,1)}), s8[1310720]{0:T(1024)(128)(4,1)S(1)}, s32[]{:S(2)}) async-start(s8[5505024]{0:T(1024)(128)(4,1)} %bitcast.37), calls=%async_computation.4 | async-start | bytes 2621440
  248.5 5.9 %slice-start.3 = ((s8[5505024]{0:T(1024)(128)(4,1)}), s8[1310720]{0:T(1024)(128)(4,1)S(1)}, s32[]{:S(2)}) async-start(s8[5505024]{0:T(1024)(128)(4,1)} %bitcast.39), calls=%async_computation.6 | async-start | bytes 2621440
  255.4 93.0 %collective-permute-start.4 = (bf16[512,1344]{0,1:T(8,128)(2,1)S(1)}, bf16[512,1344]{0,1:T(8,128)(2,1)}, u32[]{:S(2)}, u32[]{:S(2)}) collective-permute-start(bf16[512,1344]{0,1:T(8,128)(2,1)S(1)} %fusion.4), channel_id=1, source_target_pairs={{0,3},{1,0},{2,1},{3,2},{4,7},{5,4},{6,5},{7,6},{8,11},{9,8},{10,9... | collective-permute-start | bytes 4128776 | tf_op jit(solution)/shard_map/ppermute | solution.py:165
  262.1 86.2 %collective-permute-start.5 = (bf16[512,1344]{0,1:T(8,128)(2,1)}, bf16[512,1344]{0,1:T(8,128)(2,1)}, u32[]{:S(2)}, u32[]{:S(2)}) collective-permute-start(bf16[512,1344]{0,1:T(8,128)(2,1)} %fusion.5), channel_id=1, source_target_pairs={{0,2},{1,3},{2,0},{3,1},{4,6},{5,7},{6,4},{7,5},{8,10},{9,11},{10,... | collective-permute-start | bytes 4128776 | tf_op jit(solution)/shard_map/ppermute | solution.py:165
  265.8 106.6 %collective-permute-start.6 = (bf16[512,1344]{0,1:T(8,128)(2,1)}, bf16[512,1344]{0,1:T(8,128)(2,1)}, u32[]{:S(2)}, u32[]{:S(2)}) collective-permute-start(bf16[512,1344]{0,1:T(8,128)(2,1)} %fusion.6), channel_id=1, source_target_pairs={{0,1},{1,2},{2,3},{3,0},{4,5},{5,6},{6,7},{7,4},{8,9},{9,10},{10,1... | collective-permute-start | bytes 4128776 | tf_op jit(solution)/shard_map/ppermute | solution.py:165
Sparse Core Ops, SparseCore 0:
  9.6 100.8 all-gather.1
  241.5 140.0 reduce-scatter.1

commit v15 on v13

--- a/solution.py
+++ b/solution.py
@@ -128,6 +128,8 @@
     blocks = [key_value] * (hop_count + 1)
     moving = key_value
     for distance in range(1, hop_count + 1):
+        if distance > 1:
+            moving, queries = lax.optimization_barrier((moving, queries))
         moving = passed_along(moving, "seq", 1)
         blocks[hop_count - distance] = moving
     keys_all = jnp.concatenate(blocks, axis=1)

time: 395 us -> 395 us (level)
  waiting for transfers between devices: 246 us -> 251 us
  matrix products: 72.9 us -> 68.6 us
    dot_general x1, matrix products: 11.2 us -> 6.85 us  [per_device(): jnp.dot(gathered, query_weight, preferred_element_type=jnp.float32)]
    ppermute x4, waiting for transfers between devices: 39.2 us -> 43.6 us  [passed_along(): return lax.ppermute(x, axis, pairs)]
  transfers between devices with their start and end apart: 9 -> 9, of which waited for: 8 -> 8; matrix products, arithmetic and copies ran while one was open for 12% -> 10% of each run, Pallas kernels for 0% -> 0%
where the time goes in v15:
time: 395 us; the launch traced here: 393 us
  waiting for transfers between devices  251 us (64%)
  matrix products  68.6 us (17%)
  Pallas kernels  27.4 us (7%)
  starting transfers between devices  19 us (5%)
  between operations  14.4 us (4%)
  other arithmetic  9.76 us (2%)
    all_gather x1, waiting for transfers between devices, per_device(): gathered = lax.all_gather(tokens, 'head', axis=1, tiled=True)  103 us
    ppermute x3, waiting for transfers between devices, per_device(): got = lax.ppermute(sent, 'head', pairs).astype(jnp.float32)  99.8 us
    ppermute x4, waiting for transfers between devices, passed_along(): return lax.ppermute(x, axis, pairs)  43.6 us
    dot_general x12, matrix products, contract_last(): lax.dot_general(left, right, (((1,), (1,)), ((), ())), preferred_element_...  30.9 us
    pallas_call x1, Pallas kernels, attend(): pl.pallas_call(attention_kernel, grid=(kv_local,), in_specs=[pl.BlockSpec...  27.4 us
    dot_general x1, matrix products, contract_first(): lax.dot_general(left, right, (((0,), (0,)), ((), ())), preferred_element_...  17.7 us
    ppermute x4, starting transfers between devices, passed_along(): return lax.ppermute(x, axis, pairs)  13.9 us
  transfers between devices with their start and end apart: 9, of which 8 were waited for; matrix products, arithmetic and copies ran while one was open for 10% of the time, Pallas kernels for 0%

profile of v15, /device:TPU:11, one launch (start us, length us, event | category | flops | bytes accessed | tf_op | source)
XLA Modules:
  0.0 392.6 jit_solution(7790260478417878419)
XLA Ops:
  7.9 102.5 %all-gather.2.cloned.1.call-done = bf16[512,5376]{0,1:T(8,128)(2,1)} async-done(((bf16[512,1344]{0,1:T(8,128)(2,1)}), bf16[512,5376]{0,1:T(8,128)(2,1)}) %all-gather.2.cloned.1.call-update) | async-done | bytes 5505040 | tf_op jit(solution)/shard_map/all_gather | solution.py:117
  110.5 7.4 %fusion.40 = bf16[1,512,512]{2,1,0:T(8,128)(2,1)S(1)} fusion(bf16[512,5376]{0,1:T(8,128)(2,1)} %all-gather.2.cloned.1.call-done, bf16[5376,512]{1,0:T(8,128)(2,1)} %param.8), kind=kOutput, calls=%fused_computation.60 | convolution fusion | flops 2818834432 | bytes 11534336 | tf_op jit(solution)/shard_map/dot_general | solution.py:121
  117.9 5.7 %fusion.41 = bf16[1,512,512]{2,1,0:T(8,128)(2,1)S(1)} fusion(bf16[512,5376]{0,1:T(8,128)(2,1)S(1)} %copy-done.3, bf16[5376,512]{1,0:T(8,128)(2,1)} %param.9), kind=kOutput, calls=%fused_computation.61 | convolution fusion | flops 2818834432 | bytes 11534336 | tf_op jit(solution)/shard_map/dot_general | solution.py:124
  123.7 3.7 collective-permute-start
  127.5 6.8 %convolution_convert_fusion.1.q_ref = bf16[512,1024]{1,0:T(8,128)(2,1)} fusion(bf16[512,5376]{0,1:T(8,128)(2,1)S(1)} %copy-done.3, bf16[5376,1024]{1,0:T(8,128)(2,1)S(1)} %bitcast.42), kind=kOutput, calls=%fused_computation.49 | convolution fusion | flops 5637668864 | bytes 17563648 | tf_op jit(solution)/shard_map/dot_general | solution.py:118
  134.3 4.8 %collective-permute-done = bf16[2,512,512]{2,1,0:T(8,128)(2,1)S(1)} collective-permute-done((bf16[2,512,512]{2,1,0:T(8,128)(2,1)S(1)}, bf16[2,512,512]{2,1,0:T(8,128)(2,1)S(1)}, u32[]{:S(2)}, u32[]{:S(2)}) %collective-permute-start) | collective-permute-done | bytes 1048608 | tf_op jit(solution)/shard_map/ppermute | solution.py:22
  139.1 5.5 %collective-permute-start.1 = (bf16[2,512,512]{2,1,0:T(8,128)(2,1)S(1)}, bf16[2,512,512]{2,1,0:T(8,128)(2,1)S(1)}, u32[]{:S(2)}, u32[]{:S(2)}) collective-permute-start(bf16[2,512,512]{2,1,0:T(8,128)(2,1)S(1)} %collective-permute-done), channel_id=1, source_target_pairs={{0,4},{4,8},{8,12},{12,16},{16,20},{20,24},{24,28},{1,5},{5,9},{9,... | collective-permute-start | bytes 3145736 | tf_op jit(solution)/shard_map/ppermute | solution.py:22
  144.8 2.8 fusion.3.mask_ref
  147.6 8.5 %collective-permute-done.1 = bf16[2,512,512]{2,1,0:T(8,128)(2,1)S(1)} collective-permute-done((bf16[2,512,512]{2,1,0:T(8,128)(2,1)S(1)}, bf16[2,512,512]{2,1,0:T(8,128)(2,1)S(1)}, u32[]{:S(2)}, u32[]{:S(2)}) %collective-permute-start.1) | collective-permute-done | bytes 1048608 | tf_op jit(solution)/shard_map/ppermute | solution.py:22
  157.9 27.4 %shard_map.93 = (bf16[512,1024]{1,0:T(8,128)(2,1)}, f32[1536,512]{1,0:T(8,128)}, f32[1536,512]{1,0:T(8,128)}) custom-call(f32[512,1536]{1,0:T(8,128)} %fusion.3.mask_ref, bf16[512,1024]{1,0:T(8,128)(2,1)} %convolution_convert_fusion.1.q_ref, bf16[2,1536,512]{2,1,0:T(8,128)(2,1)} %maximum_maximum_fusion.k_ref.v_ref, ...), custom_call_target="tpu_custom_call" | custom-call | tf_op jit(solution)/shard_map/pallas_call | solution.py:92
  187.1 2.5 collective-permute-start.2
  189.7 15.4 %collective-permute-done.2 = bf16[2,512,512]{2,1,0:T(8,128)(2,1)S(1)} collective-permute-done((bf16[2,512,512]{2,1,0:T(8,128)(2,1)S(1)}, bf16[2,512,512]{2,1,0:T(8,128)(2,1)S(1)}, u32[]{:S(2)}, u32[]{:S(2)}) %collective-permute-start.2) | collective-permute-done | bytes 1048608 | tf_op jit(solution)/shard_map/ppermute | solution.py:22
  207.7 14.9 %collective-permute-done.3 = bf16[2,512,512]{2,1,0:T(8,128)(2,1)S(1)} collective-permute-done((bf16[2,512,512]{2,1,0:T(8,128)(2,1)S(1)}, bf16[2,512,512]{2,1,0:T(8,128)(2,1)S(1)}, u32[]{:S(2)}, u32[]{:S(2)}) %collective-permute-start.3) | collective-permute-done | bytes 1048608 | tf_op jit(solution)/shard_map/ppermute | solution.py:22
  223.0 17.7 %convolution_convert_fusion = bf16[2048,5376]{0,1:T(8,128)(2,1)} fusion(bf16[512,5376]{0,1:T(8,128)(2,1)} %all-gather.2.cloned.1.call-done, bf16[512,512]{1,0:T(8,128)(2,1)S(1)} %get-tuple-element.17, bf16[512,512]{1,0:T(8,128)(2,1)S(1)} %get-tuple-element.16, bf16[512,1024]{1,0:T(8,128)(2,1)S(1)} %copy-done.4), kind=kOutput, calls=%fused_computation | convolution fusion | flops 11291590656 | bytes 29622272 | tf_op jit(solution)/shard_map/dot_general | solution.py:32
  240.8 3.4 fusion.16
  244.2 3.6 fusion.14
  247.8 4.9 %fusion.12 = f32[512,1344]{0,1:T(8,128)S(1)} fusion(bf16[512,1024]{1,0:T(8,128)(2,1)S(1)} %copy-done.4, bf16[5376,1024]{1,0:T(8,128)(2,1)} %param.7, s32[]{:T(128)S(6)} %select_n.48), kind=kOutput, calls=%fused_computation.30 | convolution fusion | flops 1409286144 | bytes 6553604 | tf_op jit(solution)/shard_map/dot_general | solution.py:26
  254.7 3.8 collective-permute-start.4
  265.6 4.0 %fusion.10 = f32[512,1344]{0,1:T(8,128)S(1)} fusion(bf16[512,1024]{1,0:T(8,128)(2,1)S(1)} %copy-done.4, bf16[5376,1024]{1,0:T(8,128)(2,1)} %param.7, s32[]{:T(128)S(6)} %select_n.49), kind=kOutput, calls=%fused_computation.28 | convolution fusion | flops 1409286144 | bytes 6553604 | tf_op jit(solution)/shard_map/dot_general | solution.py:26
  272.0 75.7 %collective-permute-done.4 = bf16[512,1344]{0,1:T(8,128)(2,1)} collective-permute-done((bf16[512,1344]{0,1:T(8,128)(2,1)S(1)}, bf16[512,1344]{0,1:T(8,128)(2,1)}, u32[]{:S(2)}, u32[]{:S(2)}) %collective-permute-start.4) | collective-permute-done | bytes 1376288 | tf_op jit(solution)/shard_map/ppermute | solution.py:169
  347.7 24.1 %collective-permute-done.6 = bf16[512,1344]{0,1:T(8,128)(2,1)} collective-permute-done((bf16[512,1344]{0,1:T(8,128)(2,1)}, bf16[512,1344]{0,1:T(8,128)(2,1)}, u32[]{:S(2)}, u32[]{:S(2)}) %collective-permute-start.6) | collective-permute-done | bytes 1376288 | tf_op jit(solution)/shard_map/ppermute | solution.py:169
  371.8 5.0 %add_convert_fusion = bf16[512,1344]{0,1:T(8,128)(2,1)} fusion(bf16[512,1344]{0,1:T(8,128)(2,1)} %collective-permute-done.6, bf16[512,1344]{0,1:T(8,128)(2,1)} %collective-permute-done.5, bf16[512,1344]{0,1:T(8,128)(2,1)} %collective-permute-done.4, f32[512,1344]{0,1:T(8,128)S(1)} %convolution_add_fusion.1, bf16[5376,512]{1,0:T(8,128)(2,1)} %param.9, ...), kind=kOutput, calls=%fused_computation.27 | convolution fusion | flops 711524352 | bytes 10158084 | tf_op jit(solution)/shard_map/dot_general | solution.py:26
  376.8 4.2 %reduce-scatter.2.cloned.1.call-done = bf16[2048,672]{0,1:T(8,128)(2,1)} async-done(((bf16[2048,5376]{0,1:T(8,128)(2,1)}), bf16[2048,672]{0,1:T(8,128)(2,1)}) %reduce-scatter.2.cloned.1.call-update) | async-done | bytes 2752528 | tf_op jit(solution)/shard_map/reduce_scatter | solution.py:174
  381.0 2.4 fusion.9
  (54 shorter events, 21.5 us)
Async XLA Ops:
  7.2 103.3 %all-gather.2.cloned.1.call-start = ((), (), s32[]{:S(2)}) async-start(), calls=%async_computation.1 | async-start | bytes 6881280 | tf_op jit(solution)/shard_map/all_gather | solution.py:117
  7.9 373.1 %reduce-scatter.2.cloned.1.call-start = ((), (), s32[]{:S(2)}) async-start(), calls=%async_computation.2 | async-start | bytes 24772608 | tf_op jit(solution)/shard_map/reduce_scatter | solution.py:174
  110.5 7.4 %copy-start.3 = (bf16[512,5376]{0,1:T(8,128)(2,1)S(1)}, bf16[512,5376]{0,1:T(8,128)(2,1)}, u32[]{:S(2)}) copy-start(bf16[512,5376]{0,1:T(8,128)(2,1)} %all-gather.2.cloned.1.call-done) | copy-start | bytes 16515076
  110.5 16.9 %slice-start.4 = ((s8[11010048]{0:T(1024)(128)(4,1)}), s8[4194304]{0:T(1024)(128)(4,1)S(1)}, s32[]{:S(2)}) async-start(s8[11010048]{0:T(1024)(128)(4,1)} %bitcast.41), calls=%async_computation.7 | async-start | bytes 8388608
  110.5 16.9 %slice-start.5 = ((s8[11010048]{0:T(1024)(128)(4,1)}), s8[4194304]{0:T(1024)(128)(4,1)S(1)}, s32[]{:S(2)}) async-start(s8[11010048]{0:T(1024)(128)(4,1)} %bitcast.41), calls=%async_computation.8 | async-start | bytes 8388608
  117.9 9.6 %slice-start.6 = ((s8[11010048]{0:T(1024)(128)(4,1)}), s8[2621440]{0:T(1024)(128)(4,1)S(1)}, s32[]{:S(2)}) async-start(s8[11010048]{0:T(1024)(128)(4,1)} %bitcast.41), calls=%async_computation.9 | async-start | bytes 5242880
  123.7 20.9 %copy-start.2 = (s32[4096]{0:T(1024)S(1)}, s32[4096]{0:T(1024)}, u32[]{:S(2)}) copy-start(s32[4096]{0:T(1024)} %param.11) | copy-start | bytes 49156
  123.7 15.4 %collective-permute-start = (bf16[2,512,512]{2,1,0:T(8,128)(2,1)S(1)}, bf16[2,512,512]{2,1,0:T(8,128)(2,1)S(1)}, u32[]{:S(2)}, u32[]{:S(2)}) collective-permute-start(bf16[2,512,512]{2,1,0:T(8,128)(2,1)S(1)} %pad_maximum_fusion.1), channel_id=1, source_target_pairs={{0,4},{4,8},{8,12},{12,16},{16,20},{20,24},{24,28},{1,5},{5,9},{9,... | collective-permute-start | bytes 3145736 | tf_op jit(solution)/shard_map/ppermute | solution.py:22
  139.1 17.0 %collective-permute-start.1 = (bf16[2,512,512]{2,1,0:T(8,128)(2,1)S(1)}, bf16[2,512,512]{2,1,0:T(8,128)(2,1)S(1)}, u32[]{:S(2)}, u32[]{:S(2)}) collective-permute-start(bf16[2,512,512]{2,1,0:T(8,128)(2,1)S(1)} %collective-permute-done), channel_id=1, source_target_pairs={{0,4},{4,8},{8,12},{12,16},{16,20},{20,24},{24,28},{1,5},{5,9},{9,... | collective-permute-start | bytes 3145736 | tf_op jit(solution)/shard_map/ppermute | solution.py:22
  185.3 19.7 %copy-start = (f32[1536,512]{1,0:T(8,128)S(1)}, f32[1536,512]{1,0:T(8,128)}, u32[]{:S(2)}) copy-start(f32[1536,512]{1,0:T(8,128)} %get-tuple-element.12) | copy-start | bytes 9437188
  185.3 19.7 %copy-start.1 = (f32[1536,512]{1,0:T(8,128)S(1)}, f32[1536,512]{1,0:T(8,128)}, u32[]{:S(2)}) copy-start(f32[1536,512]{1,0:T(8,128)} %get-tuple-element.13) | copy-start | bytes 9437188
  187.1 17.9 %collective-permute-start.2 = (bf16[2,512,512]{2,1,0:T(8,128)(2,1)S(1)}, bf16[2,512,512]{2,1,0:T(8,128)(2,1)S(1)}, u32[]{:S(2)}, u32[]{:S(2)}) collective-permute-start(bf16[2,512,512]{2,1,0:T(8,128)(2,1)S(1)} %fusion.24), channel_id=1, source_target_pairs={{4,0},{8,4},{12,8},{16,12},{20,16},{24,20},{28,24},{5,1},{9,5},{13... | collective-permute-start | bytes 3145736 | tf_op jit(solution)/shard_map/ppermute | solution.py:22
  205.4 17.6 %copy-start.4 = (bf16[512,1024]{1,0:T(8,128)(2,1)S(1)}, bf16[512,1024]{1,0:T(8,128)(2,1)}, u32[]{:S(2)}) copy-start(bf16[512,1024]{1,0:T(8,128)(2,1)} %get-tuple-element.11) | copy-start | bytes 3145732
  205.4 17.1 %collective-permute-start.3 = (bf16[2,512,512]{2,1,0:T(8,128)(2,1)S(1)}, bf16[2,512,512]{2,1,0:T(8,128)(2,1)S(1)}, u32[]{:S(2)}, u32[]{:S(2)}) collective-permute-start(bf16[2,512,512]{2,1,0:T(8,128)(2,1)S(1)} %fusion.20), channel_id=1, source_target_pairs={{4,0},{8,4},{12,8},{16,12},{20,16},{24,20},{28,24},{5,1},{9,5},{13... | collective-permute-start | bytes 3145736 | tf_op jit(solution)/shard_map/ppermute | solution.py:22
  244.2 8.6 %slice-start = ((s8[5505024]{0:T(1024)(128)(4,1)}), s8[4194304]{0:T(1024)(128)(4,1)S(1)}, s32[]{:S(2)}) async-start(s8[5505024]{0:T(1024)(128)(4,1)} %bitcast.37), calls=%async_computation.3 | async-start | bytes 8388608
  244.2 9.5 %slice-start.2 = ((s8[5505024]{0:T(1024)(128)(4,1)}), s8[4194304]{0:T(1024)(128)(4,1)S(1)}, s32[]{:S(2)}) async-start(s8[5505024]{0:T(1024)(128)(4,1)} %bitcast.39), calls=%async_computation.5 | async-start | bytes 8388608
  247.8 5.0 %slice-start.1 = ((s8[5505024]{0:T(1024)(128)(4,1)}), s8[1310720]{0:T(1024)(128)(4,1)S(1)}, s32[]{:S(2)}) async-start(s8[5505024]{0:T(1024)(128)(4,1)} %bitcast.37), calls=%async_computation.4 | async-start | bytes 2621440
  247.8 5.9 %slice-start.3 = ((s8[5505024]{0:T(1024)(128)(4,1)}), s8[1310720]{0:T(1024)(128)(4,1)S(1)}, s32[]{:S(2)}) async-start(s8[5505024]{0:T(1024)(128)(4,1)} %bitcast.39), calls=%async_computation.6 | async-start | bytes 2621440
  254.7 93.0 %collective-permute-start.4 = (bf16[512,1344]{0,1:T(8,128)(2,1)S(1)}, bf16[512,1344]{0,1:T(8,128)(2,1)}, u32[]{:S(2)}, u32[]{:S(2)}) collective-permute-start(bf16[512,1344]{0,1:T(8,128)(2,1)S(1)} %fusion.4), channel_id=1, source_target_pairs={{0,3},{1,0},{2,1},{3,2},{4,7},{5,4},{6,5},{7,6},{8,11},{9,8},{10,9... | collective-permute-start | bytes 4128776 | tf_op jit(solution)/shard_map/ppermute | solution.py:169
  261.5 86.2 %collective-permute-start.5 = (bf16[512,1344]{0,1:T(8,128)(2,1)}, bf16[512,1344]{0,1:T(8,128)(2,1)}, u32[]{:S(2)}, u32[]{:S(2)}) collective-permute-start(bf16[512,1344]{0,1:T(8,128)(2,1)} %fusion.5), channel_id=1, source_target_pairs={{0,2},{1,3},{2,0},{3,1},{4,6},{5,7},{6,4},{7,5},{8,10},{9,11},{10,... | collective-permute-start | bytes 4128776 | tf_op jit(solution)/shard_map/ppermute | solution.py:169
  265.1 106.7 %collective-permute-start.6 = (bf16[512,1344]{0,1:T(8,128)(2,1)}, bf16[512,1344]{0,1:T(8,128)(2,1)}, u32[]{:S(2)}, u32[]{:S(2)}) collective-permute-start(bf16[512,1344]{0,1:T(8,128)(2,1)} %fusion.6), channel_id=1, source_target_pairs={{0,1},{1,2},{2,3},{3,0},{4,5},{5,6},{6,7},{7,4},{8,9},{9,10},{10,1... | collective-permute-start | bytes 4128776 | tf_op jit(solution)/shard_map/ppermute | solution.py:169
Sparse Core Ops, SparseCore 0:
  9.6 100.8 all-gather.1
  240.9 140.0 reduce-scatter.1

commit v16 on v13

--- a/solution.py
+++ b/solution.py
@@ -57,8 +57,8 @@
             scores = contract_last(queries, keys) * score_scale
             masked = jnp.where(allowed, scores, neg_large)
             row_max = jnp.max(masked, axis=-1, keepdims=True)
-            expo = jnp.where(allowed, jnp.exp(masked - row_max), 0.0)
-            probs = expo / jnp.sum(expo, axis=-1, keepdims=True)
+            expo = jnp.exp(masked - row_max)
+            probs = expo * (1.0 / jnp.sum(expo, axis=-1, keepdims=True))
             dprobs = contract_last(grads, values)
             center = jnp.sum(probs * dprobs, axis=-1, keepdims=True)
             dscores = (probs * (dprobs - center)).astype(jnp.bfloat16)

time: 395 us -> 394 us (level)
  no operation moved by 1% of the time
where the time goes in v16:
time: 394 us; the launch traced here: 392 us
  waiting for transfers between devices  246 us (62%)
  matrix products  72.9 us (19%)
  Pallas kernels  26.4 us (7%)
  starting transfers between devices  19 us (5%)
  between operations  14.4 us (4%)
  other arithmetic  9.76 us (2%)
    all_gather x1, waiting for transfers between devices, per_device(): gathered = lax.all_gather(tokens, 'head', axis=1, tiled=True)  103 us
    ppermute x3, waiting for transfers between devices, per_device(): got = lax.ppermute(sent, 'head', pairs).astype(jnp.float32)  99.8 us
    ppermute x4, waiting for transfers between devices, passed_along(): return lax.ppermute(x, axis, pairs)  39.2 us
    dot_general x12, matrix products, contract_last(): lax.dot_general(left, right, (((1,), (1,)), ((), ())), preferred_element_...  31 us
    pallas_call x1, Pallas kernels, attend(): pl.pallas_call(attention_kernel, grid=(kv_local,), in_specs=[pl.BlockSpec...  26.4 us
    dot_general x1, matrix products, contract_first(): lax.dot_general(left, right, (((0,), (0,)), ((), ())), preferred_element_...  17.7 us
    ppermute x4, starting transfers between devices, passed_along(): return lax.ppermute(x, axis, pairs)  13.9 us
    dot_general x1, matrix products, per_device(): jnp.dot(gathered, query_weight, preferred_element_type=jnp.float32)  11.2 us
  transfers between devices with their start and end apart: 9, of which 8 were waited for; matrix products, arithmetic and copies ran while one was open for 12% of the time, Pallas kernels for 0%

profile of v16, /device:TPU:11, one launch (start us, length us, event | category | flops | bytes accessed | tf_op | source)
XLA Modules:
  0.0 391.5 jit_solution(15066588963212645614)
XLA Ops:
  7.9 102.5 %all-gather.2.cloned.1.call-done = bf16[512,5376]{0,1:T(8,128)(2,1)} async-done(((bf16[512,1344]{0,1:T(8,128)(2,1)}), bf16[512,5376]{0,1:T(8,128)(2,1)}) %all-gather.2.cloned.1.call-update) | async-done | bytes 5505040 | tf_op jit(solution)/shard_map/all_gather | solution.py:117
  110.5 7.4 %fusion.40 = bf16[1,512,512]{2,1,0:T(8,128)(2,1)S(1)} fusion(bf16[512,5376]{0,1:T(8,128)(2,1)} %all-gather.2.cloned.1.call-done, bf16[5376,512]{1,0:T(8,128)(2,1)} %param.8), kind=kOutput, calls=%fused_computation.60 | convolution fusion | flops 2818834432 | bytes 11534336 | tf_op jit(solution)/shard_map/dot_general | solution.py:121
  117.9 5.6 %fusion.41 = bf16[1,512,512]{2,1,0:T(8,128)(2,1)S(1)} fusion(bf16[512,5376]{0,1:T(8,128)(2,1)S(1)} %copy-done.3, bf16[5376,512]{1,0:T(8,128)(2,1)} %param.9), kind=kOutput, calls=%fused_computation.61 | convolution fusion | flops 2818834432 | bytes 11534336 | tf_op jit(solution)/shard_map/dot_general | solution.py:124
  123.6 3.6 collective-permute-start
  127.4 2.8 fusion.3.mask_ref
  130.3 8.7 %collective-permute-done = bf16[2,512,512]{2,1,0:T(8,128)(2,1)S(1)} collective-permute-done((bf16[2,512,512]{2,1,0:T(8,128)(2,1)S(1)}, bf16[2,512,512]{2,1,0:T(8,128)(2,1)S(1)}, u32[]{:S(2)}, u32[]{:S(2)}) %collective-permute-start) | collective-permute-done | bytes 1048608 | tf_op jit(solution)/shard_map/ppermute | solution.py:22
  139.0 5.5 %collective-permute-start.1 = (bf16[2,512,512]{2,1,0:T(8,128)(2,1)S(1)}, bf16[2,512,512]{2,1,0:T(8,128)(2,1)S(1)}, u32[]{:S(2)}, u32[]{:S(2)}) collective-permute-start(bf16[2,512,512]{2,1,0:T(8,128)(2,1)S(1)} %collective-permute-done), channel_id=1, source_target_pairs={{0,4},{4,8},{8,12},{12,16},{16,20},{20,24},{24,28},{1,5},{5,9},{9,... | collective-permute-start | bytes 3145736 | tf_op jit(solution)/shard_map/ppermute | solution.py:22
  144.4 11.2 %convolution_convert_fusion.1.q_ref = bf16[512,1024]{1,0:T(8,128)(2,1)} fusion(bf16[512,5376]{0,1:T(8,128)(2,1)} %all-gather.2.cloned.1.call-done, bf16[5376,1024]{1,0:T(8,128)(2,1)} %param.7), kind=kOutput, calls=%fused_computation.49 | convolution fusion | flops 5637668864 | bytes 17563648 | tf_op jit(solution)/shard_map/dot_general | solution.py:118
  157.8 26.4 %shard_map.93 = (bf16[512,1024]{1,0:T(8,128)(2,1)}, f32[1536,512]{1,0:T(8,128)}, f32[1536,512]{1,0:T(8,128)}) custom-call(f32[512,1536]{1,0:T(8,128)} %fusion.3.mask_ref, bf16[512,1024]{1,0:T(8,128)(2,1)} %convolution_convert_fusion.1.q_ref, bf16[2,1536,512]{2,1,0:T(8,128)(2,1)} %maximum_maximum_fusion.k_ref.v_ref, ...), custom_call_target="tpu_custom_call" | custom-call | tf_op jit(solution)/shard_map/pallas_call | solution.py:92
  186.0 2.6 collective-permute-start.2
  188.5 15.3 %collective-permute-done.2 = bf16[2,512,512]{2,1,0:T(8,128)(2,1)S(1)} collective-permute-done((bf16[2,512,512]{2,1,0:T(8,128)(2,1)S(1)}, bf16[2,512,512]{2,1,0:T(8,128)(2,1)S(1)}, u32[]{:S(2)}, u32[]{:S(2)}) %collective-permute-start.2) | collective-permute-done | bytes 1048608 | tf_op jit(solution)/shard_map/ppermute | solution.py:22
  206.5 14.9 %collective-permute-done.3 = bf16[2,512,512]{2,1,0:T(8,128)(2,1)S(1)} collective-permute-done((bf16[2,512,512]{2,1,0:T(8,128)(2,1)S(1)}, bf16[2,512,512]{2,1,0:T(8,128)(2,1)S(1)}, u32[]{:S(2)}, u32[]{:S(2)}) %collective-permute-start.3) | collective-permute-done | bytes 1048608 | tf_op jit(solution)/shard_map/ppermute | solution.py:22
  221.9 17.7 %convolution_convert_fusion = bf16[2048,5376]{0,1:T(8,128)(2,1)} fusion(bf16[512,5376]{0,1:T(8,128)(2,1)} %all-gather.2.cloned.1.call-done, bf16[512,512]{1,0:T(8,128)(2,1)S(1)} %get-tuple-element.13, bf16[512,512]{1,0:T(8,128)(2,1)S(1)} %get-tuple-element.12, bf16[512,1024]{1,0:T(8,128)(2,1)S(1)} %copy-done.4), kind=kOutput, calls=%fused_computation | convolution fusion | flops 11291590656 | bytes 29622272 | tf_op jit(solution)/shard_map/dot_general | solution.py:32
  239.6 3.4 fusion.16
  243.1 3.6 fusion.14
  246.7 5.0 %fusion.12 = f32[512,1344]{0,1:T(8,128)S(1)} fusion(bf16[512,1024]{1,0:T(8,128)(2,1)S(1)} %copy-done.4, bf16[5376,1024]{1,0:T(8,128)(2,1)} %param.7, s32[]{:T(128)S(6)} %select_n.48), kind=kOutput, calls=%fused_computation.30 | convolution fusion | flops 1409286144 | bytes 6553604 | tf_op jit(solution)/shard_map/dot_general | solution.py:26
  253.6 3.8 collective-permute-start.4
  264.5 4.0 %fusion.10 = f32[512,1344]{0,1:T(8,128)S(1)} fusion(bf16[512,1024]{1,0:T(8,128)(2,1)S(1)} %copy-done.4, bf16[5376,1024]{1,0:T(8,128)(2,1)} %param.7, s32[]{:T(128)S(6)} %select_n.49), kind=kOutput, calls=%fused_computation.28 | convolution fusion | flops 1409286144 | bytes 6553604 | tf_op jit(solution)/shard_map/dot_general | solution.py:26
  268.5 2.4 convolution_add_fusion.1
  270.9 75.7 %collective-permute-done.4 = bf16[512,1344]{0,1:T(8,128)(2,1)} collective-permute-done((bf16[512,1344]{0,1:T(8,128)(2,1)S(1)}, bf16[512,1344]{0,1:T(8,128)(2,1)}, u32[]{:S(2)}, u32[]{:S(2)}) %collective-permute-start.4) | collective-permute-done | bytes 1376288 | tf_op jit(solution)/shard_map/ppermute | solution.py:167
  346.5 24.1 %collective-permute-done.6 = bf16[512,1344]{0,1:T(8,128)(2,1)} collective-permute-done((bf16[512,1344]{0,1:T(8,128)(2,1)}, bf16[512,1344]{0,1:T(8,128)(2,1)}, u32[]{:S(2)}, u32[]{:S(2)}) %collective-permute-start.6) | collective-permute-done | bytes 1376288 | tf_op jit(solution)/shard_map/ppermute | solution.py:167
  370.6 5.0 %add_convert_fusion = bf16[512,1344]{0,1:T(8,128)(2,1)} fusion(bf16[512,1344]{0,1:T(8,128)(2,1)} %collective-permute-done.6, bf16[512,1344]{0,1:T(8,128)(2,1)} %collective-permute-done.5, bf16[512,1344]{0,1:T(8,128)(2,1)} %collective-permute-done.4, f32[512,1344]{0,1:T(8,128)S(1)} %convolution_add_fusion.1, bf16[5376,512]{1,0:T(8,128)(2,1)} %param.9, ...), kind=kOutput, calls=%fused_computation.27 | convolution fusion | flops 711524352 | bytes 10158084 | tf_op jit(solution)/shard_map/dot_general | solution.py:26
  375.6 4.2 %reduce-scatter.2.cloned.1.call-done = bf16[2048,672]{0,1:T(8,128)(2,1)} async-done(((bf16[2048,5376]{0,1:T(8,128)(2,1)}), bf16[2048,672]{0,1:T(8,128)(2,1)}) %reduce-scatter.2.cloned.1.call-update) | async-done | bytes 2752528 | tf_op jit(solution)/shard_map/reduce_scatter | solution.py:172
  379.8 2.4 fusion.9
  (47 shorter events, 19.4 us)
Async XLA Ops:
  7.2 103.3 %all-gather.2.cloned.1.call-start = ((), (), s32[]{:S(2)}) async-start(), calls=%async_computation.1 | async-start | bytes 6881280 | tf_op jit(solution)/shard_map/all_gather | solution.py:117
  7.9 371.9 %reduce-scatter.2.cloned.1.call-start = ((), (), s32[]{:S(2)}) async-start(), calls=%async_computation.2 | async-start | bytes 24772608 | tf_op jit(solution)/shard_map/reduce_scatter | solution.py:172
  110.5 7.4 %copy-start.3 = (bf16[512,5376]{0,1:T(8,128)(2,1)S(1)}, bf16[512,5376]{0,1:T(8,128)(2,1)}, u32[]{:S(2)}) copy-start(bf16[512,5376]{0,1:T(8,128)(2,1)} %all-gather.2.cloned.1.call-done) | copy-start | bytes 16515076
  117.9 9.4 %copy-start.2 = (s32[4096]{0:T(1024)S(1)}, s32[4096]{0:T(1024)}, u32[]{:S(2)}) copy-start(s32[4096]{0:T(1024)} %param.11) | copy-start | bytes 49156
  123.6 15.4 %collective-permute-start = (bf16[2,512,512]{2,1,0:T(8,128)(2,1)S(1)}, bf16[2,512,512]{2,1,0:T(8,128)(2,1)S(1)}, u32[]{:S(2)}, u32[]{:S(2)}) collective-permute-start(bf16[2,512,512]{2,1,0:T(8,128)(2,1)S(1)} %pad_maximum_fusion.1), channel_id=1, source_target_pairs={{0,4},{4,8},{8,12},{12,16},{16,20},{20,24},{24,28},{1,5},{5,9},{9,... | collective-permute-start | bytes 3145736 | tf_op jit(solution)/shard_map/ppermute | solution.py:22
  139.0 17.0 %collective-permute-start.1 = (bf16[2,512,512]{2,1,0:T(8,128)(2,1)S(1)}, bf16[2,512,512]{2,1,0:T(8,128)(2,1)S(1)}, u32[]{:S(2)}, u32[]{:S(2)}) collective-permute-start(bf16[2,512,512]{2,1,0:T(8,128)(2,1)S(1)} %collective-permute-done), channel_id=1, source_target_pairs={{0,4},{4,8},{8,12},{12,16},{16,20},{20,24},{24,28},{1,5},{5,9},{9,... | collective-permute-start | bytes 3145736 | tf_op jit(solution)/shard_map/ppermute | solution.py:22
  184.1 19.7 %copy-start = (f32[1536,512]{1,0:T(8,128)S(1)}, f32[1536,512]{1,0:T(8,128)}, u32[]{:S(2)}) copy-start(f32[1536,512]{1,0:T(8,128)} %get-tuple-element.8) | copy-start | bytes 9437188
  184.1 19.7 %copy-start.1 = (f32[1536,512]{1,0:T(8,128)S(1)}, f32[1536,512]{1,0:T(8,128)}, u32[]{:S(2)}) copy-start(f32[1536,512]{1,0:T(8,128)} %get-tuple-element.9) | copy-start | bytes 9437188
  186.0 17.9 %collective-permute-start.2 = (bf16[2,512,512]{2,1,0:T(8,128)(2,1)S(1)}, bf16[2,512,512]{2,1,0:T(8,128)(2,1)S(1)}, u32[]{:S(2)}, u32[]{:S(2)}) collective-permute-start(bf16[2,512,512]{2,1,0:T(8,128)(2,1)S(1)} %fusion.24), channel_id=1, source_target_pairs={{4,0},{8,4},{12,8},{16,12},{20,16},{24,20},{28,24},{5,1},{9,5},{13... | collective-permute-start | bytes 3145736 | tf_op jit(solution)/shard_map/ppermute | solution.py:22
  204.2 17.6 %copy-start.4 = (bf16[512,1024]{1,0:T(8,128)(2,1)S(1)}, bf16[512,1024]{1,0:T(8,128)(2,1)}, u32[]{:S(2)}) copy-start(bf16[512,1024]{1,0:T(8,128)(2,1)} %get-tuple-element.7) | copy-start | bytes 3145732
  204.3 17.1 %collective-permute-start.3 = (bf16[2,512,512]{2,1,0:T(8,128)(2,1)S(1)}, bf16[2,512,512]{2,1,0:T(8,128)(2,1)S(1)}, u32[]{:S(2)}, u32[]{:S(2)}) collective-permute-start(bf16[2,512,512]{2,1,0:T(8,128)(2,1)S(1)} %fusion.20), channel_id=1, source_target_pairs={{4,0},{8,4},{12,8},{16,12},{20,16},{24,20},{28,24},{5,1},{9,5},{13... | collective-permute-start | bytes 3145736 | tf_op jit(solution)/shard_map/ppermute | solution.py:22
  243.0 8.6 %slice-start = ((s8[5505024]{0:T(1024)(128)(4,1)}), s8[4194304]{0:T(1024)(128)(4,1)S(1)}, s32[]{:S(2)}) async-start(s8[5505024]{0:T(1024)(128)(4,1)} %bitcast.37), calls=%async_computation.3 | async-start | bytes 8388608
  243.1 9.5 %slice-start.2 = ((s8[5505024]{0:T(1024)(128)(4,1)}), s8[4194304]{0:T(1024)(128)(4,1)S(1)}, s32[]{:S(2)}) async-start(s8[5505024]{0:T(1024)(128)(4,1)} %bitcast.39), calls=%async_computation.5 | async-start | bytes 8388608
  246.6 5.0 %slice-start.1 = ((s8[5505024]{0:T(1024)(128)(4,1)}), s8[1310720]{0:T(1024)(128)(4,1)S(1)}, s32[]{:S(2)}) async-start(s8[5505024]{0:T(1024)(128)(4,1)} %bitcast.37), calls=%async_computation.4 | async-start | bytes 2621440
  246.7 5.9 %slice-start.3 = ((s8[5505024]{0:T(1024)(128)(4,1)}), s8[1310720]{0:T(1024)(128)(4,1)S(1)}, s32[]{:S(2)}) async-start(s8[5505024]{0:T(1024)(128)(4,1)} %bitcast.39), calls=%async_computation.6 | async-start | bytes 2621440
  253.6 93.0 %collective-permute-start.4 = (bf16[512,1344]{0,1:T(8,128)(2,1)S(1)}, bf16[512,1344]{0,1:T(8,128)(2,1)}, u32[]{:S(2)}, u32[]{:S(2)}) collective-permute-start(bf16[512,1344]{0,1:T(8,128)(2,1)S(1)} %fusion.4), channel_id=1, source_target_pairs={{0,3},{1,0},{2,1},{3,2},{4,7},{5,4},{6,5},{7,6},{8,11},{9,8},{10,9... | collective-permute-start | bytes 4128776 | tf_op jit(solution)/shard_map/ppermute | solution.py:167
  260.3 86.2 %collective-permute-start.5 = (bf16[512,1344]{0,1:T(8,128)(2,1)}, bf16[512,1344]{0,1:T(8,128)(2,1)}, u32[]{:S(2)}, u32[]{:S(2)}) collective-permute-start(bf16[512,1344]{0,1:T(8,128)(2,1)} %fusion.5), channel_id=1, source_target_pairs={{0,2},{1,3},{2,0},{3,1},{4,6},{5,7},{6,4},{7,5},{8,10},{9,11},{10,... | collective-permute-start | bytes 4128776 | tf_op jit(solution)/shard_map/ppermute | solution.py:167
  264.0 106.6 %collective-permute-start.6 = (bf16[512,1344]{0,1:T(8,128)(2,1)}, bf16[512,1344]{0,1:T(8,128)(2,1)}, u32[]{:S(2)}, u32[]{:S(2)}) collective-permute-start(bf16[512,1344]{0,1:T(8,128)(2,1)} %fusion.6), channel_id=1, source_target_pairs={{0,1},{1,2},{2,3},{3,0},{4,5},{5,6},{6,7},{7,4},{8,9},{9,10},{10,1... | collective-permute-start | bytes 4128776 | tf_op jit(solution)/shard_map/ppermute | solution.py:167
Sparse Core Ops, SparseCore 0:
  9.6 100.8 all-gather.1
  239.7 140.0 reduce-scatter.1

commit v17 on v16

--- a/solution.py
+++ b/solution.py
@@ -86,7 +86,7 @@
         & (seg_query[:, None] == seg_key[None, :])
     )
     assert key_rows == WINDOW + tok_rows and tok_rows % 256 == 0
-    mask = allowed.astype(jnp.float32)
+    mask = allowed.astype(jnp.bfloat16)
     q_spec = pl.BlockSpec((tok_rows, groups * HEAD_DIM), lambda h: (0, h))
     kv_out_spec = pl.BlockSpec((key_rows, HEAD_DIM), lambda h: (0, h))
     query_grad, key_grad, value_grad = pl.pallas_call(

time: 394 us -> 393 us (level)
  transfers between devices with their start and end apart: 9 -> 9, of which waited for: 8 -> 8; matrix products, arithmetic and copies ran while one was open for 12% -> 11% of each run, Pallas kernels for 0% -> 0%
where the time goes in v17:
time: 393 us; the launch traced here: 391 us
  waiting for transfers between devices  247 us (63%)
  matrix products  72.8 us (19%)
  Pallas kernels  26.2 us (7%)
  starting transfers between devices  19 us (5%)
  between operations  14.4 us (4%)
  other arithmetic  9.31 us (2%)
    all_gather x1, waiting for transfers between devices, per_device(): gathered = lax.all_gather(tokens, 'head', axis=1, tiled=True)  103 us
    ppermute x3, waiting for transfers between devices, per_device(): got = lax.ppermute(sent, 'head', pairs).astype(jnp.float32)  99.8 us
    ppermute x4, waiting for transfers between devices, passed_along(): return lax.ppermute(x, axis, pairs)  39.7 us
    dot_general x12, matrix products, contract_last(): lax.dot_general(left, right, (((1,), (1,)), ((), ())), preferred_element_...  31 us
    pallas_call x1, Pallas kernels, attend(): pl.pallas_call(attention_kernel, grid=(kv_local,), in_specs=[pl.BlockSpec...  26.2 us
    dot_general x1, matrix products, contract_first(): lax.dot_general(left, right, (((0,), (0,)), ((), ())), preferred_element_...  17.7 us
    ppermute x4, starting transfers between devices, passed_along(): return lax.ppermute(x, axis, pairs)  13.9 us
    dot_general x1, matrix products, per_device(): jnp.dot(gathered, query_weight, preferred_element_type=jnp.float32)  11.2 us
  transfers between devices with their start and end apart: 9, of which 8 were waited for; matrix products, arithmetic and copies ran while one was open for 11% of the time, Pallas kernels for 0%

profile of v17, /device:TPU:11, one launch (start us, length us, event | category | flops | bytes accessed | tf_op | source)
XLA Modules:
  0.0 391.4 jit_solution(2182088060889184470)
XLA Ops:
  7.9 102.5 %all-gather.2.cloned.1.call-done = bf16[512,5376]{0,1:T(8,128)(2,1)} async-done(((bf16[512,1344]{0,1:T(8,128)(2,1)}), bf16[512,5376]{0,1:T(8,128)(2,1)}) %all-gather.2.cloned.1.call-update) | async-done | bytes 5505040 | tf_op jit(solution)/shard_map/all_gather | solution.py:117
  110.5 7.4 %fusion.40 = bf16[1,512,512]{2,1,0:T(8,128)(2,1)S(1)} fusion(bf16[512,5376]{0,1:T(8,128)(2,1)} %all-gather.2.cloned.1.call-done, bf16[5376,512]{1,0:T(8,128)(2,1)} %param.8), kind=kOutput, calls=%fused_computation.60 | convolution fusion | flops 2818834432 | bytes 11534336 | tf_op jit(solution)/shard_map/dot_general | solution.py:121
  117.9 5.6 %fusion.41 = bf16[1,512,512]{2,1,0:T(8,128)(2,1)S(1)} fusion(bf16[512,5376]{0,1:T(8,128)(2,1)S(1)} %copy-done.3, bf16[5376,512]{1,0:T(8,128)(2,1)} %param.9), kind=kOutput, calls=%fused_computation.61 | convolution fusion | flops 2818834432 | bytes 11534336 | tf_op jit(solution)/shard_map/dot_general | solution.py:124
  123.6 3.6 collective-permute-start
  127.4 2.4 fusion.3.mask_ref
  129.8 9.1 %collective-permute-done = bf16[2,512,512]{2,1,0:T(8,128)(2,1)S(1)} collective-permute-done((bf16[2,512,512]{2,1,0:T(8,128)(2,1)S(1)}, bf16[2,512,512]{2,1,0:T(8,128)(2,1)S(1)}, u32[]{:S(2)}, u32[]{:S(2)}) %collective-permute-start) | collective-permute-done | bytes 1048608 | tf_op jit(solution)/shard_map/ppermute | solution.py:22
  139.0 5.5 %collective-permute-start.1 = (bf16[2,512,512]{2,1,0:T(8,128)(2,1)S(1)}, bf16[2,512,512]{2,1,0:T(8,128)(2,1)S(1)}, u32[]{:S(2)}, u32[]{:S(2)}) collective-permute-start(bf16[2,512,512]{2,1,0:T(8,128)(2,1)S(1)} %collective-permute-done), channel_id=1, source_target_pairs={{0,4},{4,8},{8,12},{12,16},{16,20},{20,24},{24,28},{1,5},{5,9},{9,... | collective-permute-start | bytes 3145736 | tf_op jit(solution)/shard_map/ppermute | solution.py:22
  144.4 11.2 %convolution_convert_fusion.1.q_ref = bf16[512,1024]{1,0:T(8,128)(2,1)} fusion(bf16[512,5376]{0,1:T(8,128)(2,1)} %all-gather.2.cloned.1.call-done, bf16[5376,1024]{1,0:T(8,128)(2,1)} %param.7), kind=kOutput, calls=%fused_computation.49 | convolution fusion | flops 5637668864 | bytes 17563648 | tf_op jit(solution)/shard_map/dot_general | solution.py:118
  157.7 26.2 %shard_map.93 = (bf16[512,1024]{1,0:T(8,128)(2,1)}, f32[1536,512]{1,0:T(8,128)}, f32[1536,512]{1,0:T(8,128)}) custom-call(bf16[512,1536]{1,0:T(8,128)(2,1)} %fusion.3.mask_ref, bf16[512,1024]{1,0:T(8,128)(2,1)} %convolution_convert_fusion.1.q_ref, bf16[2,1536,512]{2,1,0:T(8,128)(2,1)} %maximum_maximum_fusion.k_ref.v_ref, ...), custom_call_target="tpu_custom_call" | custom-call | tf_op jit(solution)/shard_map/pallas_call | solution.py:92
  185.8 2.5 collective-permute-start.2
  188.4 15.3 %collective-permute-done.2 = bf16[2,512,512]{2,1,0:T(8,128)(2,1)S(1)} collective-permute-done((bf16[2,512,512]{2,1,0:T(8,128)(2,1)S(1)}, bf16[2,512,512]{2,1,0:T(8,128)(2,1)S(1)}, u32[]{:S(2)}, u32[]{:S(2)}) %collective-permute-start.2) | collective-permute-done | bytes 1048608 | tf_op jit(solution)/shard_map/ppermute | solution.py:22
  206.4 14.9 %collective-permute-done.3 = bf16[2,512,512]{2,1,0:T(8,128)(2,1)S(1)} collective-permute-done((bf16[2,512,512]{2,1,0:T(8,128)(2,1)S(1)}, bf16[2,512,512]{2,1,0:T(8,128)(2,1)S(1)}, u32[]{:S(2)}, u32[]{:S(2)}) %collective-permute-start.3) | collective-permute-done | bytes 1048608 | tf_op jit(solution)/shard_map/ppermute | solution.py:22
  221.7 17.7 %convolution_convert_fusion = bf16[2048,5376]{0,1:T(8,128)(2,1)} fusion(bf16[512,5376]{0,1:T(8,128)(2,1)} %all-gather.2.cloned.1.call-done, bf16[512,512]{1,0:T(8,128)(2,1)S(1)} %get-tuple-element.13, bf16[512,512]{1,0:T(8,128)(2,1)S(1)} %get-tuple-element.12, bf16[512,1024]{1,0:T(8,128)(2,1)S(1)} %copy-done.4), kind=kOutput, calls=%fused_computation | convolution fusion | flops 11291590656 | bytes 29622272 | tf_op jit(solution)/shard_map/dot_general | solution.py:32
  239.5 3.4 fusion.16
  242.9 3.6 fusion.14
  246.5 5.0 %fusion.12 = f32[512,1344]{0,1:T(8,128)S(1)} fusion(bf16[512,1024]{1,0:T(8,128)(2,1)S(1)} %copy-done.4, bf16[5376,1024]{1,0:T(8,128)(2,1)} %param.7, s32[]{:T(128)S(6)} %select_n.48), kind=kOutput, calls=%fused_computation.30 | convolution fusion | flops 1409286144 | bytes 6553604 | tf_op jit(solution)/shard_map/dot_general | solution.py:26
  253.4 3.8 collective-permute-start.4
  264.3 4.0 %fusion.10 = f32[512,1344]{0,1:T(8,128)S(1)} fusion(bf16[512,1024]{1,0:T(8,128)(2,1)S(1)} %copy-done.4, bf16[5376,1024]{1,0:T(8,128)(2,1)} %param.7, s32[]{:T(128)S(6)} %select_n.49), kind=kOutput, calls=%fused_computation.28 | convolution fusion | flops 1409286144 | bytes 6553604 | tf_op jit(solution)/shard_map/dot_general | solution.py:26
  268.3 2.4 convolution_add_fusion.1
  270.7 75.7 %collective-permute-done.4 = bf16[512,1344]{0,1:T(8,128)(2,1)} collective-permute-done((bf16[512,1344]{0,1:T(8,128)(2,1)S(1)}, bf16[512,1344]{0,1:T(8,128)(2,1)}, u32[]{:S(2)}, u32[]{:S(2)}) %collective-permute-start.4) | collective-permute-done | bytes 1376288 | tf_op jit(solution)/shard_map/ppermute | solution.py:167
  346.4 24.1 %collective-permute-done.6 = bf16[512,1344]{0,1:T(8,128)(2,1)} collective-permute-done((bf16[512,1344]{0,1:T(8,128)(2,1)}, bf16[512,1344]{0,1:T(8,128)(2,1)}, u32[]{:S(2)}, u32[]{:S(2)}) %collective-permute-start.6) | collective-permute-done | bytes 1376288 | tf_op jit(solution)/shard_map/ppermute | solution.py:167
  370.5 5.0 %add_convert_fusion = bf16[512,1344]{0,1:T(8,128)(2,1)} fusion(bf16[512,1344]{0,1:T(8,128)(2,1)} %collective-permute-done.6, bf16[512,1344]{0,1:T(8,128)(2,1)} %collective-permute-done.5, bf16[512,1344]{0,1:T(8,128)(2,1)} %collective-permute-done.4, f32[512,1344]{0,1:T(8,128)S(1)} %convolution_add_fusion.1, bf16[5376,512]{1,0:T(8,128)(2,1)} %param.9, ...), kind=kOutput, calls=%fused_computation.27 | convolution fusion | flops 711524352 | bytes 10158084 | tf_op jit(solution)/shard_map/dot_general | solution.py:26
  375.4 4.3 %reduce-scatter.2.cloned.1.call-done = bf16[2048,672]{0,1:T(8,128)(2,1)} async-done(((bf16[2048,5376]{0,1:T(8,128)(2,1)}), bf16[2048,672]{0,1:T(8,128)(2,1)}) %reduce-scatter.2.cloned.1.call-update) | async-done | bytes 2752528 | tf_op jit(solution)/shard_map/reduce_scatter | solution.py:172
  379.7 2.4 fusion.9
  (47 shorter events, 19.4 us)
Async XLA Ops:
  7.2 103.3 %all-gather.2.cloned.1.call-start = ((), (), s32[]{:S(2)}) async-start(), calls=%async_computation.1 | async-start | bytes 6881280 | tf_op jit(solution)/shard_map/all_gather | solution.py:117
  7.9 371.8 %reduce-scatter.2.cloned.1.call-start = ((), (), s32[]{:S(2)}) async-start(), calls=%async_computation.2 | async-start | bytes 24772608 | tf_op jit(solution)/shard_map/reduce_scatter | solution.py:172
  110.5 7.4 %copy-start.3 = (bf16[512,5376]{0,1:T(8,128)(2,1)S(1)}, bf16[512,5376]{0,1:T(8,128)(2,1)}, u32[]{:S(2)}) copy-start(bf16[512,5376]{0,1:T(8,128)(2,1)} %all-gather.2.cloned.1.call-done) | copy-start | bytes 16515076
  117.9 9.4 %copy-start.2 = (s32[4096]{0:T(1024)S(1)}, s32[4096]{0:T(1024)}, u32[]{:S(2)}) copy-start(s32[4096]{0:T(1024)} %param.11) | copy-start | bytes 49156
  123.6 15.4 %collective-permute-start = (bf16[2,512,512]{2,1,0:T(8,128)(2,1)S(1)}, bf16[2,512,512]{2,1,0:T(8,128)(2,1)S(1)}, u32[]{:S(2)}, u32[]{:S(2)}) collective-permute-start(bf16[2,512,512]{2,1,0:T(8,128)(2,1)S(1)} %pad_maximum_fusion.1), channel_id=1, source_target_pairs={{0,4},{4,8},{8,12},{12,16},{16,20},{20,24},{24,28},{1,5},{5,9},{9,... | collective-permute-start | bytes 3145736 | tf_op jit(solution)/shard_map/ppermute | solution.py:22
  139.0 17.0 %collective-permute-start.1 = (bf16[2,512,512]{2,1,0:T(8,128)(2,1)S(1)}, bf16[2,512,512]{2,1,0:T(8,128)(2,1)S(1)}, u32[]{:S(2)}, u32[]{:S(2)}) collective-permute-start(bf16[2,512,512]{2,1,0:T(8,128)(2,1)S(1)} %collective-permute-done), channel_id=1, source_target_pairs={{0,4},{4,8},{8,12},{12,16},{16,20},{20,24},{24,28},{1,5},{5,9},{9,... | collective-permute-start | bytes 3145736 | tf_op jit(solution)/shard_map/ppermute | solution.py:22
  184.0 19.7 %copy-start = (f32[1536,512]{1,0:T(8,128)S(1)}, f32[1536,512]{1,0:T(8,128)}, u32[]{:S(2)}) copy-start(f32[1536,512]{1,0:T(8,128)} %get-tuple-element.8) | copy-start | bytes 9437188
  184.0 19.7 %copy-start.1 = (f32[1536,512]{1,0:T(8,128)S(1)}, f32[1536,512]{1,0:T(8,128)}, u32[]{:S(2)}) copy-start(f32[1536,512]{1,0:T(8,128)} %get-tuple-element.9) | copy-start | bytes 9437188
  185.8 17.9 %collective-permute-start.2 = (bf16[2,512,512]{2,1,0:T(8,128)(2,1)S(1)}, bf16[2,512,512]{2,1,0:T(8,128)(2,1)S(1)}, u32[]{:S(2)}, u32[]{:S(2)}) collective-permute-start(bf16[2,512,512]{2,1,0:T(8,128)(2,1)S(1)} %fusion.24), channel_id=1, source_target_pairs={{4,0},{8,4},{12,8},{16,12},{20,16},{24,20},{28,24},{5,1},{9,5},{13... | collective-permute-start | bytes 3145736 | tf_op jit(solution)/shard_map/ppermute | solution.py:22
  204.1 17.6 %copy-start.4 = (bf16[512,1024]{1,0:T(8,128)(2,1)S(1)}, bf16[512,1024]{1,0:T(8,128)(2,1)}, u32[]{:S(2)}) copy-start(bf16[512,1024]{1,0:T(8,128)(2,1)} %get-tuple-element.7) | copy-start | bytes 3145732
  204.1 17.1 %collective-permute-start.3 = (bf16[2,512,512]{2,1,0:T(8,128)(2,1)S(1)}, bf16[2,512,512]{2,1,0:T(8,128)(2,1)S(1)}, u32[]{:S(2)}, u32[]{:S(2)}) collective-permute-start(bf16[2,512,512]{2,1,0:T(8,128)(2,1)S(1)} %fusion.20), channel_id=1, source_target_pairs={{4,0},{8,4},{12,8},{16,12},{20,16},{24,20},{28,24},{5,1},{9,5},{13... | collective-permute-start | bytes 3145736 | tf_op jit(solution)/shard_map/ppermute | solution.py:22
  242.9 8.6 %slice-start = ((s8[5505024]{0:T(1024)(128)(4,1)}), s8[4194304]{0:T(1024)(128)(4,1)S(1)}, s32[]{:S(2)}) async-start(s8[5505024]{0:T(1024)(128)(4,1)} %bitcast.37), calls=%async_computation.3 | async-start | bytes 8388608
  242.9 9.5 %slice-start.2 = ((s8[5505024]{0:T(1024)(128)(4,1)}), s8[4194304]{0:T(1024)(128)(4,1)S(1)}, s32[]{:S(2)}) async-start(s8[5505024]{0:T(1024)(128)(4,1)} %bitcast.39), calls=%async_computation.5 | async-start | bytes 8388608
  246.5 5.0 %slice-start.1 = ((s8[5505024]{0:T(1024)(128)(4,1)}), s8[1310720]{0:T(1024)(128)(4,1)S(1)}, s32[]{:S(2)}) async-start(s8[5505024]{0:T(1024)(128)(4,1)} %bitcast.37), calls=%async_computation.4 | async-start | bytes 2621440
  246.5 5.9 %slice-start.3 = ((s8[5505024]{0:T(1024)(128)(4,1)}), s8[1310720]{0:T(1024)(128)(4,1)S(1)}, s32[]{:S(2)}) async-start(s8[5505024]{0:T(1024)(128)(4,1)} %bitcast.39), calls=%async_computation.6 | async-start | bytes 2621440
  253.4 93.0 %collective-permute-start.4 = (bf16[512,1344]{0,1:T(8,128)(2,1)S(1)}, bf16[512,1344]{0,1:T(8,128)(2,1)}, u32[]{:S(2)}, u32[]{:S(2)}) collective-permute-start(bf16[512,1344]{0,1:T(8,128)(2,1)S(1)} %fusion.4), channel_id=1, source_target_pairs={{0,3},{1,0},{2,1},{3,2},{4,7},{5,4},{6,5},{7,6},{8,11},{9,8},{10,9... | collective-permute-start | bytes 4128776 | tf_op jit(solution)/shard_map/ppermute | solution.py:167
  260.2 86.2 %collective-permute-start.5 = (bf16[512,1344]{0,1:T(8,128)(2,1)}, bf16[512,1344]{0,1:T(8,128)(2,1)}, u32[]{:S(2)}, u32[]{:S(2)}) collective-permute-start(bf16[512,1344]{0,1:T(8,128)(2,1)} %fusion.5), channel_id=1, source_target_pairs={{0,2},{1,3},{2,0},{3,1},{4,6},{5,7},{6,4},{7,5},{8,10},{9,11},{10,... | collective-permute-start | bytes 4128776 | tf_op jit(solution)/shard_map/ppermute | solution.py:167
  263.8 106.6 %collective-permute-start.6 = (bf16[512,1344]{0,1:T(8,128)(2,1)}, bf16[512,1344]{0,1:T(8,128)(2,1)}, u32[]{:S(2)}, u32[]{:S(2)}) collective-permute-start(bf16[512,1344]{0,1:T(8,128)(2,1)} %fusion.6), channel_id=1, source_target_pairs={{0,1},{1,2},{2,3},{3,0},{4,5},{5,6},{6,7},{7,4},{8,9},{9,10},{10,1... | collective-permute-start | bytes 4128776 | tf_op jit(solution)/shard_map/ppermute | solution.py:167
Sparse Core Ops, SparseCore 0:
  9.6 100.8 all-gather.1
  239.6 140.0 reduce-scatter.1
